TPU v7x, 32 devices: a whole 2x2x4 slice. The times are simulated.
32 devices in a mesh: groups: 2 (over x), freq: 16 (over z, y, core).
Axes of the slice: x: 2, y: 2, z: 4, core: 2. Of those that a mesh axis runs over, the one named last changes fastest.
Arguments:
- encoder_input: bfloat16 [64, 2048], P(('groups', 'freq')), parts along dimension 0, may hold values from -6 to 6
- desired_responses: bfloat16 [64, 384, 512], P('groups', 'freq'), parts along dimension 0, may hold values from -6 to 6
- sample_index: int32 [64], P('groups'), parts along dimension 0, may hold values from 0 to 31, each once
- encoder_weight: bfloat16 [2048, 512], replicated, may hold values from -0.125 to 0.125
- decoder_weight: bfloat16 [512, 512], replicated, may hold values from -0.25 to 0.25
- frequency_amplitude: bfloat16 [384, 512], P('freq'), may hold values from -4 to 4
- spectral_filter_weight: float32 [2, 256], replicated, may hold values from -4 to 4
- output_weight: bfloat16 [512, 512], replicated, may hold values from -0.25 to 0.25
Outputs:
- grad_enc: float32 [4096, 512], P('groups'), parts along dimension 0
- grad_dec: float32 [1024, 512], P('groups'), parts along dimension 0
- grad_out: float32 [1024, 512], P('groups'), parts along dimension 0
- grad_filter: float32 [4, 256], P('groups'), parts along dimension 0
There are 2 independent parts, one for each index of `groups`. A program takes and returns all parts, laid end to end along the dimension named above; an argument that names none is the same for every part. Nothing has to cross between parts.
Inputs may be any that keep to these rules, and one draw needn't show every extreme that they name: sample_index names each of the 32 samples once.
All inputs are finite; a program needn't handle non-finite values.
Results may differ from a plain program's by a relative error of at most 0.0065.
Values may be sent and summed in bfloat16 or wider, within the bound.
No kernel may reach another device: no remote copies, remote signals or barrier semaphores. Data moves between devices by JAX's collectives and lax.ppermute only.
A program may use at most 128 MiB of HBM per device.

v0:
```python
import math

import jax
import jax.numpy as jnp
from jax import lax
from jax.sharding import PartitionSpec as P


def rotation_tables(antennas):
    indices = jnp.arange(antennas, dtype=jnp.int32)
    products_mod = indices[:, None] * indices[None, :] % antennas
    angle_table = products_mod.astype(jnp.float32) * (2.0 * math.pi / antennas)
    cosine_table = jnp.cos(angle_table) / math.sqrt(antennas)
    sine_table = jnp.sin(angle_table) / math.sqrt(antennas)
    forward_transform = jnp.concatenate(
        [
            jnp.concatenate([cosine_table, -sine_table], 1),
            jnp.concatenate([sine_table, cosine_table], 1),
        ],
        0,
    )
    inverse_transform = jnp.concatenate(
        [
            jnp.concatenate([cosine_table, sine_table], 1),
            jnp.concatenate([-sine_table, cosine_table], 1),
        ],
        0,
    )
    return (forward_transform.astype(jnp.bfloat16), inverse_transform.astype(jnp.bfloat16))


def decode_rows(
    mixed_in,
    wanted_lines,
    output_weight,
    spectral_filter_weight,
    forward_transform,
    inverse_transform,
    loss_scale,
):
    filter_re = spectral_filter_weight[0]
    filter_im = spectral_filter_weight[1]
    spectrum = jnp.dot(mixed_in, forward_transform, preferred_element_type=jnp.float32)
    half_width = spectrum.shape[1] // 2
    spec_re = spectrum[:, :half_width]
    spec_im = spectrum[:, half_width:]
    filtered = jnp.concatenate(
        [spec_re * filter_re - spec_im * filter_im, spec_re * filter_im + spec_im * filter_re], 1
    ).astype(jnp.bfloat16)
    mixed_back = jnp.dot(filtered, inverse_transform, preferred_element_type=jnp.float32)
    hidden = (mixed_in.astype(jnp.float32) + jax.nn.gelu(mixed_back)).astype(jnp.bfloat16)
    rebuilt = hidden.astype(jnp.float32) + jnp.dot(
        hidden, output_weight, preferred_element_type=jnp.float32
    )
    residual = loss_scale * (rebuilt - wanted_lines.astype(jnp.float32))
    residual_half = residual.astype(jnp.bfloat16)
    grad_out = lax.dot_general(
        hidden, residual_half, (((0,), (0,)), ((), ())), preferred_element_type=jnp.float32
    )
    grad_hidden = residual + lax.dot_general(
        residual_half, output_weight, (((1,), (1,)), ((), ())), preferred_element_type=jnp.float32
    )
    grad_mixed = jax.vjp(jax.nn.gelu, mixed_back)[1](grad_hidden)[0].astype(jnp.bfloat16)
    grad_filtered = lax.dot_general(
        grad_mixed, inverse_transform, (((1,), (1,)), ((), ())), preferred_element_type=jnp.float32
    )
    grad_re = grad_filtered[:, :half_width]
    grad_im = grad_filtered[:, half_width:]
    grad_filter = jnp.stack(
        [
            jnp.sum(grad_re * spec_re + grad_im * spec_im, 0),
            jnp.sum(grad_im * spec_re - grad_re * spec_im, 0),
        ]
    )
    grad_spec = jnp.concatenate(
        [grad_re * filter_re + grad_im * filter_im, grad_im * filter_re - grad_re * filter_im], 1
    ).astype(jnp.bfloat16)
    derivative_entering = grad_hidden + lax.dot_general(
        grad_spec, forward_transform, (((1,), (1,)), ((), ())), preferred_element_type=jnp.float32
    )
    return (derivative_entering, grad_out, grad_filter)


def encoder_grads(inputs_rows, codewords, latent_sums, decoder_weight):
    latent_half = latent_sums.astype(jnp.bfloat16)
    grad_dec = lax.dot_general(
        codewords, latent_half, (((0,), (0,)), ((), ())), preferred_element_type=jnp.float32
    )
    grad_codes = lax.dot_general(
        latent_half, decoder_weight, (((1,), (1,)), ((), ())), preferred_element_type=jnp.float32
    )
    grad_pre = (grad_codes * (1.0 - jnp.square(codewords.astype(jnp.float32)))).astype(jnp.bfloat16)
    grad_enc = lax.dot_general(
        inputs_rows, grad_pre, (((0,), (0,)), ((), ())), preferred_element_type=jnp.float32
    )
    return (grad_enc, grad_dec)


def local(
    encoder_input,
    desired_responses,
    sample_index,
    encoder_weight,
    decoder_weight,
    frequency_amplitude,
    spectral_filter_weight,
    output_weight,
):
    samples = sample_index.shape[0]
    sub_dev = desired_responses.shape[1]
    width = desired_responses.shape[2]
    forward_transform, inverse_transform = rotation_tables(width // 2)
    loss_scale = 1.0 / math.sqrt(samples * sub_dev * lax.axis_size("freq"))
    codes_own = jnp.tanh(
        jnp.dot(encoder_input, encoder_weight, preferred_element_type=jnp.float32)
    ).astype(jnp.bfloat16)
    all_codes = lax.all_gather(codes_own, "freq", axis=0, tiled=True)
    inverse_ids = (
        jnp.zeros((samples,), jnp.int32).at[sample_index].set(jnp.arange(samples, dtype=jnp.int32))
    )
    latent = jnp.dot(all_codes[inverse_ids], decoder_weight, preferred_element_type=jnp.float32)
    gain_row_values = frequency_amplitude.astype(jnp.float32)
    mixed_in = (latent[:, None, :] * gain_row_values[None]).astype(jnp.bfloat16).reshape(-1, width)
    wanted_lines = desired_responses.reshape(-1, width)
    derivative_entering, grad_out, grad_filter = decode_rows(
        mixed_in,
        wanted_lines,
        output_weight,
        spectral_filter_weight,
        forward_transform,
        inverse_transform,
        loss_scale,
    )
    derivative_bottleneck = jnp.einsum(
        "orm,rm->om", derivative_entering.reshape(samples, sub_dev, width), gain_row_values
    )
    enc_order = derivative_bottleneck[sample_index]
    owned_rows = lax.psum_scatter(enc_order, "freq", scatter_dimension=0, tiled=True)
    grad_enc, grad_dec = encoder_grads(encoder_input, codes_own, owned_rows, decoder_weight)
    grad_enc, grad_dec, grad_out, grad_filter = lax.psum(
        (grad_enc, grad_dec, grad_out, grad_filter), "freq"
    )
    return (grad_enc, grad_dec, grad_out, grad_filter)


def solution(mesh):
    return jax.shard_map(
        local,
        mesh=mesh,
        in_specs=(
            P(("groups", "freq"), None),
            P("groups", "freq", None),
            P("groups"),
            P(),
            P(),
            P("freq", None),
            P(),
            P(),
        ),
        out_specs=(P("groups", None), P("groups", None), P("groups", None), P("groups", None)),
        check_vma=False,
    )
```

profile of v0, /device:TPU:0, one launch (start us, length us, event | category | flops | bytes accessed | tf_op | source)
XLA Modules:
  0.0 264.4 jit_solution(11074158935546057527)
XLA Ops:
  7.3 1.0 fusion.30
  8.3 1.1 negate_convert_fusion
  9.4 0.7 compare_select_fusion.1
  10.1 0.7 scatter_custom_fusion
  10.8 0.8 fusion.54
  11.6 1.1 fusion.8
  12.7 23.2 %all-gather = bf16[16,2,512]{2,1,0:T(2,128)(2,1)S(1)} all-gather(bf16[1,2,512]{2,1,0:T(2,128)(2,1)S(1)} %bitcast.34), channel_id=1, replica_groups=mesh['groups'=2,'freq'=16] {'freq'}, dimensions={0}, use_global_device_ids=true | all-gather | bytes 34816 | tf_op jit(solution)/shard_map/all_gather | solution.py:117
  35.9 0.6 gather_fusion
  36.9 0.6 fusion.34
  37.7 1.0 add_convert_fusion
  39.0 0.6 fusion.7
  39.6 1.6 fusion.21
  41.2 0.6 convolution_add_fusion.1
  41.8 1.2 fusion.17
  43.7 0.6 dynamic-slice
  45.0 2.3 convolution_add_fusion
  47.6 0.6 gather_fusion.1
  48.2 59.2 %all-reduce.1 = (bf16[32,512]{1,0:T(8,128)(2,1)S(1)}, f32[2,256]{1,0:T(2,128)}) all-reduce(f32[32,512]{1,0:T(8,128)S(1)} %gather_fusion.1, f32[2,256]{1,0:T(2,128)S(1)} %pad_maximum_fusion.4), channel_id=2, replica_groups=mesh['groups'=2,'freq'=16] {'freq'}, use_global_device_ids=true, to_apply=%region_1.2.clone | all-reduce | flops 16896 | bytes 102400
  107.4 1.3 fusion.53
  108.7 3.0 %convolution_bitcast_fusion = f32[2048,512]{0,1:T(8,128)} fusion(bf16[2,2048]{1,0:T(2,128)(2,1)S(1)} %copy-done.8, bf16[512,512]{1,0:T(8,128)(2,1)S(1)} %copy-done.1, bf16[2,512]{1,0:T(2,128)(2,1)S(1)} %fusion.8, bf16[32,512]{1,0:T(8,128)(2,1)S(1)} %get-tuple-element.14, u32[]{:T(128)S(6)} %multiply.6), kind=kOutput, calls=%fused_computation.3 | convolution fusion | flops 5248000 | bytes 4730884 | tf_op jit(solution)/shard_map/dot_general | solution.py:93
  111.8 137.2 %all-reduce.5.cloned.1.call-done = (f32[2048,512]{0,1:T(8,128)}, f32[512,512]{1,0:T(8,128)}, f32[512,512]{1,0:T(8,128)}) async-done(((f32[2048,512]{0,1:T(8,128)}, f32[512,512]{1,0:T(8,128)}, f32[512,512]{1,0:T(8,128)}), (f32[2048,512]{0,1:T(8,128)}, f32[512,512]{1,0:T(8,128)}, f32[512,512]{1,0:T(8,128)})) %all-reduce.5.cloned.1.call-update) | async-done | bytes 6291472 | tf_op jit(solution)/shard_map/psum | solution.py:140
  248.9 5.3 %copy.13 = f32[2048,512]{1,0:T(8,128)} copy(f32[2048,512]{0,1:T(8,128)} %get-tuple-element.16) | data formatting | bytes 8388608
  254.3 2.4 copy.25
  256.6 1.0 copy.26
  (38 shorter events, 2.0 us)
Async XLA Ops:
  7.2 4.4 %copy-start = (bf16[2048,512]{1,0:T(8,128)(2,1)S(1)}, bf16[2048,512]{1,0:T(8,128)(2,1)}, u32[]{:S(2)}) copy-start(bf16[2048,512]{1,0:T(8,128)(2,1)} %param.11) | copy-start | bytes 6291460
  7.2 28.7 %copy-start.9 = (bf16[24,512]{1,0:T(8,128)(2,1)S(1)}, bf16[24,512]{1,0:T(8,128)(2,1)}, u32[]{:S(2)}) copy-start(bf16[24,512]{1,0:T(8,128)(2,1)} %param.13) | copy-start | bytes 73732
  7.2 29.3 %copy-start.1 = (bf16[512,512]{1,0:T(8,128)(2,1)S(1)}, bf16[512,512]{1,0:T(8,128)(2,1)}, u32[]{:S(2)}) copy-start(bf16[512,512]{1,0:T(8,128)(2,1)} %param.12) | copy-start | bytes 1572868
  7.2 241.7 %all-reduce.5.cloned.1.call-start = ((), (), s32[]{:S(2)}) async-start(), calls=%async_computation | async-start | bytes 12582912 | tf_op jit(solution)/shard_map/psum | solution.py:140
  8.3 33.6 %copy-start.5 = (bf16[256,256]{1,0:T(8,128)(2,1)}, bf16[256,256]{1,0:T(8,128)(2,1)S(1)}, u32[]{:S(2)}) copy-start(bf16[256,256]{1,0:T(8,128)(2,1)S(1)} %fusion.30) | copy-start | bytes 393220
  9.4 32.4 %copy-start.6 = (bf16[256,256]{1,0:T(8,128)(2,1)}, bf16[256,256]{1,0:T(8,128)(2,1)S(1)}, u32[]{:S(2)}) copy-start(bf16[256,256]{1,0:T(8,128)(2,1)S(1)} %get-tuple-element.31) | copy-start | bytes 393220
  9.4 32.4 %copy-start.7 = (bf16[256,256]{1,0:T(8,128)(2,1)}, bf16[256,256]{1,0:T(8,128)(2,1)S(1)}, u32[]{:S(2)}) copy-start(bf16[256,256]{1,0:T(8,128)(2,1)S(1)} %get-tuple-element.32) | copy-start | bytes 393220
  37.7 1.0 copy-start.4
  37.7 1.3 copy-start.10
  41.8 1.3 copy-start.2
  43.1 0.7 copy-start.11
  47.2 61.5 %copy-start.8 = (bf16[2,2048]{1,0:T(2,128)(2,1)S(1)}, bf16[2,2048]{1,0:T(2,128)(2,1)}, u32[]{:S(2)}) copy-start(bf16[2,2048]{1,0:T(2,128)(2,1)} %param.8) | copy-start | bytes 24580
  254.3 2.4 copy-start.3
Sparse Core Ops, SparseCore 0:
  111.9 136.9 all-reduce.4
where the time goes:
time: 265 us; the launch traced here: 264 us
  waiting for transfers between devices  137 us (52%)
  blocking collectives  82.4 us (31%)
  between operations  14.9 us (6%)
  matrix products  13.4 us (5%)
  local copies, waits for them, and re-layouts  12.5 us (5%)
  other arithmetic  3.97 us (1%)
    psum x1, waiting for transfers between devices, local(): lax.psum((grad_enc, grad_dec, grad_out, grad_filter), 'freq')  137 us
    unnamed x1, blocking collectives  59.2 us
    all_gather x1, blocking collectives, local(): all_codes = lax.all_gather(codes_own, 'freq', axis=0, tiled=True)  23.2 us
    unnamed x29, local copies, waits for them, and re-layouts  9.8 us
  transfers between devices with their start and end apart: 1, of which 1 were waited for; matrix products, arithmetic and copies ran while one was open for 0% of the time, Pallas kernels for 0%

commit v1 on v0

--- a/solution.py
+++ b/solution.py
@@ -111,14 +111,14 @@
     width = desired_responses.shape[2]
     forward_transform, inverse_transform = rotation_tables(width // 2)
     loss_scale = 1.0 / math.sqrt(samples * sub_dev * lax.axis_size("freq"))
-    codes_own = jnp.tanh(
-        jnp.dot(encoder_input, encoder_weight, preferred_element_type=jnp.float32)
+    all_inputs = lax.all_gather(encoder_input, "freq", axis=0, tiled=True)
+    codes = jnp.tanh(
+        jnp.dot(all_inputs, encoder_weight, preferred_element_type=jnp.float32)
     ).astype(jnp.bfloat16)
-    all_codes = lax.all_gather(codes_own, "freq", axis=0, tiled=True)
     inverse_ids = (
         jnp.zeros((samples,), jnp.int32).at[sample_index].set(jnp.arange(samples, dtype=jnp.int32))
     )
-    latent = jnp.dot(all_codes[inverse_ids], decoder_weight, preferred_element_type=jnp.float32)
+    latent = jnp.dot(codes[inverse_ids], decoder_weight, preferred_element_type=jnp.float32)
     gain_row_values = frequency_amplitude.astype(jnp.float32)
     mixed_in = (latent[:, None, :] * gain_row_values[None]).astype(jnp.bfloat16).reshape(-1, width)
     wanted_lines = desired_responses.reshape(-1, width)
@@ -134,11 +134,11 @@
     derivative_bottleneck = jnp.einsum(
         "orm,rm->om", derivative_entering.reshape(samples, sub_dev, width), gain_row_values
     )
-    enc_order = derivative_bottleneck[sample_index]
-    owned_rows = lax.psum_scatter(enc_order, "freq", scatter_dimension=0, tiled=True)
-    grad_enc, grad_dec = encoder_grads(encoder_input, codes_own, owned_rows, decoder_weight)
-    grad_enc, grad_dec, grad_out, grad_filter = lax.psum(
-        (grad_enc, grad_dec, grad_out, grad_filter), "freq"
+    derivative_bottleneck, grad_out, grad_filter = lax.psum(
+        (derivative_bottleneck, grad_out, grad_filter), "freq"
+    )
+    grad_enc, grad_dec = encoder_grads(
+        all_inputs, codes, derivative_bottleneck[sample_index], decoder_weight
     )
     return (grad_enc, grad_dec, grad_out, grad_filter)
 

time: 265 us -> 146 us (0.55)
  waiting for transfers between devices: 137 us -> 15.5 us
    psum x1, waiting for transfers between devices: 137 us -> 15.5 us  [local(): lax.psum((derivative_bottleneck, grad_out, grad_filter), 'freq')]
    psum x0 -> x1, blocking collectives: none -> 59.7 us  [local(): lax.psum((derivative_bottleneck, grad_out, grad_filter), 'freq')]
    unnamed x1 -> x0, blocking collectives: 59.2 us -> none
    unnamed x29 -> x31, local copies, waits for them, and re-layouts: 9.8 us -> 10.2 us
  transfers between devices with their start and end apart: 1 -> 1, of which waited for: 1 -> 1; matrix products, arithmetic and copies ran while one was open for 0% -> 11% of each run, Pallas kernels for 0% -> 0%
where the time goes in v1:
time: 146 us; the launch traced here: 145 us
  blocking collectives  83.4 us (57%)
  waiting for transfers between devices  15.5 us (11%)
  between operations  14.3 us (10%)
  matrix products  14.2 us (10%)
  local copies, waits for them, and re-layouts  12.9 us (9%)
  other arithmetic  4.82 us (3%)
    psum x1, blocking collectives, local(): lax.psum((derivative_bottleneck, grad_out, grad_filter), 'freq')  59.7 us
    all_gather x1, blocking collectives, local(): all_inputs = lax.all_gather(encoder_input, 'freq', axis=0, tiled=True)  23.7 us
    psum x1, waiting for transfers between devices, local(): lax.psum((derivative_bottleneck, grad_out, grad_filter), 'freq')  15.5 us
    unnamed x31, local copies, waits for them, and re-layouts  10.2 us
    dot_general x1, matrix products, encoder_grads(): lax.dot_general(inputs_rows, grad_pre, (((0,), (0,)), ((), ())), preferre...  2.94 us
  transfers between devices with their start and end apart: 1, of which 1 were waited for; matrix products, arithmetic and copies ran while one was open for 11% of the time, Pallas kernels for 0%

profile of v1, /device:TPU:0, one launch (start us, length us, event | category | flops | bytes accessed | tf_op | source)
XLA Modules:
  0.0 145.1 jit_solution(4982865574990150116)
XLA Ops:
  7.2 1.0 fusion.30
  8.2 1.1 negate_convert_fusion
  9.4 0.8 compare_select_fusion.1
  10.1 0.7 scatter_custom_fusion
  10.8 0.8 fusion.57
  11.6 0.8 bitcast_convert_fusion
  12.4 23.7 %all-gather = bf16[16,2,2048]{2,1,0:T(2,128)(2,1)S(1)} all-gather(bf16[1,2,2048]{2,1,0:T(2,128)(2,1)} %bitcast.39), channel_id=1, replica_groups=mesh['groups'=2,'freq'=16] {'freq'}, dimensions={0}, use_global_device_ids=true | all-gather | bytes 139264 | tf_op jit(solution)/shard_map/all_gather | solution.py:114
  36.6 0.6 gather_fusion
  37.7 0.6 fusion.34
  38.3 1.1 copy-done.2
  39.6 2.0 %add_convert_fusion = (bf16[768,512]{1,0:T(8,128)(2,1)S(1)}, f32[768,512]{1,0:T(8,128)}) fusion(bf16[32,24,512]{2,1,0:T(8,128)(2,1)S(1)} %multiply_convert_fusion, bf16[256,256]{1,0:T(8,128)(2,1)S(1)} %copy-done.10, bf16[256,256]{1,0:T(8,128)(2,1)S(1)} %copy-done.7, bf16[256,256]{1,0:T(8,128)(2,1)S(1)} %fusion.30, ...), kind=kOutput, calls=%fused_computation.16 | convolution fusion | flops 410648576 | bytes 4325376 | tf_op jit(solution)/shard_map/dot_general | solution.py:50
  41.7 0.6 fusion.7
  42.3 1.1 copy-done.1
  43.5 1.6 %fusion.21 = f32[512,512]{1,0:T(8,128)} fusion(bf16[768,512]{1,0:T(8,128)(2,1)S(1)} %get-tuple-element.26, f32[768,512]{1,0:T(8,128)S(1)} %fusion.7), kind=kOutput, calls=%fused_computation.44 | convolution fusion | flops 403046400 | bytes 3407872 | tf_op jit(solution)/shard_map/dot_general | solution.py:57
  45.2 2.6 %convolution_add_fusion.1 = f32[768,512]{1,0:T(8,128)S(1)} fusion(f32[768,512]{1,0:T(8,128)} %copy-done.1, bf16[512,512]{1,0:T(8,128)(2,1)S(1)} %copy-done.5), kind=kOutput, calls=%fused_computation.19 | convolution fusion | flops 403439616 | bytes 3670016 | tf_op jit(solution)/shard_map/dot_general | solution.py:60
  47.8 1.2 fusion.17
  49.7 0.6 convolution_add_fusion
  50.6 59.7 %all-reduce = (bf16[32,512]{1,0:T(8,128)(2,1)S(1)}, f32[2,256]{1,0:T(2,128)}) all-reduce(f32[32,512]{1,0:T(8,128)S(1)} %bitcast.34, f32[2,256]{1,0:T(2,128)S(1)} %pad_maximum_fusion.4), channel_id=1, replica_groups=mesh['groups'=2,'freq'=16] {'freq'}, use_global_device_ids=true, to_apply=%region_1.2 | all-reduce | flops 16896 | bytes 102400 | tf_op jit(solution)/shard_map/psum | solution.py:137
  110.3 0.6 gather_fusion.1
  110.9 2.9 %convolution_bitcast_fusion = f32[2048,512]{0,1:T(8,128)} fusion(bf16[32,2048]{1,0:T(8,128)(2,1)S(1)} %reshape.51, bf16[512,512]{1,0:T(8,128)(2,1)S(1)} %copy-done.4, bf16[32,512]{1,0:T(8,128)(2,1)S(1)} %fusion.8, bf16[32,512]{1,0:T(8,128)(2,1)S(1)} %gather_fusion.1), kind=kOutput, calls=%fused_computation.3 | convolution fusion | flops 83968000 | bytes 4915200 | tf_op jit(solution)/shard_map/dot_general | solution.py:93
  113.9 5.3 %copy.13 = f32[2048,512]{1,0:T(8,128)} copy(f32[2048,512]{0,1:T(8,128)} %convolution_bitcast_fusion) | data formatting | bytes 8388608
  119.2 1.3 fusion.59
  120.5 15.5 %all-reduce.3.cloned.1.call-done = f32[512,512]{1,0:T(8,128)} async-done(((f32[512,512]{1,0:T(8,128)}), f32[512,512]{1,0:T(8,128)}) %all-reduce.3.cloned.1.call-update) | async-done | bytes 1048592 | tf_op jit(solution)/shard_map/psum | solution.py:137
  136.0 2.3 %copy.23 = f32[512,512]{1,0:T(8,128)} copy(f32[512,512]{1,0:T(8,128)} %all-reduce.3.cloned.1.call-done) | data formatting | bytes 2097152
  (40 shorter events, 2.2 us)
Async XLA Ops:
  7.2 29.0 %copy-start = (bf16[2048,512]{1,0:T(8,128)(2,1)S(1)}, bf16[2048,512]{1,0:T(8,128)(2,1)}, u32[]{:S(2)}) copy-start(bf16[2048,512]{1,0:T(8,128)(2,1)} %param.11) | copy-start | bytes 6291460
  7.2 128.8 %all-reduce.3.cloned.1.call-start = ((), (), s32[]{:S(2)}) async-start(), calls=%async_computation | async-start | bytes 2097152 | tf_op jit(solution)/shard_map/psum | solution.py:137
  9.3 28.3 %copy-start.6 = (bf16[256,256]{1,0:T(8,128)(2,1)}, bf16[256,256]{1,0:T(8,128)(2,1)S(1)}, u32[]{:S(2)}) copy-start(bf16[256,256]{1,0:T(8,128)(2,1)S(1)} %get-tuple-element.28) | copy-start | bytes 393220
  9.3 28.3 %copy-start.9 = (bf16[256,256]{1,0:T(8,128)(2,1)}, bf16[256,256]{1,0:T(8,128)(2,1)S(1)}, u32[]{:S(2)}) copy-start(bf16[256,256]{1,0:T(8,128)(2,1)S(1)} %get-tuple-element.29) | copy-start | bytes 393220
  9.4 27.9 %copy-start.4 = (bf16[512,512]{1,0:T(8,128)(2,1)S(1)}, bf16[512,512]{1,0:T(8,128)(2,1)}, u32[]{:S(2)}) copy-start(bf16[512,512]{1,0:T(8,128)(2,1)} %param.12) | copy-start | bytes 1572868
  38.2 1.1 copy-start.2
  38.2 1.4 copy-start.7
  38.3 1.4 copy-start.10
  39.6 2.1 %copy-start.5 = (bf16[512,512]{1,0:T(8,128)(2,1)S(1)}, bf16[512,512]{1,0:T(8,128)(2,1)}, u32[]{:S(2)}) copy-start(bf16[512,512]{1,0:T(8,128)(2,1)} %param.15) | copy-start | bytes 1572868
  39.6 2.1 %copy-start.12 = (bf16[32,24,512]{2,1,0:T(8,128)(2,1)S(1)}, bf16[32,24,512]{2,1,0:T(8,128)(2,1)}, u32[]{:S(2)}) copy-start(bf16[32,24,512]{2,1,0:T(8,128)(2,1)} %param.9) | copy-start | bytes 2359300
  42.3 1.2 copy-start.1
  45.1 2.7 %copy-start.8 = (bf16[256,256]{1,0:T(8,128)(2,1)S(1)}, bf16[256,256]{1,0:T(8,128)(2,1)}, u32[]{:S(2)}) copy-start(bf16[256,256]{1,0:T(8,128)(2,1)} %copy-done.6) | copy-start | bytes 393220
  45.1 2.7 %copy-start.11 = (bf16[256,256]{1,0:T(8,128)(2,1)S(1)}, bf16[256,256]{1,0:T(8,128)(2,1)}, u32[]{:S(2)}) copy-start(bf16[256,256]{1,0:T(8,128)(2,1)} %copy-done.9) | copy-start | bytes 393220
  45.2 2.7 %copy-start.13 = (f32[768,512]{1,0:T(8,128)S(1)}, f32[768,512]{1,0:T(8,128)}, u32[]{:S(2)}) copy-start(f32[768,512]{1,0:T(8,128)} %get-tuple-element.27) | copy-start | bytes 4718596
  47.8 1.4 copy-start.3
Sparse Core Ops, SparseCore 0:
  45.2 90.7 all-reduce.2

commit v2 on v1

--- a/solution.py
+++ b/solution.py
@@ -96,6 +96,65 @@
     return (grad_enc, grad_dec)
 
 
+def _exchange_pairs(count, distance):
+    return [(i, i ^ distance) for i in range(count)]
+
+
+def _is_power_of_two(count):
+    return count > 0 and count & (count - 1) == 0
+
+
+def gather_rows(block, axis_name):
+    count = lax.axis_size(axis_name)
+    if not _is_power_of_two(count):
+        return lax.all_gather(block, axis_name, axis=0, tiled=True)
+    position = lax.axis_index(axis_name)
+    distance = 1
+    while distance < count:
+        other = lax.ppermute(block, axis_name, _exchange_pairs(count, distance))
+        lower = (position // distance) % 2 == 0
+        block = jnp.where(
+            lower, jnp.concatenate([block, other], 0), jnp.concatenate([other, block], 0)
+        )
+        distance *= 2
+    return block
+
+
+def sum_whole(values, axis_name):
+    count = lax.axis_size(axis_name)
+    if not _is_power_of_two(count):
+        return lax.psum(values, axis_name)
+    distance = 1
+    while distance < count:
+        values = values + lax.ppermute(values, axis_name, _exchange_pairs(count, distance))
+        distance *= 2
+    return values
+
+
+def sum_halving(values, axis_name):
+    count = lax.axis_size(axis_name)
+    if not _is_power_of_two(count) or values.shape[0] % count != 0:
+        return lax.psum(values, axis_name)
+    position = lax.axis_index(axis_name)
+    distance = 1
+    while distance < count:
+        half = values.shape[0] // 2
+        lower = (position // distance) % 2 == 0
+        keep = jnp.where(lower, values[:half], values[half:])
+        send = jnp.where(lower, values[half:], values[:half])
+        values = keep + lax.ppermute(send, axis_name, _exchange_pairs(count, distance))
+        distance *= 2
+    distance = count // 2
+    while distance >= 1:
+        other = lax.ppermute(values, axis_name, _exchange_pairs(count, distance))
+        lower = (position // distance) % 2 == 0
+        values = jnp.where(
+            lower, jnp.concatenate([values, other], 0), jnp.concatenate([other, values], 0)
+        )
+        distance //= 2
+    return values
+
+
 def local(
     encoder_input,
     desired_responses,
@@ -111,7 +170,7 @@
     width = desired_responses.shape[2]
     forward_transform, inverse_transform = rotation_tables(width // 2)
     loss_scale = 1.0 / math.sqrt(samples * sub_dev * lax.axis_size("freq"))
-    all_inputs = lax.all_gather(encoder_input, "freq", axis=0, tiled=True)
+    all_inputs = gather_rows(encoder_input, "freq")
     codes = jnp.tanh(
         jnp.dot(all_inputs, encoder_weight, preferred_element_type=jnp.float32)
     ).astype(jnp.bfloat16)
@@ -134,9 +193,12 @@
     derivative_bottleneck = jnp.einsum(
         "orm,rm->om", derivative_entering.reshape(samples, sub_dev, width), gain_row_values
     )
-    derivative_bottleneck, grad_out, grad_filter = lax.psum(
-        (derivative_bottleneck, grad_out, grad_filter), "freq"
-    )
+    grad_out = sum_halving(grad_out, "freq")
+    packed = sum_whole(
+        jnp.concatenate([derivative_bottleneck, grad_filter.reshape(1, -1)], 0), "freq"
+    )
+    derivative_bottleneck = packed[:samples]
+    grad_filter = packed[samples:].reshape(grad_filter.shape)
     grad_enc, grad_dec = encoder_grads(
         all_inputs, codes, derivative_bottleneck[sample_index], decoder_weight
     )

time: 146 us -> 80.1 us (0.55)
  blocking collectives: 83.4 us -> 0 us
  starting transfers between devices: 0.04 us -> 27.7 us
  between operations: 14.3 us -> 1.01 us
  waiting for transfers between devices: 15.5 us -> 26.1 us
  local copies, waits for them, and re-layouts: 12.9 us -> 4.26 us
  other arithmetic: 4.82 us -> 9.57 us
  matrix products: 14.2 us -> 11 us
    psum x1 -> x0, blocking collectives: 59.7 us -> none  [local(): lax.psum((derivative_bottleneck, grad_out, grad_filter), 'freq')]
    ppermute x0 -> x16, starting transfers between devices: none -> 27.7 us  [the longest x4 8.41 us: gather_rows(): other = lax.ppermute(block, axis_name, _exchange_pairs(count, distance))]
    ppermute x0 -> x16, waiting for transfers between devices: none -> 26.1 us  [the longest x4 11.5 us: sum_halving(): lax.ppermute(send, axis_name, _exchange_pairs(count, distance))]
    all_gather x1 -> x0, blocking collectives: 23.7 us -> none  [local(): all_inputs = lax.all_gather(encoder_input, 'freq', axis=0, tiled=True)]
    psum x1 -> x0, waiting for transfers between devices: 15.5 us -> none  [local(): lax.psum((derivative_bottleneck, grad_out, grad_filter), 'freq')]
    unnamed x31 -> x11, local copies, waits for them, and re-layouts: 10.2 us -> 0.95 us
    select_n x0 -> x11, other arithmetic: none -> 4.46 us  [the longest x4 3.45 us: sum_halving(): jnp.where(lower, jnp.concatenate([values, other], 0), jnp.concatenate([ot...]
    dot_general x1, matrix products: 2.62 us -> 0.61 us  [decode_rows(): lax.dot_general(residual_half, output_weight, (((1,), (1,)), ((), ())), p...]
  transfers between devices with their start and end apart: 1 -> 16, of which waited for: 1 -> 11; matrix products, arithmetic and copies ran while one was open for 11% -> 18% of each run, Pallas kernels for 0% -> 0%
where the time goes in v2:
time: 80.1 us; the launch traced here: 79.7 us
  starting transfers between devices  27.7 us (35%)
  waiting for transfers between devices  26.1 us (33%)
  matrix products  11 us (14%)
  other arithmetic  9.57 us (12%)
  local copies, waits for them, and re-layouts  4.26 us (5%)
  between operations  1.01 us (1%)
    ppermute x4, waiting for transfers between devices, sum_halving(): lax.ppermute(send, axis_name, _exchange_pairs(count, distance))  11.5 us
    ppermute x4, waiting for transfers between devices, sum_whole(): lax.ppermute(values, axis_name, _exchange_pairs(count, distance))  8.81 us
    ppermute x4, starting transfers between devices, gather_rows(): other = lax.ppermute(block, axis_name, _exchange_pairs(count, distance))  8.41 us
    ppermute x4, starting transfers between devices, sum_halving(): lax.ppermute(send, axis_name, _exchange_pairs(count, distance))  7.03 us
    ppermute x4, starting transfers between devices, sum_halving(): other = lax.ppermute(values, axis_name, _exchange_pairs(count, distance))  6.88 us
    ppermute x4, starting transfers between devices, sum_whole(): lax.ppermute(values, axis_name, _exchange_pairs(count, distance))  5.41 us
    dot_general x1, matrix products, encoder_grads(): lax.dot_general(inputs_rows, grad_pre, (((0,), (0,)), ((), ())), preferre...  3.87 us
    ppermute x4, waiting for transfers between devices, gather_rows(): other = lax.ppermute(block, axis_name, _exchange_pairs(count, distance))  3.64 us
  transfers between devices with their start and end apart: 16, of which 11 were waited for; matrix products, arithmetic and copies ran while one was open for 18% of the time, Pallas kernels for 0%

profile of v2, /device:TPU:0, one launch (start us, length us, event | category | flops | bytes accessed | tf_op | source)
XLA Modules:
  0.0 79.7 jit_solution(12374071463894562074)
XLA Ops:
  5.0 2.6 %collective-permute-start.1 = (bf16[4,2048]{1,0:T(4,128)(2,1)S(1)}, bf16[4,2048]{1,0:T(4,128)(2,1)S(1)}, u32[]{:S(2)}, u32[]{:S(2)}) collective-permute-start(bf16[4,2048]{1,0:T(4,128)(2,1)S(1)} %maximum_select_fusion.9), channel_id=1, source_target_pairs={{0,2},{1,3},{2,0},{3,1},{4,6},{5,7},{6,4},{7,5},{8,10},{9,11},{10,... | collective-permute-start | bytes 49160 | tf_op jit(solution)/shard_map/ppermute | solution.py:114
  7.7 1.1 %negate_convert_fusion = (bf16[256,256]{1,0:T(8,128)(2,1)S(1)}, bf16[256,256]{1,0:T(8,128)(2,1)S(1)}) fusion(), kind=kLoop, calls=%fused_computation.59 | loop fusion | flops 1245184 | bytes 262144 | tf_op jit(solution)/shard_map/convert.16
  9.4 2.2 %collective-permute-start.2 = (bf16[8,2048]{1,0:T(8,128)(2,1)S(1)}, bf16[8,2048]{1,0:T(8,128)(2,1)S(1)}, u32[]{:S(2)}, u32[]{:S(2)}) collective-permute-start(bf16[8,2048]{1,0:T(8,128)(2,1)S(1)} %maximum_select_fusion.6), channel_id=1, source_target_pairs={{0,4},{1,5},{2,6},{3,7},{4,0},{5,1},{6,2},{7,3},{8,12},{9,13},{10,... | collective-permute-start | bytes 98312 | tf_op jit(solution)/shard_map/ppermute | solution.py:114
  13.5 3.1 %collective-permute-start.3 = (bf16[16,2048]{1,0:T(8,128)(2,1)S(1)}, bf16[16,2048]{1,0:T(8,128)(2,1)S(1)}, u32[]{:S(2)}, u32[]{:S(2)}) collective-permute-start(bf16[16,2048]{1,0:T(8,128)(2,1)S(1)} %maximum_select_fusion.5), channel_id=1, source_target_pairs={{0,8},{1,9},{2,10},{3,11},{4,12},{5,13},{6,14},{7,15},{8,0},{9,1},... | collective-permute-start | bytes 196616 | tf_op jit(solution)/shard_map/ppermute | solution.py:114
  16.6 2.2 %collective-permute-done.3 = bf16[16,2048]{1,0:T(8,128)(2,1)S(1)} collective-permute-done((bf16[16,2048]{1,0:T(8,128)(2,1)S(1)}, bf16[16,2048]{1,0:T(8,128)(2,1)S(1)}, u32[]{:S(2)}, u32[]{:S(2)}) %collective-permute-start.3) | collective-permute-done | bytes 65568 | tf_op jit(solution)/shard_map/ppermute | solution.py:114
  25.1 1.2 %fusion.18 = f32[768,512]{1,0:T(8,128)S(1)} fusion(f32[768,512]{1,0:T(8,128)S(1)} %get-tuple-element.17, f32[768,512]{1,0:T(8,128)S(1)} %convolution_add_fusion.1, bf16[256,256]{1,0:T(8,128)(2,1)S(1)} %get-tuple-element.19, bf16[256,256]{1,0:T(8,128)(2,1)S(1)} %get-tuple-element.18, bf16[256,256]{1,0:T(8,128)(2,1)S(1)} %fusion.31), kind=kOutput, calls=%fused_computation.38 | convolution fusion | flops 412614656 | bytes 5111808 | tf_op jit(solution)/shard_map/dot_general | solution.py:64
  27.2 1.9 %collective-permute-start.9 = (f32[128,512]{1,0:T(8,128)S(1)}, f32[128,512]{1,0:T(8,128)S(1)}, u32[]{:S(2)}, u32[]{:S(2)}) collective-permute-start(f32[128,512]{1,0:T(8,128)S(1)} %slice_select_fusion.1), channel_id=1, source_target_pairs={{0,2},{1,3},{2,0},{3,1},{4,6},{5,7},{6,4},{7,5},{8,10},{9,11},{10,... | collective-permute-start | bytes 786440 | tf_op jit(solution)/shard_map/ppermute | solution.py:145
  29.7 6.1 %collective-permute-done.9 = f32[128,512]{1,0:T(8,128)S(1)} collective-permute-done((f32[128,512]{1,0:T(8,128)S(1)}, f32[128,512]{1,0:T(8,128)S(1)}, u32[]{:S(2)}, u32[]{:S(2)}) %collective-permute-start.9) | collective-permute-done | bytes 262176 | tf_op jit(solution)/shard_map/ppermute | solution.py:145
  35.9 1.9 %collective-permute-start.10 = (f32[64,512]{1,0:T(8,128)S(1)}, f32[64,512]{1,0:T(8,128)S(1)}, u32[]{:S(2)}, u32[]{:S(2)}) collective-permute-start(f32[64,512]{1,0:T(8,128)S(1)} %slice_select_fusion.2), channel_id=1, source_target_pairs={{0,4},{1,5},{2,6},{3,7},{4,0},{5,1},{6,2},{7,3},{8,12},{9,13},{10,... | collective-permute-start | bytes 393224 | tf_op jit(solution)/shard_map/ppermute | solution.py:145
  38.0 2.9 %collective-permute-done.10 = f32[64,512]{1,0:T(8,128)S(1)} collective-permute-done((f32[64,512]{1,0:T(8,128)S(1)}, f32[64,512]{1,0:T(8,128)S(1)}, u32[]{:S(2)}, u32[]{:S(2)}) %collective-permute-start.10) | collective-permute-done | bytes 131104 | tf_op jit(solution)/shard_map/ppermute | solution.py:145
  41.0 3.2 %collective-permute-start.11 = (f32[32,512]{1,0:T(8,128)S(1)}, f32[32,512]{1,0:T(8,128)S(1)}, u32[]{:S(2)}, u32[]{:S(2)}) collective-permute-start(f32[32,512]{1,0:T(8,128)S(1)} %slice_select_fusion.3), channel_id=1, source_target_pairs={{0,8},{1,9},{2,10},{3,11},{4,12},{5,13},{6,14},{7,15},{8,0},{9,1},... | collective-permute-start | bytes 196616 | tf_op jit(solution)/shard_map/ppermute | solution.py:145
  44.2 2.2 %collective-permute-done.11 = f32[32,512]{1,0:T(8,128)S(1)} collective-permute-done((f32[32,512]{1,0:T(8,128)S(1)}, f32[32,512]{1,0:T(8,128)S(1)}, u32[]{:S(2)}, u32[]{:S(2)}) %collective-permute-start.11) | collective-permute-done | bytes 65568 | tf_op jit(solution)/shard_map/ppermute | solution.py:145
  46.4 3.0 %collective-permute-start.12 = (f32[32,512]{1,0:T(8,128)S(1)}, f32[32,512]{1,0:T(8,128)S(1)}, u32[]{:S(2)}, u32[]{:S(2)}) collective-permute-start(f32[32,512]{1,0:T(8,128)S(1)} %select_add_fusion.3), channel_id=1, source_target_pairs={{0,8},{1,9},{2,10},{3,11},{4,12},{5,13},{6,14},{7,15},{8,0},{9,1},... | collective-permute-start | bytes 196616 | tf_op jit(solution)/shard_map/ppermute | solution.py:149
  49.5 2.2 %collective-permute-done.12 = f32[32,512]{1,0:T(8,128)S(1)} collective-permute-done((f32[32,512]{1,0:T(8,128)S(1)}, f32[32,512]{1,0:T(8,128)S(1)}, u32[]{:S(2)}, u32[]{:S(2)}) %collective-permute-start.12) | collective-permute-done | bytes 65568 | tf_op jit(solution)/shard_map/ppermute | solution.py:149
  51.7 2.2 %collective-permute-start.13 = (f32[64,512]{1,0:T(8,128)S(1)}, f32[64,512]{1,0:T(8,128)S(1)}, u32[]{:S(2)}, u32[]{:S(2)}) collective-permute-start(f32[64,512]{1,0:T(8,128)S(1)} %maximum_select_fusion.4), channel_id=1, source_target_pairs={{0,4},{1,5},{2,6},{3,7},{4,0},{5,1},{6,2},{7,3},{8,12},{9,13},{10,... | collective-permute-start | bytes 393224 | tf_op jit(solution)/shard_map/ppermute | solution.py:149
  53.9 1.6 %collective-permute-start.5 = (f32[33,512]{1,0:T(8,128)S(1)}, f32[33,512]{1,0:T(8,128)S(1)}, u32[]{:S(2)}, u32[]{:S(2)}) collective-permute-start(f32[33,512]{1,0:T(8,128)S(1)} %fusion.60), channel_id=1, source_target_pairs={{0,2},{1,3},{2,0},{3,1},{4,6},{5,7},{6,4},{7,5},{8,10},{9,11},{10,... | collective-permute-start | bytes 202760 | tf_op jit(solution)/shard_map/ppermute | solution.py:129
  55.5 2.9 %collective-permute-done.5 = f32[33,512]{1,0:T(8,128)S(1)} collective-permute-done((f32[33,512]{1,0:T(8,128)S(1)}, f32[33,512]{1,0:T(8,128)S(1)}, u32[]{:S(2)}, u32[]{:S(2)}) %collective-permute-start.5) | collective-permute-done | bytes 67616 | tf_op jit(solution)/shard_map/ppermute | solution.py:129
  58.6 1.6 %collective-permute-start.14 = (f32[128,512]{1,0:T(8,128)S(1)}, f32[128,512]{1,0:T(8,128)}, u32[]{:S(2)}, u32[]{:S(2)}) collective-permute-start(f32[128,512]{1,0:T(8,128)S(1)} %maximum_select_fusion.2), channel_id=1, source_target_pairs={{0,2},{1,3},{2,0},{3,1},{4,6},{5,7},{6,4},{7,5},{8,10},{9,11},{10,... | collective-permute-start | bytes 786440 | tf_op jit(solution)/shard_map/ppermute | solution.py:149
  60.1 3.2 %collective-permute-done.6 = f32[33,512]{1,0:T(8,128)S(1)} collective-permute-done((f32[33,512]{1,0:T(8,128)S(1)}, f32[33,512]{1,0:T(8,128)S(1)}, u32[]{:S(2)}, u32[]{:S(2)}) %collective-permute-start.6) | collective-permute-done | bytes 67616 | tf_op jit(solution)/shard_map/ppermute | solution.py:129
  63.3 3.7 %collective-permute-start.7 = (f32[33,512]{1,0:T(8,128)S(1)}, f32[33,512]{1,0:T(8,128)S(1)}, u32[]{:S(2)}, u32[]{:S(2)}) collective-permute-start(f32[33,512]{1,0:T(8,128)S(1)} %add.124), channel_id=1, source_target_pairs={{0,8},{1,9},{2,10},{3,11},{4,12},{5,13},{6,14},{7,15},{8,0},{9,1},... | collective-permute-start | bytes 202760 | tf_op jit(solution)/shard_map/ppermute | solution.py:129
  67.0 2.7 %collective-permute-done.7 = f32[33,512]{1,0:T(8,128)S(1)} collective-permute-done((f32[33,512]{1,0:T(8,128)S(1)}, f32[33,512]{1,0:T(8,128)S(1)}, u32[]{:S(2)}, u32[]{:S(2)}) %collective-permute-start.7) | collective-permute-done | bytes 67616 | tf_op jit(solution)/shard_map/ppermute | solution.py:129
  72.2 1.3 %fusion.63 = f32[512,512]{1,0:T(8,128)} fusion(bf16[32,512]{1,0:T(8,128)(2,1)S(1)} %fusion.8, bf16[32,512]{1,0:T(8,128)(2,1)S(1)} %gather_fusion.1), kind=kOutput, calls=%fused_computation.110 | convolution fusion | flops 16777216 | bytes 1114112 | tf_op jit(solution)/shard_map/dot_general | solution.py:86
  73.5 3.9 %fusion.10 = f32[2048,512]{1,0:T(8,128)} fusion(bf16[512,512]{1,0:T(8,128)(2,1)S(1)} %copy-done.1, bf16[32,512]{1,0:T(8,128)(2,1)S(1)} %fusion.8, bf16[16,2048]{1,0:T(8,128)(2,1)} %copy-done.3, bf16[16,2048]{1,0:T(8,128)(2,1)S(1)} %maximum_select_fusion.5, pred[]{:T(512)S(6)} %eq.35, bf16[32,512]{1,0:T(8,128)(2,1)S(1)} %gather_fusion.1), kind=kOutput, calls=%fused_computation.23 | convolution fusion | flops 84557824 | bytes 4915201 | tf_op jit(solution)/shard_map/dot_general | solution.py:93
  77.3 2.3 %maximum_select_fusion = f32[512,512]{1,0:T(8,128)} fusion(f32[256,512]{1,0:T(8,128)} %collective-permute-done.15, f32[256,512]{1,0:T(8,128)S(1)} %maximum_select_fusion.1, pred[]{:T(512)S(6)} %eq.38), kind=kLoop, calls=%fused_computation.24 | loop fusion | flops 786432 | bytes 2097153 | tf_op jit(solution)/shard_map/jit(_where)/select_n | solution.py:151
  (70 shorter events, 17.5 us)
Async XLA Ops:
  0.6 18.8 %copy-start = (bf16[2048,512]{1,0:T(8,128)(2,1)S(1)}, bf16[2048,512]{1,0:T(8,128)(2,1)}, u32[]{:S(2)}) copy-start(bf16[2048,512]{1,0:T(8,128)(2,1)} %param.11) | copy-start | bytes 6291460
  0.6 3.6 %collective-permute-start = (bf16[2,2048]{1,0:T(2,128)(2,1)}, bf16[2,2048]{1,0:T(2,128)(2,1)S(1)}, u32[]{:S(2)}, u32[]{:S(2)}) collective-permute-start(bf16[2,2048]{1,0:T(2,128)(2,1)} %param.8), channel_id=1, source_target_pairs={{0,1},{1,0},{2,3},{3,2},{4,5},{5,4},{6,7},{7,6},{8,9},{9,8},{10,11... | collective-permute-start | bytes 24584 | tf_op jit(solution)/shard_map/ppermute | solution.py:114
  5.0 4.3 %collective-permute-start.1 = (bf16[4,2048]{1,0:T(4,128)(2,1)S(1)}, bf16[4,2048]{1,0:T(4,128)(2,1)S(1)}, u32[]{:S(2)}, u32[]{:S(2)}) collective-permute-start(bf16[4,2048]{1,0:T(4,128)(2,1)S(1)} %maximum_select_fusion.9), channel_id=1, source_target_pairs={{0,2},{1,3},{2,0},{3,1},{4,6},{5,7},{6,4},{7,5},{8,10},{9,11},{10,... | collective-permute-start | bytes 49160 | tf_op jit(solution)/shard_map/ppermute | solution.py:114
  8.8 11.8 %copy-start.1 = (bf16[512,512]{1,0:T(8,128)(2,1)S(1)}, bf16[512,512]{1,0:T(8,128)(2,1)}, u32[]{:S(2)}) copy-start(bf16[512,512]{1,0:T(8,128)(2,1)} %param.12) | copy-start | bytes 1572868
  9.4 4.1 %collective-permute-start.2 = (bf16[8,2048]{1,0:T(8,128)(2,1)S(1)}, bf16[8,2048]{1,0:T(8,128)(2,1)S(1)}, u32[]{:S(2)}, u32[]{:S(2)}) collective-permute-start(bf16[8,2048]{1,0:T(8,128)(2,1)S(1)} %maximum_select_fusion.6), channel_id=1, source_target_pairs={{0,4},{1,5},{2,6},{3,7},{4,0},{5,1},{6,2},{7,3},{8,12},{9,13},{10,... | collective-permute-start | bytes 98312 | tf_op jit(solution)/shard_map/ppermute | solution.py:114
  13.5 5.3 %collective-permute-start.3 = (bf16[16,2048]{1,0:T(8,128)(2,1)S(1)}, bf16[16,2048]{1,0:T(8,128)(2,1)S(1)}, u32[]{:S(2)}, u32[]{:S(2)}) collective-permute-start(bf16[16,2048]{1,0:T(8,128)(2,1)S(1)} %maximum_select_fusion.5), channel_id=1, source_target_pairs={{0,8},{1,9},{2,10},{3,11},{4,12},{5,13},{6,14},{7,15},{8,0},{9,1},... | collective-permute-start | bytes 196616 | tf_op jit(solution)/shard_map/ppermute | solution.py:114
  18.8 0.6 copy-start.3
  21.7 1.0 %copy-start.2 = (bf16[512,512]{1,0:T(8,128)(2,1)S(1)}, bf16[512,512]{1,0:T(8,128)(2,1)}, u32[]{:S(2)}) copy-start(bf16[512,512]{1,0:T(8,128)(2,1)} %param.15) | copy-start | bytes 1572868
  21.8 1.3 %copy-start.4 = (bf16[32,24,512]{2,1,0:T(8,128)(2,1)S(1)}, bf16[32,24,512]{2,1,0:T(8,128)(2,1)}, u32[]{:S(2)}) copy-start(bf16[32,24,512]{2,1,0:T(8,128)(2,1)} %param.9) | copy-start | bytes 2359300
  25.0 2.0 %collective-permute-start.8 = (f32[256,512]{1,0:T(8,128)S(1)}, f32[256,512]{1,0:T(8,128)S(1)}, u32[]{:S(2)}, u32[]{:S(2)}) collective-permute-start(f32[256,512]{1,0:T(8,128)S(1)} %slice_select_fusion), channel_id=1, source_target_pairs={{0,1},{1,0},{2,3},{3,2},{4,5},{5,4},{6,7},{7,6},{8,9},{9,8},{10,11... | collective-permute-start | bytes 1572872 | tf_op jit(solution)/shard_map/ppermute | solution.py:145
  27.2 8.6 %collective-permute-start.9 = (f32[128,512]{1,0:T(8,128)S(1)}, f32[128,512]{1,0:T(8,128)S(1)}, u32[]{:S(2)}, u32[]{:S(2)}) collective-permute-start(f32[128,512]{1,0:T(8,128)S(1)} %slice_select_fusion.1), channel_id=1, source_target_pairs={{0,2},{1,3},{2,0},{3,1},{4,6},{5,7},{6,4},{7,5},{8,10},{9,11},{10,... | collective-permute-start | bytes 786440 | tf_op jit(solution)/shard_map/ppermute | solution.py:145
  35.9 5.0 %collective-permute-start.10 = (f32[64,512]{1,0:T(8,128)S(1)}, f32[64,512]{1,0:T(8,128)S(1)}, u32[]{:S(2)}, u32[]{:S(2)}) collective-permute-start(f32[64,512]{1,0:T(8,128)S(1)} %slice_select_fusion.2), channel_id=1, source_target_pairs={{0,4},{1,5},{2,6},{3,7},{4,0},{5,1},{6,2},{7,3},{8,12},{9,13},{10,... | collective-permute-start | bytes 393224 | tf_op jit(solution)/shard_map/ppermute | solution.py:145
  41.0 5.4 %collective-permute-start.11 = (f32[32,512]{1,0:T(8,128)S(1)}, f32[32,512]{1,0:T(8,128)S(1)}, u32[]{:S(2)}, u32[]{:S(2)}) collective-permute-start(f32[32,512]{1,0:T(8,128)S(1)} %slice_select_fusion.3), channel_id=1, source_target_pairs={{0,8},{1,9},{2,10},{3,11},{4,12},{5,13},{6,14},{7,15},{8,0},{9,1},... | collective-permute-start | bytes 196616 | tf_op jit(solution)/shard_map/ppermute | solution.py:145
  46.4 5.3 %collective-permute-start.12 = (f32[32,512]{1,0:T(8,128)S(1)}, f32[32,512]{1,0:T(8,128)S(1)}, u32[]{:S(2)}, u32[]{:S(2)}) collective-permute-start(f32[32,512]{1,0:T(8,128)S(1)} %select_add_fusion.3), channel_id=1, source_target_pairs={{0,8},{1,9},{2,10},{3,11},{4,12},{5,13},{6,14},{7,15},{8,0},{9,1},... | collective-permute-start | bytes 196616 | tf_op jit(solution)/shard_map/ppermute | solution.py:149
  49.4 4.5 %collective-permute-start.4 = (f32[33,512]{1,0:T(8,128)S(1)}, f32[33,512]{1,0:T(8,128)S(1)}, u32[]{:S(2)}, u32[]{:S(2)}) collective-permute-start(f32[33,512]{1,0:T(8,128)S(1)} %pad_maximum_fusion.4), channel_id=1, source_target_pairs={{0,1},{1,0},{2,3},{3,2},{4,5},{5,4},{6,7},{7,6},{8,9},{9,8},{10,11... | collective-permute-start | bytes 202760 | tf_op jit(solution)/shard_map/ppermute | solution.py:129
  51.7 6.8 %collective-permute-start.13 = (f32[64,512]{1,0:T(8,128)S(1)}, f32[64,512]{1,0:T(8,128)S(1)}, u32[]{:S(2)}, u32[]{:S(2)}) collective-permute-start(f32[64,512]{1,0:T(8,128)S(1)} %maximum_select_fusion.4), channel_id=1, source_target_pairs={{0,4},{1,5},{2,6},{3,7},{4,0},{5,1},{6,2},{7,3},{8,12},{9,13},{10,... | collective-permute-start | bytes 393224 | tf_op jit(solution)/shard_map/ppermute | solution.py:149
  53.9 4.5 %collective-permute-start.5 = (f32[33,512]{1,0:T(8,128)S(1)}, f32[33,512]{1,0:T(8,128)S(1)}, u32[]{:S(2)}, u32[]{:S(2)}) collective-permute-start(f32[33,512]{1,0:T(8,128)S(1)} %fusion.60), channel_id=1, source_target_pairs={{0,2},{1,3},{2,0},{3,1},{4,6},{5,7},{6,4},{7,5},{8,10},{9,11},{10,... | collective-permute-start | bytes 202760 | tf_op jit(solution)/shard_map/ppermute | solution.py:129
  58.4 4.9 %collective-permute-start.6 = (f32[33,512]{1,0:T(8,128)S(1)}, f32[33,512]{1,0:T(8,128)S(1)}, u32[]{:S(2)}, u32[]{:S(2)}) collective-permute-start(f32[33,512]{1,0:T(8,128)S(1)} %add.123), channel_id=1, source_target_pairs={{0,4},{1,5},{2,6},{3,7},{4,0},{5,1},{6,2},{7,3},{8,12},{9,13},{10,... | collective-permute-start | bytes 202760 | tf_op jit(solution)/shard_map/ppermute | solution.py:129
  58.6 12.4 %collective-permute-start.14 = (f32[128,512]{1,0:T(8,128)S(1)}, f32[128,512]{1,0:T(8,128)}, u32[]{:S(2)}, u32[]{:S(2)}) collective-permute-start(f32[128,512]{1,0:T(8,128)S(1)} %maximum_select_fusion.2), channel_id=1, source_target_pairs={{0,2},{1,3},{2,0},{3,1},{4,6},{5,7},{6,4},{7,5},{8,10},{9,11},{10,... | collective-permute-start | bytes 786440 | tf_op jit(solution)/shard_map/ppermute | solution.py:149
  63.3 6.4 %collective-permute-start.7 = (f32[33,512]{1,0:T(8,128)S(1)}, f32[33,512]{1,0:T(8,128)S(1)}, u32[]{:S(2)}, u32[]{:S(2)}) collective-permute-start(f32[33,512]{1,0:T(8,128)S(1)} %add.124), channel_id=1, source_target_pairs={{0,8},{1,9},{2,10},{3,11},{4,12},{5,13},{6,14},{7,15},{8,0},{9,1},... | collective-permute-start | bytes 202760 | tf_op jit(solution)/shard_map/ppermute | solution.py:129
  72.1 5.2 %collective-permute-start.15 = (f32[256,512]{1,0:T(8,128)S(1)}, f32[256,512]{1,0:T(8,128)}, u32[]{:S(2)}, u32[]{:S(2)}) collective-permute-start(f32[256,512]{1,0:T(8,128)S(1)} %maximum_select_fusion.1), channel_id=1, source_target_pairs={{0,1},{1,0},{2,3},{3,2},{4,5},{5,4},{6,7},{7,6},{8,9},{9,8},{10,11... | collective-permute-start | bytes 1572872 | tf_op jit(solution)/shard_map/ppermute | solution.py:149

commit v3 on v2

--- a/solution.py
+++ b/solution.py
@@ -193,12 +193,22 @@
     derivative_bottleneck = jnp.einsum(
         "orm,rm->om", derivative_entering.reshape(samples, sub_dev, width), gain_row_values
     )
-    grad_out = sum_halving(grad_out, "freq")
-    packed = sum_whole(
-        jnp.concatenate([derivative_bottleneck, grad_filter.reshape(1, -1)], 0), "freq"
-    )
+    count = lax.axis_size("freq")
+    packed_rows = samples + 1 + grad_out.shape[0]
+    padding = -packed_rows % count
+    packed = jnp.concatenate(
+        [
+            derivative_bottleneck,
+            grad_filter.reshape(1, -1),
+            grad_out,
+            jnp.zeros((padding, width), jnp.float32),
+        ],
+        0,
+    )
+    packed = sum_halving(packed, "freq")
     derivative_bottleneck = packed[:samples]
-    grad_filter = packed[samples:].reshape(grad_filter.shape)
+    grad_filter = packed[samples].reshape(grad_filter.shape)
+    grad_out = packed[samples + 1 : packed_rows]
     grad_enc, grad_dec = encoder_grads(
         all_inputs, codes, derivative_bottleneck[sample_index], decoder_weight
     )

time: 80.1 us -> 76.5 us (0.955)
  waiting for transfers between devices: 26.1 us -> 31.5 us
  starting transfers between devices: 27.7 us -> 22.4 us
  other arithmetic: 9.57 us -> 6.4 us
  matrix products: 11 us -> 10.1 us
    ppermute x4, waiting for transfers between devices: 2.17 us -> 12.8 us  [sum_halving(): other = lax.ppermute(values, axis_name, _exchange_pairs(count, distance))]
    ppermute x4 -> x0, waiting for transfers between devices: 8.81 us -> none  [sum_whole(): lax.ppermute(values, axis_name, _exchange_pairs(count, distance))]
    ppermute x4 -> x0, starting transfers between devices: 5.41 us -> none  [sum_whole(): lax.ppermute(values, axis_name, _exchange_pairs(count, distance))]
    ppermute x4, waiting for transfers between devices: 11.5 us -> 15.1 us  [sum_halving(): lax.ppermute(send, axis_name, _exchange_pairs(count, distance))]
    select_n x4, other arithmetic: 3.45 us -> 0.26 us  [sum_halving(): jnp.where(lower, jnp.concatenate([values, other], 0), jnp.concatenate([ot...]
    slice x1 -> x2, local copies, waits for them, and re-layouts: 0.02 us -> 1.11 us  [the longest x1 1.09 us: local(): grad_out = packed[samples + 1:packed_rows]]
    dot_general x1, matrix products: 3.87 us -> 2.96 us  [encoder_grads(): lax.dot_general(inputs_rows, grad_pre, (((0,), (0,)), ((), ())), preferre...]
  transfers between devices with their start and end apart: 16 -> 12, of which waited for: 11 -> 11; matrix products, arithmetic and copies ran while one was open for 18% -> 7% of each run, Pallas kernels for 0% -> 0%
where the time goes in v3:
time: 76.5 us; the launch traced here: 76.1 us
  waiting for transfers between devices  31.5 us (41%)
  starting transfers between devices  22.4 us (29%)
  matrix products  10.1 us (13%)
  other arithmetic  6.4 us (8%)
  local copies, waits for them, and re-layouts  4.71 us (6%)
  between operations  1.01 us (1%)
    ppermute x4, waiting for transfers between devices, sum_halving(): lax.ppermute(send, axis_name, _exchange_pairs(count, distance))  15.1 us
    ppermute x4, waiting for transfers between devices, sum_halving(): other = lax.ppermute(values, axis_name, _exchange_pairs(count, distance))  12.8 us
    ppermute x4, starting transfers between devices, gather_rows(): other = lax.ppermute(block, axis_name, _exchange_pairs(count, distance))  8.38 us
    ppermute x4, starting transfers between devices, sum_halving(): lax.ppermute(send, axis_name, _exchange_pairs(count, distance))  7.01 us
    ppermute x4, starting transfers between devices, sum_halving(): other = lax.ppermute(values, axis_name, _exchange_pairs(count, distance))  6.98 us
    ppermute x4, waiting for transfers between devices, gather_rows(): other = lax.ppermute(block, axis_name, _exchange_pairs(count, distance))  3.65 us
    dot_general x1, matrix products, encoder_grads(): lax.dot_general(inputs_rows, grad_pre, (((0,), (0,)), ((), ())), preferre...  2.96 us
    another operation x4, other arithmetic  2.75 us
  transfers between devices with their start and end apart: 12, of which 11 were waited for; matrix products, arithmetic and copies ran while one was open for 7% of the time, Pallas kernels for 0%

profile of v3, /device:TPU:0, one launch (start us, length us, event | category | flops | bytes accessed | tf_op | source)
XLA Modules:
  0.0 76.1 jit_solution(3370565770969013209)
XLA Ops:
  5.0 2.6 %collective-permute-start.1 = (bf16[4,2048]{1,0:T(4,128)(2,1)S(1)}, bf16[4,2048]{1,0:T(4,128)(2,1)S(1)}, u32[]{:S(2)}, u32[]{:S(2)}) collective-permute-start(bf16[4,2048]{1,0:T(4,128)(2,1)S(1)} %maximum_select_fusion.9), channel_id=1, source_target_pairs={{0,2},{1,3},{2,0},{3,1},{4,6},{5,7},{6,4},{7,5},{8,10},{9,11},{10,... | collective-permute-start | bytes 49160 | tf_op jit(solution)/shard_map/ppermute | solution.py:114
  7.6 1.1 %negate_convert_fusion = (bf16[256,256]{1,0:T(8,128)(2,1)S(1)}, bf16[256,256]{1,0:T(8,128)(2,1)S(1)}) fusion(), kind=kLoop, calls=%fused_computation.63 | loop fusion | flops 1245184 | bytes 262144 | tf_op jit(solution)/shard_map/convert.16
  9.4 2.1 %collective-permute-start.2 = (bf16[8,2048]{1,0:T(8,128)(2,1)S(1)}, bf16[8,2048]{1,0:T(8,128)(2,1)S(1)}, u32[]{:S(2)}, u32[]{:S(2)}) collective-permute-start(bf16[8,2048]{1,0:T(8,128)(2,1)S(1)} %maximum_select_fusion.6), channel_id=1, source_target_pairs={{0,4},{1,5},{2,6},{3,7},{4,0},{5,1},{6,2},{7,3},{8,12},{9,13},{10,... | collective-permute-start | bytes 98312 | tf_op jit(solution)/shard_map/ppermute | solution.py:114
  11.5 1.0 %fusion.32 = bf16[256,256]{1,0:T(8,128)(2,1)S(1)} fusion(), kind=kLoop, calls=%fused_computation.69 | loop fusion | flops 1048576 | bytes 131072 | tf_op jit(solution)/shard_map/convert.13
  13.4 3.1 %collective-permute-start.3 = (bf16[16,2048]{1,0:T(8,128)(2,1)S(1)}, bf16[16,2048]{1,0:T(8,128)(2,1)S(1)}, u32[]{:S(2)}, u32[]{:S(2)}) collective-permute-start(bf16[16,2048]{1,0:T(8,128)(2,1)S(1)} %maximum_select_fusion.5), channel_id=1, source_target_pairs={{0,8},{1,9},{2,10},{3,11},{4,12},{5,13},{6,14},{7,15},{8,0},{9,1},... | collective-permute-start | bytes 196616 | tf_op jit(solution)/shard_map/ppermute | solution.py:114
  16.5 2.2 %collective-permute-done.3 = bf16[16,2048]{1,0:T(8,128)(2,1)S(1)} collective-permute-done((bf16[16,2048]{1,0:T(8,128)(2,1)S(1)}, bf16[16,2048]{1,0:T(8,128)(2,1)S(1)}, u32[]{:S(2)}, u32[]{:S(2)}) %collective-permute-start.3) | collective-permute-done | bytes 65568 | tf_op jit(solution)/shard_map/ppermute | solution.py:114
  24.2 1.2 %fusion.18 = f32[768,512]{1,0:T(8,128)S(1)} fusion(f32[768,512]{1,0:T(8,128)S(1)} %get-tuple-element.17, f32[768,512]{1,0:T(8,128)S(1)} %convolution_add_fusion.1, bf16[256,256]{1,0:T(8,128)(2,1)S(1)} %get-tuple-element.19, bf16[256,256]{1,0:T(8,128)(2,1)S(1)} %get-tuple-element.18, bf16[256,256]{1,0:T(8,128)(2,1)S(1)} %fusion.32), kind=kOutput, calls=%fused_computation.39 | convolution fusion | flops 412614656 | bytes 5111808 | tf_op jit(solution)/shard_map/dot_general | solution.py:64
  27.0 2.0 %collective-permute-done.4 = f32[280,512]{1,0:T(8,128)S(1)} collective-permute-done((f32[280,512]{1,0:T(8,128)S(1)}, f32[280,512]{1,0:T(8,128)S(1)}, u32[]{:S(2)}, u32[]{:S(2)}) %collective-permute-start.4) | collective-permute-done | bytes 573472 | tf_op jit(solution)/shard_map/ppermute | solution.py:145
  29.2 1.9 %collective-permute-start.5 = (f32[140,512]{1,0:T(8,128)S(1)}, f32[140,512]{1,0:T(8,128)S(1)}, u32[]{:S(2)}, u32[]{:S(2)}) collective-permute-start(f32[140,512]{1,0:T(8,128)S(1)} %slice_select_fusion), channel_id=1, source_target_pairs={{0,2},{1,3},{2,0},{3,1},{4,6},{5,7},{6,4},{7,5},{8,10},{9,11},{10,... | collective-permute-start | bytes 860168 | tf_op jit(solution)/shard_map/ppermute | solution.py:145
  31.1 7.3 %collective-permute-done.5 = f32[140,512]{1,0:T(8,128)S(1)} collective-permute-done((f32[140,512]{1,0:T(8,128)S(1)}, f32[140,512]{1,0:T(8,128)S(1)}, u32[]{:S(2)}, u32[]{:S(2)}) %collective-permute-start.5) | collective-permute-done | bytes 286752 | tf_op jit(solution)/shard_map/ppermute | solution.py:145
  38.6 1.9 %collective-permute-start.6 = (f32[70,512]{1,0:T(8,128)S(1)}, f32[70,512]{1,0:T(8,128)S(1)}, u32[]{:S(2)}, u32[]{:S(2)}) collective-permute-start(f32[70,512]{1,0:T(8,128)S(1)} %slice_select_fusion.1), channel_id=1, source_target_pairs={{0,4},{1,5},{2,6},{3,7},{4,0},{5,1},{6,2},{7,3},{8,12},{9,13},{10,... | collective-permute-start | bytes 430088 | tf_op jit(solution)/shard_map/ppermute | solution.py:145
  40.4 3.4 %collective-permute-done.6 = f32[70,512]{1,0:T(8,128)S(1)} collective-permute-done((f32[70,512]{1,0:T(8,128)S(1)}, f32[70,512]{1,0:T(8,128)S(1)}, u32[]{:S(2)}, u32[]{:S(2)}) %collective-permute-start.6) | collective-permute-done | bytes 143392 | tf_op jit(solution)/shard_map/ppermute | solution.py:145
  43.9 3.2 %collective-permute-start.7 = (f32[35,512]{1,0:T(8,128)S(1)}, f32[35,512]{1,0:T(8,128)S(1)}, u32[]{:S(2)}, u32[]{:S(2)}) collective-permute-start(f32[35,512]{1,0:T(8,128)S(1)} %slice_select_fusion.2), channel_id=1, source_target_pairs={{0,8},{1,9},{2,10},{3,11},{4,12},{5,13},{6,14},{7,15},{8,0},{9,1},... | collective-permute-start | bytes 215048 | tf_op jit(solution)/shard_map/ppermute | solution.py:145
  47.0 2.4 %collective-permute-done.7 = f32[35,512]{1,0:T(8,128)S(1)} collective-permute-done((f32[35,512]{1,0:T(8,128)S(1)}, f32[35,512]{1,0:T(8,128)S(1)}, u32[]{:S(2)}, u32[]{:S(2)}) %collective-permute-start.7) | collective-permute-done | bytes 71712 | tf_op jit(solution)/shard_map/ppermute | solution.py:145
  49.5 3.0 %collective-permute-start.8 = (f32[35,512]{1,0:T(8,128)S(1)}, f32[35,512]{1,0:T(8,128)S(1)}, u32[]{:S(2)}, u32[]{:S(2)}) collective-permute-start(f32[35,512]{1,0:T(8,128)S(1)} %select_add_fusion.3), channel_id=1, source_target_pairs={{0,8},{1,9},{2,10},{3,11},{4,12},{5,13},{6,14},{7,15},{8,0},{9,1},... | collective-permute-start | bytes 215048 | tf_op jit(solution)/shard_map/ppermute | solution.py:149
  52.5 2.5 %collective-permute-done.8 = f32[35,512]{1,0:T(8,128)S(1)} collective-permute-done((f32[35,512]{1,0:T(8,128)S(1)}, f32[35,512]{1,0:T(8,128)S(1)}, u32[]{:S(2)}, u32[]{:S(2)}) %collective-permute-start.8) | collective-permute-done | bytes 71712 | tf_op jit(solution)/shard_map/ppermute | solution.py:149
  55.0 2.3 %collective-permute-start.9 = (f32[70,512]{1,0:T(8,128)S(1)}, f32[70,512]{1,0:T(8,128)S(1)}, u32[]{:S(2)}, u32[]{:S(2)}) collective-permute-start(f32[70,512]{1,0:T(8,128)S(1)} %maximum_select_fusion.3), channel_id=1, source_target_pairs={{0,4},{1,5},{2,6},{3,7},{4,0},{5,1},{6,2},{7,3},{8,12},{9,13},{10,... | collective-permute-start | bytes 430088 | tf_op jit(solution)/shard_map/ppermute | solution.py:149
  57.3 3.1 %collective-permute-done.9 = f32[70,512]{1,0:T(8,128)S(1)} collective-permute-done((f32[70,512]{1,0:T(8,128)S(1)}, f32[70,512]{1,0:T(8,128)S(1)}, u32[]{:S(2)}, u32[]{:S(2)}) %collective-permute-start.9) | collective-permute-done | bytes 143392 | tf_op jit(solution)/shard_map/ppermute | solution.py:149
  60.5 1.6 %collective-permute-start.10 = (f32[140,512]{1,0:T(8,128)S(1)}, f32[140,512]{1,0:T(8,128)S(1)}, u32[]{:S(2)}, u32[]{:S(2)}) collective-permute-start(f32[140,512]{1,0:T(8,128)S(1)} %maximum_select_fusion.2), channel_id=1, source_target_pairs={{0,2},{1,3},{2,0},{3,1},{4,6},{5,7},{6,4},{7,5},{8,10},{9,11},{10,... | collective-permute-start | bytes 860168 | tf_op jit(solution)/shard_map/ppermute | solution.py:149
  62.1 5.2 %collective-permute-done.10 = f32[140,512]{1,0:T(8,128)S(1)} collective-permute-done((f32[140,512]{1,0:T(8,128)S(1)}, f32[140,512]{1,0:T(8,128)S(1)}, u32[]{:S(2)}, u32[]{:S(2)}) %collective-permute-start.10) | collective-permute-done | bytes 286752 | tf_op jit(solution)/shard_map/ppermute | solution.py:149
  67.5 2.0 %collective-permute-done.11 = f32[280,512]{1,0:T(8,128)S(1)} collective-permute-done((f32[280,512]{1,0:T(8,128)S(1)}, f32[280,512]{1,0:T(8,128)S(1)}, u32[]{:S(2)}, u32[]{:S(2)}) %collective-permute-start.11) | collective-permute-done | bytes 573472 | tf_op jit(solution)/shard_map/ppermute | solution.py:149
  69.6 1.1 %slice.93 = f32[512,512]{1,0:T(8,128)} slice(f32[560,512]{1,0:T(8,128)S(1)} %maximum_select_fusion), slice={[33:545], [0:512]} | slice | bytes 2097152 | tf_op jit(solution)/shard_map/slice | solution.py:211
  71.3 1.3 %fusion.63 = f32[512,512]{1,0:T(8,128)} fusion(bf16[32,512]{1,0:T(8,128)(2,1)S(1)} %fusion.8, bf16[32,512]{1,0:T(8,128)(2,1)S(1)} %gather_fusion.1), kind=kOutput, calls=%fused_computation.111 | convolution fusion | flops 16777216 | bytes 1114112 | tf_op jit(solution)/shard_map/dot_general | solution.py:86
  73.2 3.0 %fusion.10 = f32[2048,512]{1,0:T(8,128)} fusion(bf16[512,512]{1,0:T(8,128)(2,1)S(1)} %copy-done.1, bf16[32,512]{1,0:T(8,128)(2,1)S(1)} %fusion.8, bf16[16,2048]{1,0:T(8,128)(2,1)S(1)} %collective-permute-done.3, bf16[16,2048]{1,0:T(8,128)(2,1)S(1)} %maximum_select_fusion.5, pred[]{:T(512)S(6)} %eq.35, bf16[32,512]{1,0:T(8,128)(2,1)S(1)} %gather_fusion.1), kind=kOutput, calls=%fused_computation.24 | convolution fusion | flops 84557824 | bytes 4915201 | tf_op jit(solution)/shard_map/dot_general | solution.py:93
  (56 shorter events, 14.6 us)
Async XLA Ops:
  0.6 18.1 %copy-start = (bf16[2048,512]{1,0:T(8,128)(2,1)S(1)}, bf16[2048,512]{1,0:T(8,128)(2,1)}, u32[]{:S(2)}) copy-start(bf16[2048,512]{1,0:T(8,128)(2,1)} %param.11) | copy-start | bytes 6291460
  0.6 3.5 %collective-permute-start = (bf16[2,2048]{1,0:T(2,128)(2,1)}, bf16[2,2048]{1,0:T(2,128)(2,1)S(1)}, u32[]{:S(2)}, u32[]{:S(2)}) collective-permute-start(bf16[2,2048]{1,0:T(2,128)(2,1)} %param.8), channel_id=1, source_target_pairs={{0,1},{1,0},{2,3},{3,2},{4,5},{5,4},{6,7},{7,6},{8,9},{9,8},{10,11... | collective-permute-start | bytes 24584 | tf_op jit(solution)/shard_map/ppermute | solution.py:114
  5.0 4.3 %collective-permute-start.1 = (bf16[4,2048]{1,0:T(4,128)(2,1)S(1)}, bf16[4,2048]{1,0:T(4,128)(2,1)S(1)}, u32[]{:S(2)}, u32[]{:S(2)}) collective-permute-start(bf16[4,2048]{1,0:T(4,128)(2,1)S(1)} %maximum_select_fusion.9), channel_id=1, source_target_pairs={{0,2},{1,3},{2,0},{3,1},{4,6},{5,7},{6,4},{7,5},{8,10},{9,11},{10,... | collective-permute-start | bytes 49160 | tf_op jit(solution)/shard_map/ppermute | solution.py:114
  8.7 11.2 %copy-start.1 = (bf16[512,512]{1,0:T(8,128)(2,1)S(1)}, bf16[512,512]{1,0:T(8,128)(2,1)}, u32[]{:S(2)}) copy-start(bf16[512,512]{1,0:T(8,128)(2,1)} %param.12) | copy-start | bytes 1572868
  9.4 4.0 %collective-permute-start.2 = (bf16[8,2048]{1,0:T(8,128)(2,1)S(1)}, bf16[8,2048]{1,0:T(8,128)(2,1)S(1)}, u32[]{:S(2)}, u32[]{:S(2)}) collective-permute-start(bf16[8,2048]{1,0:T(8,128)(2,1)S(1)} %maximum_select_fusion.6), channel_id=1, source_target_pairs={{0,4},{1,5},{2,6},{3,7},{4,0},{5,1},{6,2},{7,3},{8,12},{9,13},{10,... | collective-permute-start | bytes 98312 | tf_op jit(solution)/shard_map/ppermute | solution.py:114
  13.4 5.3 %collective-permute-start.3 = (bf16[16,2048]{1,0:T(8,128)(2,1)S(1)}, bf16[16,2048]{1,0:T(8,128)(2,1)S(1)}, u32[]{:S(2)}, u32[]{:S(2)}) collective-permute-start(bf16[16,2048]{1,0:T(8,128)(2,1)S(1)} %maximum_select_fusion.5), channel_id=1, source_target_pairs={{0,8},{1,9},{2,10},{3,11},{4,12},{5,13},{6,14},{7,15},{8,0},{9,1},... | collective-permute-start | bytes 196616 | tf_op jit(solution)/shard_map/ppermute | solution.py:114
  21.0 1.0 %copy-start.2 = (bf16[512,512]{1,0:T(8,128)(2,1)S(1)}, bf16[512,512]{1,0:T(8,128)(2,1)}, u32[]{:S(2)}) copy-start(bf16[512,512]{1,0:T(8,128)(2,1)} %param.15) | copy-start | bytes 1572868
  21.1 1.3 %copy-start.3 = (bf16[32,24,512]{2,1,0:T(8,128)(2,1)S(1)}, bf16[32,24,512]{2,1,0:T(8,128)(2,1)}, u32[]{:S(2)}) copy-start(bf16[32,24,512]{2,1,0:T(8,128)(2,1)} %param.9) | copy-start | bytes 2359300
  26.9 2.0 %collective-permute-start.4 = (f32[280,512]{1,0:T(8,128)S(1)}, f32[280,512]{1,0:T(8,128)S(1)}, u32[]{:S(2)}, u32[]{:S(2)}) collective-permute-start(f32[280,512]{1,0:T(8,128)S(1)} %fusion.22), channel_id=1, source_target_pairs={{0,1},{1,0},{2,3},{3,2},{4,5},{5,4},{6,7},{7,6},{8,9},{9,8},{10,11... | collective-permute-start | bytes 1720328 | tf_op jit(solution)/shard_map/ppermute | solution.py:145
  29.2 9.2 %collective-permute-start.5 = (f32[140,512]{1,0:T(8,128)S(1)}, f32[140,512]{1,0:T(8,128)S(1)}, u32[]{:S(2)}, u32[]{:S(2)}) collective-permute-start(f32[140,512]{1,0:T(8,128)S(1)} %slice_select_fusion), channel_id=1, source_target_pairs={{0,2},{1,3},{2,0},{3,1},{4,6},{5,7},{6,4},{7,5},{8,10},{9,11},{10,... | collective-permute-start | bytes 860168 | tf_op jit(solution)/shard_map/ppermute | solution.py:145
  38.6 5.3 %collective-permute-start.6 = (f32[70,512]{1,0:T(8,128)S(1)}, f32[70,512]{1,0:T(8,128)S(1)}, u32[]{:S(2)}, u32[]{:S(2)}) collective-permute-start(f32[70,512]{1,0:T(8,128)S(1)} %slice_select_fusion.1), channel_id=1, source_target_pairs={{0,4},{1,5},{2,6},{3,7},{4,0},{5,1},{6,2},{7,3},{8,12},{9,13},{10,... | collective-permute-start | bytes 430088 | tf_op jit(solution)/shard_map/ppermute | solution.py:145
  43.9 5.6 %collective-permute-start.7 = (f32[35,512]{1,0:T(8,128)S(1)}, f32[35,512]{1,0:T(8,128)S(1)}, u32[]{:S(2)}, u32[]{:S(2)}) collective-permute-start(f32[35,512]{1,0:T(8,128)S(1)} %slice_select_fusion.2), channel_id=1, source_target_pairs={{0,8},{1,9},{2,10},{3,11},{4,12},{5,13},{6,14},{7,15},{8,0},{9,1},... | collective-permute-start | bytes 215048 | tf_op jit(solution)/shard_map/ppermute | solution.py:145
  49.5 5.5 %collective-permute-start.8 = (f32[35,512]{1,0:T(8,128)S(1)}, f32[35,512]{1,0:T(8,128)S(1)}, u32[]{:S(2)}, u32[]{:S(2)}) collective-permute-start(f32[35,512]{1,0:T(8,128)S(1)} %select_add_fusion.3), channel_id=1, source_target_pairs={{0,8},{1,9},{2,10},{3,11},{4,12},{5,13},{6,14},{7,15},{8,0},{9,1},... | collective-permute-start | bytes 215048 | tf_op jit(solution)/shard_map/ppermute | solution.py:149
  55.0 5.4 %collective-permute-start.9 = (f32[70,512]{1,0:T(8,128)S(1)}, f32[70,512]{1,0:T(8,128)S(1)}, u32[]{:S(2)}, u32[]{:S(2)}) collective-permute-start(f32[70,512]{1,0:T(8,128)S(1)} %maximum_select_fusion.3), channel_id=1, source_target_pairs={{0,4},{1,5},{2,6},{3,7},{4,0},{5,1},{6,2},{7,3},{8,12},{9,13},{10,... | collective-permute-start | bytes 430088 | tf_op jit(solution)/shard_map/ppermute | solution.py:149
  60.5 6.8 %collective-permute-start.10 = (f32[140,512]{1,0:T(8,128)S(1)}, f32[140,512]{1,0:T(8,128)S(1)}, u32[]{:S(2)}, u32[]{:S(2)}) collective-permute-start(f32[140,512]{1,0:T(8,128)S(1)} %maximum_select_fusion.2), channel_id=1, source_target_pairs={{0,2},{1,3},{2,0},{3,1},{4,6},{5,7},{6,4},{7,5},{8,10},{9,11},{10,... | collective-permute-start | bytes 860168 | tf_op jit(solution)/shard_map/ppermute | solution.py:149
  67.4 2.0 %collective-permute-start.11 = (f32[280,512]{1,0:T(8,128)S(1)}, f32[280,512]{1,0:T(8,128)S(1)}, u32[]{:S(2)}, u32[]{:S(2)}) collective-permute-start(f32[280,512]{1,0:T(8,128)S(1)} %maximum_select_fusion.1), channel_id=1, source_target_pairs={{0,1},{1,0},{2,3},{3,2},{4,5},{5,4},{6,7},{7,6},{8,9},{9,8},{10,11... | collective-permute-start | bytes 1720328 | tf_op jit(solution)/shard_map/ppermute | solution.py:149

commit v4 on v3

--- a/solution.py
+++ b/solution.py
@@ -131,7 +131,7 @@
     return values
 
 
-def sum_halving(values, axis_name):
+def sum_halving(values, axis_name, wire=jnp.bfloat16):
     count = lax.axis_size(axis_name)
     if not _is_power_of_two(count) or values.shape[0] % count != 0:
         return lax.psum(values, axis_name)
@@ -141,9 +141,11 @@
         half = values.shape[0] // 2
         lower = (position // distance) % 2 == 0
         keep = jnp.where(lower, values[:half], values[half:])
-        send = jnp.where(lower, values[half:], values[:half])
-        values = keep + lax.ppermute(send, axis_name, _exchange_pairs(count, distance))
+        send = jnp.where(lower, values[half:], values[:half]).astype(wire)
+        arrived = lax.ppermute(send, axis_name, _exchange_pairs(count, distance))
+        values = keep + arrived.astype(keep.dtype)
         distance *= 2
+    values = values.astype(wire)
     distance = count // 2
     while distance >= 1:
         other = lax.ppermute(values, axis_name, _exchange_pairs(count, distance))
@@ -205,7 +207,7 @@
         ],
         0,
     )
-    packed = sum_halving(packed, "freq")
+    packed = sum_halving(packed, "freq").astype(jnp.float32)
     derivative_bottleneck = packed[:samples]
     grad_filter = packed[samples].reshape(grad_filter.shape)
     grad_out = packed[samples + 1 : packed_rows]

time: 76.5 us -> 68.1 us (0.89)
  waiting for transfers between devices: 31.5 us -> 23.3 us
    ppermute x4, waiting for transfers between devices: 15.1 us -> 10.3 us  [sum_halving(): arrived = lax.ppermute(send, axis_name, _exchange_pairs(count, distance))]
    ppermute x4, waiting for transfers between devices: 12.8 us -> 9.44 us  [sum_halving(): other = lax.ppermute(values, axis_name, _exchange_pairs(count, distance))]
where the time goes in v4:
time: 68.1 us; the launch traced here: 67.8 us
  waiting for transfers between devices  23.3 us (34%)
  starting transfers between devices  22.2 us (33%)
  matrix products  10.1 us (15%)
  other arithmetic  6.45 us (9%)
  local copies, waits for them, and re-layouts  4.71 us (7%)
  between operations  1.01 us (1%)
    ppermute x4, waiting for transfers between devices, sum_halving(): arrived = lax.ppermute(send, axis_name, _exchange_pairs(count, distance))  10.3 us
    ppermute x4, waiting for transfers between devices, sum_halving(): other = lax.ppermute(values, axis_name, _exchange_pairs(count, distance))  9.44 us
    ppermute x4, starting transfers between devices, gather_rows(): other = lax.ppermute(block, axis_name, _exchange_pairs(count, distance))  8.38 us
    ppermute x4, starting transfers between devices, sum_halving(): other = lax.ppermute(values, axis_name, _exchange_pairs(count, distance))  6.91 us
    ppermute x4, starting transfers between devices, sum_halving(): arrived = lax.ppermute(send, axis_name, _exchange_pairs(count, distance))  6.86 us
    ppermute x4, waiting for transfers between devices, gather_rows(): other = lax.ppermute(block, axis_name, _exchange_pairs(count, distance))  3.65 us
    dot_general x1, matrix products, encoder_grads(): lax.dot_general(inputs_rows, grad_pre, (((0,), (0,)), ((), ())), preferre...  2.96 us
    another operation x4, other arithmetic  2.75 us
  transfers between devices with their start and end apart: 12, of which 11 were waited for; matrix products, arithmetic and copies ran while one was open for 7% of the time, Pallas kernels for 0%

profile of v4, /device:TPU:0, one launch (start us, length us, event | category | flops | bytes accessed | tf_op | source)
XLA Modules:
  0.0 67.8 jit_solution(11530870113944617116)
XLA Ops:
  5.0 2.6 %collective-permute-start.1 = (bf16[4,2048]{1,0:T(4,128)(2,1)S(1)}, bf16[4,2048]{1,0:T(4,128)(2,1)S(1)}, u32[]{:S(2)}, u32[]{:S(2)}) collective-permute-start(bf16[4,2048]{1,0:T(4,128)(2,1)S(1)} %maximum_select_fusion.9), channel_id=1, source_target_pairs={{0,2},{1,3},{2,0},{3,1},{4,6},{5,7},{6,4},{7,5},{8,10},{9,11},{10,... | collective-permute-start | bytes 49160 | tf_op jit(solution)/shard_map/ppermute | solution.py:114
  7.6 1.1 %negate_convert_fusion = (bf16[256,256]{1,0:T(8,128)(2,1)S(1)}, bf16[256,256]{1,0:T(8,128)(2,1)S(1)}) fusion(), kind=kLoop, calls=%fused_computation.63 | loop fusion | flops 1245184 | bytes 262144 | tf_op jit(solution)/shard_map/convert.16
  9.4 2.1 %collective-permute-start.2 = (bf16[8,2048]{1,0:T(8,128)(2,1)S(1)}, bf16[8,2048]{1,0:T(8,128)(2,1)S(1)}, u32[]{:S(2)}, u32[]{:S(2)}) collective-permute-start(bf16[8,2048]{1,0:T(8,128)(2,1)S(1)} %maximum_select_fusion.6), channel_id=1, source_target_pairs={{0,4},{1,5},{2,6},{3,7},{4,0},{5,1},{6,2},{7,3},{8,12},{9,13},{10,... | collective-permute-start | bytes 98312 | tf_op jit(solution)/shard_map/ppermute | solution.py:114
  11.5 1.0 %fusion.32 = bf16[256,256]{1,0:T(8,128)(2,1)S(1)} fusion(), kind=kLoop, calls=%fused_computation.69 | loop fusion | flops 1048576 | bytes 131072 | tf_op jit(solution)/shard_map/convert.13
  13.4 3.1 %collective-permute-start.3 = (bf16[16,2048]{1,0:T(8,128)(2,1)S(1)}, bf16[16,2048]{1,0:T(8,128)(2,1)S(1)}, u32[]{:S(2)}, u32[]{:S(2)}) collective-permute-start(bf16[16,2048]{1,0:T(8,128)(2,1)S(1)} %maximum_select_fusion.5), channel_id=1, source_target_pairs={{0,8},{1,9},{2,10},{3,11},{4,12},{5,13},{6,14},{7,15},{8,0},{9,1},... | collective-permute-start | bytes 196616 | tf_op jit(solution)/shard_map/ppermute | solution.py:114
  16.5 2.2 %collective-permute-done.3 = bf16[16,2048]{1,0:T(8,128)(2,1)S(1)} collective-permute-done((bf16[16,2048]{1,0:T(8,128)(2,1)S(1)}, bf16[16,2048]{1,0:T(8,128)(2,1)S(1)}, u32[]{:S(2)}, u32[]{:S(2)}) %collective-permute-start.3) | collective-permute-done | bytes 65568 | tf_op jit(solution)/shard_map/ppermute | solution.py:114
  24.2 1.2 %fusion.18 = f32[768,512]{1,0:T(8,128)S(1)} fusion(f32[768,512]{1,0:T(8,128)S(1)} %get-tuple-element.17, f32[768,512]{1,0:T(8,128)S(1)} %convolution_add_fusion.1, bf16[256,256]{1,0:T(8,128)(2,1)S(1)} %get-tuple-element.19, bf16[256,256]{1,0:T(8,128)(2,1)S(1)} %get-tuple-element.18, bf16[256,256]{1,0:T(8,128)(2,1)S(1)} %fusion.32), kind=kOutput, calls=%fused_computation.38 | convolution fusion | flops 412614656 | bytes 5111808 | tf_op jit(solution)/shard_map/dot_general | solution.py:64
  27.0 1.6 %collective-permute-done.4 = bf16[280,512]{1,0:T(8,128)(2,1)S(1)} collective-permute-done((bf16[280,512]{1,0:T(8,128)(2,1)S(1)}, bf16[280,512]{1,0:T(8,128)(2,1)S(1)}, u32[]{:S(2)}, u32[]{:S(2)}) %collective-permute-start.4) | collective-permute-done | bytes 286752 | tf_op jit(solution)/shard_map/ppermute | solution.py:145
  28.8 1.9 %collective-permute-start.5 = (bf16[140,512]{1,0:T(8,128)(2,1)S(1)}, bf16[140,512]{1,0:T(8,128)(2,1)S(1)}, u32[]{:S(2)}, u32[]{:S(2)}) collective-permute-start(bf16[140,512]{1,0:T(8,128)(2,1)S(1)} %select_convert_fusion.1), channel_id=1, source_target_pairs={{0,2},{1,3},{2,0},{3,1},{4,6},{5,7},{6,4},{7,5},{8,10},{9,11},{10,... | collective-permute-start | bytes 430088 | tf_op jit(solution)/shard_map/ppermute | solution.py:145
  30.7 4.1 %collective-permute-done.5 = bf16[140,512]{1,0:T(8,128)(2,1)S(1)} collective-permute-done((bf16[140,512]{1,0:T(8,128)(2,1)S(1)}, bf16[140,512]{1,0:T(8,128)(2,1)S(1)}, u32[]{:S(2)}, u32[]{:S(2)}) %collective-permute-start.5) | collective-permute-done | bytes 143392 | tf_op jit(solution)/shard_map/ppermute | solution.py:145
  35.0 1.9 %collective-permute-start.6 = (bf16[70,512]{1,0:T(8,128)(2,1)S(1)}, bf16[70,512]{1,0:T(8,128)(2,1)S(1)}, u32[]{:S(2)}, u32[]{:S(2)}) collective-permute-start(bf16[70,512]{1,0:T(8,128)(2,1)S(1)} %select_convert_fusion.2), channel_id=1, source_target_pairs={{0,4},{1,5},{2,6},{3,7},{4,0},{5,1},{6,2},{7,3},{8,12},{9,13},{10,... | collective-permute-start | bytes 215048 | tf_op jit(solution)/shard_map/ppermute | solution.py:145
  36.8 2.6 %collective-permute-done.6 = bf16[70,512]{1,0:T(8,128)(2,1)S(1)} collective-permute-done((bf16[70,512]{1,0:T(8,128)(2,1)S(1)}, bf16[70,512]{1,0:T(8,128)(2,1)S(1)}, u32[]{:S(2)}, u32[]{:S(2)}) %collective-permute-start.6) | collective-permute-done | bytes 71712 | tf_op jit(solution)/shard_map/ppermute | solution.py:145
  39.4 3.0 %collective-permute-start.7 = (bf16[35,512]{1,0:T(8,128)(2,1)S(1)}, bf16[35,512]{1,0:T(8,128)(2,1)S(1)}, u32[]{:S(2)}, u32[]{:S(2)}) collective-permute-start(bf16[35,512]{1,0:T(8,128)(2,1)S(1)} %select_convert_fusion.3), channel_id=1, source_target_pairs={{0,8},{1,9},{2,10},{3,11},{4,12},{5,13},{6,14},{7,15},{8,0},{9,1},... | collective-permute-start | bytes 107528 | tf_op jit(solution)/shard_map/ppermute | solution.py:145
  42.4 2.0 %collective-permute-done.7 = bf16[35,512]{1,0:T(8,128)(2,1)S(1)} collective-permute-done((bf16[35,512]{1,0:T(8,128)(2,1)S(1)}, bf16[35,512]{1,0:T(8,128)(2,1)S(1)}, u32[]{:S(2)}, u32[]{:S(2)}) %collective-permute-start.7) | collective-permute-done | bytes 35872 | tf_op jit(solution)/shard_map/ppermute | solution.py:145
  44.5 3.0 %collective-permute-start.8 = (bf16[35,512]{1,0:T(8,128)(2,1)S(1)}, bf16[35,512]{1,0:T(8,128)(2,1)S(1)}, u32[]{:S(2)}, u32[]{:S(2)}) collective-permute-start(bf16[35,512]{1,0:T(8,128)(2,1)S(1)} %add_convert_fusion.3), channel_id=1, source_target_pairs={{0,8},{1,9},{2,10},{3,11},{4,12},{5,13},{6,14},{7,15},{8,0},{9,1},... | collective-permute-start | bytes 107528 | tf_op jit(solution)/shard_map/ppermute | solution.py:151
  47.4 2.1 %collective-permute-done.8 = bf16[35,512]{1,0:T(8,128)(2,1)S(1)} collective-permute-done((bf16[35,512]{1,0:T(8,128)(2,1)S(1)}, bf16[35,512]{1,0:T(8,128)(2,1)S(1)}, u32[]{:S(2)}, u32[]{:S(2)}) %collective-permute-start.8) | collective-permute-done | bytes 35872 | tf_op jit(solution)/shard_map/ppermute | solution.py:151
  49.6 2.1 %collective-permute-start.9 = (bf16[70,512]{1,0:T(8,128)(2,1)S(1)}, bf16[70,512]{1,0:T(8,128)(2,1)S(1)}, u32[]{:S(2)}, u32[]{:S(2)}) collective-permute-start(bf16[70,512]{1,0:T(8,128)(2,1)S(1)} %maximum_select_fusion.4), channel_id=1, source_target_pairs={{0,4},{1,5},{2,6},{3,7},{4,0},{5,1},{6,2},{7,3},{8,12},{9,13},{10,... | collective-permute-start | bytes 215048 | tf_op jit(solution)/shard_map/ppermute | solution.py:151
  51.7 2.3 %collective-permute-done.9 = bf16[70,512]{1,0:T(8,128)(2,1)S(1)} collective-permute-done((bf16[70,512]{1,0:T(8,128)(2,1)S(1)}, bf16[70,512]{1,0:T(8,128)(2,1)S(1)}, u32[]{:S(2)}, u32[]{:S(2)}) %collective-permute-start.9) | collective-permute-done | bytes 71712 | tf_op jit(solution)/shard_map/ppermute | solution.py:151
  54.1 1.7 %collective-permute-start.10 = (bf16[140,512]{1,0:T(8,128)(2,1)S(1)}, bf16[140,512]{1,0:T(8,128)(2,1)S(1)}, u32[]{:S(2)}, u32[]{:S(2)}) collective-permute-start(bf16[140,512]{1,0:T(8,128)(2,1)S(1)} %maximum_select_fusion.2), channel_id=1, source_target_pairs={{0,2},{1,3},{2,0},{3,1},{4,6},{5,7},{6,4},{7,5},{8,10},{9,11},{10,... | collective-permute-start | bytes 430088 | tf_op jit(solution)/shard_map/ppermute | solution.py:151
  55.8 3.5 %collective-permute-done.10 = bf16[140,512]{1,0:T(8,128)(2,1)S(1)} collective-permute-done((bf16[140,512]{1,0:T(8,128)(2,1)S(1)}, bf16[140,512]{1,0:T(8,128)(2,1)S(1)}, u32[]{:S(2)}, u32[]{:S(2)}) %collective-permute-start.10) | collective-permute-done | bytes 143392 | tf_op jit(solution)/shard_map/ppermute | solution.py:151
  59.5 1.5 %collective-permute-done.11 = bf16[280,512]{1,0:T(8,128)(2,1)S(1)} collective-permute-done((bf16[280,512]{1,0:T(8,128)(2,1)S(1)}, bf16[280,512]{1,0:T(8,128)(2,1)S(1)}, u32[]{:S(2)}, u32[]{:S(2)}) %collective-permute-start.11) | collective-permute-done | bytes 286752 | tf_op jit(solution)/shard_map/ppermute | solution.py:151
  61.2 1.1 %slice.93 = f32[512,512]{1,0:T(8,128)} slice(f32[560,512]{1,0:T(8,128)S(1)} %fusion.20), slice={[33:545], [0:512]} | slice | bytes 2097152 | tf_op jit(solution)/shard_map/slice | solution.py:213
  62.9 1.3 %fusion.63 = f32[512,512]{1,0:T(8,128)} fusion(bf16[32,512]{1,0:T(8,128)(2,1)S(1)} %fusion.8, bf16[32,512]{1,0:T(8,128)(2,1)S(1)} %gather_fusion.1), kind=kOutput, calls=%fused_computation.112 | convolution fusion | flops 16777216 | bytes 1114112 | tf_op jit(solution)/shard_map/dot_general | solution.py:86
  64.8 3.0 %fusion.10 = f32[2048,512]{1,0:T(8,128)} fusion(bf16[512,512]{1,0:T(8,128)(2,1)S(1)} %copy-done.1, bf16[32,512]{1,0:T(8,128)(2,1)S(1)} %fusion.8, bf16[16,2048]{1,0:T(8,128)(2,1)S(1)} %collective-permute-done.3, bf16[16,2048]{1,0:T(8,128)(2,1)S(1)} %maximum_select_fusion.5, pred[]{:T(512)S(6)} %eq.35, bf16[32,512]{1,0:T(8,128)(2,1)S(1)} %gather_fusion.1), kind=kOutput, calls=%fused_computation.23 | convolution fusion | flops 84557824 | bytes 4915201 | tf_op jit(solution)/shard_map/dot_general | solution.py:93
  (56 shorter events, 14.7 us)
Async XLA Ops:
  0.6 18.1 %copy-start = (bf16[2048,512]{1,0:T(8,128)(2,1)S(1)}, bf16[2048,512]{1,0:T(8,128)(2,1)}, u32[]{:S(2)}) copy-start(bf16[2048,512]{1,0:T(8,128)(2,1)} %param.11) | copy-start | bytes 6291460
  0.6 3.5 %collective-permute-start = (bf16[2,2048]{1,0:T(2,128)(2,1)}, bf16[2,2048]{1,0:T(2,128)(2,1)S(1)}, u32[]{:S(2)}, u32[]{:S(2)}) collective-permute-start(bf16[2,2048]{1,0:T(2,128)(2,1)} %param.8), channel_id=1, source_target_pairs={{0,1},{1,0},{2,3},{3,2},{4,5},{5,4},{6,7},{7,6},{8,9},{9,8},{10,11... | collective-permute-start | bytes 24584 | tf_op jit(solution)/shard_map/ppermute | solution.py:114
  5.0 4.3 %collective-permute-start.1 = (bf16[4,2048]{1,0:T(4,128)(2,1)S(1)}, bf16[4,2048]{1,0:T(4,128)(2,1)S(1)}, u32[]{:S(2)}, u32[]{:S(2)}) collective-permute-start(bf16[4,2048]{1,0:T(4,128)(2,1)S(1)} %maximum_select_fusion.9), channel_id=1, source_target_pairs={{0,2},{1,3},{2,0},{3,1},{4,6},{5,7},{6,4},{7,5},{8,10},{9,11},{10,... | collective-permute-start | bytes 49160 | tf_op jit(solution)/shard_map/ppermute | solution.py:114
  8.7 11.2 %copy-start.1 = (bf16[512,512]{1,0:T(8,128)(2,1)S(1)}, bf16[512,512]{1,0:T(8,128)(2,1)}, u32[]{:S(2)}) copy-start(bf16[512,512]{1,0:T(8,128)(2,1)} %param.12) | copy-start | bytes 1572868
  9.4 4.0 %collective-permute-start.2 = (bf16[8,2048]{1,0:T(8,128)(2,1)S(1)}, bf16[8,2048]{1,0:T(8,128)(2,1)S(1)}, u32[]{:S(2)}, u32[]{:S(2)}) collective-permute-start(bf16[8,2048]{1,0:T(8,128)(2,1)S(1)} %maximum_select_fusion.6), channel_id=1, source_target_pairs={{0,4},{1,5},{2,6},{3,7},{4,0},{5,1},{6,2},{7,3},{8,12},{9,13},{10,... | collective-permute-start | bytes 98312 | tf_op jit(solution)/shard_map/ppermute | solution.py:114
  13.4 5.3 %collective-permute-start.3 = (bf16[16,2048]{1,0:T(8,128)(2,1)S(1)}, bf16[16,2048]{1,0:T(8,128)(2,1)S(1)}, u32[]{:S(2)}, u32[]{:S(2)}) collective-permute-start(bf16[16,2048]{1,0:T(8,128)(2,1)S(1)} %maximum_select_fusion.5), channel_id=1, source_target_pairs={{0,8},{1,9},{2,10},{3,11},{4,12},{5,13},{6,14},{7,15},{8,0},{9,1},... | collective-permute-start | bytes 196616 | tf_op jit(solution)/shard_map/ppermute | solution.py:114
  21.0 1.0 %copy-start.2 = (bf16[512,512]{1,0:T(8,128)(2,1)S(1)}, bf16[512,512]{1,0:T(8,128)(2,1)}, u32[]{:S(2)}) copy-start(bf16[512,512]{1,0:T(8,128)(2,1)} %param.15) | copy-start | bytes 1572868
  21.1 1.3 %copy-start.3 = (bf16[32,24,512]{2,1,0:T(8,128)(2,1)S(1)}, bf16[32,24,512]{2,1,0:T(8,128)(2,1)}, u32[]{:S(2)}) copy-start(bf16[32,24,512]{2,1,0:T(8,128)(2,1)} %param.9) | copy-start | bytes 2359300
  26.9 1.6 %collective-permute-start.4 = (bf16[280,512]{1,0:T(8,128)(2,1)S(1)}, bf16[280,512]{1,0:T(8,128)(2,1)S(1)}, u32[]{:S(2)}, u32[]{:S(2)}) collective-permute-start(bf16[280,512]{1,0:T(8,128)(2,1)S(1)} %select_convert_fusion), channel_id=1, source_target_pairs={{0,1},{1,0},{2,3},{3,2},{4,5},{5,4},{6,7},{7,6},{8,9},{9,8},{10,11... | collective-permute-start | bytes 860168 | tf_op jit(solution)/shard_map/ppermute | solution.py:145
  28.8 6.1 %collective-permute-start.5 = (bf16[140,512]{1,0:T(8,128)(2,1)S(1)}, bf16[140,512]{1,0:T(8,128)(2,1)S(1)}, u32[]{:S(2)}, u32[]{:S(2)}) collective-permute-start(bf16[140,512]{1,0:T(8,128)(2,1)S(1)} %select_convert_fusion.1), channel_id=1, source_target_pairs={{0,2},{1,3},{2,0},{3,1},{4,6},{5,7},{6,4},{7,5},{8,10},{9,11},{10,... | collective-permute-start | bytes 430088 | tf_op jit(solution)/shard_map/ppermute | solution.py:145
  35.0 4.4 %collective-permute-start.6 = (bf16[70,512]{1,0:T(8,128)(2,1)S(1)}, bf16[70,512]{1,0:T(8,128)(2,1)S(1)}, u32[]{:S(2)}, u32[]{:S(2)}) collective-permute-start(bf16[70,512]{1,0:T(8,128)(2,1)S(1)} %select_convert_fusion.2), channel_id=1, source_target_pairs={{0,4},{1,5},{2,6},{3,7},{4,0},{5,1},{6,2},{7,3},{8,12},{9,13},{10,... | collective-permute-start | bytes 215048 | tf_op jit(solution)/shard_map/ppermute | solution.py:145
  39.4 5.0 %collective-permute-start.7 = (bf16[35,512]{1,0:T(8,128)(2,1)S(1)}, bf16[35,512]{1,0:T(8,128)(2,1)S(1)}, u32[]{:S(2)}, u32[]{:S(2)}) collective-permute-start(bf16[35,512]{1,0:T(8,128)(2,1)S(1)} %select_convert_fusion.3), channel_id=1, source_target_pairs={{0,8},{1,9},{2,10},{3,11},{4,12},{5,13},{6,14},{7,15},{8,0},{9,1},... | collective-permute-start | bytes 107528 | tf_op jit(solution)/shard_map/ppermute | solution.py:145
  44.5 5.1 %collective-permute-start.8 = (bf16[35,512]{1,0:T(8,128)(2,1)S(1)}, bf16[35,512]{1,0:T(8,128)(2,1)S(1)}, u32[]{:S(2)}, u32[]{:S(2)}) collective-permute-start(bf16[35,512]{1,0:T(8,128)(2,1)S(1)} %add_convert_fusion.3), channel_id=1, source_target_pairs={{0,8},{1,9},{2,10},{3,11},{4,12},{5,13},{6,14},{7,15},{8,0},{9,1},... | collective-permute-start | bytes 107528 | tf_op jit(solution)/shard_map/ppermute | solution.py:151
  49.6 4.5 %collective-permute-start.9 = (bf16[70,512]{1,0:T(8,128)(2,1)S(1)}, bf16[70,512]{1,0:T(8,128)(2,1)S(1)}, u32[]{:S(2)}, u32[]{:S(2)}) collective-permute-start(bf16[70,512]{1,0:T(8,128)(2,1)S(1)} %maximum_select_fusion.4), channel_id=1, source_target_pairs={{0,4},{1,5},{2,6},{3,7},{4,0},{5,1},{6,2},{7,3},{8,12},{9,13},{10,... | collective-permute-start | bytes 215048 | tf_op jit(solution)/shard_map/ppermute | solution.py:151
  54.1 5.2 %collective-permute-start.10 = (bf16[140,512]{1,0:T(8,128)(2,1)S(1)}, bf16[140,512]{1,0:T(8,128)(2,1)S(1)}, u32[]{:S(2)}, u32[]{:S(2)}) collective-permute-start(bf16[140,512]{1,0:T(8,128)(2,1)S(1)} %maximum_select_fusion.2), channel_id=1, source_target_pairs={{0,2},{1,3},{2,0},{3,1},{4,6},{5,7},{6,4},{7,5},{8,10},{9,11},{10,... | collective-permute-start | bytes 430088 | tf_op jit(solution)/shard_map/ppermute | solution.py:151
  59.4 1.6 %collective-permute-start.11 = (bf16[280,512]{1,0:T(8,128)(2,1)S(1)}, bf16[280,512]{1,0:T(8,128)(2,1)S(1)}, u32[]{:S(2)}, u32[]{:S(2)}) collective-permute-start(bf16[280,512]{1,0:T(8,128)(2,1)S(1)} %maximum_select_fusion.1), channel_id=1, source_target_pairs={{0,1},{1,0},{2,3},{3,2},{4,5},{5,4},{6,7},{7,6},{8,9},{9,8},{10,11... | collective-permute-start | bytes 860168 | tf_op jit(solution)/shard_map/ppermute | solution.py:151

commit v5 on v4

--- a/solution.py
+++ b/solution.py
@@ -131,13 +131,13 @@
     return values
 
 
-def sum_halving(values, axis_name, wire=jnp.bfloat16):
+def sum_halving(values, axis_name, wire=jnp.bfloat16, halving_levels=2):
     count = lax.axis_size(axis_name)
     if not _is_power_of_two(count) or values.shape[0] % count != 0:
         return lax.psum(values, axis_name)
     position = lax.axis_index(axis_name)
     distance = 1
-    while distance < count:
+    while distance < count and distance < 2**halving_levels:
         half = values.shape[0] // 2
         lower = (position // distance) % 2 == 0
         keep = jnp.where(lower, values[:half], values[half:])
@@ -145,8 +145,13 @@
         arrived = lax.ppermute(send, axis_name, _exchange_pairs(count, distance))
         values = keep + arrived.astype(keep.dtype)
         distance *= 2
+    top = distance
     values = values.astype(wire)
-    distance = count // 2
+    while distance < count:
+        arrived = lax.ppermute(values, axis_name, _exchange_pairs(count, distance))
+        values = (values.astype(jnp.float32) + arrived.astype(jnp.float32)).astype(wire)
+        distance *= 2
+    distance = top // 2
     while distance >= 1:
         other = lax.ppermute(values, axis_name, _exchange_pairs(count, distance))
         lower = (position // distance) % 2 == 0
@@ -200,17 +205,18 @@
     padding = -packed_rows % count
     packed = jnp.concatenate(
         [
+            grad_out,
             derivative_bottleneck,
             grad_filter.reshape(1, -1),
-            grad_out,
             jnp.zeros((padding, width), jnp.float32),
         ],
         0,
     )
     packed = sum_halving(packed, "freq").astype(jnp.float32)
-    derivative_bottleneck = packed[:samples]
-    grad_filter = packed[samples].reshape(grad_filter.shape)
-    grad_out = packed[samples + 1 : packed_rows]
+    rows_out = grad_out.shape[0]
+    grad_out = packed[:rows_out]
+    derivative_bottleneck = packed[rows_out : rows_out + samples]
+    grad_filter = packed[rows_out + samples].reshape(grad_filter.shape)
     grad_enc, grad_dec = encoder_grads(
         all_inputs, codes, derivative_bottleneck[sample_index], decoder_weight
     )

time: 68.1 us -> 64.3 us (0.944)
  starting transfers between devices: 22.2 us -> 17.1 us
  waiting for transfers between devices: 23.3 us -> 24.9 us
    ppermute x0 -> x2, waiting for transfers between devices: none -> 9.23 us  [sum_halving(): arrived = lax.ppermute(values, axis_name, _exchange_pairs(count, distance))]
    ppermute x4 -> x2, starting transfers between devices: 6.91 us -> 1.65 us  [sum_halving(): other = lax.ppermute(values, axis_name, _exchange_pairs(count, distance))]
    ppermute x0 -> x2, starting transfers between devices: none -> 5.05 us  [sum_halving(): arrived = lax.ppermute(values, axis_name, _exchange_pairs(count, distance))]
    ppermute x4 -> x2, starting transfers between devices: 6.86 us -> 1.98 us  [sum_halving(): arrived = lax.ppermute(send, axis_name, _exchange_pairs(count, distance))]
    ppermute x4 -> x2, waiting for transfers between devices: 10.3 us -> 5.71 us  [sum_halving(): arrived = lax.ppermute(send, axis_name, _exchange_pairs(count, distance))]
    ppermute x4 -> x2, waiting for transfers between devices: 9.44 us -> 5.17 us  [sum_halving(): other = lax.ppermute(values, axis_name, _exchange_pairs(count, distance))]
    ppermute x4, waiting for transfers between devices: 3.65 us -> 4.75 us  [gather_rows(): other = lax.ppermute(block, axis_name, _exchange_pairs(count, distance))]
  transfers between devices with their start and end apart: 12 -> 10, of which waited for: 11 -> 9; matrix products, arithmetic and copies ran while one was open for 7% -> 8% of each run, Pallas kernels for 0% -> 0%
where the time goes in v5:
time: 64.3 us; the launch traced here: 64 us
  waiting for transfers between devices  24.9 us (39%)
  starting transfers between devices  17.1 us (27%)
  matrix products  10.1 us (16%)
  other arithmetic  6.31 us (10%)
  local copies, waits for them, and re-layouts  4.74 us (7%)
  between operations  0.94 us (1%)
    ppermute x2, waiting for transfers between devices, sum_halving(): arrived = lax.ppermute(values, axis_name, _exchange_pairs(count, distance))  9.23 us
    ppermute x4, starting transfers between devices, gather_rows(): other = lax.ppermute(block, axis_name, _exchange_pairs(count, distance))  8.38 us
    ppermute x2, waiting for transfers between devices, sum_halving(): arrived = lax.ppermute(send, axis_name, _exchange_pairs(count, distance))  5.71 us
    ppermute x2, waiting for transfers between devices, sum_halving(): other = lax.ppermute(values, axis_name, _exchange_pairs(count, distance))  5.17 us
    ppermute x2, starting transfers between devices, sum_halving(): arrived = lax.ppermute(values, axis_name, _exchange_pairs(count, distance))  5.05 us
    ppermute x4, waiting for transfers between devices, gather_rows(): other = lax.ppermute(block, axis_name, _exchange_pairs(count, distance))  4.75 us
    dot_general x1, matrix products, encoder_grads(): lax.dot_general(inputs_rows, grad_pre, (((0,), (0,)), ((), ())), preferre...  2.96 us
    another operation x4, other arithmetic  2.76 us
  transfers between devices with their start and end apart: 10, of which 9 were waited for; matrix products, arithmetic and copies ran while one was open for 8% of the time, Pallas kernels for 0%

profile of v5, /device:TPU:0, one launch (start us, length us, event | category | flops | bytes accessed | tf_op | source)
XLA Modules:
  0.0 64.0 jit_solution(9423952383976096878)
XLA Ops:
  1.2 0.9 %bitcast_convert_fusion = (f32[512,24]{0,1:T(8,128)S(1)}, f32[24,512]{1,0:T(8,128)S(1)}) fusion(bf16[24,512]{1,0:T(8,128)(2,1)} %param.13), kind=kLoop, calls=%fused_computation.80 | loop fusion | flops 24576 | bytes 122880
  4.1 1.1 %negate_convert_fusion = (bf16[256,256]{1,0:T(8,128)(2,1)S(1)}, bf16[256,256]{1,0:T(8,128)(2,1)S(1)}) fusion(), kind=kLoop, calls=%fused_computation.65 | loop fusion | flops 1245184 | bytes 262144 | tf_op jit(solution)/shard_map/convert.16
  5.3 0.8 %maximum_select_fusion.7 = bf16[4,2048]{1,0:T(4,128)(2,1)S(1)} fusion(bf16[2,2048]{1,0:T(2,128)(2,1)S(1)} %collective-permute-done, bf16[2,2048]{1,0:T(2,128)(2,1)} %param.8, pred[]{:T(512)S(6)} %eq.30), kind=kLoop, calls=%fused_computation.81 | loop fusion | flops 73728 | bytes 32769 | tf_op jit(solution)/shard_map/jit(_where)/select_n | solution.py:116
  6.1 2.6 %collective-permute-start.1 = (bf16[4,2048]{1,0:T(4,128)(2,1)S(1)}, bf16[4,2048]{1,0:T(4,128)(2,1)S(1)}, u32[]{:S(2)}, u32[]{:S(2)}) collective-permute-start(bf16[4,2048]{1,0:T(4,128)(2,1)S(1)} %maximum_select_fusion.7), channel_id=1, source_target_pairs={{0,2},{1,3},{2,0},{3,1},{4,6},{5,7},{6,4},{7,5},{8,10},{9,11},{10,... | collective-permute-start | bytes 49160 | tf_op jit(solution)/shard_map/ppermute | solution.py:114
  8.7 1.0 %fusion.33 = bf16[256,256]{1,0:T(8,128)(2,1)S(1)} fusion(), kind=kLoop, calls=%fused_computation.71 | loop fusion | flops 1048576 | bytes 131072 | tf_op jit(solution)/shard_map/convert.13
  10.5 2.1 %collective-permute-start.2 = (bf16[8,2048]{1,0:T(8,128)(2,1)S(1)}, bf16[8,2048]{1,0:T(8,128)(2,1)S(1)}, u32[]{:S(2)}, u32[]{:S(2)}) collective-permute-start(bf16[8,2048]{1,0:T(8,128)(2,1)S(1)} %maximum_select_fusion.4), channel_id=1, source_target_pairs={{0,4},{1,5},{2,6},{3,7},{4,0},{5,1},{6,2},{7,3},{8,12},{9,13},{10,... | collective-permute-start | bytes 98312 | tf_op jit(solution)/shard_map/ppermute | solution.py:114
  12.6 1.9 %collective-permute-done.2 = bf16[8,2048]{1,0:T(8,128)(2,1)S(1)} collective-permute-done((bf16[8,2048]{1,0:T(8,128)(2,1)S(1)}, bf16[8,2048]{1,0:T(8,128)(2,1)S(1)}, u32[]{:S(2)}, u32[]{:S(2)}) %collective-permute-start.2) | collective-permute-done | bytes 32800 | tf_op jit(solution)/shard_map/ppermute | solution.py:114
  14.5 3.1 %collective-permute-start.3 = (bf16[16,2048]{1,0:T(8,128)(2,1)S(1)}, bf16[16,2048]{1,0:T(8,128)(2,1)S(1)}, u32[]{:S(2)}, u32[]{:S(2)}) collective-permute-start(bf16[16,2048]{1,0:T(8,128)(2,1)S(1)} %maximum_select_fusion.3), channel_id=1, source_target_pairs={{0,8},{1,9},{2,10},{3,11},{4,12},{5,13},{6,14},{7,15},{8,0},{9,1},... | collective-permute-start | bytes 196616 | tf_op jit(solution)/shard_map/ppermute | solution.py:114
  17.7 2.2 %collective-permute-done.3 = bf16[16,2048]{1,0:T(8,128)(2,1)S(1)} collective-permute-done((bf16[16,2048]{1,0:T(8,128)(2,1)S(1)}, bf16[16,2048]{1,0:T(8,128)(2,1)S(1)}, u32[]{:S(2)}, u32[]{:S(2)}) %collective-permute-start.3) | collective-permute-done | bytes 65568 | tf_op jit(solution)/shard_map/ppermute | solution.py:114
  22.2 1.0 %add_convert_fusion = (bf16[768,512]{1,0:T(8,128)(2,1)S(1)}, f32[768,512]{1,0:T(8,128)S(1)}) fusion(bf16[32,24,512]{2,1,0:T(8,128)(2,1)S(1)} %multiply_convert_fusion, bf16[256,256]{1,0:T(8,128)(2,1)S(1)} %get-tuple-element.19, bf16[256,256]{1,0:T(8,128)(2,1)S(1)} %get-tuple-element.18, bf16[256,256]{1,0:T(8,128)(2,1)S(1)} %fusion.33, ...), kind=kOutput, calls=%fused_computation.15 | convolution fusion | flops 410648576 | bytes 4325376 | tf_op jit(solution)/shard_map/dot_general | solution.py:50
  25.3 1.2 %fusion.18 = f32[768,512]{1,0:T(8,128)S(1)} fusion(f32[768,512]{1,0:T(8,128)S(1)} %get-tuple-element.17, f32[768,512]{1,0:T(8,128)S(1)} %convolution_add_fusion.1, bf16[256,256]{1,0:T(8,128)(2,1)S(1)} %get-tuple-element.19, bf16[256,256]{1,0:T(8,128)(2,1)S(1)} %get-tuple-element.18, bf16[256,256]{1,0:T(8,128)(2,1)S(1)} %fusion.33), kind=kOutput, calls=%fused_computation.37 | convolution fusion | flops 412614656 | bytes 5111808 | tf_op jit(solution)/shard_map/dot_general | solution.py:64
  28.1 1.6 %collective-permute-done.4 = bf16[280,512]{1,0:T(8,128)(2,1)S(1)} collective-permute-done((bf16[280,512]{1,0:T(8,128)(2,1)S(1)}, bf16[280,512]{1,0:T(8,128)(2,1)S(1)}, u32[]{:S(2)}, u32[]{:S(2)}) %collective-permute-start.4) | collective-permute-done | bytes 286752 | tf_op jit(solution)/shard_map/ppermute | solution.py:145
  29.9 1.9 %collective-permute-start.5 = (bf16[140,512]{1,0:T(8,128)(2,1)S(1)}, bf16[140,512]{1,0:T(8,128)(2,1)S(1)}, u32[]{:S(2)}, u32[]{:S(2)}) collective-permute-start(bf16[140,512]{1,0:T(8,128)(2,1)S(1)} %select_convert_fusion.1), channel_id=1, source_target_pairs={{0,2},{1,3},{2,0},{3,1},{4,6},{5,7},{6,4},{7,5},{8,10},{9,11},{10,... | collective-permute-start | bytes 430088 | tf_op jit(solution)/shard_map/ppermute | solution.py:145
  31.8 4.1 %collective-permute-done.5 = bf16[140,512]{1,0:T(8,128)(2,1)S(1)} collective-permute-done((bf16[140,512]{1,0:T(8,128)(2,1)S(1)}, bf16[140,512]{1,0:T(8,128)(2,1)S(1)}, u32[]{:S(2)}, u32[]{:S(2)}) %collective-permute-start.5) | collective-permute-done | bytes 143392 | tf_op jit(solution)/shard_map/ppermute | solution.py:145
  36.0 1.9 %collective-permute-start.6 = (bf16[140,512]{1,0:T(8,128)(2,1)S(1)}, bf16[140,512]{1,0:T(8,128)(2,1)S(1)}, u32[]{:S(2)}, u32[]{:S(2)}) collective-permute-start(bf16[140,512]{1,0:T(8,128)(2,1)S(1)} %add_convert_fusion.5), channel_id=1, source_target_pairs={{0,4},{1,5},{2,6},{3,7},{4,0},{5,1},{6,2},{7,3},{8,12},{9,13},{10,... | collective-permute-start | bytes 430088 | tf_op jit(solution)/shard_map/ppermute | solution.py:151
  37.9 3.4 %collective-permute-done.6 = bf16[140,512]{1,0:T(8,128)(2,1)S(1)} collective-permute-done((bf16[140,512]{1,0:T(8,128)(2,1)S(1)}, bf16[140,512]{1,0:T(8,128)(2,1)S(1)}, u32[]{:S(2)}, u32[]{:S(2)}) %collective-permute-start.6) | collective-permute-done | bytes 143392 | tf_op jit(solution)/shard_map/ppermute | solution.py:151
  41.3 3.2 %collective-permute-start.7 = (bf16[140,512]{1,0:T(8,128)(2,1)S(1)}, bf16[140,512]{1,0:T(8,128)(2,1)S(1)}, u32[]{:S(2)}, u32[]{:S(2)}) collective-permute-start(bf16[140,512]{1,0:T(8,128)(2,1)S(1)} %add_convert_fusion.4), channel_id=1, source_target_pairs={{0,8},{1,9},{2,10},{3,11},{4,12},{5,13},{6,14},{7,15},{8,0},{9,1},... | collective-permute-start | bytes 430088 | tf_op jit(solution)/shard_map/ppermute | solution.py:151
  44.5 5.9 %collective-permute-done.7 = bf16[140,512]{1,0:T(8,128)(2,1)S(1)} collective-permute-done((bf16[140,512]{1,0:T(8,128)(2,1)S(1)}, bf16[140,512]{1,0:T(8,128)(2,1)S(1)}, u32[]{:S(2)}, u32[]{:S(2)}) %collective-permute-start.7) | collective-permute-done | bytes 143392 | tf_op jit(solution)/shard_map/ppermute | solution.py:151
  50.4 1.6 %collective-permute-start.8 = (bf16[140,512]{1,0:T(8,128)(2,1)S(1)}, bf16[140,512]{1,0:T(8,128)(2,1)S(1)}, u32[]{:S(2)}, u32[]{:S(2)}) collective-permute-start(bf16[140,512]{1,0:T(8,128)(2,1)S(1)} %add_convert_fusion.3), channel_id=1, source_target_pairs={{0,2},{1,3},{2,0},{3,1},{4,6},{5,7},{6,4},{7,5},{8,10},{9,11},{10,... | collective-permute-start | bytes 430088 | tf_op jit(solution)/shard_map/ppermute | solution.py:156
  52.0 3.6 %collective-permute-done.8 = bf16[140,512]{1,0:T(8,128)(2,1)S(1)} collective-permute-done((bf16[140,512]{1,0:T(8,128)(2,1)S(1)}, bf16[140,512]{1,0:T(8,128)(2,1)S(1)}, u32[]{:S(2)}, u32[]{:S(2)}) %collective-permute-start.8) | collective-permute-done | bytes 143392 | tf_op jit(solution)/shard_map/ppermute | solution.py:156
  55.8 1.5 %collective-permute-done.9 = bf16[280,512]{1,0:T(8,128)(2,1)S(1)} collective-permute-done((bf16[280,512]{1,0:T(8,128)(2,1)S(1)}, bf16[280,512]{1,0:T(8,128)(2,1)S(1)}, u32[]{:S(2)}, u32[]{:S(2)}) %collective-permute-start.9) | collective-permute-done | bytes 286752 | tf_op jit(solution)/shard_map/ppermute | solution.py:156
  57.5 1.0 %slice.69 = f32[512,512]{1,0:T(8,128)} slice(f32[560,512]{1,0:T(8,128)S(1)} %fusion.21), slice={[0:512], [0:512]} | slice | bytes 2097152 | tf_op jit(solution)/shard_map/slice | solution.py:217
  59.2 1.3 %fusion.64 = f32[512,512]{1,0:T(8,128)} fusion(bf16[32,512]{1,0:T(8,128)(2,1)S(1)} %fusion.8, bf16[32,512]{1,0:T(8,128)(2,1)S(1)} %gather_fusion.1), kind=kOutput, calls=%fused_computation.109 | convolution fusion | flops 16777216 | bytes 1114112 | tf_op jit(solution)/shard_map/dot_general | solution.py:86
  61.1 3.0 %fusion.10 = f32[2048,512]{1,0:T(8,128)} fusion(bf16[512,512]{1,0:T(8,128)(2,1)S(1)} %copy-done.1, bf16[32,512]{1,0:T(8,128)(2,1)S(1)} %fusion.8, bf16[16,2048]{1,0:T(8,128)(2,1)S(1)} %collective-permute-done.3, bf16[16,2048]{1,0:T(8,128)(2,1)S(1)} %maximum_select_fusion.3, pred[]{:T(512)S(6)} %eq.27, bf16[32,512]{1,0:T(8,128)(2,1)S(1)} %gather_fusion.1), kind=kOutput, calls=%fused_computation.23 | convolution fusion | flops 84557824 | bytes 4915201 | tf_op jit(solution)/shard_map/dot_general | solution.py:93
  (50 shorter events, 11.3 us)
Async XLA Ops:
  0.6 19.3 %copy-start = (bf16[2048,512]{1,0:T(8,128)(2,1)S(1)}, bf16[2048,512]{1,0:T(8,128)(2,1)}, u32[]{:S(2)}) copy-start(bf16[2048,512]{1,0:T(8,128)(2,1)} %param.11) | copy-start | bytes 6291460
  0.6 4.6 %collective-permute-start = (bf16[2,2048]{1,0:T(2,128)(2,1)}, bf16[2,2048]{1,0:T(2,128)(2,1)S(1)}, u32[]{:S(2)}, u32[]{:S(2)}) collective-permute-start(bf16[2,2048]{1,0:T(2,128)(2,1)} %param.8), channel_id=1, source_target_pairs={{0,1},{1,0},{2,3},{3,2},{4,5},{5,4},{6,7},{7,6},{8,9},{9,8},{10,11... | collective-permute-start | bytes 24584 | tf_op jit(solution)/shard_map/ppermute | solution.py:114
  5.3 15.8 %copy-start.1 = (bf16[512,512]{1,0:T(8,128)(2,1)S(1)}, bf16[512,512]{1,0:T(8,128)(2,1)}, u32[]{:S(2)}) copy-start(bf16[512,512]{1,0:T(8,128)(2,1)} %param.12) | copy-start | bytes 1572868
  6.1 4.3 %collective-permute-start.1 = (bf16[4,2048]{1,0:T(4,128)(2,1)S(1)}, bf16[4,2048]{1,0:T(4,128)(2,1)S(1)}, u32[]{:S(2)}, u32[]{:S(2)}) collective-permute-start(bf16[4,2048]{1,0:T(4,128)(2,1)S(1)} %maximum_select_fusion.7), channel_id=1, source_target_pairs={{0,2},{1,3},{2,0},{3,1},{4,6},{5,7},{6,4},{7,5},{8,10},{9,11},{10,... | collective-permute-start | bytes 49160 | tf_op jit(solution)/shard_map/ppermute | solution.py:114
  10.5 4.0 %collective-permute-start.2 = (bf16[8,2048]{1,0:T(8,128)(2,1)S(1)}, bf16[8,2048]{1,0:T(8,128)(2,1)S(1)}, u32[]{:S(2)}, u32[]{:S(2)}) collective-permute-start(bf16[8,2048]{1,0:T(8,128)(2,1)S(1)} %maximum_select_fusion.4), channel_id=1, source_target_pairs={{0,4},{1,5},{2,6},{3,7},{4,0},{5,1},{6,2},{7,3},{8,12},{9,13},{10,... | collective-permute-start | bytes 98312 | tf_op jit(solution)/shard_map/ppermute | solution.py:114
  14.5 5.3 %collective-permute-start.3 = (bf16[16,2048]{1,0:T(8,128)(2,1)S(1)}, bf16[16,2048]{1,0:T(8,128)(2,1)S(1)}, u32[]{:S(2)}, u32[]{:S(2)}) collective-permute-start(bf16[16,2048]{1,0:T(8,128)(2,1)S(1)} %maximum_select_fusion.3), channel_id=1, source_target_pairs={{0,8},{1,9},{2,10},{3,11},{4,12},{5,13},{6,14},{7,15},{8,0},{9,1},... | collective-permute-start | bytes 196616 | tf_op jit(solution)/shard_map/ppermute | solution.py:114
  22.2 1.0 %copy-start.2 = (bf16[512,512]{1,0:T(8,128)(2,1)S(1)}, bf16[512,512]{1,0:T(8,128)(2,1)}, u32[]{:S(2)}) copy-start(bf16[512,512]{1,0:T(8,128)(2,1)} %param.15) | copy-start | bytes 1572868
  22.2 1.3 %copy-start.3 = (bf16[32,24,512]{2,1,0:T(8,128)(2,1)S(1)}, bf16[32,24,512]{2,1,0:T(8,128)(2,1)}, u32[]{:S(2)}) copy-start(bf16[32,24,512]{2,1,0:T(8,128)(2,1)} %param.9) | copy-start | bytes 2359300
  28.0 1.6 %collective-permute-start.4 = (bf16[280,512]{1,0:T(8,128)(2,1)S(1)}, bf16[280,512]{1,0:T(8,128)(2,1)S(1)}, u32[]{:S(2)}, u32[]{:S(2)}) collective-permute-start(bf16[280,512]{1,0:T(8,128)(2,1)S(1)} %select_convert_fusion), channel_id=1, source_target_pairs={{0,1},{1,0},{2,3},{3,2},{4,5},{5,4},{6,7},{7,6},{8,9},{9,8},{10,11... | collective-permute-start | bytes 860168 | tf_op jit(solution)/shard_map/ppermute | solution.py:145
  29.9 6.1 %collective-permute-start.5 = (bf16[140,512]{1,0:T(8,128)(2,1)S(1)}, bf16[140,512]{1,0:T(8,128)(2,1)S(1)}, u32[]{:S(2)}, u32[]{:S(2)}) collective-permute-start(bf16[140,512]{1,0:T(8,128)(2,1)S(1)} %select_convert_fusion.1), channel_id=1, source_target_pairs={{0,2},{1,3},{2,0},{3,1},{4,6},{5,7},{6,4},{7,5},{8,10},{9,11},{10,... | collective-permute-start | bytes 430088 | tf_op jit(solution)/shard_map/ppermute | solution.py:145
  36.0 5.2 %collective-permute-start.6 = (bf16[140,512]{1,0:T(8,128)(2,1)S(1)}, bf16[140,512]{1,0:T(8,128)(2,1)S(1)}, u32[]{:S(2)}, u32[]{:S(2)}) collective-permute-start(bf16[140,512]{1,0:T(8,128)(2,1)S(1)} %add_convert_fusion.5), channel_id=1, source_target_pairs={{0,4},{1,5},{2,6},{3,7},{4,0},{5,1},{6,2},{7,3},{8,12},{9,13},{10,... | collective-permute-start | bytes 430088 | tf_op jit(solution)/shard_map/ppermute | solution.py:151
  41.3 9.0 %collective-permute-start.7 = (bf16[140,512]{1,0:T(8,128)(2,1)S(1)}, bf16[140,512]{1,0:T(8,128)(2,1)S(1)}, u32[]{:S(2)}, u32[]{:S(2)}) collective-permute-start(bf16[140,512]{1,0:T(8,128)(2,1)S(1)} %add_convert_fusion.4), channel_id=1, source_target_pairs={{0,8},{1,9},{2,10},{3,11},{4,12},{5,13},{6,14},{7,15},{8,0},{9,1},... | collective-permute-start | bytes 430088 | tf_op jit(solution)/shard_map/ppermute | solution.py:151
  50.4 5.2 %collective-permute-start.8 = (bf16[140,512]{1,0:T(8,128)(2,1)S(1)}, bf16[140,512]{1,0:T(8,128)(2,1)S(1)}, u32[]{:S(2)}, u32[]{:S(2)}) collective-permute-start(bf16[140,512]{1,0:T(8,128)(2,1)S(1)} %add_convert_fusion.3), channel_id=1, source_target_pairs={{0,2},{1,3},{2,0},{3,1},{4,6},{5,7},{6,4},{7,5},{8,10},{9,11},{10,... | collective-permute-start | bytes 430088 | tf_op jit(solution)/shard_map/ppermute | solution.py:156
  55.7 1.6 %collective-permute-start.9 = (bf16[280,512]{1,0:T(8,128)(2,1)S(1)}, bf16[280,512]{1,0:T(8,128)(2,1)S(1)}, u32[]{:S(2)}, u32[]{:S(2)}) collective-permute-start(bf16[280,512]{1,0:T(8,128)(2,1)S(1)} %maximum_select_fusion.1), channel_id=1, source_target_pairs={{0,1},{1,0},{2,3},{3,2},{4,5},{5,4},{6,7},{7,6},{8,9},{9,8},{10,11... | collective-permute-start | bytes 860168 | tf_op jit(solution)/shard_map/ppermute | solution.py:156

commit v6 on v2

--- a/solution.py
+++ b/solution.py
@@ -131,20 +131,43 @@
     return values
 
 
-def sum_halving(values, axis_name):
+def reduce_grads(grad_out, small, axis_name, wire=jnp.bfloat16, halving_levels=2):
     count = lax.axis_size(axis_name)
-    if not _is_power_of_two(count) or values.shape[0] % count != 0:
-        return lax.psum(values, axis_name)
+    parts = min(2**halving_levels, count)
+    rows_out, width = grad_out.shape
+    if not _is_power_of_two(count) or rows_out % parts != 0:
+        return lax.psum(grad_out, axis_name), lax.psum(small, axis_name)
+    chunk = rows_out // parts
+    block = chunk + small.shape[0]
+    block += -block % 16
+    filler = jnp.zeros((block - chunk - small.shape[0], width), jnp.float32)
+    values = jnp.concatenate(
+        [
+            piece
+            for index in range(parts)
+            for piece in (grad_out[index * chunk : (index + 1) * chunk], small, filler)
+        ],
+        0,
+    )
     position = lax.axis_index(axis_name)
     distance = 1
-    while distance < count:
+    while distance < parts:
         half = values.shape[0] // 2
         lower = (position // distance) % 2 == 0
         keep = jnp.where(lower, values[:half], values[half:])
-        send = jnp.where(lower, values[half:], values[:half])
-        values = keep + lax.ppermute(send, axis_name, _exchange_pairs(count, distance))
-        distance *= 2
-    distance = count // 2
+        send = jnp.where(lower, values[half:], values[:half]).astype(wire)
+        arrived = lax.ppermute(send, axis_name, _exchange_pairs(count, distance))
+        shared = (jnp.arange(half) % block >= chunk)[:, None]
+        keep = jnp.where(shared, keep.astype(wire).astype(keep.dtype), keep)
+        values = keep + arrived.astype(keep.dtype)
+        distance *= 2
+    values = values.astype(wire)
+    while distance < count:
+        arrived = lax.ppermute(values, axis_name, _exchange_pairs(count, distance))
+        values = (values.astype(jnp.float32) + arrived.astype(jnp.float32)).astype(wire)
+        distance *= 2
+    small_total = values[chunk : chunk + small.shape[0]].astype(jnp.float32)
+    distance = parts // 2
     while distance >= 1:
         other = lax.ppermute(values, axis_name, _exchange_pairs(count, distance))
         lower = (position // distance) % 2 == 0
@@ -152,7 +175,8 @@
             lower, jnp.concatenate([values, other], 0), jnp.concatenate([other, values], 0)
         )
         distance //= 2
-    return values
+    grad_total = values.reshape(parts, block, width)[:, :chunk].reshape(rows_out, width)
+    return grad_total.astype(jnp.float32), small_total
 
 
 def local(
@@ -193,12 +217,13 @@
     derivative_bottleneck = jnp.einsum(
         "orm,rm->om", derivative_entering.reshape(samples, sub_dev, width), gain_row_values
     )
-    grad_out = sum_halving(grad_out, "freq")
-    packed = sum_whole(
-        jnp.concatenate([derivative_bottleneck, grad_filter.reshape(1, -1)], 0), "freq"
-    )
-    derivative_bottleneck = packed[:samples]
-    grad_filter = packed[samples:].reshape(grad_filter.shape)
+    grad_out, small = reduce_grads(
+        grad_out,
+        jnp.concatenate([derivative_bottleneck, grad_filter.reshape(1, -1)], 0),
+        "freq",
+    )
+    derivative_bottleneck = small[:samples]
+    grad_filter = small[samples].reshape(grad_filter.shape)
     grad_enc, grad_dec = encoder_grads(
         all_inputs, codes, derivative_bottleneck[sample_index], decoder_weight
     )

time: 80.1 us -> 73.2 us (0.914)
  starting transfers between devices: 27.7 us -> 17.1 us
  local copies, waits for them, and re-layouts: 4.26 us -> 11.9 us
  waiting for transfers between devices: 26.1 us -> 23.5 us
  matrix products: 11 us -> 10.1 us
    ppermute x12 -> x6, starting transfers between devices: 19.3 us -> 8.69 us  [the longest x2 5.05 us: reduce_grads(): arrived = lax.ppermute(values, axis_name, _exchange_pairs(count, distance))]
    concatenate x0 -> x2, local copies, waits for them, and re-layouts: none -> 5.61 us  [reduce_grads(): jnp.concatenate([piece for index in range(parts) for piece in (grad_out[i...]
    ppermute x12 -> x6, waiting for transfers between devices: 22.5 us -> 19.9 us  [the longest x2 11.3 us: reduce_grads(): arrived = lax.ppermute(values, axis_name, _exchange_pairs(count, distance))]
    select_n x8 -> x2, other arithmetic: 3.6 us -> 1.42 us  [reduce_grads(): jnp.where(lower, jnp.concatenate([values, other], 0), jnp.concatenate([ot...]
    slice x2 -> x4, local copies, waits for them, and re-layouts: 0.03 us -> 1.66 us  [the longest x1 0.88 us: reduce_grads(): grad_out[index * chunk:(index + 1) * chunk]]
    convert_element_type x0 -> x7, other arithmetic: none -> 1.53 us  [the longest x1 1.14 us: reduce_grads(): return (grad_total.astype(jnp.float32), small_total)]
    dot_general x1, matrix products: 3.87 us -> 2.96 us  [encoder_grads(): lax.dot_general(inputs_rows, grad_pre, (((0,), (0,)), ((), ())), preferre...]
    another operation x4 -> x3, other arithmetic: 2.75 us -> 2.33 us
  transfers between devices with their start and end apart: 16 -> 10, of which waited for: 11 -> 8; matrix products, arithmetic and copies ran while one was open for 18% -> 16% of each run, Pallas kernels for 0% -> 0%
where the time goes in v6:
time: 73.2 us; the launch traced here: 72.5 us
  waiting for transfers between devices  23.5 us (32%)
  starting transfers between devices  17.1 us (23%)
  local copies, waits for them, and re-layouts  11.9 us (16%)
  matrix products  10.1 us (14%)
  other arithmetic  8.77 us (12%)
  between operations  1.15 us (2%)
    ppermute x2, waiting for transfers between devices, reduce_grads(): arrived = lax.ppermute(values, axis_name, _exchange_pairs(count, distance))  11.3 us
    ppermute x4, starting transfers between devices, gather_rows(): other = lax.ppermute(block, axis_name, _exchange_pairs(count, distance))  8.38 us
    ppermute x2, waiting for transfers between devices, reduce_grads(): arrived = lax.ppermute(send, axis_name, _exchange_pairs(count, distance))  6.49 us
    concatenate x2, local copies, waits for them, and re-layouts, reduce_grads(): jnp.concatenate([piece for index in range(parts) for piece in (grad_out[i...  5.61 us
    ppermute x2, starting transfers between devices, reduce_grads(): arrived = lax.ppermute(values, axis_name, _exchange_pairs(count, distance))  5.05 us
    ppermute x4, waiting for transfers between devices, gather_rows(): other = lax.ppermute(block, axis_name, _exchange_pairs(count, distance))  3.63 us
    dot_general x1, matrix products, encoder_grads(): lax.dot_general(inputs_rows, grad_pre, (((0,), (0,)), ((), ())), preferre...  2.96 us
    another operation x3, other arithmetic  2.33 us
  transfers between devices with their start and end apart: 10, of which 8 were waited for; matrix products, arithmetic and copies ran while one was open for 16% of the time, Pallas kernels for 0%

profile of v6, /device:TPU:0, one launch (start us, length us, event | category | flops | bytes accessed | tf_op | source)
XLA Modules:
  0.0 72.5 jit_solution(15547282534705338007)
XLA Ops:
  1.2 0.9 %bitcast_convert_fusion.1 = (f32[512,24]{0,1:T(8,128)S(1)}, f32[24,512]{1,0:T(8,128)S(1)}) fusion(bf16[24,512]{1,0:T(8,128)(2,1)} %param.13), kind=kLoop, calls=%fused_computation.79 | loop fusion | flops 24576 | bytes 122880
  5.0 2.6 %collective-permute-start.1 = (bf16[4,2048]{1,0:T(4,128)(2,1)S(1)}, bf16[4,2048]{1,0:T(4,128)(2,1)S(1)}, u32[]{:S(2)}, u32[]{:S(2)}) collective-permute-start(bf16[4,2048]{1,0:T(4,128)(2,1)S(1)} %maximum_select_fusion.7), channel_id=1, source_target_pairs={{0,2},{1,3},{2,0},{3,1},{4,6},{5,7},{6,4},{7,5},{8,10},{9,11},{10,... | collective-permute-start | bytes 49160 | tf_op jit(solution)/shard_map/ppermute | solution.py:114
  7.6 1.1 %negate_convert_fusion = (bf16[256,256]{1,0:T(8,128)(2,1)S(1)}, bf16[256,256]{1,0:T(8,128)(2,1)S(1)}) fusion(), kind=kLoop, calls=%fused_computation.63 | loop fusion | flops 1245184 | bytes 262144 | tf_op jit(solution)/shard_map/convert.17
  9.4 2.1 %collective-permute-start.2 = (bf16[8,2048]{1,0:T(8,128)(2,1)S(1)}, bf16[8,2048]{1,0:T(8,128)(2,1)S(1)}, u32[]{:S(2)}, u32[]{:S(2)}) collective-permute-start(bf16[8,2048]{1,0:T(8,128)(2,1)S(1)} %maximum_select_fusion.4), channel_id=1, source_target_pairs={{0,4},{1,5},{2,6},{3,7},{4,0},{5,1},{6,2},{7,3},{8,12},{9,13},{10,... | collective-permute-start | bytes 98312 | tf_op jit(solution)/shard_map/ppermute | solution.py:114
  11.5 1.0 %fusion.31 = bf16[256,256]{1,0:T(8,128)(2,1)S(1)} fusion(), kind=kLoop, calls=%fused_computation.69 | loop fusion | flops 1048576 | bytes 131072 | tf_op jit(solution)/shard_map/convert.14
  13.4 3.1 %collective-permute-start.3 = (bf16[16,2048]{1,0:T(8,128)(2,1)S(1)}, bf16[16,2048]{1,0:T(8,128)(2,1)S(1)}, u32[]{:S(2)}, u32[]{:S(2)}) collective-permute-start(bf16[16,2048]{1,0:T(8,128)(2,1)S(1)} %maximum_select_fusion.3), channel_id=1, source_target_pairs={{0,8},{1,9},{2,10},{3,11},{4,12},{5,13},{6,14},{7,15},{8,0},{9,1},... | collective-permute-start | bytes 196616 | tf_op jit(solution)/shard_map/ppermute | solution.py:114
  16.5 2.2 %collective-permute-done.3 = bf16[16,2048]{1,0:T(8,128)(2,1)S(1)} collective-permute-done((bf16[16,2048]{1,0:T(8,128)(2,1)S(1)}, bf16[16,2048]{1,0:T(8,128)(2,1)S(1)}, u32[]{:S(2)}, u32[]{:S(2)}) %collective-permute-start.3) | collective-permute-done | bytes 65568 | tf_op jit(solution)/shard_map/ppermute | solution.py:114
  21.7 1.0 %add_convert_fusion = (bf16[768,512]{1,0:T(8,128)(2,1)S(1)}, f32[768,512]{1,0:T(8,128)S(1)}) fusion(bf16[32,24,512]{2,1,0:T(8,128)(2,1)S(1)} %multiply_convert_fusion, bf16[256,256]{1,0:T(8,128)(2,1)S(1)} %get-tuple-element.23, bf16[256,256]{1,0:T(8,128)(2,1)S(1)} %get-tuple-element.22, bf16[256,256]{1,0:T(8,128)(2,1)S(1)} %fusion.31, ...), kind=kOutput, calls=%fused_computation.15 | convolution fusion | flops 410648576 | bytes 4325376 | tf_op jit(solution)/shard_map/dot_general | solution.py:50
  24.9 0.9 %fusion.64 = (f32[128,512]{1,0:T(8,128)}, f32[128,512]{1,0:T(8,128)S(1)}, f32[128,512]{1,0:T(8,128)S(1)}, f32[128,512]{1,0:T(8,128)}) fusion(f32[512,512]{1,0:T(8,128)S(1)} %fusion.23), kind=kLoop, calls=%fused_computation.112 | loop fusion | bytes 2097152 | tf_op jit(solution)/shard_map/slice | solution.py:148
  25.8 1.2 %fusion.18 = f32[768,512]{1,0:T(8,128)S(1)} fusion(f32[768,512]{1,0:T(8,128)S(1)} %get-tuple-element.21, f32[768,512]{1,0:T(8,128)S(1)} %convolution_add_fusion.1, bf16[256,256]{1,0:T(8,128)(2,1)S(1)} %copy-done.14, bf16[256,256]{1,0:T(8,128)(2,1)S(1)} %get-tuple-element.22, bf16[256,256]{1,0:T(8,128)(2,1)S(1)} %copy-done.16), kind=kOutput, calls=%fused_computation.37 | convolution fusion | flops 412614656 | bytes 5111808 | tf_op jit(solution)/shard_map/dot_general | solution.py:64
  29.1 5.3 %concatenate.93 = f32[352,512]{1,0:T(8,128)S(1)} concatenate(f32[128,512]{1,0:T(8,128)} %get-tuple-element.15, f32[32,512]{1,0:T(8,128)} %bitcast.37, f32[1,512]{1,0:T(1,128)S(1)} %bitcast.43, f32[15,512]{1,0:T(8,128)} %copy-done.6, f32[128,512]{1,0:T(8,128)} %get-tuple-element.12, f32[32,512]{1,0:T(8,128)} %bitcast.38, f32[1,512]{1,0:T(1,128)S(1)} %bitcast.44, f32[15,512]{1,0:T(8,128)} %copy-done.6), dimensions={0} | concatenate | bytes 1441792 | tf_op jit(solution)/shard_map/concatenate | solution.py:144
  34.6 1.6 %collective-permute-done.4 = bf16[352,512]{1,0:T(8,128)(2,1)S(1)} collective-permute-done((bf16[352,512]{1,0:T(8,128)(2,1)S(1)}, bf16[352,512]{1,0:T(8,128)(2,1)S(1)}, u32[]{:S(2)}, u32[]{:S(2)}) %collective-permute-start.4) | collective-permute-done | bytes 360480 | tf_op jit(solution)/shard_map/ppermute | solution.py:159
  36.5 1.9 %collective-permute-start.5 = (bf16[176,512]{1,0:T(8,128)(2,1)S(1)}, bf16[176,512]{1,0:T(8,128)(2,1)S(1)}, u32[]{:S(2)}, u32[]{:S(2)}) collective-permute-start(bf16[176,512]{1,0:T(8,128)(2,1)S(1)} %select_convert_fusion.1), channel_id=1, source_target_pairs={{0,2},{1,3},{2,0},{3,1},{4,6},{5,7},{6,4},{7,5},{8,10},{9,11},{10,... | collective-permute-start | bytes 540680 | tf_op jit(solution)/shard_map/ppermute | solution.py:159
  38.4 4.8 %collective-permute-done.5 = bf16[176,512]{1,0:T(8,128)(2,1)S(1)} collective-permute-done((bf16[176,512]{1,0:T(8,128)(2,1)S(1)}, bf16[176,512]{1,0:T(8,128)(2,1)S(1)}, u32[]{:S(2)}, u32[]{:S(2)}) %collective-permute-start.5) | collective-permute-done | bytes 180256 | tf_op jit(solution)/shard_map/ppermute | solution.py:159
  43.4 1.9 %collective-permute-start.6 = (bf16[176,512]{1,0:T(8,128)(2,1)S(1)}, bf16[176,512]{1,0:T(8,128)(2,1)S(1)}, u32[]{:S(2)}, u32[]{:S(2)}) collective-permute-start(bf16[176,512]{1,0:T(8,128)(2,1)S(1)} %add_convert_fusion.5), channel_id=1, source_target_pairs={{0,4},{1,5},{2,6},{3,7},{4,0},{5,1},{6,2},{7,3},{8,12},{9,13},{10,... | collective-permute-start | bytes 540680 | tf_op jit(solution)/shard_map/ppermute | solution.py:166
  45.3 4.1 %collective-permute-done.6 = bf16[176,512]{1,0:T(8,128)(2,1)S(1)} collective-permute-done((bf16[176,512]{1,0:T(8,128)(2,1)S(1)}, bf16[176,512]{1,0:T(8,128)(2,1)S(1)}, u32[]{:S(2)}, u32[]{:S(2)}) %collective-permute-start.6) | collective-permute-done | bytes 180256 | tf_op jit(solution)/shard_map/ppermute | solution.py:166
  49.4 3.2 %collective-permute-start.7 = (bf16[176,512]{1,0:T(8,128)(2,1)S(1)}, bf16[176,512]{1,0:T(8,128)(2,1)S(1)}, u32[]{:S(2)}, u32[]{:S(2)}) collective-permute-start(bf16[176,512]{1,0:T(8,128)(2,1)S(1)} %add_convert_fusion.4), channel_id=1, source_target_pairs={{0,8},{1,9},{2,10},{3,11},{4,12},{5,13},{6,14},{7,15},{8,0},{9,1},... | collective-permute-start | bytes 540680 | tf_op jit(solution)/shard_map/ppermute | solution.py:166
  52.6 7.3 %collective-permute-done.7 = bf16[176,512]{1,0:T(8,128)(2,1)S(1)} collective-permute-done((bf16[176,512]{1,0:T(8,128)(2,1)S(1)}, bf16[176,512]{1,0:T(8,128)(2,1)S(1)}, u32[]{:S(2)}, u32[]{:S(2)}) %collective-permute-start.7) | collective-permute-done | bytes 180256 | tf_op jit(solution)/shard_map/ppermute | solution.py:166
  60.0 1.6 %collective-permute-start.8 = (bf16[176,512]{1,0:T(8,128)(2,1)S(1)}, bf16[176,512]{1,0:T(8,128)(2,1)S(1)}, u32[]{:S(2)}, u32[]{:S(2)}) collective-permute-start(bf16[176,512]{1,0:T(8,128)(2,1)S(1)} %add_convert_fusion.3), channel_id=1, source_target_pairs={{0,2},{1,3},{2,0},{3,1},{4,6},{5,7},{6,4},{7,5},{8,10},{9,11},{10,... | collective-permute-start | bytes 540680 | tf_op jit(solution)/shard_map/ppermute | solution.py:172
  62.2 1.3 %fusion.67 = f32[512,512]{1,0:T(8,128)} fusion(bf16[32,512]{1,0:T(8,128)(2,1)S(1)} %copy-done.2, bf16[32,512]{1,0:T(8,128)(2,1)S(1)} %gather_fusion.1), kind=kOutput, calls=%fused_computation.115 | convolution fusion | flops 16777216 | bytes 1114112 | tf_op jit(solution)/shard_map/dot_general | solution.py:86
  63.5 2.1 %collective-permute-done.8 = bf16[176,512]{1,0:T(8,128)(2,1)S(1)} collective-permute-done((bf16[176,512]{1,0:T(8,128)(2,1)S(1)}, bf16[176,512]{1,0:T(8,128)(2,1)S(1)}, u32[]{:S(2)}, u32[]{:S(2)}) %collective-permute-start.8) | collective-permute-done | bytes 180256 | tf_op jit(solution)/shard_map/ppermute | solution.py:172
  67.1 3.0 %fusion.10 = f32[2048,512]{1,0:T(8,128)} fusion(bf16[512,512]{1,0:T(8,128)(2,1)S(1)} %copy-done.4, bf16[32,512]{1,0:T(8,128)(2,1)S(1)} %copy-done.2, bf16[16,2048]{1,0:T(8,128)(2,1)S(1)} %copy-done.11, bf16[16,2048]{1,0:T(8,128)(2,1)S(1)} %copy-done.8, pred[]{:T(512)S(6)} %eq.31, bf16[32,512]{1,0:T(8,128)(2,1)S(1)} %gather_fusion.1), kind=kOutput, calls=%fused_computation.23 | convolution fusion | flops 84557824 | bytes 4915201 | tf_op jit(solution)/shard_map/dot_general | solution.py:93
  70.0 1.3 %maximum_select_fusion = bf16[704,512]{1,0:T(8,128)(2,1)S(1)} fusion(bf16[352,512]{1,0:T(8,128)(2,1)} %collective-permute-done.9, bf16[352,512]{1,0:T(8,128)(2,1)S(1)} %maximum_select_fusion.1, pred[]{:T(512)S(6)} %eq.34), kind=kLoop, calls=%fused_computation.38 | loop fusion | flops 3244032 | bytes 1441793 | tf_op jit(solution)/shard_map/jit(_where)/select_n | solution.py:174
  71.4 1.1 %bitcast_convert_fusion = f32[512,512]{1,0:T(8,128)} fusion(bf16[4,128,512]{2,1,0:T(8,128)(2,1)S(1)} %slice.88), kind=kLoop, calls=%fused_computation.47 | loop fusion | flops 262144 | bytes 1572864 | tf_op jit(solution)/shard_map/convert_element_type | solution.py:179
  (84 shorter events, 14.8 us)
Async XLA Ops:
  0.6 18.8 %copy-start = (bf16[2048,512]{1,0:T(8,128)(2,1)S(1)}, bf16[2048,512]{1,0:T(8,128)(2,1)}, u32[]{:S(2)}) copy-start(bf16[2048,512]{1,0:T(8,128)(2,1)} %param.11) | copy-start | bytes 6291460
  0.6 3.5 %collective-permute-start = (bf16[2,2048]{1,0:T(2,128)(2,1)}, bf16[2,2048]{1,0:T(2,128)(2,1)S(1)}, u32[]{:S(2)}, u32[]{:S(2)}) collective-permute-start(bf16[2,2048]{1,0:T(2,128)(2,1)} %param.8), channel_id=1, source_target_pairs={{0,1},{1,0},{2,3},{3,2},{4,5},{5,4},{6,7},{7,6},{8,9},{9,8},{10,11... | collective-permute-start | bytes 24584 | tf_op jit(solution)/shard_map/ppermute | solution.py:114
  5.0 4.3 %collective-permute-start.1 = (bf16[4,2048]{1,0:T(4,128)(2,1)S(1)}, bf16[4,2048]{1,0:T(4,128)(2,1)S(1)}, u32[]{:S(2)}, u32[]{:S(2)}) collective-permute-start(bf16[4,2048]{1,0:T(4,128)(2,1)S(1)} %maximum_select_fusion.7), channel_id=1, source_target_pairs={{0,2},{1,3},{2,0},{3,1},{4,6},{5,7},{6,4},{7,5},{8,10},{9,11},{10,... | collective-permute-start | bytes 49160 | tf_op jit(solution)/shard_map/ppermute | solution.py:114
  8.7 13.0 %copy-start.13 = (bf16[256,256]{1,0:T(8,128)(2,1)}, bf16[256,256]{1,0:T(8,128)(2,1)S(1)}, u32[]{:S(2)}) copy-start(bf16[256,256]{1,0:T(8,128)(2,1)S(1)} %get-tuple-element.23) | copy-start | bytes 393220
  8.7 11.8 %copy-start.3 = (bf16[512,512]{1,0:T(8,128)(2,1)S(1)}, bf16[512,512]{1,0:T(8,128)(2,1)}, u32[]{:S(2)}) copy-start(bf16[512,512]{1,0:T(8,128)(2,1)} %param.12) | copy-start | bytes 1572868
  9.4 4.0 %collective-permute-start.2 = (bf16[8,2048]{1,0:T(8,128)(2,1)S(1)}, bf16[8,2048]{1,0:T(8,128)(2,1)S(1)}, u32[]{:S(2)}, u32[]{:S(2)}) collective-permute-start(bf16[8,2048]{1,0:T(8,128)(2,1)S(1)} %maximum_select_fusion.4), channel_id=1, source_target_pairs={{0,4},{1,5},{2,6},{3,7},{4,0},{5,1},{6,2},{7,3},{8,12},{9,13},{10,... | collective-permute-start | bytes 98312 | tf_op jit(solution)/shard_map/ppermute | solution.py:114
  12.5 9.2 %copy-start.15 = (bf16[256,256]{1,0:T(8,128)(2,1)}, bf16[256,256]{1,0:T(8,128)(2,1)S(1)}, u32[]{:S(2)}) copy-start(bf16[256,256]{1,0:T(8,128)(2,1)S(1)} %fusion.31) | copy-start | bytes 393220
  13.4 5.4 %copy-start.7 = (bf16[16,2048]{1,0:T(8,128)(2,1)}, bf16[16,2048]{1,0:T(8,128)(2,1)S(1)}, u32[]{:S(2)}) copy-start(bf16[16,2048]{1,0:T(8,128)(2,1)S(1)} %maximum_select_fusion.3) | copy-start | bytes 196612
  13.4 5.3 %collective-permute-start.3 = (bf16[16,2048]{1,0:T(8,128)(2,1)S(1)}, bf16[16,2048]{1,0:T(8,128)(2,1)S(1)}, u32[]{:S(2)}, u32[]{:S(2)}) collective-permute-start(bf16[16,2048]{1,0:T(8,128)(2,1)S(1)} %maximum_select_fusion.3), channel_id=1, source_target_pairs={{0,8},{1,9},{2,10},{3,11},{4,12},{5,13},{6,14},{7,15},{8,0},{9,1},... | collective-permute-start | bytes 196616 | tf_op jit(solution)/shard_map/ppermute | solution.py:114
  19.9 1.6 %copy-start.1 = (bf16[32,512]{1,0:T(8,128)(2,1)}, bf16[32,512]{1,0:T(8,128)(2,1)S(1)}, u32[]{:S(2)}) copy-start(bf16[32,512]{1,0:T(8,128)(2,1)S(1)} %fusion.8) | copy-start | bytes 98308
  21.7 1.0 %copy-start.9 = (bf16[512,512]{1,0:T(8,128)(2,1)S(1)}, bf16[512,512]{1,0:T(8,128)(2,1)}, u32[]{:S(2)}) copy-start(bf16[512,512]{1,0:T(8,128)(2,1)} %param.15) | copy-start | bytes 1572868
  21.7 1.3 %copy-start.17 = (bf16[32,24,512]{2,1,0:T(8,128)(2,1)S(1)}, bf16[32,24,512]{2,1,0:T(8,128)(2,1)}, u32[]{:S(2)}) copy-start(bf16[32,24,512]{2,1,0:T(8,128)(2,1)} %param.9) | copy-start | bytes 2359300
  24.9 1.0 %copy-start.16 = (bf16[256,256]{1,0:T(8,128)(2,1)S(1)}, bf16[256,256]{1,0:T(8,128)(2,1)}, u32[]{:S(2)}) copy-start(bf16[256,256]{1,0:T(8,128)(2,1)} %copy-done.15) | copy-start | bytes 393220
  34.6 1.7 %collective-permute-start.4 = (bf16[352,512]{1,0:T(8,128)(2,1)S(1)}, bf16[352,512]{1,0:T(8,128)(2,1)S(1)}, u32[]{:S(2)}, u32[]{:S(2)}) collective-permute-start(bf16[352,512]{1,0:T(8,128)(2,1)S(1)} %select_convert_fusion), channel_id=1, source_target_pairs={{0,1},{1,0},{2,3},{3,2},{4,5},{5,4},{6,7},{7,6},{8,9},{9,8},{10,11... | collective-permute-start | bytes 1081352 | tf_op jit(solution)/shard_map/ppermute | solution.py:159
  36.5 25.7 %copy-start.2 = (bf16[32,512]{1,0:T(8,128)(2,1)S(1)}, bf16[32,512]{1,0:T(8,128)(2,1)}, u32[]{:S(2)}) copy-start(bf16[32,512]{1,0:T(8,128)(2,1)} %copy-done.1) | copy-start | bytes 98308
  36.5 6.8 %collective-permute-start.5 = (bf16[176,512]{1,0:T(8,128)(2,1)S(1)}, bf16[176,512]{1,0:T(8,128)(2,1)S(1)}, u32[]{:S(2)}, u32[]{:S(2)}) collective-permute-start(bf16[176,512]{1,0:T(8,128)(2,1)S(1)} %select_convert_fusion.1), channel_id=1, source_target_pairs={{0,2},{1,3},{2,0},{3,1},{4,6},{5,7},{6,4},{7,5},{8,10},{9,11},{10,... | collective-permute-start | bytes 540680 | tf_op jit(solution)/shard_map/ppermute | solution.py:159
  43.4 23.7 %copy-start.4 = (bf16[512,512]{1,0:T(8,128)(2,1)S(1)}, bf16[512,512]{1,0:T(8,128)(2,1)}, u32[]{:S(2)}) copy-start(bf16[512,512]{1,0:T(8,128)(2,1)} %param.12) | copy-start | bytes 1572868
  43.4 23.7 %copy-start.8 = (bf16[16,2048]{1,0:T(8,128)(2,1)S(1)}, bf16[16,2048]{1,0:T(8,128)(2,1)}, u32[]{:S(2)}) copy-start(bf16[16,2048]{1,0:T(8,128)(2,1)} %copy-done.7) | copy-start | bytes 196612
  43.4 23.7 %copy-start.11 = (bf16[16,2048]{1,0:T(8,128)(2,1)S(1)}, bf16[16,2048]{1,0:T(8,128)(2,1)}, u32[]{:S(2)}) copy-start(bf16[16,2048]{1,0:T(8,128)(2,1)} %copy-done.10) | copy-start | bytes 196612
  43.4 5.9 %collective-permute-start.6 = (bf16[176,512]{1,0:T(8,128)(2,1)S(1)}, bf16[176,512]{1,0:T(8,128)(2,1)S(1)}, u32[]{:S(2)}, u32[]{:S(2)}) collective-permute-start(bf16[176,512]{1,0:T(8,128)(2,1)S(1)} %add_convert_fusion.5), channel_id=1, source_target_pairs={{0,4},{1,5},{2,6},{3,7},{4,0},{5,1},{6,2},{7,3},{8,12},{9,13},{10,... | collective-permute-start | bytes 540680 | tf_op jit(solution)/shard_map/ppermute | solution.py:166
  49.4 10.4 %collective-permute-start.7 = (bf16[176,512]{1,0:T(8,128)(2,1)S(1)}, bf16[176,512]{1,0:T(8,128)(2,1)S(1)}, u32[]{:S(2)}, u32[]{:S(2)}) collective-permute-start(bf16[176,512]{1,0:T(8,128)(2,1)S(1)} %add_convert_fusion.4), channel_id=1, source_target_pairs={{0,8},{1,9},{2,10},{3,11},{4,12},{5,13},{6,14},{7,15},{8,0},{9,1},... | collective-permute-start | bytes 540680 | tf_op jit(solution)/shard_map/ppermute | solution.py:166
  59.9 3.5 %copy-start.12 = (f32[33,512]{1,0:T(8,128)}, f32[33,512]{1,0:T(8,128)S(1)}, u32[]{:S(2)}) copy-start(f32[33,512]{1,0:T(8,128)S(1)} %slice_convert_fusion) | copy-start | bytes 202756
  60.0 5.6 %collective-permute-start.8 = (bf16[176,512]{1,0:T(8,128)(2,1)S(1)}, bf16[176,512]{1,0:T(8,128)(2,1)S(1)}, u32[]{:S(2)}, u32[]{:S(2)}) collective-permute-start(bf16[176,512]{1,0:T(8,128)(2,1)S(1)} %add_convert_fusion.3), channel_id=1, source_target_pairs={{0,2},{1,3},{2,0},{3,1},{4,6},{5,7},{6,4},{7,5},{8,10},{9,11},{10,... | collective-permute-start | bytes 540680 | tf_op jit(solution)/shard_map/ppermute | solution.py:172
  65.6 4.4 %collective-permute-start.9 = (bf16[352,512]{1,0:T(8,128)(2,1)S(1)}, bf16[352,512]{1,0:T(8,128)(2,1)}, u32[]{:S(2)}, u32[]{:S(2)}) collective-permute-start(bf16[352,512]{1,0:T(8,128)(2,1)S(1)} %maximum_select_fusion.1), channel_id=1, source_target_pairs={{0,1},{1,0},{2,3},{3,2},{4,5},{5,4},{6,7},{7,6},{8,9},{9,8},{10,11... | collective-permute-start | bytes 1081352 | tf_op jit(solution)/shard_map/ppermute | solution.py:172
  (4 other events, 2.8 us)

commit v7 on v5

--- a/solution.py
+++ b/solution.py
@@ -1,32 +1,37 @@
 import math
 
 import jax
+import ml_dtypes
+import numpy as np
 import jax.numpy as jnp
 from jax import lax
 from jax.sharding import PartitionSpec as P
 
 
 def rotation_tables(antennas):
-    indices = jnp.arange(antennas, dtype=jnp.int32)
+    indices = np.arange(antennas, dtype=np.int32)
     products_mod = indices[:, None] * indices[None, :] % antennas
-    angle_table = products_mod.astype(jnp.float32) * (2.0 * math.pi / antennas)
-    cosine_table = jnp.cos(angle_table) / math.sqrt(antennas)
-    sine_table = jnp.sin(angle_table) / math.sqrt(antennas)
-    forward_transform = jnp.concatenate(
-        [
-            jnp.concatenate([cosine_table, -sine_table], 1),
-            jnp.concatenate([sine_table, cosine_table], 1),
+    angle_table = products_mod.astype(np.float32) * np.float32(2.0 * math.pi / antennas)
+    cosine_table = np.cos(angle_table) / np.float32(math.sqrt(antennas))
+    sine_table = np.sin(angle_table) / np.float32(math.sqrt(antennas))
+    forward_transform = np.concatenate(
+        [
+            np.concatenate([cosine_table, -sine_table], 1),
+            np.concatenate([sine_table, cosine_table], 1),
         ],
         0,
     )
-    inverse_transform = jnp.concatenate(
-        [
-            jnp.concatenate([cosine_table, sine_table], 1),
-            jnp.concatenate([-sine_table, cosine_table], 1),
+    inverse_transform = np.concatenate(
+        [
+            np.concatenate([cosine_table, sine_table], 1),
+            np.concatenate([-sine_table, cosine_table], 1),
         ],
         0,
     )
-    return (forward_transform.astype(jnp.bfloat16), inverse_transform.astype(jnp.bfloat16))
+    return (
+        jnp.asarray(forward_transform.astype(ml_dtypes.bfloat16)),
+        jnp.asarray(inverse_transform.astype(ml_dtypes.bfloat16)),
+    )
 
 
 def decode_rows(
@@ -181,10 +186,13 @@
     codes = jnp.tanh(
         jnp.dot(all_inputs, encoder_weight, preferred_element_type=jnp.float32)
     ).astype(jnp.bfloat16)
-    inverse_ids = (
-        jnp.zeros((samples,), jnp.int32).at[sample_index].set(jnp.arange(samples, dtype=jnp.int32))
-    )
-    latent = jnp.dot(codes[inverse_ids], decoder_weight, preferred_element_type=jnp.float32)
+    selection = (
+        sample_index[None, :] == jnp.arange(samples, dtype=jnp.int32)[:, None]
+    ).astype(jnp.bfloat16)
+    codes_by_sample = jnp.dot(selection, codes, preferred_element_type=jnp.float32).astype(
+        jnp.bfloat16
+    )
+    latent = jnp.dot(codes_by_sample, decoder_weight, preferred_element_type=jnp.float32)
     gain_row_values = frequency_amplitude.astype(jnp.float32)
     mixed_in = (latent[:, None, :] * gain_row_values[None]).astype(jnp.bfloat16).reshape(-1, width)
     wanted_lines = desired_responses.reshape(-1, width)
@@ -212,11 +220,11 @@
         ],
         0,
     )
-    packed = sum_halving(packed, "freq").astype(jnp.float32)
+    packed = sum_halving(packed, "freq")
     rows_out = grad_out.shape[0]
-    grad_out = packed[:rows_out]
-    derivative_bottleneck = packed[rows_out : rows_out + samples]
-    grad_filter = packed[rows_out + samples].reshape(grad_filter.shape)
+    grad_out = packed[:rows_out].astype(jnp.float32)
+    derivative_bottleneck = packed[rows_out : rows_out + samples].astype(jnp.float32)
+    grad_filter = packed[rows_out + samples].astype(jnp.float32).reshape(grad_filter.shape)
     grad_enc, grad_dec = encoder_grads(
         all_inputs, codes, derivative_bottleneck[sample_index], decoder_weight
     )

time: 64.3 us -> 63.1 us (0.981)
  other arithmetic: 6.31 us -> 4.26 us
    another operation x4 -> x0, other arithmetic: 2.76 us -> none
    unnamed x9 -> x23, local copies, waits for them, and re-layouts: 0.32 us -> 2.14 us
    slice x3 -> x1, local copies, waits for them, and re-layouts: 1.07 us -> 0.01 us  [local(): packed[rows_out:rows_out + samples].astype(jnp.float32)]
    convert_element_type x1 -> x2, other arithmetic: 0.15 us -> 1.12 us  [the longest x1 1.1 us: local(): grad_out = packed[:rows_out].astype(jnp.float32)]
    scatter x1 -> x0, local copies, waits for them, and re-layouts: 0.67 us -> none  [local(): jnp.zeros((samples,), jnp.int32).at[sample_index]]
    select_n x2 -> x1, other arithmetic: 0.66 us -> 0.01 us  [local(): derivative_bottleneck[sample_index]]
  transfers between devices with their start and end apart: 10 -> 10, of which waited for: 9 -> 10; matrix products, arithmetic and copies ran while one was open for 8% -> 3% of each run, Pallas kernels for 0% -> 0%
where the time goes in v7:
time: 63.1 us; the launch traced here: 62.8 us
  waiting for transfers between devices  25.4 us (40%)
  starting transfers between devices  17.3 us (27%)
  matrix products  10.7 us (17%)
  other arithmetic  4.26 us (7%)
  local copies, waits for them, and re-layouts  4.19 us (7%)
  between operations  0.92 us (1%)
    ppermute x2, waiting for transfers between devices, sum_halving(): arrived = lax.ppermute(values, axis_name, _exchange_pairs(count, distance))  9.27 us
    ppermute x4, starting transfers between devices, gather_rows(): other = lax.ppermute(block, axis_name, _exchange_pairs(count, distance))  8.68 us
    ppermute x2, waiting for transfers between devices, sum_halving(): arrived = lax.ppermute(send, axis_name, _exchange_pairs(count, distance))  5.71 us
    ppermute x4, waiting for transfers between devices, gather_rows(): other = lax.ppermute(block, axis_name, _exchange_pairs(count, distance))  5.23 us
    ppermute x2, waiting for transfers between devices, sum_halving(): other = lax.ppermute(values, axis_name, _exchange_pairs(count, distance))  5.16 us
    ppermute x2, starting transfers between devices, sum_halving(): arrived = lax.ppermute(values, axis_name, _exchange_pairs(count, distance))  5.01 us
    dot_general x1, matrix products, encoder_grads(): lax.dot_general(inputs_rows, grad_pre, (((0,), (0,)), ((), ())), preferre...  2.96 us
    unnamed x23, local copies, waits for them, and re-layouts  2.14 us
  transfers between devices with their start and end apart: 10, of which 10 were waited for; matrix products, arithmetic and copies ran while one was open for 3% of the time, Pallas kernels for 0%

profile of v7, /device:TPU:0, one launch (start us, length us, event | category | flops | bytes accessed | tf_op | source)
XLA Modules:
  0.0 62.8 jit_solution(6003548849846240180)
XLA Ops:
  1.2 1.0 %collective-permute-done = bf16[2,2048]{1,0:T(2,128)(2,1)S(1)} collective-permute-done((bf16[2,2048]{1,0:T(2,128)(2,1)}, bf16[2,2048]{1,0:T(2,128)(2,1)S(1)}, u32[]{:S(2)}, u32[]{:S(2)}) %collective-permute-start) | collective-permute-done | bytes 8224 | tf_op jit(solution)/shard_map/ppermute | solution.py:119
  2.2 0.8 %maximum_select_fusion.7 = bf16[4,2048]{1,0:T(4,128)(2,1)S(1)} fusion(bf16[2,2048]{1,0:T(2,128)(2,1)S(1)} %collective-permute-done, bf16[2,2048]{1,0:T(2,128)(2,1)} %param.10, pred[]{:T(512)S(6)} %eq.41), kind=kLoop, calls=%fused_computation.66 | loop fusion | flops 73728 | bytes 32769 | tf_op jit(solution)/shard_map/jit(_where)/select_n | solution.py:121
  3.0 2.9 %collective-permute-start.1 = (bf16[4,2048]{1,0:T(4,128)(2,1)S(1)}, bf16[4,2048]{1,0:T(4,128)(2,1)S(1)}, u32[]{:S(2)}, u32[]{:S(2)}) collective-permute-start(bf16[4,2048]{1,0:T(4,128)(2,1)S(1)} %maximum_select_fusion.7), channel_id=1, source_target_pairs={{0,2},{1,3},{2,0},{3,1},{4,6},{5,7},{6,4},{7,5},{8,10},{9,11},{10,... | collective-permute-start | bytes 49160 | tf_op jit(solution)/shard_map/ppermute | solution.py:119
  6.0 0.8 %bitcast_convert_fusion = (f32[512,24]{0,1:T(8,128)S(1)}, f32[24,512]{1,0:T(8,128)S(1)}) fusion(bf16[24,512]{1,0:T(8,128)(2,1)} %param.15), kind=kLoop, calls=%fused_computation.65 | loop fusion | flops 24576 | bytes 122880
  6.8 0.9 %collective-permute-done.1 = bf16[4,2048]{1,0:T(4,128)(2,1)S(1)} collective-permute-done((bf16[4,2048]{1,0:T(4,128)(2,1)S(1)}, bf16[4,2048]{1,0:T(4,128)(2,1)S(1)}, u32[]{:S(2)}, u32[]{:S(2)}) %collective-permute-start.1) | collective-permute-done | bytes 16416 | tf_op jit(solution)/shard_map/ppermute | solution.py:119
  7.7 2.1 %collective-permute-start.2 = (bf16[8,2048]{1,0:T(8,128)(2,1)S(1)}, bf16[8,2048]{1,0:T(8,128)(2,1)S(1)}, u32[]{:S(2)}, u32[]{:S(2)}) collective-permute-start(bf16[8,2048]{1,0:T(8,128)(2,1)S(1)} %maximum_select_fusion.4), channel_id=1, source_target_pairs={{0,4},{1,5},{2,6},{3,7},{4,0},{5,1},{6,2},{7,3},{8,12},{9,13},{10,... | collective-permute-start | bytes 98312 | tf_op jit(solution)/shard_map/ppermute | solution.py:119
  10.6 1.1 %collective-permute-done.2 = bf16[8,2048]{1,0:T(8,128)(2,1)S(1)} collective-permute-done((bf16[8,2048]{1,0:T(8,128)(2,1)S(1)}, bf16[8,2048]{1,0:T(8,128)(2,1)S(1)}, u32[]{:S(2)}, u32[]{:S(2)}) %collective-permute-start.2) | collective-permute-done | bytes 32800 | tf_op jit(solution)/shard_map/ppermute | solution.py:119
  11.8 3.1 %collective-permute-start.3 = (bf16[16,2048]{1,0:T(8,128)(2,1)S(1)}, bf16[16,2048]{1,0:T(8,128)(2,1)S(1)}, u32[]{:S(2)}, u32[]{:S(2)}) collective-permute-start(bf16[16,2048]{1,0:T(8,128)(2,1)S(1)} %maximum_select_fusion.3), channel_id=1, source_target_pairs={{0,8},{1,9},{2,10},{3,11},{4,12},{5,13},{6,14},{7,15},{8,0},{9,1},... | collective-permute-start | bytes 196616 | tf_op jit(solution)/shard_map/ppermute | solution.py:119
  15.0 2.2 %collective-permute-done.3 = bf16[16,2048]{1,0:T(8,128)(2,1)S(1)} collective-permute-done((bf16[16,2048]{1,0:T(8,128)(2,1)S(1)}, bf16[16,2048]{1,0:T(8,128)(2,1)S(1)}, u32[]{:S(2)}, u32[]{:S(2)}) %collective-permute-start.3) | collective-permute-done | bytes 65568 | tf_op jit(solution)/shard_map/ppermute | solution.py:119
  19.6 0.9 %add_convert_fusion = (bf16[768,512]{1,0:T(8,128)(2,1)S(1)}, f32[768,512]{1,0:T(8,128)S(1)}) fusion(bf16[32,24,512]{2,1,0:T(8,128)(2,1)S(1)} %multiply_convert_fusion, f32[768,512]{1,0:T(8,128)S(1)} %fusion.15, bf16[256,512]{1,0:T(8,128)(2,1)S(1)} %copy-done.10, f32[768,512]{1,0:T(8,128)S(1)} %fusion.49, f32[256]{0:T(256)S(1)} %bitcast.47, f32[256]{0:T(256)S(1)} %bitcast.43), kind=kOutput, calls=%fused_computation.14 | convolution fusion | flops 206831616 | bytes 6555648 | tf_op jit(solution)/shard_map/dot_general | solution.py:55
  23.2 1.2 %fusion.12 = f32[768,512]{1,0:T(8,128)S(1)} fusion(bf16[512,512]{1,0:T(8,128)(2,1)S(1)} %copy-done.9, f32[768,512]{1,0:T(8,128)S(1)} %get-tuple-element.11, f32[768,512]{1,0:T(8,128)S(1)} %convolution_add_fusion), kind=kOutput, calls=%fused_computation.31 | convolution fusion | flops 410517504 | bytes 5242880 | tf_op jit(solution)/shard_map/dot_general | solution.py:69
  26.7 1.6 %collective-permute-done.4 = bf16[280,512]{1,0:T(8,128)(2,1)S(1)} collective-permute-done((bf16[280,512]{1,0:T(8,128)(2,1)S(1)}, bf16[280,512]{1,0:T(8,128)(2,1)S(1)}, u32[]{:S(2)}, u32[]{:S(2)}) %collective-permute-start.4) | collective-permute-done | bytes 286752 | tf_op jit(solution)/shard_map/ppermute | solution.py:150
  28.5 1.9 %collective-permute-start.5 = (bf16[140,512]{1,0:T(8,128)(2,1)S(1)}, bf16[140,512]{1,0:T(8,128)(2,1)S(1)}, u32[]{:S(2)}, u32[]{:S(2)}) collective-permute-start(bf16[140,512]{1,0:T(8,128)(2,1)S(1)} %select_convert_fusion.1), channel_id=1, source_target_pairs={{0,2},{1,3},{2,0},{3,1},{4,6},{5,7},{6,4},{7,5},{8,10},{9,11},{10,... | collective-permute-start | bytes 430088 | tf_op jit(solution)/shard_map/ppermute | solution.py:150
  30.4 4.1 %collective-permute-done.5 = bf16[140,512]{1,0:T(8,128)(2,1)S(1)} collective-permute-done((bf16[140,512]{1,0:T(8,128)(2,1)S(1)}, bf16[140,512]{1,0:T(8,128)(2,1)S(1)}, u32[]{:S(2)}, u32[]{:S(2)}) %collective-permute-start.5) | collective-permute-done | bytes 143392 | tf_op jit(solution)/shard_map/ppermute | solution.py:150
  34.6 1.8 %collective-permute-start.6 = (bf16[140,512]{1,0:T(8,128)(2,1)S(1)}, bf16[140,512]{1,0:T(8,128)(2,1)S(1)}, u32[]{:S(2)}, u32[]{:S(2)}) collective-permute-start(bf16[140,512]{1,0:T(8,128)(2,1)S(1)} %add_convert_fusion.7), channel_id=1, source_target_pairs={{0,4},{1,5},{2,6},{3,7},{4,0},{5,1},{6,2},{7,3},{8,12},{9,13},{10,... | collective-permute-start | bytes 430088 | tf_op jit(solution)/shard_map/ppermute | solution.py:156
  36.5 3.4 %collective-permute-done.6 = bf16[140,512]{1,0:T(8,128)(2,1)S(1)} collective-permute-done((bf16[140,512]{1,0:T(8,128)(2,1)S(1)}, bf16[140,512]{1,0:T(8,128)(2,1)S(1)}, u32[]{:S(2)}, u32[]{:S(2)}) %collective-permute-start.6) | collective-permute-done | bytes 143392 | tf_op jit(solution)/shard_map/ppermute | solution.py:156
  39.9 3.2 %collective-permute-start.7 = (bf16[140,512]{1,0:T(8,128)(2,1)S(1)}, bf16[140,512]{1,0:T(8,128)(2,1)S(1)}, u32[]{:S(2)}, u32[]{:S(2)}) collective-permute-start(bf16[140,512]{1,0:T(8,128)(2,1)S(1)} %add_convert_fusion.6), channel_id=1, source_target_pairs={{0,8},{1,9},{2,10},{3,11},{4,12},{5,13},{6,14},{7,15},{8,0},{9,1},... | collective-permute-start | bytes 430088 | tf_op jit(solution)/shard_map/ppermute | solution.py:156
  43.1 5.9 %collective-permute-done.7 = bf16[140,512]{1,0:T(8,128)(2,1)S(1)} collective-permute-done((bf16[140,512]{1,0:T(8,128)(2,1)S(1)}, bf16[140,512]{1,0:T(8,128)(2,1)S(1)}, u32[]{:S(2)}, u32[]{:S(2)}) %collective-permute-start.7) | collective-permute-done | bytes 143392 | tf_op jit(solution)/shard_map/ppermute | solution.py:156
  49.0 1.6 %collective-permute-start.8 = (bf16[140,512]{1,0:T(8,128)(2,1)S(1)}, bf16[140,512]{1,0:T(8,128)(2,1)S(1)}, u32[]{:S(2)}, u32[]{:S(2)}) collective-permute-start(bf16[140,512]{1,0:T(8,128)(2,1)S(1)} %add_convert_fusion.5), channel_id=1, source_target_pairs={{0,2},{1,3},{2,0},{3,1},{4,6},{5,7},{6,4},{7,5},{8,10},{9,11},{10,... | collective-permute-start | bytes 430088 | tf_op jit(solution)/shard_map/ppermute | solution.py:161
  50.6 3.6 %collective-permute-done.8 = bf16[140,512]{1,0:T(8,128)(2,1)S(1)} collective-permute-done((bf16[140,512]{1,0:T(8,128)(2,1)S(1)}, bf16[140,512]{1,0:T(8,128)(2,1)S(1)}, u32[]{:S(2)}, u32[]{:S(2)}) %collective-permute-start.8) | collective-permute-done | bytes 143392 | tf_op jit(solution)/shard_map/ppermute | solution.py:161
  54.4 1.5 %collective-permute-done.9 = bf16[280,512]{1,0:T(8,128)(2,1)S(1)} collective-permute-done((bf16[280,512]{1,0:T(8,128)(2,1)S(1)}, bf16[280,512]{1,0:T(8,128)(2,1)S(1)}, u32[]{:S(2)}, u32[]{:S(2)}) %collective-permute-start.9) | collective-permute-done | bytes 286752 | tf_op jit(solution)/shard_map/ppermute | solution.py:161
  56.2 1.1 %slice_convert_fusion = f32[512,512]{1,0:T(8,128)} fusion(bf16[560,512]{1,0:T(8,128)(2,1)S(1)} %maximum_select_fusion), kind=kLoop, calls=%fused_computation.38 | loop fusion | flops 262144 | bytes 1572864 | tf_op jit(solution)/shard_map/convert_element_type | solution.py:225
  57.9 1.3 %fusion.50 = f32[512,512]{1,0:T(8,128)} fusion(bf16[32,512]{1,0:T(8,128)(2,1)S(1)} %fusion.8, bf16[32,512]{1,0:T(8,128)(2,1)S(1)} %gather_fusion), kind=kOutput, calls=%fused_computation.89 | convolution fusion | flops 16777216 | bytes 1114112 | tf_op jit(solution)/shard_map/dot_general | solution.py:91
  59.8 3.0 %fusion.11 = f32[2048,512]{1,0:T(8,128)} fusion(bf16[512,512]{1,0:T(8,128)(2,1)S(1)} %copy-done.1, bf16[32,512]{1,0:T(8,128)(2,1)S(1)} %fusion.8, bf16[16,2048]{1,0:T(8,128)(2,1)S(1)} %collective-permute-done.3, bf16[16,2048]{1,0:T(8,128)(2,1)S(1)} %maximum_select_fusion.3, pred[]{:T(512)S(6)} %eq.38, bf16[32,512]{1,0:T(8,128)(2,1)S(1)} %gather_fusion), kind=kOutput, calls=%fused_computation.24 | convolution fusion | flops 84557824 | bytes 4915201 | tf_op jit(solution)/shard_map/dot_general | solution.py:98
  (58 shorter events, 10.7 us)
Async XLA Ops:
  0.6 16.5 %copy-start = (bf16[2048,512]{1,0:T(8,128)(2,1)S(1)}, bf16[2048,512]{1,0:T(8,128)(2,1)}, u32[]{:S(2)}) copy-start(bf16[2048,512]{1,0:T(8,128)(2,1)} %param.13) | copy-start | bytes 6291460
  0.6 17.0 %copy-start.1 = (bf16[512,512]{1,0:T(8,128)(2,1)S(1)}, bf16[512,512]{1,0:T(8,128)(2,1)}, u32[]{:S(2)}) copy-start(bf16[512,512]{1,0:T(8,128)(2,1)} %param.14) | copy-start | bytes 1572868
  0.7 17.0 %copy-start.7 = (s32[32]{0:T(128)S(1)}, s32[32]{0:T(128)}, u32[]{:S(2)}) copy-start(s32[32]{0:T(128)} %param.12) | copy-start | bytes 388
  0.7 1.6 %collective-permute-start = (bf16[2,2048]{1,0:T(2,128)(2,1)}, bf16[2,2048]{1,0:T(2,128)(2,1)S(1)}, u32[]{:S(2)}, u32[]{:S(2)}) collective-permute-start(bf16[2,2048]{1,0:T(2,128)(2,1)} %param.10), channel_id=1, source_target_pairs={{0,1},{1,0},{2,3},{3,2},{4,5},{5,4},{6,7},{7,6},{8,9},{9,8},{10,11... | collective-permute-start | bytes 24584 | tf_op jit(solution)/shard_map/ppermute | solution.py:119
  3.0 4.6 %collective-permute-start.1 = (bf16[4,2048]{1,0:T(4,128)(2,1)S(1)}, bf16[4,2048]{1,0:T(4,128)(2,1)S(1)}, u32[]{:S(2)}, u32[]{:S(2)}) collective-permute-start(bf16[4,2048]{1,0:T(4,128)(2,1)S(1)} %maximum_select_fusion.7), channel_id=1, source_target_pairs={{0,2},{1,3},{2,0},{3,1},{4,6},{5,7},{6,4},{7,5},{8,10},{9,11},{10,... | collective-permute-start | bytes 49160 | tf_op jit(solution)/shard_map/ppermute | solution.py:119
  7.7 4.0 %collective-permute-start.2 = (bf16[8,2048]{1,0:T(8,128)(2,1)S(1)}, bf16[8,2048]{1,0:T(8,128)(2,1)S(1)}, u32[]{:S(2)}, u32[]{:S(2)}) collective-permute-start(bf16[8,2048]{1,0:T(8,128)(2,1)S(1)} %maximum_select_fusion.4), channel_id=1, source_target_pairs={{0,4},{1,5},{2,6},{3,7},{4,0},{5,1},{6,2},{7,3},{8,12},{9,13},{10,... | collective-permute-start | bytes 98312 | tf_op jit(solution)/shard_map/ppermute | solution.py:119
  11.8 5.3 %collective-permute-start.3 = (bf16[16,2048]{1,0:T(8,128)(2,1)S(1)}, bf16[16,2048]{1,0:T(8,128)(2,1)S(1)}, u32[]{:S(2)}, u32[]{:S(2)}) collective-permute-start(bf16[16,2048]{1,0:T(8,128)(2,1)S(1)} %maximum_select_fusion.3), channel_id=1, source_target_pairs={{0,8},{1,9},{2,10},{3,11},{4,12},{5,13},{6,14},{7,15},{8,0},{9,1},... | collective-permute-start | bytes 196616 | tf_op jit(solution)/shard_map/ppermute | solution.py:119
  14.9 3.1 %copy-start.3 = (bf16[512,512]{1,0:T(8,128)(2,1)S(1)}, bf16[512,512]{1,0:T(8,128)(2,1)}, u32[]{:S(2)}) copy-start(bf16[512,512]{1,0:T(8,128)(2,1)} %constant.111.clone) | copy-start | bytes 1572868
  18.1 1.0 %copy-start.5 = (bf16[256,512]{1,0:T(8,128)(2,1)S(1)}, bf16[256,512]{1,0:T(8,128)(2,1)}, u32[]{:S(2)}) copy-start(bf16[256,512]{1,0:T(8,128)(2,1)} %constant.116) | copy-start | bytes 786436
  18.6 1.0 %copy-start.10 = (bf16[256,512]{1,0:T(8,128)(2,1)S(1)}, bf16[256,512]{1,0:T(8,128)(2,1)}, u32[]{:S(2)}) copy-start(bf16[256,512]{1,0:T(8,128)(2,1)} %constant.117) | copy-start | bytes 786436
  19.6 1.0 %copy-start.2 = (bf16[512,512]{1,0:T(8,128)(2,1)S(1)}, bf16[512,512]{1,0:T(8,128)(2,1)}, u32[]{:S(2)}) copy-start(bf16[512,512]{1,0:T(8,128)(2,1)} %param.17) | copy-start | bytes 1572868
  19.6 1.3 %copy-start.8 = (bf16[32,24,512]{2,1,0:T(8,128)(2,1)S(1)}, bf16[32,24,512]{2,1,0:T(8,128)(2,1)}, u32[]{:S(2)}) copy-start(bf16[32,24,512]{2,1,0:T(8,128)(2,1)} %param.11) | copy-start | bytes 2359300
  22.2 1.0 %copy-start.9 = (bf16[512,512]{1,0:T(8,128)(2,1)S(1)}, bf16[512,512]{1,0:T(8,128)(2,1)}, u32[]{:S(2)}) copy-start(bf16[512,512]{1,0:T(8,128)(2,1)} %constant.112.clone) | copy-start | bytes 1572868
  24.4 1.0 %copy-start.4 = (bf16[512,256]{1,0:T(8,128)(2,1)S(1)}, bf16[512,256]{1,0:T(8,128)(2,1)}, u32[]{:S(2)}) copy-start(bf16[512,256]{1,0:T(8,128)(2,1)} %constant.118) | copy-start | bytes 786436
  24.6 1.1 %copy-start.6 = (bf16[512,256]{1,0:T(8,128)(2,1)S(1)}, bf16[512,256]{1,0:T(8,128)(2,1)}, u32[]{:S(2)}) copy-start(bf16[512,256]{1,0:T(8,128)(2,1)} %constant.119) | copy-start | bytes 786436
  26.6 1.6 %collective-permute-start.4 = (bf16[280,512]{1,0:T(8,128)(2,1)S(1)}, bf16[280,512]{1,0:T(8,128)(2,1)S(1)}, u32[]{:S(2)}, u32[]{:S(2)}) collective-permute-start(bf16[280,512]{1,0:T(8,128)(2,1)S(1)} %select_convert_fusion), channel_id=1, source_target_pairs={{0,1},{1,0},{2,3},{3,2},{4,5},{5,4},{6,7},{7,6},{8,9},{9,8},{10,11... | collective-permute-start | bytes 860168 | tf_op jit(solution)/shard_map/ppermute | solution.py:150
  28.5 6.1 %collective-permute-start.5 = (bf16[140,512]{1,0:T(8,128)(2,1)S(1)}, bf16[140,512]{1,0:T(8,128)(2,1)S(1)}, u32[]{:S(2)}, u32[]{:S(2)}) collective-permute-start(bf16[140,512]{1,0:T(8,128)(2,1)S(1)} %select_convert_fusion.1), channel_id=1, source_target_pairs={{0,2},{1,3},{2,0},{3,1},{4,6},{5,7},{6,4},{7,5},{8,10},{9,11},{10,... | collective-permute-start | bytes 430088 | tf_op jit(solution)/shard_map/ppermute | solution.py:150
  34.6 5.3 %collective-permute-start.6 = (bf16[140,512]{1,0:T(8,128)(2,1)S(1)}, bf16[140,512]{1,0:T(8,128)(2,1)S(1)}, u32[]{:S(2)}, u32[]{:S(2)}) collective-permute-start(bf16[140,512]{1,0:T(8,128)(2,1)S(1)} %add_convert_fusion.7), channel_id=1, source_target_pairs={{0,4},{1,5},{2,6},{3,7},{4,0},{5,1},{6,2},{7,3},{8,12},{9,13},{10,... | collective-permute-start | bytes 430088 | tf_op jit(solution)/shard_map/ppermute | solution.py:156
  39.9 9.0 %collective-permute-start.7 = (bf16[140,512]{1,0:T(8,128)(2,1)S(1)}, bf16[140,512]{1,0:T(8,128)(2,1)S(1)}, u32[]{:S(2)}, u32[]{:S(2)}) collective-permute-start(bf16[140,512]{1,0:T(8,128)(2,1)S(1)} %add_convert_fusion.6), channel_id=1, source_target_pairs={{0,8},{1,9},{2,10},{3,11},{4,12},{5,13},{6,14},{7,15},{8,0},{9,1},... | collective-permute-start | bytes 430088 | tf_op jit(solution)/shard_map/ppermute | solution.py:156
  49.0 5.2 %collective-permute-start.8 = (bf16[140,512]{1,0:T(8,128)(2,1)S(1)}, bf16[140,512]{1,0:T(8,128)(2,1)S(1)}, u32[]{:S(2)}, u32[]{:S(2)}) collective-permute-start(bf16[140,512]{1,0:T(8,128)(2,1)S(1)} %add_convert_fusion.5), channel_id=1, source_target_pairs={{0,2},{1,3},{2,0},{3,1},{4,6},{5,7},{6,4},{7,5},{8,10},{9,11},{10,... | collective-permute-start | bytes 430088 | tf_op jit(solution)/shard_map/ppermute | solution.py:161
  54.3 1.6 %collective-permute-start.9 = (bf16[280,512]{1,0:T(8,128)(2,1)S(1)}, bf16[280,512]{1,0:T(8,128)(2,1)S(1)}, u32[]{:S(2)}, u32[]{:S(2)}) collective-permute-start(bf16[280,512]{1,0:T(8,128)(2,1)S(1)} %maximum_select_fusion.1), channel_id=1, source_target_pairs={{0,1},{1,0},{2,3},{3,2},{4,5},{5,4},{6,7},{7,6},{8,9},{9,8},{10,11... | collective-permute-start | bytes 860168 | tf_op jit(solution)/shard_map/ppermute | solution.py:161

commit v8 on v7

--- a/solution.py
+++ b/solution.py
@@ -1,3 +1,4 @@
+import functools
 import math
 
 import jax
@@ -5,6 +6,8 @@
 import numpy as np
 import jax.numpy as jnp
 from jax import lax
+from jax.experimental import pallas as pl
+from jax.experimental.pallas import tpu as pltpu
 from jax.sharding import PartitionSpec as P
 
 
@@ -167,6 +170,84 @@
     return values
 
 
+def _encoder_tail_kernel(
+    rows_out,
+    samples,
+    packed_ref,
+    selection_ref,
+    codes_ref,
+    codes_t_ref,
+    decoder_ref,
+    inputs_t_ref,
+    grad_enc_ref,
+    grad_dec_ref,
+    grad_out_ref,
+    grad_filter_ref,
+    grad_pre_ref,
+):
+    @pl.when(pl.program_id(0) == 0)
+    def _():
+        grad_out_ref[...] = packed_ref[pl.ds(0, rows_out), :].astype(jnp.float32)
+        sums = packed_ref[pl.ds(rows_out, samples), :]
+        latent_half = jnp.dot(
+            selection_ref[...], sums, preferred_element_type=jnp.float32
+        ).astype(jnp.bfloat16)
+        grad_dec_ref[...] = jnp.dot(
+            codes_t_ref[...], latent_half, preferred_element_type=jnp.float32
+        )
+        grad_codes = lax.dot_general(
+            latent_half,
+            decoder_ref[...],
+            (((1,), (1,)), ((), ())),
+            preferred_element_type=jnp.float32,
+        )
+        codes = codes_ref[...].astype(jnp.float32)
+        grad_pre_ref[...] = (grad_codes * (1.0 - jnp.square(codes))).astype(jnp.bfloat16)
+        filter_row = packed_ref[pl.ds(rows_out + samples, 1), :].astype(jnp.float32)
+        half = filter_row.shape[1] // 2
+        grad_filter_ref[pl.ds(0, 1), :] = filter_row[:, :half]
+        grad_filter_ref[pl.ds(1, 1), :] = filter_row[:, half:]
+
+    grad_enc_ref[...] = jnp.dot(
+        inputs_t_ref[...], grad_pre_ref[...], preferred_element_type=jnp.float32
+    )
+
+
+def encoder_tail(packed, rows_out, samples, selection_t, codes, decoder_weight, inputs_rows):
+    width = packed.shape[1]
+    enc_in = inputs_rows.shape[1]
+    code = codes.shape[1]
+    steps = 4 if enc_in % (4 * 8) == 0 else 1
+    tile = enc_in // steps
+    whole = lambda shape: pl.BlockSpec(shape, lambda i: (0,) * len(shape))
+    return pl.pallas_call(
+        functools.partial(_encoder_tail_kernel, rows_out, samples),
+        grid=(steps,),
+        in_specs=[
+            whole(packed.shape),
+            whole(selection_t.shape),
+            whole(codes.shape),
+            whole((code, samples)),
+            whole(decoder_weight.shape),
+            pl.BlockSpec((tile, samples), lambda i: (i, 0)),
+        ],
+        out_specs=[
+            pl.BlockSpec((tile, code), lambda i: (i, 0)),
+            whole((code, width)),
+            whole((rows_out, width)),
+            whole((2, width // 2)),
+        ],
+        out_shape=[
+            jax.ShapeDtypeStruct((enc_in, code), jnp.float32),
+            jax.ShapeDtypeStruct((code, width), jnp.float32),
+            jax.ShapeDtypeStruct((rows_out, width), jnp.float32),
+            jax.ShapeDtypeStruct((2, width // 2), jnp.float32),
+        ],
+        scratch_shapes=[pltpu.VMEM((samples, code), jnp.bfloat16)],
+        compiler_params=pltpu.CompilerParams(dimension_semantics=("arbitrary",)),
+    )(packed, selection_t, codes, codes.T, decoder_weight, inputs_rows.T)
+
+
 def local(
     encoder_input,
     desired_responses,
@@ -221,12 +302,11 @@
         0,
     )
     packed = sum_halving(packed, "freq")
-    rows_out = grad_out.shape[0]
-    grad_out = packed[:rows_out].astype(jnp.float32)
-    derivative_bottleneck = packed[rows_out : rows_out + samples].astype(jnp.float32)
-    grad_filter = packed[rows_out + samples].astype(jnp.float32).reshape(grad_filter.shape)
-    grad_enc, grad_dec = encoder_grads(
-        all_inputs, codes, derivative_bottleneck[sample_index], decoder_weight
+    selection_t = (
+        sample_index[:, None] == jnp.arange(samples, dtype=jnp.int32)[None, :]
+    ).astype(jnp.bfloat16)
+    grad_enc, grad_dec, grad_out, grad_filter = encoder_tail(
+        packed, grad_out.shape[0], samples, selection_t, codes, decoder_weight, all_inputs
     )
     return (grad_enc, grad_dec, grad_out, grad_filter)
 

time: 63.1 us -> 67.2 us (1.065)
  Pallas kernels: 0 us -> 5.73 us
  other arithmetic: 4.26 us -> 6.47 us
  waiting for transfers between devices: 25.4 us -> 23.3 us
  matrix products: 10.7 us -> 8.67 us
    pallas_call x0 -> x1, Pallas kernels: none -> 5.73 us  [encoder_tail(): pl.pallas_call(functools.partial(_encoder_tail_kernel, rows_out, samples)...]
    dot_general x2 -> x0, matrix products: 4.24 us -> none  [the longest x1 2.96 us: encoder_grads(): lax.dot_general(inputs_rows, grad_pre, (((0,), (0,)), ((), ())), preferre...]
    ppermute x2, waiting for transfers between devices: 5.16 us -> 3.08 us  [sum_halving(): other = lax.ppermute(values, axis_name, _exchange_pairs(count, distance))]
    select_n x2, other arithmetic: 0.32 us -> 2.12 us  [sum_halving(): jnp.where(lower, jnp.concatenate([values, other], 0), jnp.concatenate([ot...]
    dot_general x1, matrix products: 0.27 us -> 1.39 us  [local(): jnp.dot(codes_by_sample, decoder_weight, preferred_element_type=jnp.float32)]
    dot_general x1, matrix products: 0.57 us -> 1.65 us  [decode_rows(): jnp.dot(mixed_in, forward_transform, preferred_element_type=jnp.float32)]
    transpose x0 -> x1, other arithmetic: none -> 0.86 us  [encoder_tail(): return pl.pallas_call(functools.partial(_encoder_tail_kernel, rows_out, s...]
    unnamed x23 -> x21, local copies, waits for them, and re-layouts: 2.14 us -> 2.12 us
  transfers between devices with their start and end apart: 10 -> 10, of which waited for: 10 -> 10; matrix products, arithmetic and copies ran while one was open for 3% -> 6% of each run, Pallas kernels for 0% -> 0%
where the time goes in v8:
time: 67.2 us; the launch traced here: 66.7 us
  waiting for transfers between devices  23.3 us (35%)
  starting transfers between devices  17.4 us (26%)
  matrix products  8.67 us (13%)
  other arithmetic  6.47 us (10%)
  Pallas kernels  5.73 us (9%)
  local copies, waits for them, and re-layouts  4.32 us (6%)
  between operations  0.9 us (1%)
    ppermute x2, waiting for transfers between devices, sum_halving(): arrived = lax.ppermute(values, axis_name, _exchange_pairs(count, distance))  9.23 us
    ppermute x4, starting transfers between devices, gather_rows(): other = lax.ppermute(block, axis_name, _exchange_pairs(count, distance))  8.68 us
    pallas_call x1, Pallas kernels, encoder_tail(): pl.pallas_call(functools.partial(_encoder_tail_kernel, rows_out, samples)...  5.73 us
    ppermute x2, waiting for transfers between devices, sum_halving(): arrived = lax.ppermute(send, axis_name, _exchange_pairs(count, distance))  5.71 us
    ppermute x4, waiting for transfers between devices, gather_rows(): other = lax.ppermute(block, axis_name, _exchange_pairs(count, distance))  5.23 us
    ppermute x2, starting transfers between devices, sum_halving(): arrived = lax.ppermute(values, axis_name, _exchange_pairs(count, distance))  5.06 us
    ppermute x2, waiting for transfers between devices, sum_halving(): other = lax.ppermute(values, axis_name, _exchange_pairs(count, distance))  3.08 us
    select_n x2, other arithmetic, sum_halving(): jnp.where(lower, jnp.concatenate([values, other], 0), jnp.concatenate([ot...  2.12 us
  transfers between devices with their start and end apart: 10, of which 10 were waited for; matrix products, arithmetic and copies ran while one was open for 6% of the time, Pallas kernels for 0%

profile of v8, /device:TPU:0, one launch (start us, length us, event | category | flops | bytes accessed | tf_op | source)
XLA Modules:
  0.0 66.7 jit_solution(11927604802387675125)
XLA Ops:
  1.2 1.0 %collective-permute-done = bf16[2,2048]{1,0:T(2,128)(2,1)S(1)} collective-permute-done((bf16[2,2048]{1,0:T(2,128)(2,1)}, bf16[2,2048]{1,0:T(2,128)(2,1)S(1)}, u32[]{:S(2)}, u32[]{:S(2)}) %collective-permute-start) | collective-permute-done | bytes 8224 | tf_op jit(solution)/shard_map/ppermute | solution.py:122
  3.0 2.9 %collective-permute-start.1 = (bf16[4,2048]{1,0:T(4,128)(2,1)S(1)}, bf16[4,2048]{1,0:T(4,128)(2,1)S(1)}, u32[]{:S(2)}, u32[]{:S(2)}) collective-permute-start(bf16[4,2048]{1,0:T(4,128)(2,1)S(1)} %maximum_select_fusion.4), channel_id=1, source_target_pairs={{0,2},{1,3},{2,0},{3,1},{4,6},{5,7},{6,4},{7,5},{8,10},{9,11},{10,... | collective-permute-start | bytes 49160 | tf_op jit(solution)/shard_map/ppermute | solution.py:122
  6.8 0.9 %collective-permute-done.1 = bf16[4,2048]{1,0:T(4,128)(2,1)S(1)} collective-permute-done((bf16[4,2048]{1,0:T(4,128)(2,1)S(1)}, bf16[4,2048]{1,0:T(4,128)(2,1)S(1)}, u32[]{:S(2)}, u32[]{:S(2)}) %collective-permute-start.1) | collective-permute-done | bytes 16416 | tf_op jit(solution)/shard_map/ppermute | solution.py:122
  7.7 2.1 %collective-permute-start.2 = (bf16[8,2048]{1,0:T(8,128)(2,1)S(1)}, bf16[8,2048]{1,0:T(8,128)(2,1)S(1)}, u32[]{:S(2)}, u32[]{:S(2)}) collective-permute-start(bf16[8,2048]{1,0:T(8,128)(2,1)S(1)} %maximum_select_fusion.3), channel_id=1, source_target_pairs={{0,4},{1,5},{2,6},{3,7},{4,0},{5,1},{6,2},{7,3},{8,12},{9,13},{10,... | collective-permute-start | bytes 98312 | tf_op jit(solution)/shard_map/ppermute | solution.py:122
  10.6 1.1 %collective-permute-done.2 = bf16[8,2048]{1,0:T(8,128)(2,1)S(1)} collective-permute-done((bf16[8,2048]{1,0:T(8,128)(2,1)S(1)}, bf16[8,2048]{1,0:T(8,128)(2,1)S(1)}, u32[]{:S(2)}, u32[]{:S(2)}) %collective-permute-start.2) | collective-permute-done | bytes 32800 | tf_op jit(solution)/shard_map/ppermute | solution.py:122
  11.7 3.1 %collective-permute-start.3 = (bf16[16,2048]{1,0:T(8,128)(2,1)S(1)}, bf16[16,2048]{1,0:T(8,128)(2,1)S(1)}, u32[]{:S(2)}, u32[]{:S(2)}) collective-permute-start(bf16[16,2048]{1,0:T(8,128)(2,1)S(1)} %maximum_select_fusion.2), channel_id=1, source_target_pairs={{0,8},{1,9},{2,10},{3,11},{4,12},{5,13},{6,14},{7,15},{8,0},{9,1},... | collective-permute-start | bytes 196616 | tf_op jit(solution)/shard_map/ppermute | solution.py:122
  14.9 2.2 %collective-permute-done.3 = bf16[16,2048]{1,0:T(8,128)(2,1)S(1)} collective-permute-done((bf16[16,2048]{1,0:T(8,128)(2,1)S(1)}, bf16[16,2048]{1,0:T(8,128)(2,1)S(1)}, u32[]{:S(2)}, u32[]{:S(2)}) %collective-permute-start.3) | collective-permute-done | bytes 65568 | tf_op jit(solution)/shard_map/ppermute | solution.py:122
  18.4 1.4 %fusion.8 = f32[32,512]{1,0:T(8,128)S(1)} fusion(bf16[512,512]{1,0:T(8,128)(2,1)} %decoder_ref.1, bf16[32,512]{0,1:T(8,128)(2,1)S(1)} %copy.25, s32[32]{0:T(128)S(1)} %copy-done.6), kind=kOutput, calls=%fused_computation.19 | convolution fusion | flops 17843200 | bytes 622720 | tf_op jit(solution)/shard_map/dot_general | solution.py:276
  19.9 1.7 %fusion.36 = f32[768,512]{1,0:T(8,128)S(1)} fusion(bf16[768,512]{1,0:T(8,128)(2,1)S(1)} %bitcast.36, bf16[512,512]{1,0:T(8,128)(2,1)} %constant.107.clone), kind=kOutput, calls=%fused_computation.72 | convolution fusion | flops 402653184 | bytes 2883584 | tf_op jit(solution)/shard_map/dot_general | solution.py:51
  22.5 0.9 %add_convert_fusion = (bf16[768,512]{1,0:T(8,128)(2,1)S(1)}, f32[768,512]{1,0:T(8,128)S(1)}) fusion(bf16[32,24,512]{2,1,0:T(8,128)(2,1)S(1)} %multiply_convert_fusion, f32[768,512]{1,0:T(8,128)S(1)} %fusion.12, bf16[256,512]{1,0:T(8,128)(2,1)S(1)} %copy-done.9, f32[768,512]{1,0:T(8,128)S(1)} %fusion.36, f32[256]{0:T(256)S(1)} %bitcast.47, f32[256]{0:T(256)S(1)} %bitcast.43), kind=kOutput, calls=%fused_computation.13 | convolution fusion | flops 206831616 | bytes 6555648 | tf_op jit(solution)/shard_map/dot_general | solution.py:58
  26.1 1.2 %fusion.9 = f32[768,512]{1,0:T(8,128)S(1)} fusion(bf16[512,512]{1,0:T(8,128)(2,1)S(1)} %copy-done.8, f32[768,512]{1,0:T(8,128)S(1)} %get-tuple-element.13, f32[768,512]{1,0:T(8,128)S(1)} %convolution_add_fusion), kind=kOutput, calls=%fused_computation.26 | convolution fusion | flops 410517504 | bytes 5242880 | tf_op jit(solution)/shard_map/dot_general | solution.py:72
  29.6 1.6 %collective-permute-done.4 = bf16[280,512]{1,0:T(8,128)(2,1)S(1)} collective-permute-done((bf16[280,512]{1,0:T(8,128)(2,1)S(1)}, bf16[280,512]{1,0:T(8,128)(2,1)S(1)}, u32[]{:S(2)}, u32[]{:S(2)}) %collective-permute-start.4) | collective-permute-done | bytes 286752 | tf_op jit(solution)/shard_map/ppermute | solution.py:153
  31.4 1.9 %collective-permute-start.5 = (bf16[140,512]{1,0:T(8,128)(2,1)S(1)}, bf16[140,512]{1,0:T(8,128)(2,1)S(1)}, u32[]{:S(2)}, u32[]{:S(2)}) collective-permute-start(bf16[140,512]{1,0:T(8,128)(2,1)S(1)} %select_convert_fusion.1), channel_id=1, source_target_pairs={{0,2},{1,3},{2,0},{3,1},{4,6},{5,7},{6,4},{7,5},{8,10},{9,11},{10,... | collective-permute-start | bytes 430088 | tf_op jit(solution)/shard_map/ppermute | solution.py:153
  33.3 4.1 %collective-permute-done.5 = bf16[140,512]{1,0:T(8,128)(2,1)S(1)} collective-permute-done((bf16[140,512]{1,0:T(8,128)(2,1)S(1)}, bf16[140,512]{1,0:T(8,128)(2,1)S(1)}, u32[]{:S(2)}, u32[]{:S(2)}) %collective-permute-start.5) | collective-permute-done | bytes 143392 | tf_op jit(solution)/shard_map/ppermute | solution.py:153
  37.5 1.9 %collective-permute-start.6 = (bf16[140,512]{1,0:T(8,128)(2,1)S(1)}, bf16[140,512]{1,0:T(8,128)(2,1)S(1)}, u32[]{:S(2)}, u32[]{:S(2)}) collective-permute-start(bf16[140,512]{1,0:T(8,128)(2,1)S(1)} %add_convert_fusion.7), channel_id=1, source_target_pairs={{0,4},{1,5},{2,6},{3,7},{4,0},{5,1},{6,2},{7,3},{8,12},{9,13},{10,... | collective-permute-start | bytes 430088 | tf_op jit(solution)/shard_map/ppermute | solution.py:159
  39.4 3.4 %collective-permute-done.6 = bf16[140,512]{1,0:T(8,128)(2,1)S(1)} collective-permute-done((bf16[140,512]{1,0:T(8,128)(2,1)S(1)}, bf16[140,512]{1,0:T(8,128)(2,1)S(1)}, u32[]{:S(2)}, u32[]{:S(2)}) %collective-permute-start.6) | collective-permute-done | bytes 143392 | tf_op jit(solution)/shard_map/ppermute | solution.py:159
  42.8 3.2 %collective-permute-start.7 = (bf16[140,512]{1,0:T(8,128)(2,1)S(1)}, bf16[140,512]{1,0:T(8,128)(2,1)S(1)}, u32[]{:S(2)}, u32[]{:S(2)}) collective-permute-start(bf16[140,512]{1,0:T(8,128)(2,1)S(1)} %add_convert_fusion.6), channel_id=1, source_target_pairs={{0,8},{1,9},{2,10},{3,11},{4,12},{5,13},{6,14},{7,15},{8,0},{9,1},... | collective-permute-start | bytes 430088 | tf_op jit(solution)/shard_map/ppermute | solution.py:159
  46.0 5.9 %collective-permute-done.7 = bf16[140,512]{1,0:T(8,128)(2,1)S(1)} collective-permute-done((bf16[140,512]{1,0:T(8,128)(2,1)S(1)}, bf16[140,512]{1,0:T(8,128)(2,1)S(1)}, u32[]{:S(2)}, u32[]{:S(2)}) %collective-permute-start.7) | collective-permute-done | bytes 143392 | tf_op jit(solution)/shard_map/ppermute | solution.py:159
  51.9 1.6 %collective-permute-start.8 = (bf16[140,512]{1,0:T(8,128)(2,1)S(1)}, bf16[140,512]{1,0:T(8,128)(2,1)}, u32[]{:S(2)}, u32[]{:S(2)}) collective-permute-start(bf16[140,512]{1,0:T(8,128)(2,1)S(1)} %add_convert_fusion.5), channel_id=1, source_target_pairs={{0,2},{1,3},{2,0},{3,1},{4,6},{5,7},{6,4},{7,5},{8,10},{9,11},{10,... | collective-permute-start | bytes 430088 | tf_op jit(solution)/shard_map/ppermute | solution.py:164
  54.8 2.4 %collective-permute-done.8 = bf16[140,512]{1,0:T(8,128)(2,1)} collective-permute-done((bf16[140,512]{1,0:T(8,128)(2,1)S(1)}, bf16[140,512]{1,0:T(8,128)(2,1)}, u32[]{:S(2)}, u32[]{:S(2)}) %collective-permute-start.8) | collective-permute-done | bytes 143392 | tf_op jit(solution)/shard_map/ppermute | solution.py:164
  57.2 1.1 %maximum_select_fusion.1 = bf16[280,512]{1,0:T(8,128)(2,1)S(1)} fusion(bf16[140,512]{1,0:T(8,128)(2,1)} %collective-permute-done.8, bf16[140,512]{1,0:T(8,128)(2,1)S(1)} %add_convert_fusion.5, pred[]{:T(512)S(6)} %eq.52), kind=kLoop, calls=%fused_computation.51 | loop fusion | flops 1290240 | bytes 573441 | tf_op jit(solution)/shard_map/jit(_where)/select_n | solution.py:166
  58.4 0.9 %fusion.25.inputs_t_ref = bf16[2048,32]{1,0:T(8,128)(2,1)} fusion(bf16[32,2048]{0,1:T(8,128)(2,1)S(1)} %copy.23, bf16[32,2048]{0,1:T(8,128)(2,1)S(1)} %copy.24, pred[]{:T(512)S(6)} %eq.56), kind=kLoop, calls=%fused_computation.52 | loop fusion | flops 65536 | bytes 393217 | tf_op jit(solution)/shard_map/transpose | solution.py:248
  59.9 1.0 %maximum_select_fusion.packed_ref = bf16[560,512]{1,0:T(8,128)(2,1)} fusion(bf16[280,512]{1,0:T(8,128)(2,1)S(1)} %collective-permute-done.9, bf16[280,512]{1,0:T(8,128)(2,1)S(1)} %maximum_select_fusion.1, pred[]{:T(512)S(6)} %eq.51), kind=kLoop, calls=%fused_computation.30 | loop fusion | flops 2580480 | bytes 1146881 | tf_op jit(solution)/shard_map/jit(_where)/select_n | solution.py:166
  61.0 5.7 %shard_map.129 = (f32[2048,512]{1,0:T(8,128)}, f32[512,512]{1,0:T(8,128)}, f32[512,512]{1,0:T(8,128)}, f32[2,256]{1,0:T(2,128)}) custom-call(bf16[560,512]{1,0:T(8,128)(2,1)} %maximum_select_fusion.packed_ref, bf16[32,32]{1,0:T(8,128)(2,1)} %fusion.26.selection_ref, bf16[32,512]{1,0:T(8,128)(2,1)} %copy.26.codes_ref, bf16[512,32]{1,0:T(8,128)(2,1)} %bitcast.37, ...), custom_call_target="tpu_custom_call" | custom-call | tf_op jit(solution)/shard_map/pallas_call | solution.py:223
  (55 shorter events, 12.7 us)
Async XLA Ops:
  0.6 17.1 %copy-start = (bf16[2048,512]{1,0:T(8,128)(2,1)S(1)}, bf16[2048,512]{1,0:T(8,128)(2,1)}, u32[]{:S(2)}) copy-start(bf16[2048,512]{1,0:T(8,128)(2,1)} %param.13) | copy-start | bytes 6291460
  0.6 1.6 %collective-permute-start = (bf16[2,2048]{1,0:T(2,128)(2,1)}, bf16[2,2048]{1,0:T(2,128)(2,1)S(1)}, u32[]{:S(2)}, u32[]{:S(2)}) collective-permute-start(bf16[2,2048]{1,0:T(2,128)(2,1)} %param.10), channel_id=1, source_target_pairs={{0,1},{1,0},{2,3},{3,2},{4,5},{5,4},{6,7},{7,6},{8,9},{9,8},{10,11... | collective-permute-start | bytes 24584 | tf_op jit(solution)/shard_map/ppermute | solution.py:122
  3.0 4.6 %collective-permute-start.1 = (bf16[4,2048]{1,0:T(4,128)(2,1)S(1)}, bf16[4,2048]{1,0:T(4,128)(2,1)S(1)}, u32[]{:S(2)}, u32[]{:S(2)}) collective-permute-start(bf16[4,2048]{1,0:T(4,128)(2,1)S(1)} %maximum_select_fusion.4), channel_id=1, source_target_pairs={{0,2},{1,3},{2,0},{3,1},{4,6},{5,7},{6,4},{7,5},{8,10},{9,11},{10,... | collective-permute-start | bytes 49160 | tf_op jit(solution)/shard_map/ppermute | solution.py:122
  7.7 4.0 %collective-permute-start.2 = (bf16[8,2048]{1,0:T(8,128)(2,1)S(1)}, bf16[8,2048]{1,0:T(8,128)(2,1)S(1)}, u32[]{:S(2)}, u32[]{:S(2)}) collective-permute-start(bf16[8,2048]{1,0:T(8,128)(2,1)S(1)} %maximum_select_fusion.3), channel_id=1, source_target_pairs={{0,4},{1,5},{2,6},{3,7},{4,0},{5,1},{6,2},{7,3},{8,12},{9,13},{10,... | collective-permute-start | bytes 98312 | tf_op jit(solution)/shard_map/ppermute | solution.py:122
  11.7 5.3 %collective-permute-start.3 = (bf16[16,2048]{1,0:T(8,128)(2,1)S(1)}, bf16[16,2048]{1,0:T(8,128)(2,1)S(1)}, u32[]{:S(2)}, u32[]{:S(2)}) collective-permute-start(bf16[16,2048]{1,0:T(8,128)(2,1)S(1)} %maximum_select_fusion.2), channel_id=1, source_target_pairs={{0,8},{1,9},{2,10},{3,11},{4,12},{5,13},{6,14},{7,15},{8,0},{9,1},... | collective-permute-start | bytes 196616 | tf_op jit(solution)/shard_map/ppermute | solution.py:122
  17.7 0.7 copy-start.6
  18.3 35.8 %copy-start.1 = (bf16[32,512]{0,1:T(8,128)(2,1)}, bf16[32,512]{0,1:T(8,128)(2,1)S(1)}, u32[]{:S(2)}) copy-start(bf16[32,512]{0,1:T(8,128)(2,1)S(1)} %copy.25) | copy-start | bytes 98308
  19.9 1.7 %copy-start.4 = (bf16[256,512]{1,0:T(8,128)(2,1)S(1)}, bf16[256,512]{1,0:T(8,128)(2,1)}, u32[]{:S(2)}) copy-start(bf16[256,512]{1,0:T(8,128)(2,1)} %constant.112) | copy-start | bytes 786436
  21.6 1.0 %copy-start.9 = (bf16[256,512]{1,0:T(8,128)(2,1)S(1)}, bf16[256,512]{1,0:T(8,128)(2,1)}, u32[]{:S(2)}) copy-start(bf16[256,512]{1,0:T(8,128)(2,1)} %constant.113) | copy-start | bytes 786436
  22.5 1.0 %copy-start.2 = (bf16[512,512]{1,0:T(8,128)(2,1)S(1)}, bf16[512,512]{1,0:T(8,128)(2,1)}, u32[]{:S(2)}) copy-start(bf16[512,512]{1,0:T(8,128)(2,1)} %param.17) | copy-start | bytes 1572868
  22.5 1.3 %copy-start.7 = (bf16[32,24,512]{2,1,0:T(8,128)(2,1)S(1)}, bf16[32,24,512]{2,1,0:T(8,128)(2,1)}, u32[]{:S(2)}) copy-start(bf16[32,24,512]{2,1,0:T(8,128)(2,1)} %param.11) | copy-start | bytes 2359300
  25.1 1.0 %copy-start.8 = (bf16[512,512]{1,0:T(8,128)(2,1)S(1)}, bf16[512,512]{1,0:T(8,128)(2,1)}, u32[]{:S(2)}) copy-start(bf16[512,512]{1,0:T(8,128)(2,1)} %constant.108.clone) | copy-start | bytes 1572868
  27.3 1.0 %copy-start.3 = (bf16[512,256]{1,0:T(8,128)(2,1)S(1)}, bf16[512,256]{1,0:T(8,128)(2,1)}, u32[]{:S(2)}) copy-start(bf16[512,256]{1,0:T(8,128)(2,1)} %constant.114) | copy-start | bytes 786436
  27.5 1.1 %copy-start.5 = (bf16[512,256]{1,0:T(8,128)(2,1)S(1)}, bf16[512,256]{1,0:T(8,128)(2,1)}, u32[]{:S(2)}) copy-start(bf16[512,256]{1,0:T(8,128)(2,1)} %constant.115) | copy-start | bytes 786436
  29.5 1.6 %collective-permute-start.4 = (bf16[280,512]{1,0:T(8,128)(2,1)S(1)}, bf16[280,512]{1,0:T(8,128)(2,1)S(1)}, u32[]{:S(2)}, u32[]{:S(2)}) collective-permute-start(bf16[280,512]{1,0:T(8,128)(2,1)S(1)} %select_convert_fusion), channel_id=1, source_target_pairs={{0,1},{1,0},{2,3},{3,2},{4,5},{5,4},{6,7},{7,6},{8,9},{9,8},{10,11... | collective-permute-start | bytes 860168 | tf_op jit(solution)/shard_map/ppermute | solution.py:153
  31.4 6.1 %collective-permute-start.5 = (bf16[140,512]{1,0:T(8,128)(2,1)S(1)}, bf16[140,512]{1,0:T(8,128)(2,1)S(1)}, u32[]{:S(2)}, u32[]{:S(2)}) collective-permute-start(bf16[140,512]{1,0:T(8,128)(2,1)S(1)} %select_convert_fusion.1), channel_id=1, source_target_pairs={{0,2},{1,3},{2,0},{3,1},{4,6},{5,7},{6,4},{7,5},{8,10},{9,11},{10,... | collective-permute-start | bytes 430088 | tf_op jit(solution)/shard_map/ppermute | solution.py:153
  37.5 5.2 %collective-permute-start.6 = (bf16[140,512]{1,0:T(8,128)(2,1)S(1)}, bf16[140,512]{1,0:T(8,128)(2,1)S(1)}, u32[]{:S(2)}, u32[]{:S(2)}) collective-permute-start(bf16[140,512]{1,0:T(8,128)(2,1)S(1)} %add_convert_fusion.7), channel_id=1, source_target_pairs={{0,4},{1,5},{2,6},{3,7},{4,0},{5,1},{6,2},{7,3},{8,12},{9,13},{10,... | collective-permute-start | bytes 430088 | tf_op jit(solution)/shard_map/ppermute | solution.py:159
  42.8 9.1 %collective-permute-start.7 = (bf16[140,512]{1,0:T(8,128)(2,1)S(1)}, bf16[140,512]{1,0:T(8,128)(2,1)S(1)}, u32[]{:S(2)}, u32[]{:S(2)}) collective-permute-start(bf16[140,512]{1,0:T(8,128)(2,1)S(1)} %add_convert_fusion.6), channel_id=1, source_target_pairs={{0,8},{1,9},{2,10},{3,11},{4,12},{5,13},{6,14},{7,15},{8,0},{9,1},... | collective-permute-start | bytes 430088 | tf_op jit(solution)/shard_map/ppermute | solution.py:159
  51.9 5.3 %collective-permute-start.8 = (bf16[140,512]{1,0:T(8,128)(2,1)S(1)}, bf16[140,512]{1,0:T(8,128)(2,1)}, u32[]{:S(2)}, u32[]{:S(2)}) collective-permute-start(bf16[140,512]{1,0:T(8,128)(2,1)S(1)} %add_convert_fusion.5), channel_id=1, source_target_pairs={{0,2},{1,3},{2,0},{3,1},{4,6},{5,7},{6,4},{7,5},{8,10},{9,11},{10,... | collective-permute-start | bytes 430088 | tf_op jit(solution)/shard_map/ppermute | solution.py:164
  58.3 1.6 %collective-permute-start.9 = (bf16[280,512]{1,0:T(8,128)(2,1)S(1)}, bf16[280,512]{1,0:T(8,128)(2,1)S(1)}, u32[]{:S(2)}, u32[]{:S(2)}) collective-permute-start(bf16[280,512]{1,0:T(8,128)(2,1)S(1)} %maximum_select_fusion.1), channel_id=1, source_target_pairs={{0,1},{1,0},{2,3},{3,2},{4,5},{5,4},{6,7},{7,6},{8,9},{9,8},{10,11... | collective-permute-start | bytes 860168 | tf_op jit(solution)/shard_map/ppermute | solution.py:164

commit v9 on v7

--- a/solution.py
+++ b/solution.py
@@ -1,3 +1,4 @@
+import functools
 import math
 
 import jax
@@ -5,6 +6,8 @@
 import numpy as np
 import jax.numpy as jnp
 from jax import lax
+from jax.experimental import pallas as pl
+from jax.experimental.pallas import tpu as pltpu
 from jax.sharding import PartitionSpec as P
 
 
@@ -167,6 +170,129 @@
     return values
 
 
+_TRANSPOSED_RIGHT = (((1,), (1,)), ((), ()))
+
+
+def _decoder_kernel(
+    loss_scale,
+    latent_ref,
+    amplitude_ref,
+    wanted_ref,
+    filter_ref,
+    forward_ref,
+    inverse_ref,
+    output_weight_ref,
+    bottleneck_ref,
+    grad_out_ref,
+    grad_filter_ref,
+):
+    block_samples, width = latent_ref.shape
+    tones = amplitude_ref.shape[0]
+    half_width = width // 2
+    amplitude = amplitude_ref[...].astype(jnp.float32)
+    mixed_in = (
+        (latent_ref[...][:, None, :] * amplitude[None])
+        .reshape(block_samples * tones, width)
+        .astype(jnp.bfloat16)
+    )
+    wanted = wanted_ref[...].astype(jnp.float32).reshape(block_samples * tones, width)
+    filter_re = filter_ref[pl.ds(0, 1), :]
+    filter_im = filter_ref[pl.ds(1, 1), :]
+    spectrum = jnp.dot(mixed_in, forward_ref[...], preferred_element_type=jnp.float32)
+    spec_re = spectrum[:, :half_width]
+    spec_im = spectrum[:, half_width:]
+    filtered = jnp.concatenate(
+        [spec_re * filter_re - spec_im * filter_im, spec_re * filter_im + spec_im * filter_re], 1
+    ).astype(jnp.bfloat16)
+    mixed_back = jnp.dot(filtered, inverse_ref[...], preferred_element_type=jnp.float32)
+    activated, activation_vjp = jax.vjp(jax.nn.gelu, mixed_back)
+    hidden = (mixed_in.astype(jnp.float32) + activated).astype(jnp.bfloat16)
+    rebuilt = hidden.astype(jnp.float32) + jnp.dot(
+        hidden, output_weight_ref[...], preferred_element_type=jnp.float32
+    )
+    residual = loss_scale * (rebuilt - wanted)
+    residual_half = residual.astype(jnp.bfloat16)
+    grad_out_part = lax.dot_general(
+        hidden, residual_half, (((0,), (0,)), ((), ())), preferred_element_type=jnp.float32
+    )
+    grad_hidden = residual + lax.dot_general(
+        residual_half, output_weight_ref[...], _TRANSPOSED_RIGHT, preferred_element_type=jnp.float32
+    )
+    grad_mixed = activation_vjp(grad_hidden)[0].astype(jnp.bfloat16)
+    grad_filtered = lax.dot_general(
+        grad_mixed, inverse_ref[...], _TRANSPOSED_RIGHT, preferred_element_type=jnp.float32
+    )
+    grad_re = grad_filtered[:, :half_width]
+    grad_im = grad_filtered[:, half_width:]
+    filter_grad_re = jnp.sum(grad_re * spec_re + grad_im * spec_im, 0, keepdims=True)
+    filter_grad_im = jnp.sum(grad_im * spec_re - grad_re * spec_im, 0, keepdims=True)
+    grad_spec = jnp.concatenate(
+        [grad_re * filter_re + grad_im * filter_im, grad_im * filter_re - grad_re * filter_im], 1
+    ).astype(jnp.bfloat16)
+    derivative_entering = grad_hidden + lax.dot_general(
+        grad_spec, forward_ref[...], _TRANSPOSED_RIGHT, preferred_element_type=jnp.float32
+    )
+    bottleneck_ref[...] = jnp.sum(
+        derivative_entering.reshape(block_samples, tones, width) * amplitude[None], 1
+    )
+
+    @pl.when(pl.program_id(0) == 0)
+    def _():
+        grad_out_ref[...] = jnp.zeros_like(grad_out_ref)
+        grad_filter_ref[...] = jnp.zeros_like(grad_filter_ref)
+
+    grad_out_ref[...] += grad_out_part
+    grad_filter_ref[pl.ds(0, 1), :] += filter_grad_re
+    grad_filter_ref[pl.ds(1, 1), :] += filter_grad_im
+
+
+def decode_block(
+    latent,
+    frequency_amplitude,
+    desired_responses,
+    spectral_filter_weight,
+    forward_transform,
+    inverse_transform,
+    output_weight,
+    loss_scale,
+):
+    samples, tones, width = desired_responses.shape
+    block_samples = 8 if samples % 8 == 0 else samples
+    whole = lambda shape: pl.BlockSpec(shape, lambda i: (0,) * len(shape))
+    return pl.pallas_call(
+        functools.partial(_decoder_kernel, loss_scale),
+        grid=(samples // block_samples,),
+        in_specs=[
+            pl.BlockSpec((block_samples, width), lambda i: (i, 0)),
+            whole(frequency_amplitude.shape),
+            pl.BlockSpec((block_samples, tones, width), lambda i: (i, 0, 0)),
+            whole(spectral_filter_weight.shape),
+            whole(forward_transform.shape),
+            whole(inverse_transform.shape),
+            whole(output_weight.shape),
+        ],
+        out_specs=[
+            pl.BlockSpec((block_samples, width), lambda i: (i, 0)),
+            whole((width, width)),
+            whole(spectral_filter_weight.shape),
+        ],
+        out_shape=[
+            jax.ShapeDtypeStruct((samples, width), jnp.float32),
+            jax.ShapeDtypeStruct((width, width), jnp.float32),
+            jax.ShapeDtypeStruct(spectral_filter_weight.shape, jnp.float32),
+        ],
+        compiler_params=pltpu.CompilerParams(dimension_semantics=("arbitrary",)),
+    )(
+        latent,
+        frequency_amplitude,
+        desired_responses,
+        spectral_filter_weight,
+        forward_transform,
+        inverse_transform,
+        output_weight,
+    )
+
+
 def local(
     encoder_input,
     desired_responses,
@@ -193,20 +319,15 @@
         jnp.bfloat16
     )
     latent = jnp.dot(codes_by_sample, decoder_weight, preferred_element_type=jnp.float32)
-    gain_row_values = frequency_amplitude.astype(jnp.float32)
-    mixed_in = (latent[:, None, :] * gain_row_values[None]).astype(jnp.bfloat16).reshape(-1, width)
-    wanted_lines = desired_responses.reshape(-1, width)
-    derivative_entering, grad_out, grad_filter = decode_rows(
-        mixed_in,
-        wanted_lines,
-        output_weight,
+    derivative_bottleneck, grad_out, grad_filter = decode_block(
+        latent,
+        frequency_amplitude,
+        desired_responses,
         spectral_filter_weight,
         forward_transform,
         inverse_transform,
+        output_weight,
         loss_scale,
-    )
-    derivative_bottleneck = jnp.einsum(
-        "orm,rm->om", derivative_entering.reshape(samples, sub_dev, width), gain_row_values
     )
     count = lax.axis_size("freq")
     packed_rows = samples + 1 + grad_out.shape[0]

time: 63.1 us -> 67.8 us (1.074)
  Pallas kernels: 0 us -> 9.88 us
  matrix products: 10.7 us -> 5.64 us
  local copies, waits for them, and re-layouts: 4.19 us -> 2.1 us
  waiting for transfers between devices: 25.4 us -> 26.9 us
    pallas_call x0 -> x1, Pallas kernels: none -> 9.88 us  [decode_block(): pl.pallas_call(functools.partial(_decoder_kernel, loss_scale), grid=(samp...]
    dot_general x9 -> x0, matrix products: 5.71 us -> none  [the longest x2 1.26 us: decode_rows(): jnp.dot(filtered, inverse_transform, preferred_element_type=jnp.float32)]
    ppermute x4, waiting for transfers between devices: 5.23 us -> 6.82 us  [gather_rows(): other = lax.ppermute(block, axis_name, _exchange_pairs(count, distance))]
    unnamed x23 -> x9, local copies, waits for them, and re-layouts: 2.14 us -> 0.8 us
    convert_element_type x2, other arithmetic: 0.16 us -> 1.35 us  [sum_halving(): send = jnp.where(lower, values[half:], values[:half]).astype(wire)]
    add x1, other arithmetic: 0.15 us -> 0.98 us  [sum_halving(): values = keep + arrived.astype(keep.dtype)]
    unnamed x2 -> x0, other arithmetic: 0.83 us -> none
    slice x1 -> x0, local copies, waits for them, and re-layouts: 0.76 us -> none  [decode_rows(): filter_re = spectral_filter_weight[0]]
  transfers between devices with their start and end apart: 10 -> 10, of which waited for: 10 -> 10; matrix products, arithmetic and copies ran while one was open for 3% -> 0% of each run, Pallas kernels for 0% -> 0%
where the time goes in v9:
time: 67.8 us; the launch traced here: 67.5 us
  waiting for transfers between devices  26.9 us (40%)
  starting transfers between devices  17.4 us (26%)
  Pallas kernels  9.88 us (15%)
  matrix products  5.64 us (8%)
  other arithmetic  4.8 us (7%)
  local copies, waits for them, and re-layouts  2.1 us (3%)
  between operations  0.79 us (1%)
    pallas_call x1, Pallas kernels, decode_block(): pl.pallas_call(functools.partial(_decoder_kernel, loss_scale), grid=(samp...  9.88 us
    ppermute x2, waiting for transfers between devices, sum_halving(): arrived = lax.ppermute(values, axis_name, _exchange_pairs(count, distance))  9.26 us
    ppermute x4, starting transfers between devices, gather_rows(): other = lax.ppermute(block, axis_name, _exchange_pairs(count, distance))  8.68 us
    ppermute x4, waiting for transfers between devices, gather_rows(): other = lax.ppermute(block, axis_name, _exchange_pairs(count, distance))  6.82 us
    ppermute x2, waiting for transfers between devices, sum_halving(): arrived = lax.ppermute(send, axis_name, _exchange_pairs(count, distance))  5.71 us
    ppermute x2, waiting for transfers between devices, sum_halving(): other = lax.ppermute(values, axis_name, _exchange_pairs(count, distance))  5.15 us
    ppermute x2, starting transfers between devices, sum_halving(): arrived = lax.ppermute(values, axis_name, _exchange_pairs(count, distance))  5.02 us
    dot_general x1, matrix products, encoder_grads(): lax.dot_general(inputs_rows, grad_pre, (((0,), (0,)), ((), ())), preferre...  2.96 us
  transfers between devices with their start and end apart: 10, of which 10 were waited for; matrix products, arithmetic and copies ran while one was open for 0% of the time, Pallas kernels for 0%

profile of v9, /device:TPU:0, one launch (start us, length us, event | category | flops | bytes accessed | tf_op | source)
XLA Modules:
  0.0 67.5 jit_solution(10809241877966193938)
XLA Ops:
  1.2 1.0 %collective-permute-done = bf16[2,2048]{1,0:T(2,128)(2,1)S(1)} collective-permute-done((bf16[2,2048]{1,0:T(2,128)(2,1)}, bf16[2,2048]{1,0:T(2,128)(2,1)S(1)}, u32[]{:S(2)}, u32[]{:S(2)}) %collective-permute-start) | collective-permute-done | bytes 8224 | tf_op jit(solution)/shard_map/ppermute | solution.py:122
  3.0 2.9 %collective-permute-start.1 = (bf16[4,2048]{1,0:T(4,128)(2,1)S(1)}, bf16[4,2048]{1,0:T(4,128)(2,1)S(1)}, u32[]{:S(2)}, u32[]{:S(2)}) collective-permute-start(bf16[4,2048]{1,0:T(4,128)(2,1)S(1)} %maximum_select_fusion.7), channel_id=1, source_target_pairs={{0,2},{1,3},{2,0},{3,1},{4,6},{5,7},{6,4},{7,5},{8,10},{9,11},{10,... | collective-permute-start | bytes 49160 | tf_op jit(solution)/shard_map/ppermute | solution.py:122
  6.0 1.7 %collective-permute-done.1 = bf16[4,2048]{1,0:T(4,128)(2,1)S(1)} collective-permute-done((bf16[4,2048]{1,0:T(4,128)(2,1)S(1)}, bf16[4,2048]{1,0:T(4,128)(2,1)S(1)}, u32[]{:S(2)}, u32[]{:S(2)}) %collective-permute-start.1) | collective-permute-done | bytes 16416 | tf_op jit(solution)/shard_map/ppermute | solution.py:122
  7.7 2.1 %collective-permute-start.2 = (bf16[8,2048]{1,0:T(8,128)(2,1)S(1)}, bf16[8,2048]{1,0:T(8,128)(2,1)S(1)}, u32[]{:S(2)}, u32[]{:S(2)}) collective-permute-start(bf16[8,2048]{1,0:T(8,128)(2,1)S(1)} %maximum_select_fusion.4), channel_id=1, source_target_pairs={{0,4},{1,5},{2,6},{3,7},{4,0},{5,1},{6,2},{7,3},{8,12},{9,13},{10,... | collective-permute-start | bytes 98312 | tf_op jit(solution)/shard_map/ppermute | solution.py:122
  9.9 1.9 %collective-permute-done.2 = bf16[8,2048]{1,0:T(8,128)(2,1)S(1)} collective-permute-done((bf16[8,2048]{1,0:T(8,128)(2,1)S(1)}, bf16[8,2048]{1,0:T(8,128)(2,1)S(1)}, u32[]{:S(2)}, u32[]{:S(2)}) %collective-permute-start.2) | collective-permute-done | bytes 32800 | tf_op jit(solution)/shard_map/ppermute | solution.py:122
  11.8 3.1 %collective-permute-start.3 = (bf16[16,2048]{1,0:T(8,128)(2,1)S(1)}, bf16[16,2048]{1,0:T(8,128)(2,1)S(1)}, u32[]{:S(2)}, u32[]{:S(2)}) collective-permute-start(bf16[16,2048]{1,0:T(8,128)(2,1)S(1)} %maximum_select_fusion.3), channel_id=1, source_target_pairs={{0,8},{1,9},{2,10},{3,11},{4,12},{5,13},{6,14},{7,15},{8,0},{9,1},... | collective-permute-start | bytes 196616 | tf_op jit(solution)/shard_map/ppermute | solution.py:122
  14.9 2.2 %collective-permute-done.3 = bf16[16,2048]{1,0:T(8,128)(2,1)S(1)} collective-permute-done((bf16[16,2048]{1,0:T(8,128)(2,1)S(1)}, bf16[16,2048]{1,0:T(8,128)(2,1)S(1)}, u32[]{:S(2)}, u32[]{:S(2)}) %collective-permute-start.3) | collective-permute-done | bytes 65568 | tf_op jit(solution)/shard_map/ppermute | solution.py:122
  17.6 0.9 %fusion.2.latent_ref = f32[32,512]{1,0:T(8,128)} fusion(bf16[512,512]{1,0:T(8,128)(2,1)S(1)} %copy-done.2, bf16[32,512]{1,0:T(8,128)(2,1)S(1)} %fusion, s32[32]{0:T(128)S(1)} %copy-done.3), kind=kOutput, calls=%fused_computation.6 | convolution fusion | flops 17843200 | bytes 622720 | tf_op jit(solution)/shard_map/dot_general | solution.py:321
  18.5 9.9 %shard_map.129 = (f32[32,512]{1,0:T(8,128)}, f32[512,512]{1,0:T(8,128)}, f32[2,256]{1,0:T(2,128)}) custom-call(f32[32,512]{1,0:T(8,128)} %fusion.2.latent_ref, bf16[24,512]{1,0:T(8,128)(2,1)} %amplitude_ref.1, bf16[32,24,512]{2,1,0:T(8,128)(2,1)} %wanted_ref.1, f32[2,256]{1,0:T(2,128)} %filter_ref.1, bf16[512,512]{1,0:T(8,128)(2,1)} %constant.97.clone.forward_ref, ...), custom_call_target="tpu_custom_call" | custom-call | tf_op jit(solution)/shard_map/pallas_call | solution.py:262
  29.2 1.3 %select_convert_fusion = bf16[280,512]{1,0:T(8,128)(2,1)S(1)} fusion(f32[512,512]{1,0:T(8,128)} %get-tuple-element.7, pred[]{:T(512)S(6)} %eq.41, f32[280]{0:T(512)S(1)} %pad_slice_fusion, f32[1,512]{1,0:T(1,128)S(1)} %bitcast.10, f32[32,512]{1,0:T(8,128)} %get-tuple-element.8), kind=kLoop, calls=%fused_computation.13 | loop fusion | flops 1290240 | bytes 1690721 | tf_op jit(solution)/shard_map/convert_element_type | solution.py:152
  30.6 1.6 %collective-permute-done.4 = bf16[280,512]{1,0:T(8,128)(2,1)S(1)} collective-permute-done((bf16[280,512]{1,0:T(8,128)(2,1)S(1)}, bf16[280,512]{1,0:T(8,128)(2,1)S(1)}, u32[]{:S(2)}, u32[]{:S(2)}) %collective-permute-start.4) | collective-permute-done | bytes 286752 | tf_op jit(solution)/shard_map/ppermute | solution.py:153
  32.2 1.0 %convert_add_fusion = f32[280,512]{1,0:T(8,128)S(1)} fusion(bf16[280,512]{1,0:T(8,128)(2,1)S(1)} %collective-permute-done.4, f32[512,512]{1,0:T(8,128)S(1)} %copy-done.1, pred[]{:T(512)S(6)} %eq.41, f32[280]{0:T(512)S(1)} %pad_slice_fusion, f32[1,512]{1,0:T(1,128)S(1)} %bitcast.11, f32[32,512]{1,0:T(8,128)} %get-tuple-element.8), kind=kLoop, calls=%fused_computation.12 | loop fusion | flops 860160 | bytes 2551809 | tf_op jit(solution)/shard_map/add | solution.py:154
  33.2 1.9 %collective-permute-start.5 = (bf16[140,512]{1,0:T(8,128)(2,1)S(1)}, bf16[140,512]{1,0:T(8,128)(2,1)S(1)}, u32[]{:S(2)}, u32[]{:S(2)}) collective-permute-start(bf16[140,512]{1,0:T(8,128)(2,1)S(1)} %select_convert_fusion.1), channel_id=1, source_target_pairs={{0,2},{1,3},{2,0},{3,1},{4,6},{5,7},{6,4},{7,5},{8,10},{9,11},{10,... | collective-permute-start | bytes 430088 | tf_op jit(solution)/shard_map/ppermute | solution.py:153
  35.1 4.1 %collective-permute-done.5 = bf16[140,512]{1,0:T(8,128)(2,1)S(1)} collective-permute-done((bf16[140,512]{1,0:T(8,128)(2,1)S(1)}, bf16[140,512]{1,0:T(8,128)(2,1)S(1)}, u32[]{:S(2)}, u32[]{:S(2)}) %collective-permute-start.5) | collective-permute-done | bytes 143392 | tf_op jit(solution)/shard_map/ppermute | solution.py:153
  39.4 1.9 %collective-permute-start.6 = (bf16[140,512]{1,0:T(8,128)(2,1)S(1)}, bf16[140,512]{1,0:T(8,128)(2,1)S(1)}, u32[]{:S(2)}, u32[]{:S(2)}) collective-permute-start(bf16[140,512]{1,0:T(8,128)(2,1)S(1)} %add_convert_fusion.2), channel_id=1, source_target_pairs={{0,4},{1,5},{2,6},{3,7},{4,0},{5,1},{6,2},{7,3},{8,12},{9,13},{10,... | collective-permute-start | bytes 430088 | tf_op jit(solution)/shard_map/ppermute | solution.py:159
  41.2 3.4 %collective-permute-done.6 = bf16[140,512]{1,0:T(8,128)(2,1)S(1)} collective-permute-done((bf16[140,512]{1,0:T(8,128)(2,1)S(1)}, bf16[140,512]{1,0:T(8,128)(2,1)S(1)}, u32[]{:S(2)}, u32[]{:S(2)}) %collective-permute-start.6) | collective-permute-done | bytes 143392 | tf_op jit(solution)/shard_map/ppermute | solution.py:159
  44.7 3.2 %collective-permute-start.7 = (bf16[140,512]{1,0:T(8,128)(2,1)S(1)}, bf16[140,512]{1,0:T(8,128)(2,1)S(1)}, u32[]{:S(2)}, u32[]{:S(2)}) collective-permute-start(bf16[140,512]{1,0:T(8,128)(2,1)S(1)} %add_convert_fusion.1), channel_id=1, source_target_pairs={{0,8},{1,9},{2,10},{3,11},{4,12},{5,13},{6,14},{7,15},{8,0},{9,1},... | collective-permute-start | bytes 430088 | tf_op jit(solution)/shard_map/ppermute | solution.py:159
  47.8 5.9 %collective-permute-done.7 = bf16[140,512]{1,0:T(8,128)(2,1)S(1)} collective-permute-done((bf16[140,512]{1,0:T(8,128)(2,1)S(1)}, bf16[140,512]{1,0:T(8,128)(2,1)S(1)}, u32[]{:S(2)}, u32[]{:S(2)}) %collective-permute-start.7) | collective-permute-done | bytes 143392 | tf_op jit(solution)/shard_map/ppermute | solution.py:159
  53.7 1.6 %collective-permute-start.8 = (bf16[140,512]{1,0:T(8,128)(2,1)S(1)}, bf16[140,512]{1,0:T(8,128)(2,1)S(1)}, u32[]{:S(2)}, u32[]{:S(2)}) collective-permute-start(bf16[140,512]{1,0:T(8,128)(2,1)S(1)} %add_convert_fusion), channel_id=1, source_target_pairs={{0,2},{1,3},{2,0},{3,1},{4,6},{5,7},{6,4},{7,5},{8,10},{9,11},{10,... | collective-permute-start | bytes 430088 | tf_op jit(solution)/shard_map/ppermute | solution.py:164
  55.3 3.6 %collective-permute-done.8 = bf16[140,512]{1,0:T(8,128)(2,1)S(1)} collective-permute-done((bf16[140,512]{1,0:T(8,128)(2,1)S(1)}, bf16[140,512]{1,0:T(8,128)(2,1)S(1)}, u32[]{:S(2)}, u32[]{:S(2)}) %collective-permute-start.8) | collective-permute-done | bytes 143392 | tf_op jit(solution)/shard_map/ppermute | solution.py:164
  59.1 1.5 %collective-permute-done.9 = bf16[280,512]{1,0:T(8,128)(2,1)S(1)} collective-permute-done((bf16[280,512]{1,0:T(8,128)(2,1)S(1)}, bf16[280,512]{1,0:T(8,128)(2,1)S(1)}, u32[]{:S(2)}, u32[]{:S(2)}) %collective-permute-start.9) | collective-permute-done | bytes 286752 | tf_op jit(solution)/shard_map/ppermute | solution.py:164
  60.9 1.1 %slice_convert_fusion = f32[512,512]{1,0:T(8,128)} fusion(bf16[560,512]{1,0:T(8,128)(2,1)S(1)} %maximum_select_fusion), kind=kLoop, calls=%fused_computation.14 | loop fusion | flops 262144 | bytes 1572864 | tf_op jit(solution)/shard_map/convert_element_type | solution.py:346
  63.3 1.3 %fusion.19 = f32[512,512]{1,0:T(8,128)} fusion(bf16[32,512]{1,0:T(8,128)(2,1)S(1)} %fusion, bf16[32,512]{1,0:T(8,128)(2,1)S(1)} %gather_fusion), kind=kOutput, calls=%fused_computation.42 | convolution fusion | flops 16777216 | bytes 1114112 | tf_op jit(solution)/shard_map/dot_general | solution.py:94
  64.5 3.0 %fusion.3 = f32[2048,512]{1,0:T(8,128)} fusion(bf16[512,512]{1,0:T(8,128)(2,1)S(1)} %copy-done.2, bf16[32,512]{1,0:T(8,128)(2,1)S(1)} %fusion, bf16[16,2048]{1,0:T(8,128)(2,1)S(1)} %collective-permute-done.3, bf16[16,2048]{1,0:T(8,128)(2,1)S(1)} %maximum_select_fusion.3, pred[]{:T(512)S(6)} %eq.38, bf16[32,512]{1,0:T(8,128)(2,1)S(1)} %gather_fusion), kind=kOutput, calls=%fused_computation.7 | convolution fusion | flops 84557824 | bytes 4915201 | tf_op jit(solution)/shard_map/dot_general | solution.py:101
  (30 shorter events, 4.6 us)
Async XLA Ops:
  0.6 16.5 %copy-start = (bf16[2048,512]{1,0:T(8,128)(2,1)S(1)}, bf16[2048,512]{1,0:T(8,128)(2,1)}, u32[]{:S(2)}) copy-start(bf16[2048,512]{1,0:T(8,128)(2,1)} %param.13) | copy-start | bytes 6291460
  0.6 17.0 %copy-start.2 = (bf16[512,512]{1,0:T(8,128)(2,1)S(1)}, bf16[512,512]{1,0:T(8,128)(2,1)}, u32[]{:S(2)}) copy-start(bf16[512,512]{1,0:T(8,128)(2,1)} %param.14) | copy-start | bytes 1572868
  0.7 17.0 %copy-start.3 = (s32[32]{0:T(128)S(1)}, s32[32]{0:T(128)}, u32[]{:S(2)}) copy-start(s32[32]{0:T(128)} %param.12) | copy-start | bytes 388
  0.7 1.6 %collective-permute-start = (bf16[2,2048]{1,0:T(2,128)(2,1)}, bf16[2,2048]{1,0:T(2,128)(2,1)S(1)}, u32[]{:S(2)}, u32[]{:S(2)}) collective-permute-start(bf16[2,2048]{1,0:T(2,128)(2,1)} %param.10), channel_id=1, source_target_pairs={{0,1},{1,0},{2,3},{3,2},{4,5},{5,4},{6,7},{7,6},{8,9},{9,8},{10,11... | collective-permute-start | bytes 24584 | tf_op jit(solution)/shard_map/ppermute | solution.py:122
  3.0 4.6 %collective-permute-start.1 = (bf16[4,2048]{1,0:T(4,128)(2,1)S(1)}, bf16[4,2048]{1,0:T(4,128)(2,1)S(1)}, u32[]{:S(2)}, u32[]{:S(2)}) collective-permute-start(bf16[4,2048]{1,0:T(4,128)(2,1)S(1)} %maximum_select_fusion.7), channel_id=1, source_target_pairs={{0,2},{1,3},{2,0},{3,1},{4,6},{5,7},{6,4},{7,5},{8,10},{9,11},{10,... | collective-permute-start | bytes 49160 | tf_op jit(solution)/shard_map/ppermute | solution.py:122
  7.7 4.0 %collective-permute-start.2 = (bf16[8,2048]{1,0:T(8,128)(2,1)S(1)}, bf16[8,2048]{1,0:T(8,128)(2,1)S(1)}, u32[]{:S(2)}, u32[]{:S(2)}) collective-permute-start(bf16[8,2048]{1,0:T(8,128)(2,1)S(1)} %maximum_select_fusion.4), channel_id=1, source_target_pairs={{0,4},{1,5},{2,6},{3,7},{4,0},{5,1},{6,2},{7,3},{8,12},{9,13},{10,... | collective-permute-start | bytes 98312 | tf_op jit(solution)/shard_map/ppermute | solution.py:122
  11.8 5.3 %collective-permute-start.3 = (bf16[16,2048]{1,0:T(8,128)(2,1)S(1)}, bf16[16,2048]{1,0:T(8,128)(2,1)S(1)}, u32[]{:S(2)}, u32[]{:S(2)}) collective-permute-start(bf16[16,2048]{1,0:T(8,128)(2,1)S(1)} %maximum_select_fusion.3), channel_id=1, source_target_pairs={{0,8},{1,9},{2,10},{3,11},{4,12},{5,13},{6,14},{7,15},{8,0},{9,1},... | collective-permute-start | bytes 196616 | tf_op jit(solution)/shard_map/ppermute | solution.py:122
  28.4 3.7 %copy-start.1 = (f32[512,512]{1,0:T(8,128)S(1)}, f32[512,512]{1,0:T(8,128)}, u32[]{:S(2)}) copy-start(f32[512,512]{1,0:T(8,128)} %get-tuple-element.7) | copy-start | bytes 3145732
  30.5 1.6 %collective-permute-start.4 = (bf16[280,512]{1,0:T(8,128)(2,1)S(1)}, bf16[280,512]{1,0:T(8,128)(2,1)S(1)}, u32[]{:S(2)}, u32[]{:S(2)}) collective-permute-start(bf16[280,512]{1,0:T(8,128)(2,1)S(1)} %select_convert_fusion), channel_id=1, source_target_pairs={{0,1},{1,0},{2,3},{3,2},{4,5},{5,4},{6,7},{7,6},{8,9},{9,8},{10,11... | collective-permute-start | bytes 860168 | tf_op jit(solution)/shard_map/ppermute | solution.py:153
  33.2 6.1 %collective-permute-start.5 = (bf16[140,512]{1,0:T(8,128)(2,1)S(1)}, bf16[140,512]{1,0:T(8,128)(2,1)S(1)}, u32[]{:S(2)}, u32[]{:S(2)}) collective-permute-start(bf16[140,512]{1,0:T(8,128)(2,1)S(1)} %select_convert_fusion.1), channel_id=1, source_target_pairs={{0,2},{1,3},{2,0},{3,1},{4,6},{5,7},{6,4},{7,5},{8,10},{9,11},{10,... | collective-permute-start | bytes 430088 | tf_op jit(solution)/shard_map/ppermute | solution.py:153
  39.4 5.3 %collective-permute-start.6 = (bf16[140,512]{1,0:T(8,128)(2,1)S(1)}, bf16[140,512]{1,0:T(8,128)(2,1)S(1)}, u32[]{:S(2)}, u32[]{:S(2)}) collective-permute-start(bf16[140,512]{1,0:T(8,128)(2,1)S(1)} %add_convert_fusion.2), channel_id=1, source_target_pairs={{0,4},{1,5},{2,6},{3,7},{4,0},{5,1},{6,2},{7,3},{8,12},{9,13},{10,... | collective-permute-start | bytes 430088 | tf_op jit(solution)/shard_map/ppermute | solution.py:159
  44.7 9.0 %collective-permute-start.7 = (bf16[140,512]{1,0:T(8,128)(2,1)S(1)}, bf16[140,512]{1,0:T(8,128)(2,1)S(1)}, u32[]{:S(2)}, u32[]{:S(2)}) collective-permute-start(bf16[140,512]{1,0:T(8,128)(2,1)S(1)} %add_convert_fusion.1), channel_id=1, source_target_pairs={{0,8},{1,9},{2,10},{3,11},{4,12},{5,13},{6,14},{7,15},{8,0},{9,1},... | collective-permute-start | bytes 430088 | tf_op jit(solution)/shard_map/ppermute | solution.py:159
  53.7 5.2 %collective-permute-start.8 = (bf16[140,512]{1,0:T(8,128)(2,1)S(1)}, bf16[140,512]{1,0:T(8,128)(2,1)S(1)}, u32[]{:S(2)}, u32[]{:S(2)}) collective-permute-start(bf16[140,512]{1,0:T(8,128)(2,1)S(1)} %add_convert_fusion), channel_id=1, source_target_pairs={{0,2},{1,3},{2,0},{3,1},{4,6},{5,7},{6,4},{7,5},{8,10},{9,11},{10,... | collective-permute-start | bytes 430088 | tf_op jit(solution)/shard_map/ppermute | solution.py:164
  59.0 1.6 %collective-permute-start.9 = (bf16[280,512]{1,0:T(8,128)(2,1)S(1)}, bf16[280,512]{1,0:T(8,128)(2,1)S(1)}, u32[]{:S(2)}, u32[]{:S(2)}) collective-permute-start(bf16[280,512]{1,0:T(8,128)(2,1)S(1)} %maximum_select_fusion.1), channel_id=1, source_target_pairs={{0,1},{1,0},{2,3},{3,2},{4,5},{5,4},{6,7},{7,6},{8,9},{9,8},{10,11... | collective-permute-start | bytes 860168 | tf_op jit(solution)/shard_map/ppermute | solution.py:164

commit v10 on v7

--- a/solution.py
+++ b/solution.py
@@ -52,7 +52,9 @@
     filtered = jnp.concatenate(
         [spec_re * filter_re - spec_im * filter_im, spec_re * filter_im + spec_im * filter_re], 1
     ).astype(jnp.bfloat16)
-    mixed_back = jnp.dot(filtered, inverse_transform, preferred_element_type=jnp.float32)
+    mixed_back = lax.dot_general(
+        filtered, forward_transform, (((1,), (1,)), ((), ())), preferred_element_type=jnp.float32
+    )
     hidden = (mixed_in.astype(jnp.float32) + jax.nn.gelu(mixed_back)).astype(jnp.bfloat16)
     rebuilt = hidden.astype(jnp.float32) + jnp.dot(
         hidden, output_weight, preferred_element_type=jnp.float32
@@ -66,9 +68,7 @@
         residual_half, output_weight, (((1,), (1,)), ((), ())), preferred_element_type=jnp.float32
     )
     grad_mixed = jax.vjp(jax.nn.gelu, mixed_back)[1](grad_hidden)[0].astype(jnp.bfloat16)
-    grad_filtered = lax.dot_general(
-        grad_mixed, inverse_transform, (((1,), (1,)), ((), ())), preferred_element_type=jnp.float32
-    )
+    grad_filtered = jnp.dot(grad_mixed, forward_transform, preferred_element_type=jnp.float32)
     grad_re = grad_filtered[:, :half_width]
     grad_im = grad_filtered[:, half_width:]
     grad_filter = jnp.stack(

time: 63.1 us -> 61.9 us (0.981)
  local copies, waits for them, and re-layouts: 4.19 us -> 3.01 us
    unnamed x23 -> x17, local copies, waits for them, and re-layouts: 2.14 us -> 0.95 us
where the time goes in v10:
time: 61.9 us; the launch traced here: 61.6 us
  waiting for transfers between devices  25.4 us (41%)
  starting transfers between devices  17.3 us (28%)
  matrix products  10.8 us (17%)
  other arithmetic  4.26 us (7%)
  local copies, waits for them, and re-layouts  3.01 us (5%)
  between operations  0.89 us (1%)
    ppermute x2, waiting for transfers between devices, sum_halving(): arrived = lax.ppermute(values, axis_name, _exchange_pairs(count, distance))  9.27 us
    ppermute x4, starting transfers between devices, gather_rows(): other = lax.ppermute(block, axis_name, _exchange_pairs(count, distance))  8.68 us
    ppermute x2, waiting for transfers between devices, sum_halving(): arrived = lax.ppermute(send, axis_name, _exchange_pairs(count, distance))  5.71 us
    ppermute x4, waiting for transfers between devices, gather_rows(): other = lax.ppermute(block, axis_name, _exchange_pairs(count, distance))  5.23 us
    ppermute x2, waiting for transfers between devices, sum_halving(): other = lax.ppermute(values, axis_name, _exchange_pairs(count, distance))  5.16 us
    ppermute x2, starting transfers between devices, sum_halving(): arrived = lax.ppermute(values, axis_name, _exchange_pairs(count, distance))  5.01 us
    dot_general x1, matrix products, encoder_grads(): lax.dot_general(inputs_rows, grad_pre, (((0,), (0,)), ((), ())), preferre...  2.96 us
    ppermute x2, starting transfers between devices, sum_halving(): arrived = lax.ppermute(send, axis_name, _exchange_pairs(count, distance))  2 us
  transfers between devices with their start and end apart: 10, of which 10 were waited for; matrix products, arithmetic and copies ran while one was open for 3% of the time, Pallas kernels for 0%

profile of v10, /device:TPU:0, one launch (start us, length us, event | category | flops | bytes accessed | tf_op | source)
XLA Modules:
  0.0 61.6 jit_solution(17262244931957566726)
XLA Ops:
  1.2 1.0 %collective-permute-done = bf16[2,2048]{1,0:T(2,128)(2,1)S(1)} collective-permute-done((bf16[2,2048]{1,0:T(2,128)(2,1)}, bf16[2,2048]{1,0:T(2,128)(2,1)S(1)}, u32[]{:S(2)}, u32[]{:S(2)}) %collective-permute-start) | collective-permute-done | bytes 8224 | tf_op jit(solution)/shard_map/ppermute | solution.py:119
  2.2 0.8 %maximum_select_fusion.7 = bf16[4,2048]{1,0:T(4,128)(2,1)S(1)} fusion(bf16[2,2048]{1,0:T(2,128)(2,1)S(1)} %collective-permute-done, bf16[2,2048]{1,0:T(2,128)(2,1)} %param.9, pred[]{:T(512)S(6)} %eq.41), kind=kLoop, calls=%fused_computation.66 | loop fusion | flops 73728 | bytes 32769 | tf_op jit(solution)/shard_map/jit(_where)/select_n | solution.py:121
  3.0 2.9 %collective-permute-start.1 = (bf16[4,2048]{1,0:T(4,128)(2,1)S(1)}, bf16[4,2048]{1,0:T(4,128)(2,1)S(1)}, u32[]{:S(2)}, u32[]{:S(2)}) collective-permute-start(bf16[4,2048]{1,0:T(4,128)(2,1)S(1)} %maximum_select_fusion.7), channel_id=1, source_target_pairs={{0,2},{1,3},{2,0},{3,1},{4,6},{5,7},{6,4},{7,5},{8,10},{9,11},{10,... | collective-permute-start | bytes 49160 | tf_op jit(solution)/shard_map/ppermute | solution.py:119
  6.0 0.8 %bitcast_convert_fusion = (f32[512,24]{0,1:T(8,128)S(1)}, f32[24,512]{1,0:T(8,128)S(1)}) fusion(bf16[24,512]{1,0:T(8,128)(2,1)} %param.14), kind=kLoop, calls=%fused_computation.65 | loop fusion | flops 24576 | bytes 122880
  6.8 0.9 %collective-permute-done.1 = bf16[4,2048]{1,0:T(4,128)(2,1)S(1)} collective-permute-done((bf16[4,2048]{1,0:T(4,128)(2,1)S(1)}, bf16[4,2048]{1,0:T(4,128)(2,1)S(1)}, u32[]{:S(2)}, u32[]{:S(2)}) %collective-permute-start.1) | collective-permute-done | bytes 16416 | tf_op jit(solution)/shard_map/ppermute | solution.py:119
  7.7 2.1 %collective-permute-start.2 = (bf16[8,2048]{1,0:T(8,128)(2,1)S(1)}, bf16[8,2048]{1,0:T(8,128)(2,1)S(1)}, u32[]{:S(2)}, u32[]{:S(2)}) collective-permute-start(bf16[8,2048]{1,0:T(8,128)(2,1)S(1)} %maximum_select_fusion.4), channel_id=1, source_target_pairs={{0,4},{1,5},{2,6},{3,7},{4,0},{5,1},{6,2},{7,3},{8,12},{9,13},{10,... | collective-permute-start | bytes 98312 | tf_op jit(solution)/shard_map/ppermute | solution.py:119
  10.6 1.1 %collective-permute-done.2 = bf16[8,2048]{1,0:T(8,128)(2,1)S(1)} collective-permute-done((bf16[8,2048]{1,0:T(8,128)(2,1)S(1)}, bf16[8,2048]{1,0:T(8,128)(2,1)S(1)}, u32[]{:S(2)}, u32[]{:S(2)}) %collective-permute-start.2) | collective-permute-done | bytes 32800 | tf_op jit(solution)/shard_map/ppermute | solution.py:119
  11.8 3.1 %collective-permute-start.3 = (bf16[16,2048]{1,0:T(8,128)(2,1)S(1)}, bf16[16,2048]{1,0:T(8,128)(2,1)S(1)}, u32[]{:S(2)}, u32[]{:S(2)}) collective-permute-start(bf16[16,2048]{1,0:T(8,128)(2,1)S(1)} %maximum_select_fusion.3), channel_id=1, source_target_pairs={{0,8},{1,9},{2,10},{3,11},{4,12},{5,13},{6,14},{7,15},{8,0},{9,1},... | collective-permute-start | bytes 196616 | tf_op jit(solution)/shard_map/ppermute | solution.py:119
  15.0 2.2 %collective-permute-done.3 = bf16[16,2048]{1,0:T(8,128)(2,1)S(1)} collective-permute-done((bf16[16,2048]{1,0:T(8,128)(2,1)S(1)}, bf16[16,2048]{1,0:T(8,128)(2,1)S(1)}, u32[]{:S(2)}, u32[]{:S(2)}) %collective-permute-start.3) | collective-permute-done | bytes 65568 | tf_op jit(solution)/shard_map/ppermute | solution.py:119
  19.6 0.9 %add_convert_fusion = (bf16[768,512]{1,0:T(8,128)(2,1)S(1)}, f32[768,512]{1,0:T(8,128)S(1)}) fusion(bf16[32,24,512]{2,1,0:T(8,128)(2,1)S(1)} %multiply_convert_fusion, f32[768,512]{1,0:T(8,128)S(1)} %fusion.15, bf16[512,256]{1,0:T(8,128)(2,1)S(1)} %copy-done.5, f32[768,512]{1,0:T(8,128)S(1)} %fusion.49, f32[256]{0:T(256)S(1)} %bitcast.47, f32[256]{0:T(256)S(1)} %bitcast.43), kind=kOutput, calls=%fused_computation.14 | convolution fusion | flops 206831616 | bytes 6555648 | tf_op jit(solution)/shard_map/dot_general | solution.py:55
  22.8 1.2 %fusion.12 = f32[768,512]{1,0:T(8,128)S(1)} fusion(bf16[512,512]{1,0:T(8,128)(2,1)S(1)} %copy-done.4, f32[768,512]{1,0:T(8,128)S(1)} %get-tuple-element.11, f32[768,512]{1,0:T(8,128)S(1)} %convolution_add_fusion), kind=kOutput, calls=%fused_computation.31 | convolution fusion | flops 410517504 | bytes 5242880 | tf_op jit(solution)/shard_map/dot_general | solution.py:71
  25.6 1.6 %collective-permute-done.4 = bf16[280,512]{1,0:T(8,128)(2,1)S(1)} collective-permute-done((bf16[280,512]{1,0:T(8,128)(2,1)S(1)}, bf16[280,512]{1,0:T(8,128)(2,1)S(1)}, u32[]{:S(2)}, u32[]{:S(2)}) %collective-permute-start.4) | collective-permute-done | bytes 286752 | tf_op jit(solution)/shard_map/ppermute | solution.py:150
  27.3 1.9 %collective-permute-start.5 = (bf16[140,512]{1,0:T(8,128)(2,1)S(1)}, bf16[140,512]{1,0:T(8,128)(2,1)S(1)}, u32[]{:S(2)}, u32[]{:S(2)}) collective-permute-start(bf16[140,512]{1,0:T(8,128)(2,1)S(1)} %select_convert_fusion.1), channel_id=1, source_target_pairs={{0,2},{1,3},{2,0},{3,1},{4,6},{5,7},{6,4},{7,5},{8,10},{9,11},{10,... | collective-permute-start | bytes 430088 | tf_op jit(solution)/shard_map/ppermute | solution.py:150
  29.3 4.1 %collective-permute-done.5 = bf16[140,512]{1,0:T(8,128)(2,1)S(1)} collective-permute-done((bf16[140,512]{1,0:T(8,128)(2,1)S(1)}, bf16[140,512]{1,0:T(8,128)(2,1)S(1)}, u32[]{:S(2)}, u32[]{:S(2)}) %collective-permute-start.5) | collective-permute-done | bytes 143392 | tf_op jit(solution)/shard_map/ppermute | solution.py:150
  33.5 1.9 %collective-permute-start.6 = (bf16[140,512]{1,0:T(8,128)(2,1)S(1)}, bf16[140,512]{1,0:T(8,128)(2,1)S(1)}, u32[]{:S(2)}, u32[]{:S(2)}) collective-permute-start(bf16[140,512]{1,0:T(8,128)(2,1)S(1)} %add_convert_fusion.7), channel_id=1, source_target_pairs={{0,4},{1,5},{2,6},{3,7},{4,0},{5,1},{6,2},{7,3},{8,12},{9,13},{10,... | collective-permute-start | bytes 430088 | tf_op jit(solution)/shard_map/ppermute | solution.py:156
  35.3 3.4 %collective-permute-done.6 = bf16[140,512]{1,0:T(8,128)(2,1)S(1)} collective-permute-done((bf16[140,512]{1,0:T(8,128)(2,1)S(1)}, bf16[140,512]{1,0:T(8,128)(2,1)S(1)}, u32[]{:S(2)}, u32[]{:S(2)}) %collective-permute-start.6) | collective-permute-done | bytes 143392 | tf_op jit(solution)/shard_map/ppermute | solution.py:156
  38.8 3.2 %collective-permute-start.7 = (bf16[140,512]{1,0:T(8,128)(2,1)S(1)}, bf16[140,512]{1,0:T(8,128)(2,1)S(1)}, u32[]{:S(2)}, u32[]{:S(2)}) collective-permute-start(bf16[140,512]{1,0:T(8,128)(2,1)S(1)} %add_convert_fusion.6), channel_id=1, source_target_pairs={{0,8},{1,9},{2,10},{3,11},{4,12},{5,13},{6,14},{7,15},{8,0},{9,1},... | collective-permute-start | bytes 430088 | tf_op jit(solution)/shard_map/ppermute | solution.py:156
  42.0 5.9 %collective-permute-done.7 = bf16[140,512]{1,0:T(8,128)(2,1)S(1)} collective-permute-done((bf16[140,512]{1,0:T(8,128)(2,1)S(1)}, bf16[140,512]{1,0:T(8,128)(2,1)S(1)}, u32[]{:S(2)}, u32[]{:S(2)}) %collective-permute-start.7) | collective-permute-done | bytes 143392 | tf_op jit(solution)/shard_map/ppermute | solution.py:156
  47.8 1.6 %collective-permute-start.8 = (bf16[140,512]{1,0:T(8,128)(2,1)S(1)}, bf16[140,512]{1,0:T(8,128)(2,1)S(1)}, u32[]{:S(2)}, u32[]{:S(2)}) collective-permute-start(bf16[140,512]{1,0:T(8,128)(2,1)S(1)} %add_convert_fusion.5), channel_id=1, source_target_pairs={{0,2},{1,3},{2,0},{3,1},{4,6},{5,7},{6,4},{7,5},{8,10},{9,11},{10,... | collective-permute-start | bytes 430088 | tf_op jit(solution)/shard_map/ppermute | solution.py:161
  49.4 3.6 %collective-permute-done.8 = bf16[140,512]{1,0:T(8,128)(2,1)S(1)} collective-permute-done((bf16[140,512]{1,0:T(8,128)(2,1)S(1)}, bf16[140,512]{1,0:T(8,128)(2,1)S(1)}, u32[]{:S(2)}, u32[]{:S(2)}) %collective-permute-start.8) | collective-permute-done | bytes 143392 | tf_op jit(solution)/shard_map/ppermute | solution.py:161
  53.3 1.5 %collective-permute-done.9 = bf16[280,512]{1,0:T(8,128)(2,1)S(1)} collective-permute-done((bf16[280,512]{1,0:T(8,128)(2,1)S(1)}, bf16[280,512]{1,0:T(8,128)(2,1)S(1)}, u32[]{:S(2)}, u32[]{:S(2)}) %collective-permute-start.9) | collective-permute-done | bytes 286752 | tf_op jit(solution)/shard_map/ppermute | solution.py:161
  55.0 1.1 %slice_convert_fusion = f32[512,512]{1,0:T(8,128)} fusion(bf16[560,512]{1,0:T(8,128)(2,1)S(1)} %maximum_select_fusion), kind=kLoop, calls=%fused_computation.38 | loop fusion | flops 262144 | bytes 1572864 | tf_op jit(solution)/shard_map/convert_element_type | solution.py:225
  56.8 1.3 %fusion.50 = f32[512,512]{1,0:T(8,128)} fusion(bf16[32,512]{1,0:T(8,128)(2,1)S(1)} %fusion.8, bf16[32,512]{1,0:T(8,128)(2,1)S(1)} %gather_fusion), kind=kOutput, calls=%fused_computation.89 | convolution fusion | flops 16777216 | bytes 1114112 | tf_op jit(solution)/shard_map/dot_general | solution.py:91
  58.7 3.0 %fusion.11 = f32[2048,512]{1,0:T(8,128)} fusion(bf16[512,512]{1,0:T(8,128)(2,1)S(1)} %copy-done.1, bf16[32,512]{1,0:T(8,128)(2,1)S(1)} %fusion.8, bf16[16,2048]{1,0:T(8,128)(2,1)S(1)} %collective-permute-done.3, bf16[16,2048]{1,0:T(8,128)(2,1)S(1)} %maximum_select_fusion.3, pred[]{:T(512)S(6)} %eq.38, bf16[32,512]{1,0:T(8,128)(2,1)S(1)} %gather_fusion), kind=kOutput, calls=%fused_computation.24 | convolution fusion | flops 84557824 | bytes 4915201 | tf_op jit(solution)/shard_map/dot_general | solution.py:98
  (52 shorter events, 9.6 us)
Async XLA Ops:
  0.6 16.5 %copy-start = (bf16[2048,512]{1,0:T(8,128)(2,1)S(1)}, bf16[2048,512]{1,0:T(8,128)(2,1)}, u32[]{:S(2)}) copy-start(bf16[2048,512]{1,0:T(8,128)(2,1)} %param.12) | copy-start | bytes 6291460
  0.6 17.0 %copy-start.1 = (bf16[512,512]{1,0:T(8,128)(2,1)S(1)}, bf16[512,512]{1,0:T(8,128)(2,1)}, u32[]{:S(2)}) copy-start(bf16[512,512]{1,0:T(8,128)(2,1)} %param.13) | copy-start | bytes 1572868
  0.7 17.0 %copy-start.6 = (s32[32]{0:T(128)S(1)}, s32[32]{0:T(128)}, u32[]{:S(2)}) copy-start(s32[32]{0:T(128)} %param.11) | copy-start | bytes 388
  0.7 1.6 %collective-permute-start = (bf16[2,2048]{1,0:T(2,128)(2,1)}, bf16[2,2048]{1,0:T(2,128)(2,1)S(1)}, u32[]{:S(2)}, u32[]{:S(2)}) collective-permute-start(bf16[2,2048]{1,0:T(2,128)(2,1)} %param.9), channel_id=1, source_target_pairs={{0,1},{1,0},{2,3},{3,2},{4,5},{5,4},{6,7},{7,6},{8,9},{9,8},{10,11... | collective-permute-start | bytes 24584 | tf_op jit(solution)/shard_map/ppermute | solution.py:119
  3.0 4.6 %collective-permute-start.1 = (bf16[4,2048]{1,0:T(4,128)(2,1)S(1)}, bf16[4,2048]{1,0:T(4,128)(2,1)S(1)}, u32[]{:S(2)}, u32[]{:S(2)}) collective-permute-start(bf16[4,2048]{1,0:T(4,128)(2,1)S(1)} %maximum_select_fusion.7), channel_id=1, source_target_pairs={{0,2},{1,3},{2,0},{3,1},{4,6},{5,7},{6,4},{7,5},{8,10},{9,11},{10,... | collective-permute-start | bytes 49160 | tf_op jit(solution)/shard_map/ppermute | solution.py:119
  7.7 4.0 %collective-permute-start.2 = (bf16[8,2048]{1,0:T(8,128)(2,1)S(1)}, bf16[8,2048]{1,0:T(8,128)(2,1)S(1)}, u32[]{:S(2)}, u32[]{:S(2)}) collective-permute-start(bf16[8,2048]{1,0:T(8,128)(2,1)S(1)} %maximum_select_fusion.4), channel_id=1, source_target_pairs={{0,4},{1,5},{2,6},{3,7},{4,0},{5,1},{6,2},{7,3},{8,12},{9,13},{10,... | collective-permute-start | bytes 98312 | tf_op jit(solution)/shard_map/ppermute | solution.py:119
  11.8 5.3 %collective-permute-start.3 = (bf16[16,2048]{1,0:T(8,128)(2,1)S(1)}, bf16[16,2048]{1,0:T(8,128)(2,1)S(1)}, u32[]{:S(2)}, u32[]{:S(2)}) collective-permute-start(bf16[16,2048]{1,0:T(8,128)(2,1)S(1)} %maximum_select_fusion.3), channel_id=1, source_target_pairs={{0,8},{1,9},{2,10},{3,11},{4,12},{5,13},{6,14},{7,15},{8,0},{9,1},... | collective-permute-start | bytes 196616 | tf_op jit(solution)/shard_map/ppermute | solution.py:119
  14.9 3.1 %copy-start.4 = (bf16[512,512]{1,0:T(8,128)(2,1)S(1)}, bf16[512,512]{1,0:T(8,128)(2,1)}, u32[]{:S(2)}) copy-start(bf16[512,512]{1,0:T(8,128)(2,1)} %constant.109.clone) | copy-start | bytes 1572868
  18.1 1.0 %copy-start.2 = (bf16[512,256]{1,0:T(8,128)(2,1)S(1)}, bf16[512,256]{1,0:T(8,128)(2,1)}, u32[]{:S(2)}) copy-start(bf16[512,256]{1,0:T(8,128)(2,1)} %constant.113) | copy-start | bytes 786436
  18.6 1.0 %copy-start.5 = (bf16[512,256]{1,0:T(8,128)(2,1)S(1)}, bf16[512,256]{1,0:T(8,128)(2,1)}, u32[]{:S(2)}) copy-start(bf16[512,256]{1,0:T(8,128)(2,1)} %constant.114) | copy-start | bytes 786436
  19.6 1.0 %copy-start.3 = (bf16[512,512]{1,0:T(8,128)(2,1)S(1)}, bf16[512,512]{1,0:T(8,128)(2,1)}, u32[]{:S(2)}) copy-start(bf16[512,512]{1,0:T(8,128)(2,1)} %param.16) | copy-start | bytes 1572868
  19.6 1.3 %copy-start.7 = (bf16[32,24,512]{2,1,0:T(8,128)(2,1)S(1)}, bf16[32,24,512]{2,1,0:T(8,128)(2,1)}, u32[]{:S(2)}) copy-start(bf16[32,24,512]{2,1,0:T(8,128)(2,1)} %param.10) | copy-start | bytes 2359300
  25.5 1.6 %collective-permute-start.4 = (bf16[280,512]{1,0:T(8,128)(2,1)S(1)}, bf16[280,512]{1,0:T(8,128)(2,1)S(1)}, u32[]{:S(2)}, u32[]{:S(2)}) collective-permute-start(bf16[280,512]{1,0:T(8,128)(2,1)S(1)} %select_convert_fusion), channel_id=1, source_target_pairs={{0,1},{1,0},{2,3},{3,2},{4,5},{5,4},{6,7},{7,6},{8,9},{9,8},{10,11... | collective-permute-start | bytes 860168 | tf_op jit(solution)/shard_map/ppermute | solution.py:150
  27.3 6.1 %collective-permute-start.5 = (bf16[140,512]{1,0:T(8,128)(2,1)S(1)}, bf16[140,512]{1,0:T(8,128)(2,1)S(1)}, u32[]{:S(2)}, u32[]{:S(2)}) collective-permute-start(bf16[140,512]{1,0:T(8,128)(2,1)S(1)} %select_convert_fusion.1), channel_id=1, source_target_pairs={{0,2},{1,3},{2,0},{3,1},{4,6},{5,7},{6,4},{7,5},{8,10},{9,11},{10,... | collective-permute-start | bytes 430088 | tf_op jit(solution)/shard_map/ppermute | solution.py:150
  33.5 5.3 %collective-permute-start.6 = (bf16[140,512]{1,0:T(8,128)(2,1)S(1)}, bf16[140,512]{1,0:T(8,128)(2,1)S(1)}, u32[]{:S(2)}, u32[]{:S(2)}) collective-permute-start(bf16[140,512]{1,0:T(8,128)(2,1)S(1)} %add_convert_fusion.7), channel_id=1, source_target_pairs={{0,4},{1,5},{2,6},{3,7},{4,0},{5,1},{6,2},{7,3},{8,12},{9,13},{10,... | collective-permute-start | bytes 430088 | tf_op jit(solution)/shard_map/ppermute | solution.py:156
  38.8 9.0 %collective-permute-start.7 = (bf16[140,512]{1,0:T(8,128)(2,1)S(1)}, bf16[140,512]{1,0:T(8,128)(2,1)S(1)}, u32[]{:S(2)}, u32[]{:S(2)}) collective-permute-start(bf16[140,512]{1,0:T(8,128)(2,1)S(1)} %add_convert_fusion.6), channel_id=1, source_target_pairs={{0,8},{1,9},{2,10},{3,11},{4,12},{5,13},{6,14},{7,15},{8,0},{9,1},... | collective-permute-start | bytes 430088 | tf_op jit(solution)/shard_map/ppermute | solution.py:156
  47.8 5.2 %collective-permute-start.8 = (bf16[140,512]{1,0:T(8,128)(2,1)S(1)}, bf16[140,512]{1,0:T(8,128)(2,1)S(1)}, u32[]{:S(2)}, u32[]{:S(2)}) collective-permute-start(bf16[140,512]{1,0:T(8,128)(2,1)S(1)} %add_convert_fusion.5), channel_id=1, source_target_pairs={{0,2},{1,3},{2,0},{3,1},{4,6},{5,7},{6,4},{7,5},{8,10},{9,11},{10,... | collective-permute-start | bytes 430088 | tf_op jit(solution)/shard_map/ppermute | solution.py:161
  53.2 1.6 %collective-permute-start.9 = (bf16[280,512]{1,0:T(8,128)(2,1)S(1)}, bf16[280,512]{1,0:T(8,128)(2,1)S(1)}, u32[]{:S(2)}, u32[]{:S(2)}) collective-permute-start(bf16[280,512]{1,0:T(8,128)(2,1)S(1)} %maximum_select_fusion.1), channel_id=1, source_target_pairs={{0,1},{1,0},{2,3},{3,2},{4,5},{5,4},{6,7},{7,6},{8,9},{9,8},{10,11... | collective-permute-start | bytes 860168 | tf_op jit(solution)/shard_map/ppermute | solution.py:161

commit v11 on v10

--- a/solution.py
+++ b/solution.py
@@ -183,15 +183,15 @@
     forward_transform, inverse_transform = rotation_tables(width // 2)
     loss_scale = 1.0 / math.sqrt(samples * sub_dev * lax.axis_size("freq"))
     all_inputs = gather_rows(encoder_input, "freq")
-    codes = jnp.tanh(
-        jnp.dot(all_inputs, encoder_weight, preferred_element_type=jnp.float32)
-    ).astype(jnp.bfloat16)
     selection = (
         sample_index[None, :] == jnp.arange(samples, dtype=jnp.int32)[:, None]
     ).astype(jnp.bfloat16)
-    codes_by_sample = jnp.dot(selection, codes, preferred_element_type=jnp.float32).astype(
+    inputs_by_sample = jnp.dot(selection, all_inputs, preferred_element_type=jnp.float32).astype(
         jnp.bfloat16
     )
+    codes_by_sample = jnp.tanh(
+        jnp.dot(inputs_by_sample, encoder_weight, preferred_element_type=jnp.float32)
+    ).astype(jnp.bfloat16)
     latent = jnp.dot(codes_by_sample, decoder_weight, preferred_element_type=jnp.float32)
     gain_row_values = frequency_amplitude.astype(jnp.float32)
     mixed_in = (latent[:, None, :] * gain_row_values[None]).astype(jnp.bfloat16).reshape(-1, width)
@@ -209,13 +209,17 @@
         "orm,rm->om", derivative_entering.reshape(samples, sub_dev, width), gain_row_values
     )
     count = lax.axis_size("freq")
-    packed_rows = samples + 1 + grad_out.shape[0]
+    half_width = grad_filter.shape[1]
+    filter_rows = jnp.concatenate(
+        [grad_filter, jnp.zeros((grad_filter.shape[0], width - half_width), jnp.float32)], 1
+    )
+    packed_rows = grad_out.shape[0] + samples + filter_rows.shape[0]
     padding = -packed_rows % count
     packed = jnp.concatenate(
         [
             grad_out,
             derivative_bottleneck,
-            grad_filter.reshape(1, -1),
+            filter_rows,
             jnp.zeros((padding, width), jnp.float32),
         ],
         0,
@@ -224,9 +228,11 @@
     rows_out = grad_out.shape[0]
     grad_out = packed[:rows_out].astype(jnp.float32)
     derivative_bottleneck = packed[rows_out : rows_out + samples].astype(jnp.float32)
-    grad_filter = packed[rows_out + samples].astype(jnp.float32).reshape(grad_filter.shape)
+    grad_filter = packed[
+        rows_out + samples : rows_out + samples + filter_rows.shape[0], :half_width
+    ].astype(jnp.float32)
     grad_enc, grad_dec = encoder_grads(
-        all_inputs, codes, derivative_bottleneck[sample_index], decoder_weight
+        inputs_by_sample, codes_by_sample, derivative_bottleneck, decoder_weight
     )
     return (grad_enc, grad_dec, grad_out, grad_filter)
 

time: 61.9 us -> 62.2 us (level)
  local copies, waits for them, and re-layouts: 3.01 us -> 1.97 us
  matrix products: 10.8 us -> 11.5 us
    dot_general x1 -> x2, matrix products: 0.47 us -> 1.29 us  [the longest x1 0.82 us: local(): jnp.dot(selection, all_inputs, preferred_element_type=jnp.float32)]
    gather x1 -> x0, local copies, waits for them, and re-layouts: 0.63 us -> none  [local(): derivative_bottleneck[sample_index]]
where the time goes in v11:
time: 62.2 us; the launch traced here: 61.8 us
  waiting for transfers between devices  25.3 us (41%)
  starting transfers between devices  17.4 us (28%)
  matrix products  11.5 us (18%)
  other arithmetic  4.8 us (8%)
  local copies, waits for them, and re-layouts  1.97 us (3%)
  between operations  0.88 us (1%)
    ppermute x2, waiting for transfers between devices, sum_halving(): arrived = lax.ppermute(values, axis_name, _exchange_pairs(count, distance))  9.23 us
    ppermute x4, starting transfers between devices, gather_rows(): other = lax.ppermute(block, axis_name, _exchange_pairs(count, distance))  8.68 us
    ppermute x2, waiting for transfers between devices, sum_halving(): arrived = lax.ppermute(send, axis_name, _exchange_pairs(count, distance))  5.71 us
    ppermute x4, waiting for transfers between devices, gather_rows(): other = lax.ppermute(block, axis_name, _exchange_pairs(count, distance))  5.2 us
    ppermute x2, waiting for transfers between devices, sum_halving(): other = lax.ppermute(values, axis_name, _exchange_pairs(count, distance))  5.19 us
    ppermute x2, starting transfers between devices, sum_halving(): arrived = lax.ppermute(values, axis_name, _exchange_pairs(count, distance))  5.06 us
    dot_general x1, matrix products, encoder_grads(): lax.dot_general(inputs_rows, grad_pre, (((0,), (0,)), ((), ())), preferre...  2.96 us
    ppermute x2, starting transfers between devices, sum_halving(): arrived = lax.ppermute(send, axis_name, _exchange_pairs(count, distance))  1.98 us
  transfers between devices with their start and end apart: 10, of which 10 were waited for; matrix products, arithmetic and copies ran while one was open for 3% of the time, Pallas kernels for 0%

profile of v11, /device:TPU:0, one launch (start us, length us, event | category | flops | bytes accessed | tf_op | source)
XLA Modules:
  0.0 61.8 jit_solution(8020488711914015226)
XLA Ops:
  1.2 1.0 %collective-permute-done = bf16[2,2048]{1,0:T(2,128)(2,1)S(1)} collective-permute-done((bf16[2,2048]{1,0:T(2,128)(2,1)}, bf16[2,2048]{1,0:T(2,128)(2,1)S(1)}, u32[]{:S(2)}, u32[]{:S(2)}) %collective-permute-start) | collective-permute-done | bytes 8224 | tf_op jit(solution)/shard_map/ppermute | solution.py:119
  3.0 2.9 %collective-permute-start.1 = (bf16[4,2048]{1,0:T(4,128)(2,1)S(1)}, bf16[4,2048]{1,0:T(4,128)(2,1)S(1)}, u32[]{:S(2)}, u32[]{:S(2)}) collective-permute-start(bf16[4,2048]{1,0:T(4,128)(2,1)S(1)} %maximum_select_fusion.6), channel_id=1, source_target_pairs={{0,2},{1,3},{2,0},{3,1},{4,6},{5,7},{6,4},{7,5},{8,10},{9,11},{10,... | collective-permute-start | bytes 49160 | tf_op jit(solution)/shard_map/ppermute | solution.py:119
  5.9 0.8 %bitcast_convert_fusion = (f32[512,24]{0,1:T(8,128)S(1)}, f32[24,512]{1,0:T(8,128)S(1)}) fusion(bf16[24,512]{1,0:T(8,128)(2,1)} %param.14), kind=kLoop, calls=%fused_computation.71 | loop fusion | flops 24576 | bytes 122880
  6.8 0.9 %collective-permute-done.1 = bf16[4,2048]{1,0:T(4,128)(2,1)S(1)} collective-permute-done((bf16[4,2048]{1,0:T(4,128)(2,1)S(1)}, bf16[4,2048]{1,0:T(4,128)(2,1)S(1)}, u32[]{:S(2)}, u32[]{:S(2)}) %collective-permute-start.1) | collective-permute-done | bytes 16416 | tf_op jit(solution)/shard_map/ppermute | solution.py:119
  7.7 2.1 %collective-permute-start.2 = (bf16[8,2048]{1,0:T(8,128)(2,1)S(1)}, bf16[8,2048]{1,0:T(8,128)(2,1)S(1)}, u32[]{:S(2)}, u32[]{:S(2)}) collective-permute-start(bf16[8,2048]{1,0:T(8,128)(2,1)S(1)} %maximum_select_fusion.5), channel_id=1, source_target_pairs={{0,4},{1,5},{2,6},{3,7},{4,0},{5,1},{6,2},{7,3},{8,12},{9,13},{10,... | collective-permute-start | bytes 98312 | tf_op jit(solution)/shard_map/ppermute | solution.py:119
  10.6 1.1 %collective-permute-done.2 = bf16[8,2048]{1,0:T(8,128)(2,1)S(1)} collective-permute-done((bf16[8,2048]{1,0:T(8,128)(2,1)S(1)}, bf16[8,2048]{1,0:T(8,128)(2,1)S(1)}, u32[]{:S(2)}, u32[]{:S(2)}) %collective-permute-start.2) | collective-permute-done | bytes 32800 | tf_op jit(solution)/shard_map/ppermute | solution.py:119
  11.7 3.1 %collective-permute-start.3 = (bf16[16,2048]{1,0:T(8,128)(2,1)S(1)}, bf16[16,2048]{1,0:T(8,128)(2,1)S(1)}, u32[]{:S(2)}, u32[]{:S(2)}) collective-permute-start(bf16[16,2048]{1,0:T(8,128)(2,1)S(1)} %maximum_select_fusion.4), channel_id=1, source_target_pairs={{0,8},{1,9},{2,10},{3,11},{4,12},{5,13},{6,14},{7,15},{8,0},{9,1},... | collective-permute-start | bytes 196616 | tf_op jit(solution)/shard_map/ppermute | solution.py:119
  14.9 2.2 %collective-permute-done.3 = bf16[16,2048]{1,0:T(8,128)(2,1)S(1)} collective-permute-done((bf16[16,2048]{1,0:T(8,128)(2,1)S(1)}, bf16[16,2048]{1,0:T(8,128)(2,1)S(1)}, u32[]{:S(2)}, u32[]{:S(2)}) %collective-permute-start.3) | collective-permute-done | bytes 65568 | tf_op jit(solution)/shard_map/ppermute | solution.py:119
  17.1 0.8 %convolution_convert_fusion = bf16[32,2048]{1,0:T(8,128)(2,1)S(1)} fusion(bf16[16,2048]{1,0:T(8,128)(2,1)S(1)} %collective-permute-done.3, bf16[16,2048]{1,0:T(8,128)(2,1)S(1)} %maximum_select_fusion.4, pred[]{:T(512)S(6)} %eq.41, s32[32]{0:T(128)} %param.11), kind=kOutput, calls=%fused_computation.2 | convolution fusion | flops 4850688 | bytes 262273 | tf_op jit(solution)/shard_map/dot_general | solution.py:189
  20.5 0.9 %add_convert_fusion = (bf16[768,512]{1,0:T(8,128)(2,1)S(1)}, f32[768,512]{1,0:T(8,128)S(1)}) fusion(bf16[32,24,512]{2,1,0:T(8,128)(2,1)S(1)} %multiply_convert_fusion, f32[768,512]{1,0:T(8,128)S(1)} %fusion.14, bf16[512,256]{1,0:T(8,128)(2,1)S(1)} %copy-done.5, f32[768,512]{1,0:T(8,128)S(1)} %fusion.52, f32[256]{0:T(256)S(1)} %bitcast.41, f32[256]{0:T(256)S(1)} %bitcast.37), kind=kOutput, calls=%fused_computation.14 | convolution fusion | flops 206831616 | bytes 6555648 | tf_op jit(solution)/shard_map/dot_general | solution.py:55
  23.7 1.2 %fusion.11 = f32[768,512]{1,0:T(8,128)S(1)} fusion(bf16[512,512]{1,0:T(8,128)(2,1)S(1)} %copy-done.4, f32[768,512]{1,0:T(8,128)S(1)} %get-tuple-element.11, f32[768,512]{1,0:T(8,128)S(1)} %convolution_add_fusion), kind=kOutput, calls=%fused_computation.29 | convolution fusion | flops 410517504 | bytes 5242880 | tf_op jit(solution)/shard_map/dot_general | solution.py:71
  26.5 1.6 %collective-permute-done.4 = bf16[280,512]{1,0:T(8,128)(2,1)S(1)} collective-permute-done((bf16[280,512]{1,0:T(8,128)(2,1)S(1)}, bf16[280,512]{1,0:T(8,128)(2,1)S(1)}, u32[]{:S(2)}, u32[]{:S(2)}) %collective-permute-start.4) | collective-permute-done | bytes 286752 | tf_op jit(solution)/shard_map/ppermute | solution.py:150
  28.2 1.9 %collective-permute-start.5 = (bf16[140,512]{1,0:T(8,128)(2,1)S(1)}, bf16[140,512]{1,0:T(8,128)(2,1)S(1)}, u32[]{:S(2)}, u32[]{:S(2)}) collective-permute-start(bf16[140,512]{1,0:T(8,128)(2,1)S(1)} %select_convert_fusion.1), channel_id=1, source_target_pairs={{0,2},{1,3},{2,0},{3,1},{4,6},{5,7},{6,4},{7,5},{8,10},{9,11},{10,... | collective-permute-start | bytes 430088 | tf_op jit(solution)/shard_map/ppermute | solution.py:150
  30.1 4.1 %collective-permute-done.5 = bf16[140,512]{1,0:T(8,128)(2,1)S(1)} collective-permute-done((bf16[140,512]{1,0:T(8,128)(2,1)S(1)}, bf16[140,512]{1,0:T(8,128)(2,1)S(1)}, u32[]{:S(2)}, u32[]{:S(2)}) %collective-permute-start.5) | collective-permute-done | bytes 143392 | tf_op jit(solution)/shard_map/ppermute | solution.py:150
  34.4 1.9 %collective-permute-start.6 = (bf16[140,512]{1,0:T(8,128)(2,1)S(1)}, bf16[140,512]{1,0:T(8,128)(2,1)S(1)}, u32[]{:S(2)}, u32[]{:S(2)}) collective-permute-start(bf16[140,512]{1,0:T(8,128)(2,1)S(1)} %add_convert_fusion.7), channel_id=1, source_target_pairs={{0,4},{1,5},{2,6},{3,7},{4,0},{5,1},{6,2},{7,3},{8,12},{9,13},{10,... | collective-permute-start | bytes 430088 | tf_op jit(solution)/shard_map/ppermute | solution.py:156
  36.2 3.4 %collective-permute-done.6 = bf16[140,512]{1,0:T(8,128)(2,1)S(1)} collective-permute-done((bf16[140,512]{1,0:T(8,128)(2,1)S(1)}, bf16[140,512]{1,0:T(8,128)(2,1)S(1)}, u32[]{:S(2)}, u32[]{:S(2)}) %collective-permute-start.6) | collective-permute-done | bytes 143392 | tf_op jit(solution)/shard_map/ppermute | solution.py:156
  39.6 3.2 %collective-permute-start.7 = (bf16[140,512]{1,0:T(8,128)(2,1)S(1)}, bf16[140,512]{1,0:T(8,128)(2,1)S(1)}, u32[]{:S(2)}, u32[]{:S(2)}) collective-permute-start(bf16[140,512]{1,0:T(8,128)(2,1)S(1)} %add_convert_fusion.6), channel_id=1, source_target_pairs={{0,8},{1,9},{2,10},{3,11},{4,12},{5,13},{6,14},{7,15},{8,0},{9,1},... | collective-permute-start | bytes 430088 | tf_op jit(solution)/shard_map/ppermute | solution.py:156
  42.8 5.9 %collective-permute-done.7 = bf16[140,512]{1,0:T(8,128)(2,1)S(1)} collective-permute-done((bf16[140,512]{1,0:T(8,128)(2,1)S(1)}, bf16[140,512]{1,0:T(8,128)(2,1)S(1)}, u32[]{:S(2)}, u32[]{:S(2)}) %collective-permute-start.7) | collective-permute-done | bytes 143392 | tf_op jit(solution)/shard_map/ppermute | solution.py:156
  48.7 1.6 %collective-permute-start.8 = (bf16[140,512]{1,0:T(8,128)(2,1)S(1)}, bf16[140,512]{1,0:T(8,128)(2,1)S(1)}, u32[]{:S(2)}, u32[]{:S(2)}) collective-permute-start(bf16[140,512]{1,0:T(8,128)(2,1)S(1)} %add_convert_fusion.5), channel_id=1, source_target_pairs={{0,2},{1,3},{2,0},{3,1},{4,6},{5,7},{6,4},{7,5},{8,10},{9,11},{10,... | collective-permute-start | bytes 430088 | tf_op jit(solution)/shard_map/ppermute | solution.py:161
  50.3 3.6 %collective-permute-done.8 = bf16[140,512]{1,0:T(8,128)(2,1)S(1)} collective-permute-done((bf16[140,512]{1,0:T(8,128)(2,1)S(1)}, bf16[140,512]{1,0:T(8,128)(2,1)S(1)}, u32[]{:S(2)}, u32[]{:S(2)}) %collective-permute-start.8) | collective-permute-done | bytes 143392 | tf_op jit(solution)/shard_map/ppermute | solution.py:161
  54.1 1.6 %collective-permute-done.9 = bf16[280,512]{1,0:T(8,128)(2,1)S(1)} collective-permute-done((bf16[280,512]{1,0:T(8,128)(2,1)S(1)}, bf16[280,512]{1,0:T(8,128)(2,1)S(1)}, u32[]{:S(2)}, u32[]{:S(2)}) %collective-permute-start.9) | collective-permute-done | bytes 286752 | tf_op jit(solution)/shard_map/ppermute | solution.py:161
  56.5 1.3 %fusion.37 = f32[512,512]{1,0:T(8,128)} fusion(bf16[32,512]{1,0:T(8,128)(2,1)S(1)} %fusion.8, bf16[560,512]{1,0:T(8,128)(2,1)S(1)} %maximum_select_fusion), kind=kOutput, calls=%fused_computation.68 | convolution fusion | flops 16777216 | bytes 1114112 | tf_op jit(solution)/shard_map/dot_general | solution.py:91
  57.8 1.1 %slice_convert_fusion = f32[512,512]{1,0:T(8,128)} fusion(bf16[560,512]{1,0:T(8,128)(2,1)S(1)} %maximum_select_fusion), kind=kLoop, calls=%fused_computation.36 | loop fusion | flops 262144 | bytes 1572864 | tf_op jit(solution)/shard_map/convert_element_type | solution.py:229
  58.9 3.0 %fusion.10 = f32[2048,512]{1,0:T(8,128)} fusion(bf16[32,2048]{1,0:T(8,128)(2,1)S(1)} %convolution_convert_fusion, bf16[512,512]{1,0:T(8,128)(2,1)S(1)} %copy-done.1, bf16[32,512]{1,0:T(8,128)(2,1)S(1)} %fusion.8, bf16[560,512]{1,0:T(8,128)(2,1)S(1)} %maximum_select_fusion), kind=kOutput, calls=%fused_computation.22 | convolution fusion | flops 83968000 | bytes 4915200 | tf_op jit(solution)/shard_map/dot_general | solution.py:98
  (45 shorter events, 9.8 us)
Async XLA Ops:
  0.6 17.3 %copy-start = (bf16[2048,512]{1,0:T(8,128)(2,1)S(1)}, bf16[2048,512]{1,0:T(8,128)(2,1)}, u32[]{:S(2)}) copy-start(bf16[2048,512]{1,0:T(8,128)(2,1)} %param.12) | copy-start | bytes 6291460
  0.6 1.6 %collective-permute-start = (bf16[2,2048]{1,0:T(2,128)(2,1)}, bf16[2,2048]{1,0:T(2,128)(2,1)S(1)}, u32[]{:S(2)}, u32[]{:S(2)}) collective-permute-start(bf16[2,2048]{1,0:T(2,128)(2,1)} %param.9), channel_id=1, source_target_pairs={{0,1},{1,0},{2,3},{3,2},{4,5},{5,4},{6,7},{7,6},{8,9},{9,8},{10,11... | collective-permute-start | bytes 24584 | tf_op jit(solution)/shard_map/ppermute | solution.py:119
  3.0 4.6 %collective-permute-start.1 = (bf16[4,2048]{1,0:T(4,128)(2,1)S(1)}, bf16[4,2048]{1,0:T(4,128)(2,1)S(1)}, u32[]{:S(2)}, u32[]{:S(2)}) collective-permute-start(bf16[4,2048]{1,0:T(4,128)(2,1)S(1)} %maximum_select_fusion.6), channel_id=1, source_target_pairs={{0,2},{1,3},{2,0},{3,1},{4,6},{5,7},{6,4},{7,5},{8,10},{9,11},{10,... | collective-permute-start | bytes 49160 | tf_op jit(solution)/shard_map/ppermute | solution.py:119
  6.8 11.7 %copy-start.1 = (bf16[512,512]{1,0:T(8,128)(2,1)S(1)}, bf16[512,512]{1,0:T(8,128)(2,1)}, u32[]{:S(2)}) copy-start(bf16[512,512]{1,0:T(8,128)(2,1)} %param.13) | copy-start | bytes 1572868
  7.7 4.0 %collective-permute-start.2 = (bf16[8,2048]{1,0:T(8,128)(2,1)S(1)}, bf16[8,2048]{1,0:T(8,128)(2,1)S(1)}, u32[]{:S(2)}, u32[]{:S(2)}) collective-permute-start(bf16[8,2048]{1,0:T(8,128)(2,1)S(1)} %maximum_select_fusion.5), channel_id=1, source_target_pairs={{0,4},{1,5},{2,6},{3,7},{4,0},{5,1},{6,2},{7,3},{8,12},{9,13},{10,... | collective-permute-start | bytes 98312 | tf_op jit(solution)/shard_map/ppermute | solution.py:119
  11.7 5.3 %collective-permute-start.3 = (bf16[16,2048]{1,0:T(8,128)(2,1)S(1)}, bf16[16,2048]{1,0:T(8,128)(2,1)S(1)}, u32[]{:S(2)}, u32[]{:S(2)}) collective-permute-start(bf16[16,2048]{1,0:T(8,128)(2,1)S(1)} %maximum_select_fusion.4), channel_id=1, source_target_pairs={{0,8},{1,9},{2,10},{3,11},{4,12},{5,13},{6,14},{7,15},{8,0},{9,1},... | collective-permute-start | bytes 196616 | tf_op jit(solution)/shard_map/ppermute | solution.py:119
  17.9 1.0 %copy-start.4 = (bf16[512,512]{1,0:T(8,128)(2,1)S(1)}, bf16[512,512]{1,0:T(8,128)(2,1)}, u32[]{:S(2)}) copy-start(bf16[512,512]{1,0:T(8,128)(2,1)} %constant.107.clone) | copy-start | bytes 1572868
  18.8 1.0 %copy-start.2 = (bf16[512,256]{1,0:T(8,128)(2,1)S(1)}, bf16[512,256]{1,0:T(8,128)(2,1)}, u32[]{:S(2)}) copy-start(bf16[512,256]{1,0:T(8,128)(2,1)} %constant.113) | copy-start | bytes 786436
  19.5 1.0 %copy-start.5 = (bf16[512,256]{1,0:T(8,128)(2,1)S(1)}, bf16[512,256]{1,0:T(8,128)(2,1)}, u32[]{:S(2)}) copy-start(bf16[512,256]{1,0:T(8,128)(2,1)} %constant.114) | copy-start | bytes 786436
  20.5 1.0 %copy-start.3 = (bf16[512,512]{1,0:T(8,128)(2,1)S(1)}, bf16[512,512]{1,0:T(8,128)(2,1)}, u32[]{:S(2)}) copy-start(bf16[512,512]{1,0:T(8,128)(2,1)} %param.16) | copy-start | bytes 1572868
  20.5 1.3 %copy-start.6 = (bf16[32,24,512]{2,1,0:T(8,128)(2,1)S(1)}, bf16[32,24,512]{2,1,0:T(8,128)(2,1)}, u32[]{:S(2)}) copy-start(bf16[32,24,512]{2,1,0:T(8,128)(2,1)} %param.10) | copy-start | bytes 2359300
  26.4 1.6 %collective-permute-start.4 = (bf16[280,512]{1,0:T(8,128)(2,1)S(1)}, bf16[280,512]{1,0:T(8,128)(2,1)S(1)}, u32[]{:S(2)}, u32[]{:S(2)}) collective-permute-start(bf16[280,512]{1,0:T(8,128)(2,1)S(1)} %select_convert_fusion), channel_id=1, source_target_pairs={{0,1},{1,0},{2,3},{3,2},{4,5},{5,4},{6,7},{7,6},{8,9},{9,8},{10,11... | collective-permute-start | bytes 860168 | tf_op jit(solution)/shard_map/ppermute | solution.py:150
  28.2 6.1 %collective-permute-start.5 = (bf16[140,512]{1,0:T(8,128)(2,1)S(1)}, bf16[140,512]{1,0:T(8,128)(2,1)S(1)}, u32[]{:S(2)}, u32[]{:S(2)}) collective-permute-start(bf16[140,512]{1,0:T(8,128)(2,1)S(1)} %select_convert_fusion.1), channel_id=1, source_target_pairs={{0,2},{1,3},{2,0},{3,1},{4,6},{5,7},{6,4},{7,5},{8,10},{9,11},{10,... | collective-permute-start | bytes 430088 | tf_op jit(solution)/shard_map/ppermute | solution.py:150
  34.4 5.2 %collective-permute-start.6 = (bf16[140,512]{1,0:T(8,128)(2,1)S(1)}, bf16[140,512]{1,0:T(8,128)(2,1)S(1)}, u32[]{:S(2)}, u32[]{:S(2)}) collective-permute-start(bf16[140,512]{1,0:T(8,128)(2,1)S(1)} %add_convert_fusion.7), channel_id=1, source_target_pairs={{0,4},{1,5},{2,6},{3,7},{4,0},{5,1},{6,2},{7,3},{8,12},{9,13},{10,... | collective-permute-start | bytes 430088 | tf_op jit(solution)/shard_map/ppermute | solution.py:156
  39.6 9.1 %collective-permute-start.7 = (bf16[140,512]{1,0:T(8,128)(2,1)S(1)}, bf16[140,512]{1,0:T(8,128)(2,1)S(1)}, u32[]{:S(2)}, u32[]{:S(2)}) collective-permute-start(bf16[140,512]{1,0:T(8,128)(2,1)S(1)} %add_convert_fusion.6), channel_id=1, source_target_pairs={{0,8},{1,9},{2,10},{3,11},{4,12},{5,13},{6,14},{7,15},{8,0},{9,1},... | collective-permute-start | bytes 430088 | tf_op jit(solution)/shard_map/ppermute | solution.py:156
  48.7 5.2 %collective-permute-start.8 = (bf16[140,512]{1,0:T(8,128)(2,1)S(1)}, bf16[140,512]{1,0:T(8,128)(2,1)S(1)}, u32[]{:S(2)}, u32[]{:S(2)}) collective-permute-start(bf16[140,512]{1,0:T(8,128)(2,1)S(1)} %add_convert_fusion.5), channel_id=1, source_target_pairs={{0,2},{1,3},{2,0},{3,1},{4,6},{5,7},{6,4},{7,5},{8,10},{9,11},{10,... | collective-permute-start | bytes 430088 | tf_op jit(solution)/shard_map/ppermute | solution.py:161
  54.0 1.6 %collective-permute-start.9 = (bf16[280,512]{1,0:T(8,128)(2,1)S(1)}, bf16[280,512]{1,0:T(8,128)(2,1)S(1)}, u32[]{:S(2)}, u32[]{:S(2)}) collective-permute-start(bf16[280,512]{1,0:T(8,128)(2,1)S(1)} %maximum_select_fusion.1), channel_id=1, source_target_pairs={{0,1},{1,0},{2,3},{3,2},{4,5},{5,4},{6,7},{7,6},{8,9},{9,8},{10,11... | collective-permute-start | bytes 860168 | tf_op jit(solution)/shard_map/ppermute | solution.py:161

commit v12 on v11

--- a/solution.py
+++ b/solution.py
@@ -112,17 +112,24 @@
 def gather_rows(block, axis_name):
     count = lax.axis_size(axis_name)
     if not _is_power_of_two(count):
-        return lax.all_gather(block, axis_name, axis=0, tiled=True)
+        return lax.all_gather(block, axis_name, axis=0, tiled=True), np.arange(count * block.shape[0])
     position = lax.axis_index(axis_name)
-    distance = 1
-    while distance < count:
+    distance = count // 2
+    while distance >= 1:
         other = lax.ppermute(block, axis_name, _exchange_pairs(count, distance))
         lower = (position // distance) % 2 == 0
         block = jnp.where(
             lower, jnp.concatenate([block, other], 0), jnp.concatenate([other, block], 0)
         )
-        distance *= 2
-    return block
+        distance //= 2
+    bits = count.bit_length() - 1
+    rows = block.shape[0] // count
+    slots = np.arange(count)
+    owners = np.zeros(count, np.int64)
+    for bit in range(bits):
+        owners |= ((slots >> bit) & 1) << (bits - 1 - bit)
+    order = (owners[:, None] * rows + np.arange(rows)[None, :]).reshape(-1)
+    return block, order
 
 
 def sum_whole(values, axis_name):
@@ -182,9 +189,9 @@
     width = desired_responses.shape[2]
     forward_transform, inverse_transform = rotation_tables(width // 2)
     loss_scale = 1.0 / math.sqrt(samples * sub_dev * lax.axis_size("freq"))
-    all_inputs = gather_rows(encoder_input, "freq")
+    all_inputs, row_order = gather_rows(encoder_input, "freq")
     selection = (
-        sample_index[None, :] == jnp.arange(samples, dtype=jnp.int32)[:, None]
+        sample_index[row_order][None, :] == jnp.arange(samples, dtype=jnp.int32)[:, None]
     ).astype(jnp.bfloat16)
     inputs_by_sample = jnp.dot(selection, all_inputs, preferred_element_type=jnp.float32).astype(
         jnp.bfloat16

time: 62.2 us -> 60.2 us (0.968)
  waiting for transfers between devices: 25.3 us -> 22.7 us
  local copies, waits for them, and re-layouts: 1.97 us -> 3.32 us
  starting transfers between devices: 17.4 us -> 16.6 us
  matrix products: 11.5 us -> 10.8 us
  other arithmetic: 4.8 us -> 5.46 us
    ppermute x4, waiting for transfers between devices: 5.2 us -> 3.29 us  [gather_rows(): other = lax.ppermute(block, axis_name, _exchange_pairs(count, distance))]
    gather x0 -> x1, local copies, waits for them, and re-layouts: none -> 1.35 us  [local(): sample_index[row_order][None, :]]
    gather x0 -> x1, other arithmetic: none -> 0.66 us  [local(): sample_index[row_order][None, :]]
    dot_general x1, matrix products: 0.82 us -> 0.17 us  [local(): jnp.dot(selection, all_inputs, preferred_element_type=jnp.float32)]
    ppermute x4, starting transfers between devices: 8.68 us -> 8.05 us  [gather_rows(): other = lax.ppermute(block, axis_name, _exchange_pairs(count, distance))]
  transfers between devices with their start and end apart: 10 -> 10, of which waited for: 10 -> 10; matrix products, arithmetic and copies ran while one was open for 3% -> 6% of each run, Pallas kernels for 0% -> 0%
where the time goes in v12:
time: 60.2 us; the launch traced here: 59.8 us
  waiting for transfers between devices  22.7 us (38%)
  starting transfers between devices  16.6 us (28%)
  matrix products  10.8 us (18%)
  other arithmetic  5.46 us (9%)
  local copies, waits for them, and re-layouts  3.32 us (6%)
  between operations  0.87 us (1%)
    ppermute x2, waiting for transfers between devices, sum_halving(): arrived = lax.ppermute(values, axis_name, _exchange_pairs(count, distance))  8.73 us
    ppermute x4, starting transfers between devices, gather_rows(): other = lax.ppermute(block, axis_name, _exchange_pairs(count, distance))  8.05 us
    ppermute x2, waiting for transfers between devices, sum_halving(): arrived = lax.ppermute(send, axis_name, _exchange_pairs(count, distance))  5.59 us
    ppermute x2, waiting for transfers between devices, sum_halving(): other = lax.ppermute(values, axis_name, _exchange_pairs(count, distance))  5.12 us
    ppermute x2, starting transfers between devices, sum_halving(): arrived = lax.ppermute(values, axis_name, _exchange_pairs(count, distance))  4.7 us
    ppermute x4, waiting for transfers between devices, gather_rows(): other = lax.ppermute(block, axis_name, _exchange_pairs(count, distance))  3.29 us
    dot_general x1, matrix products, encoder_grads(): lax.dot_general(inputs_rows, grad_pre, (((0,), (0,)), ((), ())), preferre...  2.96 us
    ppermute x2, starting transfers between devices, sum_halving(): arrived = lax.ppermute(send, axis_name, _exchange_pairs(count, distance))  2.12 us
  transfers between devices with their start and end apart: 10, of which 10 were waited for; matrix products, arithmetic and copies ran while one was open for 6% of the time, Pallas kernels for 0%

profile of v12, /device:TPU:0, one launch (start us, length us, event | category | flops | bytes accessed | tf_op | source)
XLA Modules:
  0.0 59.8 jit_solution(8658060764500221133)
XLA Ops:
  0.6 4.1 %collective-permute-start = (bf16[2,2048]{1,0:T(2,128)(2,1)}, bf16[2,2048]{1,0:T(2,128)(2,1)S(1)}, u32[]{:S(2)}, u32[]{:S(2)}) collective-permute-start(bf16[2,2048]{1,0:T(2,128)(2,1)} %param.11), channel_id=1, source_target_pairs={{0,8},{1,9},{2,10},{3,11},{4,12},{5,13},{6,14},{7,15},{8,0},{9,1},... | collective-permute-start | bytes 24584 | tf_op jit(solution)/shard_map/ppermute | solution.py:119
  4.7 0.8 %bitcast_convert_fusion = (f32[512,24]{0,1:T(8,128)S(1)}, f32[24,512]{1,0:T(8,128)S(1)}) fusion(bf16[24,512]{1,0:T(8,128)(2,1)} %param.16), kind=kLoop, calls=%fused_computation.72 | loop fusion | flops 24576 | bytes 122880
  5.6 1.0 %collective-permute-done = bf16[2,2048]{1,0:T(2,128)(2,1)S(1)} collective-permute-done((bf16[2,2048]{1,0:T(2,128)(2,1)}, bf16[2,2048]{1,0:T(2,128)(2,1)S(1)}, u32[]{:S(2)}, u32[]{:S(2)}) %collective-permute-start) | collective-permute-done | bytes 8224 | tf_op jit(solution)/shard_map/ppermute | solution.py:119
  6.6 0.8 %maximum_select_fusion.6 = bf16[4,2048]{1,0:T(4,128)(2,1)S(1)} fusion(bf16[2,2048]{1,0:T(2,128)(2,1)S(1)} %collective-permute-done, bf16[2,2048]{1,0:T(2,128)(2,1)} %param.11, pred[]{:T(512)S(6)} %eq.44), kind=kLoop, calls=%fused_computation.73 | loop fusion | flops 73728 | bytes 32769 | tf_op jit(solution)/shard_map/jit(_where)/select_n | solution.py:121
  7.4 2.0 %collective-permute-start.1 = (bf16[4,2048]{1,0:T(4,128)(2,1)S(1)}, bf16[4,2048]{1,0:T(4,128)(2,1)S(1)}, u32[]{:S(2)}, u32[]{:S(2)}) collective-permute-start(bf16[4,2048]{1,0:T(4,128)(2,1)S(1)} %maximum_select_fusion.6), channel_id=1, source_target_pairs={{0,4},{1,5},{2,6},{3,7},{4,0},{5,1},{6,2},{7,3},{8,12},{9,13},{10,... | collective-permute-start | bytes 49160 | tf_op jit(solution)/shard_map/ppermute | solution.py:119
  10.1 1.1 %collective-permute-done.1 = bf16[4,2048]{1,0:T(4,128)(2,1)S(1)} collective-permute-done((bf16[4,2048]{1,0:T(4,128)(2,1)S(1)}, bf16[4,2048]{1,0:T(4,128)(2,1)S(1)}, u32[]{:S(2)}, u32[]{:S(2)}) %collective-permute-start.1) | collective-permute-done | bytes 16416 | tf_op jit(solution)/shard_map/ppermute | solution.py:119
  11.2 1.9 %collective-permute-start.2 = (bf16[8,2048]{1,0:T(8,128)(2,1)S(1)}, bf16[8,2048]{1,0:T(8,128)(2,1)S(1)}, u32[]{:S(2)}, u32[]{:S(2)}) collective-permute-start(bf16[8,2048]{1,0:T(8,128)(2,1)S(1)} %maximum_select_fusion.5), channel_id=1, source_target_pairs={{0,2},{1,3},{2,0},{3,1},{4,6},{5,7},{6,4},{7,5},{8,10},{9,11},{10,... | collective-permute-start | bytes 98312 | tf_op jit(solution)/shard_map/ppermute | solution.py:119
  13.8 1.4 %gather_fusion = s32[32]{0:T(128)S(1)} fusion(s32[32]{0:T(128)} %param.13, s32[1024]{0:T(1024)S(1)} %pad_clamp_fusion), kind=kCustom, calls=%fused_computation | custom fusion | bytes 384 | tf_op jit(solution)/shard_map/gather | solution.py:194
  15.4 1.2 %collective-permute-done.3 = bf16[16,2048]{1,0:T(8,128)(2,1)S(1)} collective-permute-done((bf16[16,2048]{1,0:T(8,128)(2,1)S(1)}, bf16[16,2048]{1,0:T(8,128)(2,1)S(1)}, u32[]{:S(2)}, u32[]{:S(2)}) %collective-permute-start.3) | collective-permute-done | bytes 65568 | tf_op jit(solution)/shard_map/ppermute | solution.py:119
  19.3 0.9 %add_convert_fusion = (bf16[768,512]{1,0:T(8,128)(2,1)S(1)}, f32[768,512]{1,0:T(8,128)S(1)}) fusion(bf16[32,24,512]{2,1,0:T(8,128)(2,1)S(1)} %multiply_convert_fusion, f32[768,512]{1,0:T(8,128)S(1)} %fusion.14, bf16[512,256]{1,0:T(8,128)(2,1)S(1)} %copy-done.5, f32[768,512]{1,0:T(8,128)S(1)} %fusion.52, f32[256]{0:T(256)S(1)} %bitcast.41, f32[256]{0:T(256)S(1)} %bitcast.37), kind=kOutput, calls=%fused_computation.15 | convolution fusion | flops 206831616 | bytes 6555648 | tf_op jit(solution)/shard_map/dot_general | solution.py:55
  22.5 1.2 %fusion.11 = f32[768,512]{1,0:T(8,128)S(1)} fusion(bf16[512,512]{1,0:T(8,128)(2,1)S(1)} %copy-done.4, f32[768,512]{1,0:T(8,128)S(1)} %get-tuple-element.11, f32[768,512]{1,0:T(8,128)S(1)} %convolution_add_fusion), kind=kOutput, calls=%fused_computation.30 | convolution fusion | flops 410517504 | bytes 5242880 | tf_op jit(solution)/shard_map/dot_general | solution.py:71
  25.4 1.4 %collective-permute-done.4 = bf16[280,512]{1,0:T(8,128)(2,1)S(1)} collective-permute-done((bf16[280,512]{1,0:T(8,128)(2,1)S(1)}, bf16[280,512]{1,0:T(8,128)(2,1)S(1)}, u32[]{:S(2)}, u32[]{:S(2)}) %collective-permute-start.4) | collective-permute-done | bytes 286752 | tf_op jit(solution)/shard_map/ppermute | solution.py:157
  27.0 1.9 %collective-permute-start.5 = (bf16[140,512]{1,0:T(8,128)(2,1)S(1)}, bf16[140,512]{1,0:T(8,128)(2,1)S(1)}, u32[]{:S(2)}, u32[]{:S(2)}) collective-permute-start(bf16[140,512]{1,0:T(8,128)(2,1)S(1)} %select_convert_fusion.1), channel_id=1, source_target_pairs={{0,2},{1,3},{2,0},{3,1},{4,6},{5,7},{6,4},{7,5},{8,10},{9,11},{10,... | collective-permute-start | bytes 430088 | tf_op jit(solution)/shard_map/ppermute | solution.py:157
  29.0 4.2 %collective-permute-done.5 = bf16[140,512]{1,0:T(8,128)(2,1)S(1)} collective-permute-done((bf16[140,512]{1,0:T(8,128)(2,1)S(1)}, bf16[140,512]{1,0:T(8,128)(2,1)S(1)}, u32[]{:S(2)}, u32[]{:S(2)}) %collective-permute-start.5) | collective-permute-done | bytes 143392 | tf_op jit(solution)/shard_map/ppermute | solution.py:157
  33.2 1.9 %collective-permute-start.6 = (bf16[140,512]{1,0:T(8,128)(2,1)S(1)}, bf16[140,512]{1,0:T(8,128)(2,1)S(1)}, u32[]{:S(2)}, u32[]{:S(2)}) collective-permute-start(bf16[140,512]{1,0:T(8,128)(2,1)S(1)} %add_convert_fusion.7), channel_id=1, source_target_pairs={{0,4},{1,5},{2,6},{3,7},{4,0},{5,1},{6,2},{7,3},{8,12},{9,13},{10,... | collective-permute-start | bytes 430088 | tf_op jit(solution)/shard_map/ppermute | solution.py:163
  35.1 3.4 %collective-permute-done.6 = bf16[140,512]{1,0:T(8,128)(2,1)S(1)} collective-permute-done((bf16[140,512]{1,0:T(8,128)(2,1)S(1)}, bf16[140,512]{1,0:T(8,128)(2,1)S(1)}, u32[]{:S(2)}, u32[]{:S(2)}) %collective-permute-start.6) | collective-permute-done | bytes 143392 | tf_op jit(solution)/shard_map/ppermute | solution.py:163
  38.5 2.8 %collective-permute-start.7 = (bf16[140,512]{1,0:T(8,128)(2,1)S(1)}, bf16[140,512]{1,0:T(8,128)(2,1)S(1)}, u32[]{:S(2)}, u32[]{:S(2)}) collective-permute-start(bf16[140,512]{1,0:T(8,128)(2,1)S(1)} %add_convert_fusion.6), channel_id=1, source_target_pairs={{0,8},{1,9},{2,10},{3,11},{4,12},{5,13},{6,14},{7,15},{8,0},{9,1},... | collective-permute-start | bytes 430088 | tf_op jit(solution)/shard_map/ppermute | solution.py:163
  41.3 5.3 %collective-permute-done.7 = bf16[140,512]{1,0:T(8,128)(2,1)S(1)} collective-permute-done((bf16[140,512]{1,0:T(8,128)(2,1)S(1)}, bf16[140,512]{1,0:T(8,128)(2,1)S(1)}, u32[]{:S(2)}, u32[]{:S(2)}) %collective-permute-start.7) | collective-permute-done | bytes 143392 | tf_op jit(solution)/shard_map/ppermute | solution.py:163
  46.7 1.6 %collective-permute-start.8 = (bf16[140,512]{1,0:T(8,128)(2,1)S(1)}, bf16[140,512]{1,0:T(8,128)(2,1)S(1)}, u32[]{:S(2)}, u32[]{:S(2)}) collective-permute-start(bf16[140,512]{1,0:T(8,128)(2,1)S(1)} %add_convert_fusion.5), channel_id=1, source_target_pairs={{0,2},{1,3},{2,0},{3,1},{4,6},{5,7},{6,4},{7,5},{8,10},{9,11},{10,... | collective-permute-start | bytes 430088 | tf_op jit(solution)/shard_map/ppermute | solution.py:168
  48.3 3.6 %collective-permute-done.8 = bf16[140,512]{1,0:T(8,128)(2,1)S(1)} collective-permute-done((bf16[140,512]{1,0:T(8,128)(2,1)S(1)}, bf16[140,512]{1,0:T(8,128)(2,1)S(1)}, u32[]{:S(2)}, u32[]{:S(2)}) %collective-permute-start.8) | collective-permute-done | bytes 143392 | tf_op jit(solution)/shard_map/ppermute | solution.py:168
  52.1 1.6 %collective-permute-done.9 = bf16[280,512]{1,0:T(8,128)(2,1)S(1)} collective-permute-done((bf16[280,512]{1,0:T(8,128)(2,1)S(1)}, bf16[280,512]{1,0:T(8,128)(2,1)S(1)}, u32[]{:S(2)}, u32[]{:S(2)}) %collective-permute-start.9) | collective-permute-done | bytes 286752 | tf_op jit(solution)/shard_map/ppermute | solution.py:168
  54.5 1.3 %fusion.37 = f32[512,512]{1,0:T(8,128)} fusion(bf16[32,512]{1,0:T(8,128)(2,1)S(1)} %fusion.8, bf16[560,512]{1,0:T(8,128)(2,1)S(1)} %maximum_select_fusion), kind=kOutput, calls=%fused_computation.69 | convolution fusion | flops 16777216 | bytes 1114112 | tf_op jit(solution)/shard_map/dot_general | solution.py:91
  55.7 1.1 %slice_convert_fusion = f32[512,512]{1,0:T(8,128)} fusion(bf16[560,512]{1,0:T(8,128)(2,1)S(1)} %maximum_select_fusion), kind=kLoop, calls=%fused_computation.37 | loop fusion | flops 262144 | bytes 1572864 | tf_op jit(solution)/shard_map/convert_element_type | solution.py:236
  56.8 3.0 %fusion.10 = f32[2048,512]{1,0:T(8,128)} fusion(bf16[32,2048]{1,0:T(8,128)(2,1)S(1)} %convolution_convert_fusion, bf16[512,512]{1,0:T(8,128)(2,1)S(1)} %copy-done.1, bf16[32,512]{1,0:T(8,128)(2,1)S(1)} %fusion.8, bf16[560,512]{1,0:T(8,128)(2,1)S(1)} %maximum_select_fusion), kind=kOutput, calls=%fused_computation.23 | convolution fusion | flops 83968000 | bytes 4915200 | tf_op jit(solution)/shard_map/dot_general | solution.py:98
  (47 shorter events, 9.6 us)
Async XLA Ops:
  0.6 16.1 %copy-start = (bf16[2048,512]{1,0:T(8,128)(2,1)S(1)}, bf16[2048,512]{1,0:T(8,128)(2,1)}, u32[]{:S(2)}) copy-start(bf16[2048,512]{1,0:T(8,128)(2,1)} %param.14) | copy-start | bytes 6291460
  0.6 5.9 %collective-permute-start = (bf16[2,2048]{1,0:T(2,128)(2,1)}, bf16[2,2048]{1,0:T(2,128)(2,1)S(1)}, u32[]{:S(2)}, u32[]{:S(2)}) collective-permute-start(bf16[2,2048]{1,0:T(2,128)(2,1)} %param.11), channel_id=1, source_target_pairs={{0,8},{1,9},{2,10},{3,11},{4,12},{5,13},{6,14},{7,15},{8,0},{9,1},... | collective-permute-start | bytes 24584 | tf_op jit(solution)/shard_map/ppermute | solution.py:119
  7.4 3.8 %collective-permute-start.1 = (bf16[4,2048]{1,0:T(4,128)(2,1)S(1)}, bf16[4,2048]{1,0:T(4,128)(2,1)S(1)}, u32[]{:S(2)}, u32[]{:S(2)}) collective-permute-start(bf16[4,2048]{1,0:T(4,128)(2,1)S(1)} %maximum_select_fusion.6), channel_id=1, source_target_pairs={{0,4},{1,5},{2,6},{3,7},{4,0},{5,1},{6,2},{7,3},{8,12},{9,13},{10,... | collective-permute-start | bytes 49160 | tf_op jit(solution)/shard_map/ppermute | solution.py:119
  11.2 4.0 %collective-permute-start.2 = (bf16[8,2048]{1,0:T(8,128)(2,1)S(1)}, bf16[8,2048]{1,0:T(8,128)(2,1)S(1)}, u32[]{:S(2)}, u32[]{:S(2)}) collective-permute-start(bf16[8,2048]{1,0:T(8,128)(2,1)S(1)} %maximum_select_fusion.5), channel_id=1, source_target_pairs={{0,2},{1,3},{2,0},{3,1},{4,6},{5,7},{6,4},{7,5},{8,10},{9,11},{10,... | collective-permute-start | bytes 98312 | tf_op jit(solution)/shard_map/ppermute | solution.py:119
  15.2 2.1 %copy-start.1 = (bf16[512,512]{1,0:T(8,128)(2,1)S(1)}, bf16[512,512]{1,0:T(8,128)(2,1)}, u32[]{:S(2)}) copy-start(bf16[512,512]{1,0:T(8,128)(2,1)} %param.15) | copy-start | bytes 1572868
  15.2 1.3 %collective-permute-start.3 = (bf16[16,2048]{1,0:T(8,128)(2,1)S(1)}, bf16[16,2048]{1,0:T(8,128)(2,1)S(1)}, u32[]{:S(2)}, u32[]{:S(2)}) collective-permute-start(bf16[16,2048]{1,0:T(8,128)(2,1)S(1)} %maximum_select_fusion.4), channel_id=1, source_target_pairs={{0,1},{1,0},{2,3},{3,2},{4,5},{5,4},{6,7},{7,6},{8,9},{9,8},{10,11... | collective-permute-start | bytes 196616 | tf_op jit(solution)/shard_map/ppermute | solution.py:119
  16.7 1.0 %copy-start.4 = (bf16[512,512]{1,0:T(8,128)(2,1)S(1)}, bf16[512,512]{1,0:T(8,128)(2,1)}, u32[]{:S(2)}) copy-start(bf16[512,512]{1,0:T(8,128)(2,1)} %constant.113.clone) | copy-start | bytes 1572868
  17.6 1.0 %copy-start.2 = (bf16[512,256]{1,0:T(8,128)(2,1)S(1)}, bf16[512,256]{1,0:T(8,128)(2,1)}, u32[]{:S(2)}) copy-start(bf16[512,256]{1,0:T(8,128)(2,1)} %constant.122) | copy-start | bytes 786436
  18.4 1.0 %copy-start.5 = (bf16[512,256]{1,0:T(8,128)(2,1)S(1)}, bf16[512,256]{1,0:T(8,128)(2,1)}, u32[]{:S(2)}) copy-start(bf16[512,256]{1,0:T(8,128)(2,1)} %constant.123) | copy-start | bytes 786436
  19.3 1.0 %copy-start.3 = (bf16[512,512]{1,0:T(8,128)(2,1)S(1)}, bf16[512,512]{1,0:T(8,128)(2,1)}, u32[]{:S(2)}) copy-start(bf16[512,512]{1,0:T(8,128)(2,1)} %param.18) | copy-start | bytes 1572868
  19.3 1.3 %copy-start.6 = (bf16[32,24,512]{2,1,0:T(8,128)(2,1)S(1)}, bf16[32,24,512]{2,1,0:T(8,128)(2,1)}, u32[]{:S(2)}) copy-start(bf16[32,24,512]{2,1,0:T(8,128)(2,1)} %param.12) | copy-start | bytes 2359300
  25.2 1.6 %collective-permute-start.4 = (bf16[280,512]{1,0:T(8,128)(2,1)S(1)}, bf16[280,512]{1,0:T(8,128)(2,1)S(1)}, u32[]{:S(2)}, u32[]{:S(2)}) collective-permute-start(bf16[280,512]{1,0:T(8,128)(2,1)S(1)} %select_convert_fusion), channel_id=1, source_target_pairs={{0,1},{1,0},{2,3},{3,2},{4,5},{5,4},{6,7},{7,6},{8,9},{9,8},{10,11... | collective-permute-start | bytes 860168 | tf_op jit(solution)/shard_map/ppermute | solution.py:157
  27.0 6.1 %collective-permute-start.5 = (bf16[140,512]{1,0:T(8,128)(2,1)S(1)}, bf16[140,512]{1,0:T(8,128)(2,1)S(1)}, u32[]{:S(2)}, u32[]{:S(2)}) collective-permute-start(bf16[140,512]{1,0:T(8,128)(2,1)S(1)} %select_convert_fusion.1), channel_id=1, source_target_pairs={{0,2},{1,3},{2,0},{3,1},{4,6},{5,7},{6,4},{7,5},{8,10},{9,11},{10,... | collective-permute-start | bytes 430088 | tf_op jit(solution)/shard_map/ppermute | solution.py:157
  33.2 5.3 %collective-permute-start.6 = (bf16[140,512]{1,0:T(8,128)(2,1)S(1)}, bf16[140,512]{1,0:T(8,128)(2,1)S(1)}, u32[]{:S(2)}, u32[]{:S(2)}) collective-permute-start(bf16[140,512]{1,0:T(8,128)(2,1)S(1)} %add_convert_fusion.7), channel_id=1, source_target_pairs={{0,4},{1,5},{2,6},{3,7},{4,0},{5,1},{6,2},{7,3},{8,12},{9,13},{10,... | collective-permute-start | bytes 430088 | tf_op jit(solution)/shard_map/ppermute | solution.py:163
  38.5 8.2 %collective-permute-start.7 = (bf16[140,512]{1,0:T(8,128)(2,1)S(1)}, bf16[140,512]{1,0:T(8,128)(2,1)S(1)}, u32[]{:S(2)}, u32[]{:S(2)}) collective-permute-start(bf16[140,512]{1,0:T(8,128)(2,1)S(1)} %add_convert_fusion.6), channel_id=1, source_target_pairs={{0,8},{1,9},{2,10},{3,11},{4,12},{5,13},{6,14},{7,15},{8,0},{9,1},... | collective-permute-start | bytes 430088 | tf_op jit(solution)/shard_map/ppermute | solution.py:163
  46.7 5.2 %collective-permute-start.8 = (bf16[140,512]{1,0:T(8,128)(2,1)S(1)}, bf16[140,512]{1,0:T(8,128)(2,1)S(1)}, u32[]{:S(2)}, u32[]{:S(2)}) collective-permute-start(bf16[140,512]{1,0:T(8,128)(2,1)S(1)} %add_convert_fusion.5), channel_id=1, source_target_pairs={{0,2},{1,3},{2,0},{3,1},{4,6},{5,7},{6,4},{7,5},{8,10},{9,11},{10,... | collective-permute-start | bytes 430088 | tf_op jit(solution)/shard_map/ppermute | solution.py:168
  52.0 1.6 %collective-permute-start.9 = (bf16[280,512]{1,0:T(8,128)(2,1)S(1)}, bf16[280,512]{1,0:T(8,128)(2,1)S(1)}, u32[]{:S(2)}, u32[]{:S(2)}) collective-permute-start(bf16[280,512]{1,0:T(8,128)(2,1)S(1)} %maximum_select_fusion.1), channel_id=1, source_target_pairs={{0,1},{1,0},{2,3},{3,2},{4,5},{5,4},{6,7},{7,6},{8,9},{9,8},{10,11... | collective-permute-start | bytes 860168 | tf_op jit(solution)/shard_map/ppermute | solution.py:168

commit v13 on v11

--- a/solution.py
+++ b/solution.py
@@ -114,15 +114,23 @@
     if not _is_power_of_two(count):
         return lax.all_gather(block, axis_name, axis=0, tiled=True)
     position = lax.axis_index(axis_name)
-    distance = 1
-    while distance < count:
+    distance = count // 2
+    while distance >= 1:
         other = lax.ppermute(block, axis_name, _exchange_pairs(count, distance))
         lower = (position // distance) % 2 == 0
         block = jnp.where(
             lower, jnp.concatenate([block, other], 0), jnp.concatenate([other, block], 0)
         )
-        distance *= 2
+        distance //= 2
     return block
+
+
+def bit_reversed_blocks(values, count):
+    if not _is_power_of_two(count):
+        return values
+    bits = count.bit_length() - 1
+    blocks = values.reshape((2,) * bits + (-1,))
+    return blocks.transpose(tuple(reversed(range(bits))) + (bits,)).reshape(-1)
 
 
 def sum_whole(values, axis_name):
@@ -183,8 +191,9 @@
     forward_transform, inverse_transform = rotation_tables(width // 2)
     loss_scale = 1.0 / math.sqrt(samples * sub_dev * lax.axis_size("freq"))
     all_inputs = gather_rows(encoder_input, "freq")
+    gathered_index = bit_reversed_blocks(sample_index, lax.axis_size("freq"))
     selection = (
-        sample_index[None, :] == jnp.arange(samples, dtype=jnp.int32)[:, None]
+        gathered_index[None, :] == jnp.arange(samples, dtype=jnp.int32)[:, None]
     ).astype(jnp.bfloat16)
     inputs_by_sample = jnp.dot(selection, all_inputs, preferred_element_type=jnp.float32).astype(
         jnp.bfloat16

time: 62.2 us -> 60.1 us (0.966)
  waiting for transfers between devices: 25.3 us -> 23.9 us
  local copies, waits for them, and re-layouts: 1.97 us -> 2.8 us
  starting transfers between devices: 17.4 us -> 16.6 us
  matrix products: 11.5 us -> 10.8 us
    ppermute x4, waiting for transfers between devices: 5.2 us -> 4.42 us  [gather_rows(): other = lax.ppermute(block, axis_name, _exchange_pairs(count, distance))]
    reshape x0 -> x1, local copies, waits for them, and re-layouts: none -> 0.74 us  [bit_reversed_blocks(): blocks = values.reshape((2,) * bits + (-1,))]
    dot_general x1, matrix products: 0.82 us -> 0.17 us  [local(): jnp.dot(selection, all_inputs, preferred_element_type=jnp.float32)]
  transfers between devices with their start and end apart: 10 -> 10, of which waited for: 10 -> 10; matrix products, arithmetic and copies ran while one was open for 3% -> 4% of each run, Pallas kernels for 0% -> 0%
where the time goes in v13:
time: 60.1 us; the launch traced here: 59.8 us
  waiting for transfers between devices  23.9 us (40%)
  starting transfers between devices  16.6 us (28%)
  matrix products  10.8 us (18%)
  other arithmetic  4.81 us (8%)
  local copies, waits for them, and re-layouts  2.8 us (5%)
  between operations  0.9 us (1%)
    ppermute x2, waiting for transfers between devices, sum_halving(): arrived = lax.ppermute(values, axis_name, _exchange_pairs(count, distance))  8.73 us
    ppermute x4, starting transfers between devices, gather_rows(): other = lax.ppermute(block, axis_name, _exchange_pairs(count, distance))  8.06 us
    ppermute x2, waiting for transfers between devices, sum_halving(): arrived = lax.ppermute(send, axis_name, _exchange_pairs(count, distance))  5.59 us
    ppermute x2, waiting for transfers between devices, sum_halving(): other = lax.ppermute(values, axis_name, _exchange_pairs(count, distance))  5.12 us
    ppermute x2, starting transfers between devices, sum_halving(): arrived = lax.ppermute(values, axis_name, _exchange_pairs(count, distance))  4.7 us
    ppermute x4, waiting for transfers between devices, gather_rows(): other = lax.ppermute(block, axis_name, _exchange_pairs(count, distance))  4.42 us
    dot_general x1, matrix products, encoder_grads(): lax.dot_general(inputs_rows, grad_pre, (((0,), (0,)), ((), ())), preferre...  2.96 us
    ppermute x2, starting transfers between devices, sum_halving(): arrived = lax.ppermute(send, axis_name, _exchange_pairs(count, distance))  2.12 us
  transfers between devices with their start and end apart: 10, of which 10 were waited for; matrix products, arithmetic and copies ran while one was open for 4% of the time, Pallas kernels for 0%

profile of v13, /device:TPU:0, one launch (start us, length us, event | category | flops | bytes accessed | tf_op | source)
XLA Modules:
  0.0 59.8 jit_solution(16501066250038440012)
XLA Ops:
  0.6 4.1 %collective-permute-start = (bf16[2,2048]{1,0:T(2,128)(2,1)}, bf16[2,2048]{1,0:T(2,128)(2,1)S(1)}, u32[]{:S(2)}, u32[]{:S(2)}) collective-permute-start(bf16[2,2048]{1,0:T(2,128)(2,1)} %param.9), channel_id=1, source_target_pairs={{0,8},{1,9},{2,10},{3,11},{4,12},{5,13},{6,14},{7,15},{8,0},{9,1},... | collective-permute-start | bytes 24584 | tf_op jit(solution)/shard_map/ppermute | solution.py:119
  4.7 1.8 %collective-permute-done = bf16[2,2048]{1,0:T(2,128)(2,1)S(1)} collective-permute-done((bf16[2,2048]{1,0:T(2,128)(2,1)}, bf16[2,2048]{1,0:T(2,128)(2,1)S(1)}, u32[]{:S(2)}, u32[]{:S(2)}) %collective-permute-start) | collective-permute-done | bytes 8224 | tf_op jit(solution)/shard_map/ppermute | solution.py:119
  6.6 0.8 %maximum_select_fusion.6 = bf16[4,2048]{1,0:T(4,128)(2,1)S(1)} fusion(bf16[2,2048]{1,0:T(2,128)(2,1)S(1)} %collective-permute-done, bf16[2,2048]{1,0:T(2,128)(2,1)} %param.9, pred[]{:T(512)S(6)} %eq.47), kind=kLoop, calls=%fused_computation.72 | loop fusion | flops 73728 | bytes 32769 | tf_op jit(solution)/shard_map/jit(_where)/select_n | solution.py:121
  7.4 2.0 %collective-permute-start.1 = (bf16[4,2048]{1,0:T(4,128)(2,1)S(1)}, bf16[4,2048]{1,0:T(4,128)(2,1)S(1)}, u32[]{:S(2)}, u32[]{:S(2)}) collective-permute-start(bf16[4,2048]{1,0:T(4,128)(2,1)S(1)} %maximum_select_fusion.6), channel_id=1, source_target_pairs={{0,4},{1,5},{2,6},{3,7},{4,0},{5,1},{6,2},{7,3},{8,12},{9,13},{10,... | collective-permute-start | bytes 49160 | tf_op jit(solution)/shard_map/ppermute | solution.py:119
  9.4 0.8 %bitcast_convert_fusion = (f32[512,24]{0,1:T(8,128)S(1)}, f32[24,512]{1,0:T(8,128)S(1)}) fusion(bf16[24,512]{1,0:T(8,128)(2,1)} %param.14), kind=kLoop, calls=%fused_computation.71 | loop fusion | flops 24576 | bytes 122880
  10.2 1.0 %collective-permute-done.1 = bf16[4,2048]{1,0:T(4,128)(2,1)S(1)} collective-permute-done((bf16[4,2048]{1,0:T(4,128)(2,1)S(1)}, bf16[4,2048]{1,0:T(4,128)(2,1)S(1)}, u32[]{:S(2)}, u32[]{:S(2)}) %collective-permute-start.1) | collective-permute-done | bytes 16416 | tf_op jit(solution)/shard_map/ppermute | solution.py:119
  11.2 1.9 %collective-permute-start.2 = (bf16[8,2048]{1,0:T(8,128)(2,1)S(1)}, bf16[8,2048]{1,0:T(8,128)(2,1)S(1)}, u32[]{:S(2)}, u32[]{:S(2)}) collective-permute-start(bf16[8,2048]{1,0:T(8,128)(2,1)S(1)} %maximum_select_fusion.5), channel_id=1, source_target_pairs={{0,2},{1,3},{2,0},{3,1},{4,6},{5,7},{6,4},{7,5},{8,10},{9,11},{10,... | collective-permute-start | bytes 98312 | tf_op jit(solution)/shard_map/ppermute | solution.py:119
  13.2 0.8 %fusion.50 = (f32[1,256]{1,0:T(1,128)S(1)}, f32[1,256]{1,0:T(1,128)S(1)}) fusion(f32[2,256]{1,0:T(2,128)} %param.15), kind=kLoop, calls=%fused_computation.86 | loop fusion | bytes 4096 | tf_op jit(solution)/shard_map/slice | solution.py:46
  15.4 1.2 %collective-permute-done.3 = bf16[16,2048]{1,0:T(8,128)(2,1)S(1)} collective-permute-done((bf16[16,2048]{1,0:T(8,128)(2,1)S(1)}, bf16[16,2048]{1,0:T(8,128)(2,1)S(1)}, u32[]{:S(2)}, u32[]{:S(2)}) %collective-permute-start.3) | collective-permute-done | bytes 65568 | tf_op jit(solution)/shard_map/ppermute | solution.py:119
  19.3 0.9 %add_convert_fusion = (bf16[768,512]{1,0:T(8,128)(2,1)S(1)}, f32[768,512]{1,0:T(8,128)S(1)}) fusion(bf16[32,24,512]{2,1,0:T(8,128)(2,1)S(1)} %multiply_convert_fusion, f32[768,512]{1,0:T(8,128)S(1)} %fusion.14, bf16[512,256]{1,0:T(8,128)(2,1)S(1)} %copy-done.5, f32[768,512]{1,0:T(8,128)S(1)} %fusion.52, f32[256]{0:T(256)S(1)} %bitcast.43, f32[256]{0:T(256)S(1)} %bitcast.39), kind=kOutput, calls=%fused_computation.14 | convolution fusion | flops 206831616 | bytes 6555648 | tf_op jit(solution)/shard_map/dot_general | solution.py:55
  22.5 1.2 %fusion.11 = f32[768,512]{1,0:T(8,128)S(1)} fusion(bf16[512,512]{1,0:T(8,128)(2,1)S(1)} %copy-done.4, f32[768,512]{1,0:T(8,128)S(1)} %get-tuple-element.11, f32[768,512]{1,0:T(8,128)S(1)} %convolution_add_fusion), kind=kOutput, calls=%fused_computation.29 | convolution fusion | flops 410517504 | bytes 5242880 | tf_op jit(solution)/shard_map/dot_general | solution.py:71
  25.4 1.4 %collective-permute-done.4 = bf16[280,512]{1,0:T(8,128)(2,1)S(1)} collective-permute-done((bf16[280,512]{1,0:T(8,128)(2,1)S(1)}, bf16[280,512]{1,0:T(8,128)(2,1)S(1)}, u32[]{:S(2)}, u32[]{:S(2)}) %collective-permute-start.4) | collective-permute-done | bytes 286752 | tf_op jit(solution)/shard_map/ppermute | solution.py:158
  27.0 1.9 %collective-permute-start.5 = (bf16[140,512]{1,0:T(8,128)(2,1)S(1)}, bf16[140,512]{1,0:T(8,128)(2,1)S(1)}, u32[]{:S(2)}, u32[]{:S(2)}) collective-permute-start(bf16[140,512]{1,0:T(8,128)(2,1)S(1)} %select_convert_fusion.1), channel_id=1, source_target_pairs={{0,2},{1,3},{2,0},{3,1},{4,6},{5,7},{6,4},{7,5},{8,10},{9,11},{10,... | collective-permute-start | bytes 430088 | tf_op jit(solution)/shard_map/ppermute | solution.py:158
  29.0 4.2 %collective-permute-done.5 = bf16[140,512]{1,0:T(8,128)(2,1)S(1)} collective-permute-done((bf16[140,512]{1,0:T(8,128)(2,1)S(1)}, bf16[140,512]{1,0:T(8,128)(2,1)S(1)}, u32[]{:S(2)}, u32[]{:S(2)}) %collective-permute-start.5) | collective-permute-done | bytes 143392 | tf_op jit(solution)/shard_map/ppermute | solution.py:158
  33.2 1.9 %collective-permute-start.6 = (bf16[140,512]{1,0:T(8,128)(2,1)S(1)}, bf16[140,512]{1,0:T(8,128)(2,1)S(1)}, u32[]{:S(2)}, u32[]{:S(2)}) collective-permute-start(bf16[140,512]{1,0:T(8,128)(2,1)S(1)} %add_convert_fusion.7), channel_id=1, source_target_pairs={{0,4},{1,5},{2,6},{3,7},{4,0},{5,1},{6,2},{7,3},{8,12},{9,13},{10,... | collective-permute-start | bytes 430088 | tf_op jit(solution)/shard_map/ppermute | solution.py:164
  35.1 3.4 %collective-permute-done.6 = bf16[140,512]{1,0:T(8,128)(2,1)S(1)} collective-permute-done((bf16[140,512]{1,0:T(8,128)(2,1)S(1)}, bf16[140,512]{1,0:T(8,128)(2,1)S(1)}, u32[]{:S(2)}, u32[]{:S(2)}) %collective-permute-start.6) | collective-permute-done | bytes 143392 | tf_op jit(solution)/shard_map/ppermute | solution.py:164
  38.5 2.8 %collective-permute-start.7 = (bf16[140,512]{1,0:T(8,128)(2,1)S(1)}, bf16[140,512]{1,0:T(8,128)(2,1)S(1)}, u32[]{:S(2)}, u32[]{:S(2)}) collective-permute-start(bf16[140,512]{1,0:T(8,128)(2,1)S(1)} %add_convert_fusion.6), channel_id=1, source_target_pairs={{0,8},{1,9},{2,10},{3,11},{4,12},{5,13},{6,14},{7,15},{8,0},{9,1},... | collective-permute-start | bytes 430088 | tf_op jit(solution)/shard_map/ppermute | solution.py:164
  41.3 5.3 %collective-permute-done.7 = bf16[140,512]{1,0:T(8,128)(2,1)S(1)} collective-permute-done((bf16[140,512]{1,0:T(8,128)(2,1)S(1)}, bf16[140,512]{1,0:T(8,128)(2,1)S(1)}, u32[]{:S(2)}, u32[]{:S(2)}) %collective-permute-start.7) | collective-permute-done | bytes 143392 | tf_op jit(solution)/shard_map/ppermute | solution.py:164
  46.7 1.6 %collective-permute-start.8 = (bf16[140,512]{1,0:T(8,128)(2,1)S(1)}, bf16[140,512]{1,0:T(8,128)(2,1)S(1)}, u32[]{:S(2)}, u32[]{:S(2)}) collective-permute-start(bf16[140,512]{1,0:T(8,128)(2,1)S(1)} %add_convert_fusion.5), channel_id=1, source_target_pairs={{0,2},{1,3},{2,0},{3,1},{4,6},{5,7},{6,4},{7,5},{8,10},{9,11},{10,... | collective-permute-start | bytes 430088 | tf_op jit(solution)/shard_map/ppermute | solution.py:169
  48.3 3.6 %collective-permute-done.8 = bf16[140,512]{1,0:T(8,128)(2,1)S(1)} collective-permute-done((bf16[140,512]{1,0:T(8,128)(2,1)S(1)}, bf16[140,512]{1,0:T(8,128)(2,1)S(1)}, u32[]{:S(2)}, u32[]{:S(2)}) %collective-permute-start.8) | collective-permute-done | bytes 143392 | tf_op jit(solution)/shard_map/ppermute | solution.py:169
  52.1 1.6 %collective-permute-done.9 = bf16[280,512]{1,0:T(8,128)(2,1)S(1)} collective-permute-done((bf16[280,512]{1,0:T(8,128)(2,1)S(1)}, bf16[280,512]{1,0:T(8,128)(2,1)S(1)}, u32[]{:S(2)}, u32[]{:S(2)}) %collective-permute-start.9) | collective-permute-done | bytes 286752 | tf_op jit(solution)/shard_map/ppermute | solution.py:169
  54.5 1.3 %fusion.37 = f32[512,512]{1,0:T(8,128)} fusion(bf16[32,512]{1,0:T(8,128)(2,1)S(1)} %fusion.8, bf16[560,512]{1,0:T(8,128)(2,1)S(1)} %maximum_select_fusion), kind=kOutput, calls=%fused_computation.68 | convolution fusion | flops 16777216 | bytes 1114112 | tf_op jit(solution)/shard_map/dot_general | solution.py:91
  55.7 1.1 %slice_convert_fusion = f32[512,512]{1,0:T(8,128)} fusion(bf16[560,512]{1,0:T(8,128)(2,1)S(1)} %maximum_select_fusion), kind=kLoop, calls=%fused_computation.36 | loop fusion | flops 262144 | bytes 1572864 | tf_op jit(solution)/shard_map/convert_element_type | solution.py:238
  56.8 3.0 %fusion.10 = f32[2048,512]{1,0:T(8,128)} fusion(bf16[32,2048]{1,0:T(8,128)(2,1)S(1)} %convolution_convert_fusion, bf16[512,512]{1,0:T(8,128)(2,1)S(1)} %copy-done.1, bf16[32,512]{1,0:T(8,128)(2,1)S(1)} %fusion.8, bf16[560,512]{1,0:T(8,128)(2,1)S(1)} %maximum_select_fusion), kind=kOutput, calls=%fused_computation.22 | convolution fusion | flops 83968000 | bytes 4915200 | tf_op jit(solution)/shard_map/dot_general | solution.py:98
  (48 shorter events, 9.4 us)
Async XLA Ops:
  0.6 16.1 %copy-start = (bf16[2048,512]{1,0:T(8,128)(2,1)S(1)}, bf16[2048,512]{1,0:T(8,128)(2,1)}, u32[]{:S(2)}) copy-start(bf16[2048,512]{1,0:T(8,128)(2,1)} %param.12) | copy-start | bytes 6291460
  0.6 5.9 %collective-permute-start = (bf16[2,2048]{1,0:T(2,128)(2,1)}, bf16[2,2048]{1,0:T(2,128)(2,1)S(1)}, u32[]{:S(2)}, u32[]{:S(2)}) collective-permute-start(bf16[2,2048]{1,0:T(2,128)(2,1)} %param.9), channel_id=1, source_target_pairs={{0,8},{1,9},{2,10},{3,11},{4,12},{5,13},{6,14},{7,15},{8,0},{9,1},... | collective-permute-start | bytes 24584 | tf_op jit(solution)/shard_map/ppermute | solution.py:119
  7.4 3.8 %collective-permute-start.1 = (bf16[4,2048]{1,0:T(4,128)(2,1)S(1)}, bf16[4,2048]{1,0:T(4,128)(2,1)S(1)}, u32[]{:S(2)}, u32[]{:S(2)}) collective-permute-start(bf16[4,2048]{1,0:T(4,128)(2,1)S(1)} %maximum_select_fusion.6), channel_id=1, source_target_pairs={{0,4},{1,5},{2,6},{3,7},{4,0},{5,1},{6,2},{7,3},{8,12},{9,13},{10,... | collective-permute-start | bytes 49160 | tf_op jit(solution)/shard_map/ppermute | solution.py:119
  10.2 7.0 %copy-start.1 = (bf16[512,512]{1,0:T(8,128)(2,1)S(1)}, bf16[512,512]{1,0:T(8,128)(2,1)}, u32[]{:S(2)}) copy-start(bf16[512,512]{1,0:T(8,128)(2,1)} %param.13) | copy-start | bytes 1572868
  11.2 4.0 %collective-permute-start.2 = (bf16[8,2048]{1,0:T(8,128)(2,1)S(1)}, bf16[8,2048]{1,0:T(8,128)(2,1)S(1)}, u32[]{:S(2)}, u32[]{:S(2)}) collective-permute-start(bf16[8,2048]{1,0:T(8,128)(2,1)S(1)} %maximum_select_fusion.5), channel_id=1, source_target_pairs={{0,2},{1,3},{2,0},{3,1},{4,6},{5,7},{6,4},{7,5},{8,10},{9,11},{10,... | collective-permute-start | bytes 98312 | tf_op jit(solution)/shard_map/ppermute | solution.py:119
  15.2 1.3 %collective-permute-start.3 = (bf16[16,2048]{1,0:T(8,128)(2,1)S(1)}, bf16[16,2048]{1,0:T(8,128)(2,1)S(1)}, u32[]{:S(2)}, u32[]{:S(2)}) collective-permute-start(bf16[16,2048]{1,0:T(8,128)(2,1)S(1)} %maximum_select_fusion.4), channel_id=1, source_target_pairs={{0,1},{1,0},{2,3},{3,2},{4,5},{5,4},{6,7},{7,6},{8,9},{9,8},{10,11... | collective-permute-start | bytes 196616 | tf_op jit(solution)/shard_map/ppermute | solution.py:119
  16.7 1.0 %copy-start.4 = (bf16[512,512]{1,0:T(8,128)(2,1)S(1)}, bf16[512,512]{1,0:T(8,128)(2,1)}, u32[]{:S(2)}) copy-start(bf16[512,512]{1,0:T(8,128)(2,1)} %constant.107.clone) | copy-start | bytes 1572868
  17.6 1.0 %copy-start.2 = (bf16[512,256]{1,0:T(8,128)(2,1)S(1)}, bf16[512,256]{1,0:T(8,128)(2,1)}, u32[]{:S(2)}) copy-start(bf16[512,256]{1,0:T(8,128)(2,1)} %constant.113) | copy-start | bytes 786436
  18.4 1.0 %copy-start.5 = (bf16[512,256]{1,0:T(8,128)(2,1)S(1)}, bf16[512,256]{1,0:T(8,128)(2,1)}, u32[]{:S(2)}) copy-start(bf16[512,256]{1,0:T(8,128)(2,1)} %constant.114) | copy-start | bytes 786436
  19.3 1.0 %copy-start.3 = (bf16[512,512]{1,0:T(8,128)(2,1)S(1)}, bf16[512,512]{1,0:T(8,128)(2,1)}, u32[]{:S(2)}) copy-start(bf16[512,512]{1,0:T(8,128)(2,1)} %param.16) | copy-start | bytes 1572868
  19.3 1.3 %copy-start.6 = (bf16[32,24,512]{2,1,0:T(8,128)(2,1)S(1)}, bf16[32,24,512]{2,1,0:T(8,128)(2,1)}, u32[]{:S(2)}) copy-start(bf16[32,24,512]{2,1,0:T(8,128)(2,1)} %param.10) | copy-start | bytes 2359300
  25.2 1.6 %collective-permute-start.4 = (bf16[280,512]{1,0:T(8,128)(2,1)S(1)}, bf16[280,512]{1,0:T(8,128)(2,1)S(1)}, u32[]{:S(2)}, u32[]{:S(2)}) collective-permute-start(bf16[280,512]{1,0:T(8,128)(2,1)S(1)} %select_convert_fusion), channel_id=1, source_target_pairs={{0,1},{1,0},{2,3},{3,2},{4,5},{5,4},{6,7},{7,6},{8,9},{9,8},{10,11... | collective-permute-start | bytes 860168 | tf_op jit(solution)/shard_map/ppermute | solution.py:158
  27.0 6.1 %collective-permute-start.5 = (bf16[140,512]{1,0:T(8,128)(2,1)S(1)}, bf16[140,512]{1,0:T(8,128)(2,1)S(1)}, u32[]{:S(2)}, u32[]{:S(2)}) collective-permute-start(bf16[140,512]{1,0:T(8,128)(2,1)S(1)} %select_convert_fusion.1), channel_id=1, source_target_pairs={{0,2},{1,3},{2,0},{3,1},{4,6},{5,7},{6,4},{7,5},{8,10},{9,11},{10,... | collective-permute-start | bytes 430088 | tf_op jit(solution)/shard_map/ppermute | solution.py:158
  33.2 5.3 %collective-permute-start.6 = (bf16[140,512]{1,0:T(8,128)(2,1)S(1)}, bf16[140,512]{1,0:T(8,128)(2,1)S(1)}, u32[]{:S(2)}, u32[]{:S(2)}) collective-permute-start(bf16[140,512]{1,0:T(8,128)(2,1)S(1)} %add_convert_fusion.7), channel_id=1, source_target_pairs={{0,4},{1,5},{2,6},{3,7},{4,0},{5,1},{6,2},{7,3},{8,12},{9,13},{10,... | collective-permute-start | bytes 430088 | tf_op jit(solution)/shard_map/ppermute | solution.py:164
  38.5 8.2 %collective-permute-start.7 = (bf16[140,512]{1,0:T(8,128)(2,1)S(1)}, bf16[140,512]{1,0:T(8,128)(2,1)S(1)}, u32[]{:S(2)}, u32[]{:S(2)}) collective-permute-start(bf16[140,512]{1,0:T(8,128)(2,1)S(1)} %add_convert_fusion.6), channel_id=1, source_target_pairs={{0,8},{1,9},{2,10},{3,11},{4,12},{5,13},{6,14},{7,15},{8,0},{9,1},... | collective-permute-start | bytes 430088 | tf_op jit(solution)/shard_map/ppermute | solution.py:164
  46.7 5.2 %collective-permute-start.8 = (bf16[140,512]{1,0:T(8,128)(2,1)S(1)}, bf16[140,512]{1,0:T(8,128)(2,1)S(1)}, u32[]{:S(2)}, u32[]{:S(2)}) collective-permute-start(bf16[140,512]{1,0:T(8,128)(2,1)S(1)} %add_convert_fusion.5), channel_id=1, source_target_pairs={{0,2},{1,3},{2,0},{3,1},{4,6},{5,7},{6,4},{7,5},{8,10},{9,11},{10,... | collective-permute-start | bytes 430088 | tf_op jit(solution)/shard_map/ppermute | solution.py:169
  52.0 1.6 %collective-permute-start.9 = (bf16[280,512]{1,0:T(8,128)(2,1)S(1)}, bf16[280,512]{1,0:T(8,128)(2,1)S(1)}, u32[]{:S(2)}, u32[]{:S(2)}) collective-permute-start(bf16[280,512]{1,0:T(8,128)(2,1)S(1)} %maximum_select_fusion.1), channel_id=1, source_target_pairs={{0,1},{1,0},{2,3},{3,2},{4,5},{5,4},{6,7},{7,6},{8,9},{9,8},{10,11... | collective-permute-start | bytes 860168 | tf_op jit(solution)/shard_map/ppermute | solution.py:169

commit v14 on v13

--- a/solution.py
+++ b/solution.py
@@ -144,10 +144,11 @@
     return values
 
 
-def sum_halving(values, axis_name, wire=jnp.bfloat16, halving_levels=2):
+def sum_halving(values, axis_name, split, wire=jnp.bfloat16, halving_levels=2):
     count = lax.axis_size(axis_name)
     if not _is_power_of_two(count) or values.shape[0] % count != 0:
-        return lax.psum(values, axis_name)
+        values = lax.psum(values, axis_name)
+        return values[:split], values[split:]
     position = lax.axis_index(axis_name)
     distance = 1
     while distance < count and distance < 2**halving_levels:
@@ -168,11 +169,19 @@
     while distance >= 1:
         other = lax.ppermute(values, axis_name, _exchange_pairs(count, distance))
         lower = (position // distance) % 2 == 0
+        if distance == 1 and values.shape[0] <= split < 2 * values.shape[0]:
+            cut = split - values.shape[0]
+            head = jnp.where(
+                lower,
+                jnp.concatenate([values, other[:cut]], 0),
+                jnp.concatenate([other, values[:cut]], 0),
+            )
+            return head, jnp.where(lower, other[cut:], values[cut:])
         values = jnp.where(
             lower, jnp.concatenate([values, other], 0), jnp.concatenate([other, values], 0)
         )
         distance //= 2
-    return values
+    return values[:split], values[split:]
 
 
 def local(
@@ -233,13 +242,11 @@
         ],
         0,
     )
-    packed = sum_halving(packed, "freq")
     rows_out = grad_out.shape[0]
-    grad_out = packed[:rows_out].astype(jnp.float32)
-    derivative_bottleneck = packed[rows_out : rows_out + samples].astype(jnp.float32)
-    grad_filter = packed[
-        rows_out + samples : rows_out + samples + filter_rows.shape[0], :half_width
-    ].astype(jnp.float32)
+    head, rest = sum_halving(packed, "freq", rows_out)
+    grad_out = head.astype(jnp.float32)
+    derivative_bottleneck = rest[:samples].astype(jnp.float32)
+    grad_filter = rest[samples : samples + filter_rows.shape[0], :half_width].astype(jnp.float32)
     grad_enc, grad_dec = encoder_grads(
         inputs_by_sample, codes_by_sample, derivative_bottleneck, decoder_weight
     )

time: 60.1 us -> 61 us (1.015)
  matrix products: 10.8 us -> 11.7 us
    dot_general x1, matrix products: 2.96 us -> 3.86 us  [encoder_grads(): lax.dot_general(inputs_rows, grad_pre, (((0,), (0,)), ((), ())), preferre...]
where the time goes in v14:
time: 61 us; the launch traced here: 60.6 us
  waiting for transfers between devices  23.8 us (39%)
  starting transfers between devices  16.6 us (27%)
  matrix products  11.7 us (19%)
  other arithmetic  4.61 us (8%)
  local copies, waits for them, and re-layouts  2.89 us (5%)
  between operations  0.92 us (2%)
    ppermute x2, waiting for transfers between devices, sum_halving(): arrived = lax.ppermute(values, axis_name, _exchange_pairs(count, distance))  8.74 us
    ppermute x4, starting transfers between devices, gather_rows(): other = lax.ppermute(block, axis_name, _exchange_pairs(count, distance))  8.06 us
    ppermute x2, waiting for transfers between devices, sum_halving(): arrived = lax.ppermute(send, axis_name, _exchange_pairs(count, distance))  5.59 us
    ppermute x2, waiting for transfers between devices, sum_halving(): other = lax.ppermute(values, axis_name, _exchange_pairs(count, distance))  5.1 us
    ppermute x2, starting transfers between devices, sum_halving(): arrived = lax.ppermute(values, axis_name, _exchange_pairs(count, distance))  4.68 us
    ppermute x4, waiting for transfers between devices, gather_rows(): other = lax.ppermute(block, axis_name, _exchange_pairs(count, distance))  4.42 us
    dot_general x1, matrix products, encoder_grads(): lax.dot_general(inputs_rows, grad_pre, (((0,), (0,)), ((), ())), preferre...  3.86 us
    ppermute x2, starting transfers between devices, sum_halving(): arrived = lax.ppermute(send, axis_name, _exchange_pairs(count, distance))  2.13 us
  transfers between devices with their start and end apart: 10, of which 10 were waited for; matrix products, arithmetic and copies ran while one was open for 4% of the time, Pallas kernels for 0%

profile of v14, /device:TPU:0, one launch (start us, length us, event | category | flops | bytes accessed | tf_op | source)
XLA Modules:
  0.0 60.6 jit_solution(12875194643844867345)
XLA Ops:
  0.6 4.1 %collective-permute-start = (bf16[2,2048]{1,0:T(2,128)(2,1)}, bf16[2,2048]{1,0:T(2,128)(2,1)S(1)}, u32[]{:S(2)}, u32[]{:S(2)}) collective-permute-start(bf16[2,2048]{1,0:T(2,128)(2,1)} %param.9), channel_id=1, source_target_pairs={{0,8},{1,9},{2,10},{3,11},{4,12},{5,13},{6,14},{7,15},{8,0},{9,1},... | collective-permute-start | bytes 24584 | tf_op jit(solution)/shard_map/ppermute | solution.py:119
  4.7 1.8 %collective-permute-done = bf16[2,2048]{1,0:T(2,128)(2,1)S(1)} collective-permute-done((bf16[2,2048]{1,0:T(2,128)(2,1)}, bf16[2,2048]{1,0:T(2,128)(2,1)S(1)}, u32[]{:S(2)}, u32[]{:S(2)}) %collective-permute-start) | collective-permute-done | bytes 8224 | tf_op jit(solution)/shard_map/ppermute | solution.py:119
  6.6 0.8 %maximum_select_fusion.6 = bf16[4,2048]{1,0:T(4,128)(2,1)S(1)} fusion(bf16[2,2048]{1,0:T(2,128)(2,1)S(1)} %collective-permute-done, bf16[2,2048]{1,0:T(2,128)(2,1)} %param.9, pred[]{:T(512)S(6)} %eq.47), kind=kLoop, calls=%fused_computation.73 | loop fusion | flops 73728 | bytes 32769 | tf_op jit(solution)/shard_map/jit(_where)/select_n | solution.py:121
  7.4 2.0 %collective-permute-start.1 = (bf16[4,2048]{1,0:T(4,128)(2,1)S(1)}, bf16[4,2048]{1,0:T(4,128)(2,1)S(1)}, u32[]{:S(2)}, u32[]{:S(2)}) collective-permute-start(bf16[4,2048]{1,0:T(4,128)(2,1)S(1)} %maximum_select_fusion.6), channel_id=1, source_target_pairs={{0,4},{1,5},{2,6},{3,7},{4,0},{5,1},{6,2},{7,3},{8,12},{9,13},{10,... | collective-permute-start | bytes 49160 | tf_op jit(solution)/shard_map/ppermute | solution.py:119
  9.4 0.8 %bitcast_convert_fusion = (f32[512,24]{0,1:T(8,128)S(1)}, f32[24,512]{1,0:T(8,128)S(1)}) fusion(bf16[24,512]{1,0:T(8,128)(2,1)} %param.14), kind=kLoop, calls=%fused_computation.72 | loop fusion | flops 24576 | bytes 122880
  10.2 1.0 %collective-permute-done.1 = bf16[4,2048]{1,0:T(4,128)(2,1)S(1)} collective-permute-done((bf16[4,2048]{1,0:T(4,128)(2,1)S(1)}, bf16[4,2048]{1,0:T(4,128)(2,1)S(1)}, u32[]{:S(2)}, u32[]{:S(2)}) %collective-permute-start.1) | collective-permute-done | bytes 16416 | tf_op jit(solution)/shard_map/ppermute | solution.py:119
  11.2 1.9 %collective-permute-start.2 = (bf16[8,2048]{1,0:T(8,128)(2,1)S(1)}, bf16[8,2048]{1,0:T(8,128)(2,1)S(1)}, u32[]{:S(2)}, u32[]{:S(2)}) collective-permute-start(bf16[8,2048]{1,0:T(8,128)(2,1)S(1)} %maximum_select_fusion.5), channel_id=1, source_target_pairs={{0,2},{1,3},{2,0},{3,1},{4,6},{5,7},{6,4},{7,5},{8,10},{9,11},{10,... | collective-permute-start | bytes 98312 | tf_op jit(solution)/shard_map/ppermute | solution.py:119
  13.2 0.8 %fusion.51 = (f32[1,256]{1,0:T(1,128)S(1)}, f32[1,256]{1,0:T(1,128)S(1)}) fusion(f32[2,256]{1,0:T(2,128)} %param.15), kind=kLoop, calls=%fused_computation.87 | loop fusion | bytes 4096 | tf_op jit(solution)/shard_map/slice | solution.py:46
  15.4 1.2 %collective-permute-done.3 = bf16[16,2048]{1,0:T(8,128)(2,1)S(1)} collective-permute-done((bf16[16,2048]{1,0:T(8,128)(2,1)S(1)}, bf16[16,2048]{1,0:T(8,128)(2,1)S(1)}, u32[]{:S(2)}, u32[]{:S(2)}) %collective-permute-start.3) | collective-permute-done | bytes 65568 | tf_op jit(solution)/shard_map/ppermute | solution.py:119
  19.4 0.9 %add_convert_fusion = (bf16[768,512]{1,0:T(8,128)(2,1)S(1)}, f32[768,512]{1,0:T(8,128)S(1)}) fusion(bf16[32,24,512]{2,1,0:T(8,128)(2,1)S(1)} %multiply_convert_fusion, f32[768,512]{1,0:T(8,128)S(1)} %fusion.15, bf16[512,256]{1,0:T(8,128)(2,1)S(1)} %copy-done.6, f32[768,512]{1,0:T(8,128)S(1)} %fusion.53, f32[256]{0:T(256)S(1)} %bitcast.43, f32[256]{0:T(256)S(1)} %bitcast.39), kind=kOutput, calls=%fused_computation.14 | convolution fusion | flops 206831616 | bytes 6555648 | tf_op jit(solution)/shard_map/dot_general | solution.py:55
  22.5 1.2 %fusion.11 = f32[768,512]{1,0:T(8,128)S(1)} fusion(bf16[512,512]{1,0:T(8,128)(2,1)S(1)} %copy-done.5, f32[768,512]{1,0:T(8,128)S(1)} %get-tuple-element.11, f32[768,512]{1,0:T(8,128)S(1)} %convolution_add_fusion), kind=kOutput, calls=%fused_computation.29 | convolution fusion | flops 410517504 | bytes 5242880 | tf_op jit(solution)/shard_map/dot_general | solution.py:71
  25.5 1.4 %collective-permute-done.4 = bf16[280,512]{1,0:T(8,128)(2,1)S(1)} collective-permute-done((bf16[280,512]{1,0:T(8,128)(2,1)S(1)}, bf16[280,512]{1,0:T(8,128)(2,1)S(1)}, u32[]{:S(2)}, u32[]{:S(2)}) %collective-permute-start.4) | collective-permute-done | bytes 286752 | tf_op jit(solution)/shard_map/ppermute | solution.py:159
  27.1 1.9 %collective-permute-start.5 = (bf16[140,512]{1,0:T(8,128)(2,1)S(1)}, bf16[140,512]{1,0:T(8,128)(2,1)S(1)}, u32[]{:S(2)}, u32[]{:S(2)}) collective-permute-start(bf16[140,512]{1,0:T(8,128)(2,1)S(1)} %select_convert_fusion.1), channel_id=1, source_target_pairs={{0,2},{1,3},{2,0},{3,1},{4,6},{5,7},{6,4},{7,5},{8,10},{9,11},{10,... | collective-permute-start | bytes 430088 | tf_op jit(solution)/shard_map/ppermute | solution.py:159
  29.0 4.2 %collective-permute-done.5 = bf16[140,512]{1,0:T(8,128)(2,1)S(1)} collective-permute-done((bf16[140,512]{1,0:T(8,128)(2,1)S(1)}, bf16[140,512]{1,0:T(8,128)(2,1)S(1)}, u32[]{:S(2)}, u32[]{:S(2)}) %collective-permute-start.5) | collective-permute-done | bytes 143392 | tf_op jit(solution)/shard_map/ppermute | solution.py:159
  33.3 1.9 %collective-permute-start.6 = (bf16[140,512]{1,0:T(8,128)(2,1)S(1)}, bf16[140,512]{1,0:T(8,128)(2,1)S(1)}, u32[]{:S(2)}, u32[]{:S(2)}) collective-permute-start(bf16[140,512]{1,0:T(8,128)(2,1)S(1)} %add_convert_fusion.7), channel_id=1, source_target_pairs={{0,4},{1,5},{2,6},{3,7},{4,0},{5,1},{6,2},{7,3},{8,12},{9,13},{10,... | collective-permute-start | bytes 430088 | tf_op jit(solution)/shard_map/ppermute | solution.py:165
  35.1 3.4 %collective-permute-done.6 = bf16[140,512]{1,0:T(8,128)(2,1)S(1)} collective-permute-done((bf16[140,512]{1,0:T(8,128)(2,1)S(1)}, bf16[140,512]{1,0:T(8,128)(2,1)S(1)}, u32[]{:S(2)}, u32[]{:S(2)}) %collective-permute-start.6) | collective-permute-done | bytes 143392 | tf_op jit(solution)/shard_map/ppermute | solution.py:165
  38.6 2.8 %collective-permute-start.7 = (bf16[140,512]{1,0:T(8,128)(2,1)S(1)}, bf16[140,512]{1,0:T(8,128)(2,1)S(1)}, u32[]{:S(2)}, u32[]{:S(2)}) collective-permute-start(bf16[140,512]{1,0:T(8,128)(2,1)S(1)} %add_convert_fusion.6), channel_id=1, source_target_pairs={{0,8},{1,9},{2,10},{3,11},{4,12},{5,13},{6,14},{7,15},{8,0},{9,1},... | collective-permute-start | bytes 430088 | tf_op jit(solution)/shard_map/ppermute | solution.py:165
  41.4 5.3 %collective-permute-done.7 = bf16[140,512]{1,0:T(8,128)(2,1)S(1)} collective-permute-done((bf16[140,512]{1,0:T(8,128)(2,1)S(1)}, bf16[140,512]{1,0:T(8,128)(2,1)S(1)}, u32[]{:S(2)}, u32[]{:S(2)}) %collective-permute-start.7) | collective-permute-done | bytes 143392 | tf_op jit(solution)/shard_map/ppermute | solution.py:165
  46.8 1.6 %collective-permute-start.8 = (bf16[140,512]{1,0:T(8,128)(2,1)S(1)}, bf16[140,512]{1,0:T(8,128)(2,1)S(1)}, u32[]{:S(2)}, u32[]{:S(2)}) collective-permute-start(bf16[140,512]{1,0:T(8,128)(2,1)S(1)} %add_convert_fusion.5), channel_id=1, source_target_pairs={{0,2},{1,3},{2,0},{3,1},{4,6},{5,7},{6,4},{7,5},{8,10},{9,11},{10,... | collective-permute-start | bytes 430088 | tf_op jit(solution)/shard_map/ppermute | solution.py:170
  48.4 3.6 %collective-permute-done.8 = bf16[140,512]{1,0:T(8,128)(2,1)S(1)} collective-permute-done((bf16[140,512]{1,0:T(8,128)(2,1)S(1)}, bf16[140,512]{1,0:T(8,128)(2,1)S(1)}, u32[]{:S(2)}, u32[]{:S(2)}) %collective-permute-start.8) | collective-permute-done | bytes 143392 | tf_op jit(solution)/shard_map/ppermute | solution.py:170
  52.2 1.5 %collective-permute-done.9 = bf16[280,512]{1,0:T(8,128)(2,1)S(1)} collective-permute-done((bf16[280,512]{1,0:T(8,128)(2,1)S(1)}, bf16[280,512]{1,0:T(8,128)(2,1)S(1)}, u32[]{:S(2)}, u32[]{:S(2)}) %collective-permute-start.9) | collective-permute-done | bytes 286752 | tf_op jit(solution)/shard_map/ppermute | solution.py:170
  54.3 1.3 %fusion.38 = f32[512,512]{1,0:T(8,128)} fusion(bf16[32,512]{1,0:T(8,128)(2,1)S(1)} %fusion.8, bf16[48,512]{1,0:T(8,128)(2,1)S(1)} %slice_select_fusion), kind=kOutput, calls=%fused_computation.69 | convolution fusion | flops 16777216 | bytes 1114112 | tf_op jit(solution)/shard_map/dot_general | solution.py:91
  55.6 3.9 %fusion.10 = f32[2048,512]{1,0:T(8,128)} fusion(bf16[32,2048]{1,0:T(8,128)(2,1)} %copy-done.4, bf16[512,512]{1,0:T(8,128)(2,1)S(1)} %copy-done.1, bf16[32,512]{1,0:T(8,128)(2,1)S(1)} %fusion.8, bf16[48,512]{1,0:T(8,128)(2,1)S(1)} %slice_select_fusion), kind=kOutput, calls=%fused_computation.22 | convolution fusion | flops 83968000 | bytes 4915200 | tf_op jit(solution)/shard_map/dot_general | solution.py:98
  59.5 1.1 %fusion.14 = f32[512,512]{1,0:T(8,128)} fusion(bf16[232,512]{1,0:T(8,128)(2,1)S(1)} %slice.83, bf16[280,512]{1,0:T(8,128)(2,1)S(1)} %maximum_select_fusion.1, bf16[232,512]{1,0:T(8,128)(2,1)S(1)} %slice.84, bf16[280,512]{1,0:T(8,128)(2,1)S(1)} %collective-permute-done.9, pred[]{:T(512)S(6)} %eq.44), kind=kLoop, calls=%fused_computation.36 | loop fusion | flops 2621440 | bytes 2097153 | tf_op jit(solution)/shard_map/convert_element_type | solution.py:247
  (52 shorter events, 9.3 us)
Async XLA Ops:
  0.6 16.1 %copy-start = (bf16[2048,512]{1,0:T(8,128)(2,1)S(1)}, bf16[2048,512]{1,0:T(8,128)(2,1)}, u32[]{:S(2)}) copy-start(bf16[2048,512]{1,0:T(8,128)(2,1)} %param.12) | copy-start | bytes 6291460
  0.6 5.9 %collective-permute-start = (bf16[2,2048]{1,0:T(2,128)(2,1)}, bf16[2,2048]{1,0:T(2,128)(2,1)S(1)}, u32[]{:S(2)}, u32[]{:S(2)}) collective-permute-start(bf16[2,2048]{1,0:T(2,128)(2,1)} %param.9), channel_id=1, source_target_pairs={{0,8},{1,9},{2,10},{3,11},{4,12},{5,13},{6,14},{7,15},{8,0},{9,1},... | collective-permute-start | bytes 24584 | tf_op jit(solution)/shard_map/ppermute | solution.py:119
  7.4 3.8 %collective-permute-start.1 = (bf16[4,2048]{1,0:T(4,128)(2,1)S(1)}, bf16[4,2048]{1,0:T(4,128)(2,1)S(1)}, u32[]{:S(2)}, u32[]{:S(2)}) collective-permute-start(bf16[4,2048]{1,0:T(4,128)(2,1)S(1)} %maximum_select_fusion.6), channel_id=1, source_target_pairs={{0,4},{1,5},{2,6},{3,7},{4,0},{5,1},{6,2},{7,3},{8,12},{9,13},{10,... | collective-permute-start | bytes 49160 | tf_op jit(solution)/shard_map/ppermute | solution.py:119
  10.2 7.1 %copy-start.1 = (bf16[512,512]{1,0:T(8,128)(2,1)S(1)}, bf16[512,512]{1,0:T(8,128)(2,1)}, u32[]{:S(2)}) copy-start(bf16[512,512]{1,0:T(8,128)(2,1)} %param.13) | copy-start | bytes 1572868
  11.2 4.0 %collective-permute-start.2 = (bf16[8,2048]{1,0:T(8,128)(2,1)S(1)}, bf16[8,2048]{1,0:T(8,128)(2,1)S(1)}, u32[]{:S(2)}, u32[]{:S(2)}) collective-permute-start(bf16[8,2048]{1,0:T(8,128)(2,1)S(1)} %maximum_select_fusion.5), channel_id=1, source_target_pairs={{0,2},{1,3},{2,0},{3,1},{4,6},{5,7},{6,4},{7,5},{8,10},{9,11},{10,... | collective-permute-start | bytes 98312 | tf_op jit(solution)/shard_map/ppermute | solution.py:119
  15.2 1.3 %collective-permute-start.3 = (bf16[16,2048]{1,0:T(8,128)(2,1)S(1)}, bf16[16,2048]{1,0:T(8,128)(2,1)S(1)}, u32[]{:S(2)}, u32[]{:S(2)}) collective-permute-start(bf16[16,2048]{1,0:T(8,128)(2,1)S(1)} %maximum_select_fusion.4), channel_id=1, source_target_pairs={{0,1},{1,0},{2,3},{3,2},{4,5},{5,4},{6,7},{7,6},{8,9},{9,8},{10,11... | collective-permute-start | bytes 196616 | tf_op jit(solution)/shard_map/ppermute | solution.py:119
  16.7 0.7 %copy-start.4 = (bf16[32,2048]{1,0:T(8,128)(2,1)}, bf16[32,2048]{1,0:T(8,128)(2,1)S(1)}, u32[]{:S(2)}) copy-start(bf16[32,2048]{1,0:T(8,128)(2,1)S(1)} %convolution_convert_fusion) | copy-start | bytes 393220
  16.8 1.1 %copy-start.5 = (bf16[512,512]{1,0:T(8,128)(2,1)S(1)}, bf16[512,512]{1,0:T(8,128)(2,1)}, u32[]{:S(2)}) copy-start(bf16[512,512]{1,0:T(8,128)(2,1)} %constant.107.clone) | copy-start | bytes 1572868
  17.6 1.0 %copy-start.2 = (bf16[512,256]{1,0:T(8,128)(2,1)S(1)}, bf16[512,256]{1,0:T(8,128)(2,1)}, u32[]{:S(2)}) copy-start(bf16[512,256]{1,0:T(8,128)(2,1)} %constant.113) | copy-start | bytes 786436
  18.4 1.0 %copy-start.6 = (bf16[512,256]{1,0:T(8,128)(2,1)S(1)}, bf16[512,256]{1,0:T(8,128)(2,1)}, u32[]{:S(2)}) copy-start(bf16[512,256]{1,0:T(8,128)(2,1)} %constant.114) | copy-start | bytes 786436
  19.4 1.0 %copy-start.3 = (bf16[512,512]{1,0:T(8,128)(2,1)S(1)}, bf16[512,512]{1,0:T(8,128)(2,1)}, u32[]{:S(2)}) copy-start(bf16[512,512]{1,0:T(8,128)(2,1)} %param.16) | copy-start | bytes 1572868
  19.4 1.3 %copy-start.7 = (bf16[32,24,512]{2,1,0:T(8,128)(2,1)S(1)}, bf16[32,24,512]{2,1,0:T(8,128)(2,1)}, u32[]{:S(2)}) copy-start(bf16[32,24,512]{2,1,0:T(8,128)(2,1)} %param.10) | copy-start | bytes 2359300
  25.3 1.6 %collective-permute-start.4 = (bf16[280,512]{1,0:T(8,128)(2,1)S(1)}, bf16[280,512]{1,0:T(8,128)(2,1)S(1)}, u32[]{:S(2)}, u32[]{:S(2)}) collective-permute-start(bf16[280,512]{1,0:T(8,128)(2,1)S(1)} %select_convert_fusion), channel_id=1, source_target_pairs={{0,1},{1,0},{2,3},{3,2},{4,5},{5,4},{6,7},{7,6},{8,9},{9,8},{10,11... | collective-permute-start | bytes 860168 | tf_op jit(solution)/shard_map/ppermute | solution.py:159
  27.1 6.1 %collective-permute-start.5 = (bf16[140,512]{1,0:T(8,128)(2,1)S(1)}, bf16[140,512]{1,0:T(8,128)(2,1)S(1)}, u32[]{:S(2)}, u32[]{:S(2)}) collective-permute-start(bf16[140,512]{1,0:T(8,128)(2,1)S(1)} %select_convert_fusion.1), channel_id=1, source_target_pairs={{0,2},{1,3},{2,0},{3,1},{4,6},{5,7},{6,4},{7,5},{8,10},{9,11},{10,... | collective-permute-start | bytes 430088 | tf_op jit(solution)/shard_map/ppermute | solution.py:159
  33.3 5.3 %collective-permute-start.6 = (bf16[140,512]{1,0:T(8,128)(2,1)S(1)}, bf16[140,512]{1,0:T(8,128)(2,1)S(1)}, u32[]{:S(2)}, u32[]{:S(2)}) collective-permute-start(bf16[140,512]{1,0:T(8,128)(2,1)S(1)} %add_convert_fusion.7), channel_id=1, source_target_pairs={{0,4},{1,5},{2,6},{3,7},{4,0},{5,1},{6,2},{7,3},{8,12},{9,13},{10,... | collective-permute-start | bytes 430088 | tf_op jit(solution)/shard_map/ppermute | solution.py:165
  38.6 8.2 %collective-permute-start.7 = (bf16[140,512]{1,0:T(8,128)(2,1)S(1)}, bf16[140,512]{1,0:T(8,128)(2,1)S(1)}, u32[]{:S(2)}, u32[]{:S(2)}) collective-permute-start(bf16[140,512]{1,0:T(8,128)(2,1)S(1)} %add_convert_fusion.6), channel_id=1, source_target_pairs={{0,8},{1,9},{2,10},{3,11},{4,12},{5,13},{6,14},{7,15},{8,0},{9,1},... | collective-permute-start | bytes 430088 | tf_op jit(solution)/shard_map/ppermute | solution.py:165
  46.8 5.2 %collective-permute-start.8 = (bf16[140,512]{1,0:T(8,128)(2,1)S(1)}, bf16[140,512]{1,0:T(8,128)(2,1)S(1)}, u32[]{:S(2)}, u32[]{:S(2)}) collective-permute-start(bf16[140,512]{1,0:T(8,128)(2,1)S(1)} %add_convert_fusion.5), channel_id=1, source_target_pairs={{0,2},{1,3},{2,0},{3,1},{4,6},{5,7},{6,4},{7,5},{8,10},{9,11},{10,... | collective-permute-start | bytes 430088 | tf_op jit(solution)/shard_map/ppermute | solution.py:170
  52.1 1.6 %collective-permute-start.9 = (bf16[280,512]{1,0:T(8,128)(2,1)S(1)}, bf16[280,512]{1,0:T(8,128)(2,1)S(1)}, u32[]{:S(2)}, u32[]{:S(2)}) collective-permute-start(bf16[280,512]{1,0:T(8,128)(2,1)S(1)} %maximum_select_fusion.1), channel_id=1, source_target_pairs={{0,1},{1,0},{2,3},{3,2},{4,5},{5,4},{6,7},{7,6},{8,9},{9,8},{10,11... | collective-permute-start | bytes 860168 | tf_op jit(solution)/shard_map/ppermute | solution.py:170

commit v15 on v13

--- a/solution.py
+++ b/solution.py
@@ -144,7 +144,7 @@
     return values
 
 
-def sum_halving(values, axis_name, wire=jnp.bfloat16, halving_levels=2):
+def sum_halving(values, axis_name, wire=jnp.bfloat16, halving_levels=3):
     count = lax.axis_size(axis_name)
     if not _is_power_of_two(count) or values.shape[0] % count != 0:
         return lax.psum(values, axis_name)

time: 60.1 us -> 60.9 us (1.013)
  starting transfers between devices: 16.6 us -> 18.7 us
  waiting for transfers between devices: 23.9 us -> 22.5 us
    ppermute x2 -> x1, waiting for transfers between devices: 8.73 us -> 2.44 us  [sum_halving(): arrived = lax.ppermute(values, axis_name, _exchange_pairs(count, distance))]
    ppermute x2 -> x3, waiting for transfers between devices: 5.59 us -> 8.13 us  [sum_halving(): arrived = lax.ppermute(send, axis_name, _exchange_pairs(count, distance))]
    ppermute x2 -> x3, waiting for transfers between devices: 5.12 us -> 7.48 us  [sum_halving(): other = lax.ppermute(values, axis_name, _exchange_pairs(count, distance))]
    ppermute x2 -> x3, starting transfers between devices: 1.71 us -> 3.78 us  [sum_halving(): other = lax.ppermute(values, axis_name, _exchange_pairs(count, distance))]
    ppermute x2 -> x3, starting transfers between devices: 2.12 us -> 4 us  [sum_halving(): arrived = lax.ppermute(send, axis_name, _exchange_pairs(count, distance))]
    ppermute x2 -> x1, starting transfers between devices: 4.7 us -> 2.87 us  [sum_halving(): arrived = lax.ppermute(values, axis_name, _exchange_pairs(count, distance))]
  transfers between devices with their start and end apart: 10 -> 11, of which waited for: 10 -> 11; matrix products, arithmetic and copies ran while one was open for 4% -> 4% of each run, Pallas kernels for 0% -> 0%
where the time goes in v15:
time: 60.9 us; the launch traced here: 60.6 us
  waiting for transfers between devices  22.5 us (37%)
  starting transfers between devices  18.7 us (31%)
  matrix products  10.8 us (18%)
  other arithmetic  4.86 us (8%)
  local copies, waits for them, and re-layouts  2.8 us (5%)
  between operations  0.92 us (2%)
    ppermute x3, waiting for transfers between devices, sum_halving(): arrived = lax.ppermute(send, axis_name, _exchange_pairs(count, distance))  8.13 us
    ppermute x4, starting transfers between devices, gather_rows(): other = lax.ppermute(block, axis_name, _exchange_pairs(count, distance))  8.06 us
    ppermute x3, waiting for transfers between devices, sum_halving(): other = lax.ppermute(values, axis_name, _exchange_pairs(count, distance))  7.48 us
    ppermute x4, waiting for transfers between devices, gather_rows(): other = lax.ppermute(block, axis_name, _exchange_pairs(count, distance))  4.42 us
    ppermute x3, starting transfers between devices, sum_halving(): arrived = lax.ppermute(send, axis_name, _exchange_pairs(count, distance))  4 us
    ppermute x3, starting transfers between devices, sum_halving(): other = lax.ppermute(values, axis_name, _exchange_pairs(count, distance))  3.78 us
    dot_general x1, matrix products, encoder_grads(): lax.dot_general(inputs_rows, grad_pre, (((0,), (0,)), ((), ())), preferre...  2.96 us
    ppermute x1, starting transfers between devices, sum_halving(): arrived = lax.ppermute(values, axis_name, _exchange_pairs(count, distance))  2.87 us
  transfers between devices with their start and end apart: 11, of which 11 were waited for; matrix products, arithmetic and copies ran while one was open for 4% of the time, Pallas kernels for 0%

profile of v15, /device:TPU:0, one launch (start us, length us, event | category | flops | bytes accessed | tf_op | source)
XLA Modules:
  0.0 60.6 jit_solution(15563845269609069653)
XLA Ops:
  0.6 4.1 %collective-permute-start = (bf16[2,2048]{1,0:T(2,128)(2,1)}, bf16[2,2048]{1,0:T(2,128)(2,1)S(1)}, u32[]{:S(2)}, u32[]{:S(2)}) collective-permute-start(bf16[2,2048]{1,0:T(2,128)(2,1)} %param.9), channel_id=1, source_target_pairs={{0,8},{1,9},{2,10},{3,11},{4,12},{5,13},{6,14},{7,15},{8,0},{9,1},... | collective-permute-start | bytes 24584 | tf_op jit(solution)/shard_map/ppermute | solution.py:119
  4.7 1.8 %collective-permute-done = bf16[2,2048]{1,0:T(2,128)(2,1)S(1)} collective-permute-done((bf16[2,2048]{1,0:T(2,128)(2,1)}, bf16[2,2048]{1,0:T(2,128)(2,1)S(1)}, u32[]{:S(2)}, u32[]{:S(2)}) %collective-permute-start) | collective-permute-done | bytes 8224 | tf_op jit(solution)/shard_map/ppermute | solution.py:119
  7.4 2.0 %collective-permute-start.1 = (bf16[4,2048]{1,0:T(4,128)(2,1)S(1)}, bf16[4,2048]{1,0:T(4,128)(2,1)S(1)}, u32[]{:S(2)}, u32[]{:S(2)}) collective-permute-start(bf16[4,2048]{1,0:T(4,128)(2,1)S(1)} %maximum_select_fusion.7), channel_id=1, source_target_pairs={{0,4},{1,5},{2,6},{3,7},{4,0},{5,1},{6,2},{7,3},{8,12},{9,13},{10,... | collective-permute-start | bytes 49160 | tf_op jit(solution)/shard_map/ppermute | solution.py:119
  9.4 0.8 %bitcast_convert_fusion = (f32[512,24]{0,1:T(8,128)S(1)}, f32[24,512]{1,0:T(8,128)S(1)}) fusion(bf16[24,512]{1,0:T(8,128)(2,1)} %param.14), kind=kLoop, calls=%fused_computation.73 | loop fusion | flops 24576 | bytes 122880
  10.2 1.0 %collective-permute-done.1 = bf16[4,2048]{1,0:T(4,128)(2,1)S(1)} collective-permute-done((bf16[4,2048]{1,0:T(4,128)(2,1)S(1)}, bf16[4,2048]{1,0:T(4,128)(2,1)S(1)}, u32[]{:S(2)}, u32[]{:S(2)}) %collective-permute-start.1) | collective-permute-done | bytes 16416 | tf_op jit(solution)/shard_map/ppermute | solution.py:119
  11.2 1.9 %collective-permute-start.2 = (bf16[8,2048]{1,0:T(8,128)(2,1)S(1)}, bf16[8,2048]{1,0:T(8,128)(2,1)S(1)}, u32[]{:S(2)}, u32[]{:S(2)}) collective-permute-start(bf16[8,2048]{1,0:T(8,128)(2,1)S(1)} %maximum_select_fusion.6), channel_id=1, source_target_pairs={{0,2},{1,3},{2,0},{3,1},{4,6},{5,7},{6,4},{7,5},{8,10},{9,11},{10,... | collective-permute-start | bytes 98312 | tf_op jit(solution)/shard_map/ppermute | solution.py:119
  15.4 1.2 %collective-permute-done.3 = bf16[16,2048]{1,0:T(8,128)(2,1)S(1)} collective-permute-done((bf16[16,2048]{1,0:T(8,128)(2,1)S(1)}, bf16[16,2048]{1,0:T(8,128)(2,1)S(1)}, u32[]{:S(2)}, u32[]{:S(2)}) %collective-permute-start.3) | collective-permute-done | bytes 65568 | tf_op jit(solution)/shard_map/ppermute | solution.py:119
  19.3 0.9 %add_convert_fusion = (bf16[768,512]{1,0:T(8,128)(2,1)S(1)}, f32[768,512]{1,0:T(8,128)S(1)}) fusion(bf16[32,24,512]{2,1,0:T(8,128)(2,1)S(1)} %multiply_convert_fusion, f32[768,512]{1,0:T(8,128)S(1)} %fusion.14, bf16[512,256]{1,0:T(8,128)(2,1)S(1)} %copy-done.5, f32[768,512]{1,0:T(8,128)S(1)} %fusion.52, f32[256]{0:T(256)S(1)} %bitcast.43, f32[256]{0:T(256)S(1)} %bitcast.39), kind=kOutput, calls=%fused_computation.14 | convolution fusion | flops 206831616 | bytes 6555648 | tf_op jit(solution)/shard_map/dot_general | solution.py:55
  22.5 1.2 %fusion.11 = f32[768,512]{1,0:T(8,128)S(1)} fusion(bf16[512,512]{1,0:T(8,128)(2,1)S(1)} %copy-done.4, f32[768,512]{1,0:T(8,128)S(1)} %get-tuple-element.11, f32[768,512]{1,0:T(8,128)S(1)} %convolution_add_fusion), kind=kOutput, calls=%fused_computation.29 | convolution fusion | flops 410517504 | bytes 5242880 | tf_op jit(solution)/shard_map/dot_general | solution.py:71
  25.4 1.4 %collective-permute-done.4 = bf16[280,512]{1,0:T(8,128)(2,1)S(1)} collective-permute-done((bf16[280,512]{1,0:T(8,128)(2,1)S(1)}, bf16[280,512]{1,0:T(8,128)(2,1)S(1)}, u32[]{:S(2)}, u32[]{:S(2)}) %collective-permute-start.4) | collective-permute-done | bytes 286752 | tf_op jit(solution)/shard_map/ppermute | solution.py:158
  27.0 1.9 %collective-permute-start.5 = (bf16[140,512]{1,0:T(8,128)(2,1)S(1)}, bf16[140,512]{1,0:T(8,128)(2,1)S(1)}, u32[]{:S(2)}, u32[]{:S(2)}) collective-permute-start(bf16[140,512]{1,0:T(8,128)(2,1)S(1)} %select_convert_fusion.1), channel_id=1, source_target_pairs={{0,2},{1,3},{2,0},{3,1},{4,6},{5,7},{6,4},{7,5},{8,10},{9,11},{10,... | collective-permute-start | bytes 430088 | tf_op jit(solution)/shard_map/ppermute | solution.py:158
  29.0 4.2 %collective-permute-done.5 = bf16[140,512]{1,0:T(8,128)(2,1)S(1)} collective-permute-done((bf16[140,512]{1,0:T(8,128)(2,1)S(1)}, bf16[140,512]{1,0:T(8,128)(2,1)S(1)}, u32[]{:S(2)}, u32[]{:S(2)}) %collective-permute-start.5) | collective-permute-done | bytes 143392 | tf_op jit(solution)/shard_map/ppermute | solution.py:158
  33.2 1.9 %collective-permute-start.6 = (bf16[70,512]{1,0:T(8,128)(2,1)S(1)}, bf16[70,512]{1,0:T(8,128)(2,1)S(1)}, u32[]{:S(2)}, u32[]{:S(2)}) collective-permute-start(bf16[70,512]{1,0:T(8,128)(2,1)S(1)} %select_convert_fusion.2), channel_id=1, source_target_pairs={{0,4},{1,5},{2,6},{3,7},{4,0},{5,1},{6,2},{7,3},{8,12},{9,13},{10,... | collective-permute-start | bytes 215048 | tf_op jit(solution)/shard_map/ppermute | solution.py:158
  35.1 2.5 %collective-permute-done.6 = bf16[70,512]{1,0:T(8,128)(2,1)S(1)} collective-permute-done((bf16[70,512]{1,0:T(8,128)(2,1)S(1)}, bf16[70,512]{1,0:T(8,128)(2,1)S(1)}, u32[]{:S(2)}, u32[]{:S(2)}) %collective-permute-start.6) | collective-permute-done | bytes 71712 | tf_op jit(solution)/shard_map/ppermute | solution.py:158
  37.7 2.9 %collective-permute-start.7 = (bf16[70,512]{1,0:T(8,128)(2,1)S(1)}, bf16[70,512]{1,0:T(8,128)(2,1)S(1)}, u32[]{:S(2)}, u32[]{:S(2)}) collective-permute-start(bf16[70,512]{1,0:T(8,128)(2,1)S(1)} %add_convert_fusion.6), channel_id=1, source_target_pairs={{0,8},{1,9},{2,10},{3,11},{4,12},{5,13},{6,14},{7,15},{8,0},{9,1},... | collective-permute-start | bytes 215048 | tf_op jit(solution)/shard_map/ppermute | solution.py:164
  40.6 2.4 %collective-permute-done.7 = bf16[70,512]{1,0:T(8,128)(2,1)S(1)} collective-permute-done((bf16[70,512]{1,0:T(8,128)(2,1)S(1)}, bf16[70,512]{1,0:T(8,128)(2,1)S(1)}, u32[]{:S(2)}, u32[]{:S(2)}) %collective-permute-start.7) | collective-permute-done | bytes 71712 | tf_op jit(solution)/shard_map/ppermute | solution.py:164
  43.0 1.9 %collective-permute-start.8 = (bf16[70,512]{1,0:T(8,128)(2,1)S(1)}, bf16[70,512]{1,0:T(8,128)(2,1)S(1)}, u32[]{:S(2)}, u32[]{:S(2)}) collective-permute-start(bf16[70,512]{1,0:T(8,128)(2,1)S(1)} %add_convert_fusion.5), channel_id=1, source_target_pairs={{0,4},{1,5},{2,6},{3,7},{4,0},{5,1},{6,2},{7,3},{8,12},{9,13},{10,... | collective-permute-start | bytes 215048 | tf_op jit(solution)/shard_map/ppermute | solution.py:169
  44.9 2.5 %collective-permute-done.8 = bf16[70,512]{1,0:T(8,128)(2,1)S(1)} collective-permute-done((bf16[70,512]{1,0:T(8,128)(2,1)S(1)}, bf16[70,512]{1,0:T(8,128)(2,1)S(1)}, u32[]{:S(2)}, u32[]{:S(2)}) %collective-permute-start.8) | collective-permute-done | bytes 71712 | tf_op jit(solution)/shard_map/ppermute | solution.py:169
  47.5 1.8 %collective-permute-start.9 = (bf16[140,512]{1,0:T(8,128)(2,1)S(1)}, bf16[140,512]{1,0:T(8,128)(2,1)S(1)}, u32[]{:S(2)}, u32[]{:S(2)}) collective-permute-start(bf16[140,512]{1,0:T(8,128)(2,1)S(1)} %maximum_select_fusion.2), channel_id=1, source_target_pairs={{0,2},{1,3},{2,0},{3,1},{4,6},{5,7},{6,4},{7,5},{8,10},{9,11},{10,... | collective-permute-start | bytes 430088 | tf_op jit(solution)/shard_map/ppermute | solution.py:169
  49.3 3.4 %collective-permute-done.9 = bf16[140,512]{1,0:T(8,128)(2,1)S(1)} collective-permute-done((bf16[140,512]{1,0:T(8,128)(2,1)S(1)}, bf16[140,512]{1,0:T(8,128)(2,1)S(1)}, u32[]{:S(2)}, u32[]{:S(2)}) %collective-permute-start.9) | collective-permute-done | bytes 143392 | tf_op jit(solution)/shard_map/ppermute | solution.py:169
  52.9 1.6 %collective-permute-done.10 = bf16[280,512]{1,0:T(8,128)(2,1)S(1)} collective-permute-done((bf16[280,512]{1,0:T(8,128)(2,1)S(1)}, bf16[280,512]{1,0:T(8,128)(2,1)S(1)}, u32[]{:S(2)}, u32[]{:S(2)}) %collective-permute-start.10) | collective-permute-done | bytes 286752 | tf_op jit(solution)/shard_map/ppermute | solution.py:169
  55.3 1.3 %fusion.37 = f32[512,512]{1,0:T(8,128)} fusion(bf16[32,512]{1,0:T(8,128)(2,1)S(1)} %fusion.8, bf16[560,512]{1,0:T(8,128)(2,1)S(1)} %maximum_select_fusion), kind=kOutput, calls=%fused_computation.70 | convolution fusion | flops 16777216 | bytes 1114112 | tf_op jit(solution)/shard_map/dot_general | solution.py:91
  56.5 1.1 %slice_convert_fusion = f32[512,512]{1,0:T(8,128)} fusion(bf16[560,512]{1,0:T(8,128)(2,1)S(1)} %maximum_select_fusion), kind=kLoop, calls=%fused_computation.36 | loop fusion | flops 262144 | bytes 1572864 | tf_op jit(solution)/shard_map/convert_element_type | solution.py:238
  57.6 3.0 %fusion.10 = f32[2048,512]{1,0:T(8,128)} fusion(bf16[32,2048]{1,0:T(8,128)(2,1)S(1)} %convolution_convert_fusion, bf16[512,512]{1,0:T(8,128)(2,1)S(1)} %copy-done.1, bf16[32,512]{1,0:T(8,128)(2,1)S(1)} %fusion.8, bf16[560,512]{1,0:T(8,128)(2,1)S(1)} %maximum_select_fusion), kind=kOutput, calls=%fused_computation.22 | convolution fusion | flops 83968000 | bytes 4915200 | tf_op jit(solution)/shard_map/dot_general | solution.py:98
  (52 shorter events, 11.0 us)
Async XLA Ops:
  0.6 16.1 %copy-start = (bf16[2048,512]{1,0:T(8,128)(2,1)S(1)}, bf16[2048,512]{1,0:T(8,128)(2,1)}, u32[]{:S(2)}) copy-start(bf16[2048,512]{1,0:T(8,128)(2,1)} %param.12) | copy-start | bytes 6291460
  0.6 5.9 %collective-permute-start = (bf16[2,2048]{1,0:T(2,128)(2,1)}, bf16[2,2048]{1,0:T(2,128)(2,1)S(1)}, u32[]{:S(2)}, u32[]{:S(2)}) collective-permute-start(bf16[2,2048]{1,0:T(2,128)(2,1)} %param.9), channel_id=1, source_target_pairs={{0,8},{1,9},{2,10},{3,11},{4,12},{5,13},{6,14},{7,15},{8,0},{9,1},... | collective-permute-start | bytes 24584 | tf_op jit(solution)/shard_map/ppermute | solution.py:119
  7.4 3.8 %collective-permute-start.1 = (bf16[4,2048]{1,0:T(4,128)(2,1)S(1)}, bf16[4,2048]{1,0:T(4,128)(2,1)S(1)}, u32[]{:S(2)}, u32[]{:S(2)}) collective-permute-start(bf16[4,2048]{1,0:T(4,128)(2,1)S(1)} %maximum_select_fusion.7), channel_id=1, source_target_pairs={{0,4},{1,5},{2,6},{3,7},{4,0},{5,1},{6,2},{7,3},{8,12},{9,13},{10,... | collective-permute-start | bytes 49160 | tf_op jit(solution)/shard_map/ppermute | solution.py:119
  10.2 7.0 %copy-start.1 = (bf16[512,512]{1,0:T(8,128)(2,1)S(1)}, bf16[512,512]{1,0:T(8,128)(2,1)}, u32[]{:S(2)}) copy-start(bf16[512,512]{1,0:T(8,128)(2,1)} %param.13) | copy-start | bytes 1572868
  11.2 4.0 %collective-permute-start.2 = (bf16[8,2048]{1,0:T(8,128)(2,1)S(1)}, bf16[8,2048]{1,0:T(8,128)(2,1)S(1)}, u32[]{:S(2)}, u32[]{:S(2)}) collective-permute-start(bf16[8,2048]{1,0:T(8,128)(2,1)S(1)} %maximum_select_fusion.6), channel_id=1, source_target_pairs={{0,2},{1,3},{2,0},{3,1},{4,6},{5,7},{6,4},{7,5},{8,10},{9,11},{10,... | collective-permute-start | bytes 98312 | tf_op jit(solution)/shard_map/ppermute | solution.py:119
  15.2 1.3 %collective-permute-start.3 = (bf16[16,2048]{1,0:T(8,128)(2,1)S(1)}, bf16[16,2048]{1,0:T(8,128)(2,1)S(1)}, u32[]{:S(2)}, u32[]{:S(2)}) collective-permute-start(bf16[16,2048]{1,0:T(8,128)(2,1)S(1)} %maximum_select_fusion.5), channel_id=1, source_target_pairs={{0,1},{1,0},{2,3},{3,2},{4,5},{5,4},{6,7},{7,6},{8,9},{9,8},{10,11... | collective-permute-start | bytes 196616 | tf_op jit(solution)/shard_map/ppermute | solution.py:119
  16.7 1.0 %copy-start.4 = (bf16[512,512]{1,0:T(8,128)(2,1)S(1)}, bf16[512,512]{1,0:T(8,128)(2,1)}, u32[]{:S(2)}) copy-start(bf16[512,512]{1,0:T(8,128)(2,1)} %constant.115.clone) | copy-start | bytes 1572868
  17.6 1.0 %copy-start.2 = (bf16[512,256]{1,0:T(8,128)(2,1)S(1)}, bf16[512,256]{1,0:T(8,128)(2,1)}, u32[]{:S(2)}) copy-start(bf16[512,256]{1,0:T(8,128)(2,1)} %constant.121) | copy-start | bytes 786436
  18.4 1.0 %copy-start.5 = (bf16[512,256]{1,0:T(8,128)(2,1)S(1)}, bf16[512,256]{1,0:T(8,128)(2,1)}, u32[]{:S(2)}) copy-start(bf16[512,256]{1,0:T(8,128)(2,1)} %constant.122) | copy-start | bytes 786436
  19.3 1.0 %copy-start.3 = (bf16[512,512]{1,0:T(8,128)(2,1)S(1)}, bf16[512,512]{1,0:T(8,128)(2,1)}, u32[]{:S(2)}) copy-start(bf16[512,512]{1,0:T(8,128)(2,1)} %param.16) | copy-start | bytes 1572868
  19.3 1.3 %copy-start.6 = (bf16[32,24,512]{2,1,0:T(8,128)(2,1)S(1)}, bf16[32,24,512]{2,1,0:T(8,128)(2,1)}, u32[]{:S(2)}) copy-start(bf16[32,24,512]{2,1,0:T(8,128)(2,1)} %param.10) | copy-start | bytes 2359300
  25.2 1.6 %collective-permute-start.4 = (bf16[280,512]{1,0:T(8,128)(2,1)S(1)}, bf16[280,512]{1,0:T(8,128)(2,1)S(1)}, u32[]{:S(2)}, u32[]{:S(2)}) collective-permute-start(bf16[280,512]{1,0:T(8,128)(2,1)S(1)} %select_convert_fusion), channel_id=1, source_target_pairs={{0,1},{1,0},{2,3},{3,2},{4,5},{5,4},{6,7},{7,6},{8,9},{9,8},{10,11... | collective-permute-start | bytes 860168 | tf_op jit(solution)/shard_map/ppermute | solution.py:158
  27.0 6.1 %collective-permute-start.5 = (bf16[140,512]{1,0:T(8,128)(2,1)S(1)}, bf16[140,512]{1,0:T(8,128)(2,1)S(1)}, u32[]{:S(2)}, u32[]{:S(2)}) collective-permute-start(bf16[140,512]{1,0:T(8,128)(2,1)S(1)} %select_convert_fusion.1), channel_id=1, source_target_pairs={{0,2},{1,3},{2,0},{3,1},{4,6},{5,7},{6,4},{7,5},{8,10},{9,11},{10,... | collective-permute-start | bytes 430088 | tf_op jit(solution)/shard_map/ppermute | solution.py:158
  33.2 4.4 %collective-permute-start.6 = (bf16[70,512]{1,0:T(8,128)(2,1)S(1)}, bf16[70,512]{1,0:T(8,128)(2,1)S(1)}, u32[]{:S(2)}, u32[]{:S(2)}) collective-permute-start(bf16[70,512]{1,0:T(8,128)(2,1)S(1)} %select_convert_fusion.2), channel_id=1, source_target_pairs={{0,4},{1,5},{2,6},{3,7},{4,0},{5,1},{6,2},{7,3},{8,12},{9,13},{10,... | collective-permute-start | bytes 215048 | tf_op jit(solution)/shard_map/ppermute | solution.py:158
  37.7 5.3 %collective-permute-start.7 = (bf16[70,512]{1,0:T(8,128)(2,1)S(1)}, bf16[70,512]{1,0:T(8,128)(2,1)S(1)}, u32[]{:S(2)}, u32[]{:S(2)}) collective-permute-start(bf16[70,512]{1,0:T(8,128)(2,1)S(1)} %add_convert_fusion.6), channel_id=1, source_target_pairs={{0,8},{1,9},{2,10},{3,11},{4,12},{5,13},{6,14},{7,15},{8,0},{9,1},... | collective-permute-start | bytes 215048 | tf_op jit(solution)/shard_map/ppermute | solution.py:164
  43.0 4.4 %collective-permute-start.8 = (bf16[70,512]{1,0:T(8,128)(2,1)S(1)}, bf16[70,512]{1,0:T(8,128)(2,1)S(1)}, u32[]{:S(2)}, u32[]{:S(2)}) collective-permute-start(bf16[70,512]{1,0:T(8,128)(2,1)S(1)} %add_convert_fusion.5), channel_id=1, source_target_pairs={{0,4},{1,5},{2,6},{3,7},{4,0},{5,1},{6,2},{7,3},{8,12},{9,13},{10,... | collective-permute-start | bytes 215048 | tf_op jit(solution)/shard_map/ppermute | solution.py:169
  47.5 5.2 %collective-permute-start.9 = (bf16[140,512]{1,0:T(8,128)(2,1)S(1)}, bf16[140,512]{1,0:T(8,128)(2,1)S(1)}, u32[]{:S(2)}, u32[]{:S(2)}) collective-permute-start(bf16[140,512]{1,0:T(8,128)(2,1)S(1)} %maximum_select_fusion.2), channel_id=1, source_target_pairs={{0,2},{1,3},{2,0},{3,1},{4,6},{5,7},{6,4},{7,5},{8,10},{9,11},{10,... | collective-permute-start | bytes 430088 | tf_op jit(solution)/shard_map/ppermute | solution.py:169
  52.8 1.6 %collective-permute-start.10 = (bf16[280,512]{1,0:T(8,128)(2,1)S(1)}, bf16[280,512]{1,0:T(8,128)(2,1)S(1)}, u32[]{:S(2)}, u32[]{:S(2)}) collective-permute-start(bf16[280,512]{1,0:T(8,128)(2,1)S(1)} %maximum_select_fusion.1), channel_id=1, source_target_pairs={{0,1},{1,0},{2,3},{3,2},{4,5},{5,4},{6,7},{7,6},{8,9},{9,8},{10,11... | collective-permute-start | bytes 860168 | tf_op jit(solution)/shard_map/ppermute | solution.py:169

commit v16 on v13

--- a/solution.py
+++ b/solution.py
@@ -190,16 +190,20 @@
     width = desired_responses.shape[2]
     forward_transform, inverse_transform = rotation_tables(width // 2)
     loss_scale = 1.0 / math.sqrt(samples * sub_dev * lax.axis_size("freq"))
-    all_inputs = gather_rows(encoder_input, "freq")
+    codes_own = jnp.tanh(
+        jnp.dot(encoder_input, encoder_weight, preferred_element_type=jnp.float32)
+    ).astype(jnp.bfloat16)
+    enc_in = encoder_input.shape[1]
+    gathered = gather_rows(jnp.concatenate([encoder_input, codes_own], 1), "freq")
     gathered_index = bit_reversed_blocks(sample_index, lax.axis_size("freq"))
     selection = (
         gathered_index[None, :] == jnp.arange(samples, dtype=jnp.int32)[:, None]
     ).astype(jnp.bfloat16)
-    inputs_by_sample = jnp.dot(selection, all_inputs, preferred_element_type=jnp.float32).astype(
-        jnp.bfloat16
-    )
-    codes_by_sample = jnp.tanh(
-        jnp.dot(inputs_by_sample, encoder_weight, preferred_element_type=jnp.float32)
+    codes_by_sample = jnp.dot(
+        selection, gathered[:, enc_in:], preferred_element_type=jnp.float32
+    ).astype(jnp.bfloat16)
+    inputs_by_sample = jnp.dot(
+        selection, gathered[:, :enc_in], preferred_element_type=jnp.float32
     ).astype(jnp.bfloat16)
     latent = jnp.dot(codes_by_sample, decoder_weight, preferred_element_type=jnp.float32)
     gain_row_values = frequency_amplitude.astype(jnp.float32)

time: 60.1 us -> 61.5 us (1.023)
  waiting for transfers between devices: 23.9 us -> 26.1 us
  other arithmetic: 4.81 us -> 3.29 us
  matrix products: 10.8 us -> 11.6 us
    ppermute x4, waiting for transfers between devices: 4.42 us -> 6.6 us  [gather_rows(): other = lax.ppermute(block, axis_name, _exchange_pairs(count, distance))]
    unnamed x14 -> x22, local copies, waits for them, and re-layouts: 1.13 us -> 2.5 us
    unnamed x1, other arithmetic: 0.82 us -> 0.01 us
    dot_general x2 -> x3, matrix products: 0.64 us -> 1.44 us  [the longest x1 1.07 us: local(): jnp.dot(encoder_input, encoder_weight, preferred_element_type=jnp.float32)]
    slice x1, local copies, waits for them, and re-layouts: 0.76 us -> 0.01 us  [decode_rows(): filter_re = spectral_filter_weight[0]]
    select_n x3 -> x4, other arithmetic: 0.86 us -> 0.13 us  [gather_rows(): jnp.where(lower, jnp.concatenate([block, other], 0), jnp.concatenate([oth...]
    reshape x1, local copies, waits for them, and re-layouts: 0.74 us -> 0.09 us  [bit_reversed_blocks(): blocks = values.reshape((2,) * bits + (-1,))]
  transfers between devices with their start and end apart: 10 -> 10, of which waited for: 10 -> 10; matrix products, arithmetic and copies ran while one was open for 4% -> 0% of each run, Pallas kernels for 0% -> 0%
where the time goes in v16:
time: 61.5 us; the launch traced here: 61.2 us
  waiting for transfers between devices  26.1 us (42%)
  starting transfers between devices  16.6 us (27%)
  matrix products  11.6 us (19%)
  other arithmetic  3.29 us (5%)
  local copies, waits for them, and re-layouts  2.76 us (4%)
  between operations  0.96 us (2%)
    ppermute x2, waiting for transfers between devices, sum_halving(): arrived = lax.ppermute(values, axis_name, _exchange_pairs(count, distance))  8.77 us
    ppermute x4, starting transfers between devices, gather_rows(): other = lax.ppermute(block, axis_name, _exchange_pairs(count, distance))  8.06 us
    ppermute x4, waiting for transfers between devices, gather_rows(): other = lax.ppermute(block, axis_name, _exchange_pairs(count, distance))  6.6 us
    ppermute x2, waiting for transfers between devices, sum_halving(): arrived = lax.ppermute(send, axis_name, _exchange_pairs(count, distance))  5.58 us
    ppermute x2, waiting for transfers between devices, sum_halving(): other = lax.ppermute(values, axis_name, _exchange_pairs(count, distance))  5.13 us
    ppermute x2, starting transfers between devices, sum_halving(): arrived = lax.ppermute(values, axis_name, _exchange_pairs(count, distance))  4.65 us
    dot_general x1, matrix products, encoder_grads(): lax.dot_general(inputs_rows, grad_pre, (((0,), (0,)), ((), ())), preferre...  2.89 us
    unnamed x22, local copies, waits for them, and re-layouts  2.5 us
  transfers between devices with their start and end apart: 10, of which 10 were waited for; matrix products, arithmetic and copies ran while one was open for 0% of the time, Pallas kernels for 0%

profile of v16, /device:TPU:0, one launch (start us, length us, event | category | flops | bytes accessed | tf_op | source)
XLA Modules:
  0.0 61.2 jit_solution(2632790980036869130)
XLA Ops:
  0.7 1.5 %copy-done = bf16[2048,512]{1,0:T(8,128)(2,1)S(1)} copy-done((bf16[2048,512]{1,0:T(8,128)(2,1)S(1)}, bf16[2048,512]{1,0:T(8,128)(2,1)}, u32[]{:S(2)}) %copy-start) | copy-done | bytes 2097176
  2.2 1.1 %fusion.10 = bf16[2,512]{1,0:T(2,128)(2,1)S(1)} fusion(bf16[2,2048]{1,0:T(2,128)(2,1)} %param.9, bf16[2048,512]{1,0:T(8,128)(2,1)S(1)} %copy-done), kind=kOutput, calls=%fused_computation.23 | convolution fusion | flops 4195328 | bytes 2107392 | tf_op jit(solution)/shard_map/dot_general | solution.py:194
  3.3 4.1 %collective-permute-start = (bf16[2,2560]{1,0:T(2,128)(2,1)S(1)}, bf16[2,2560]{1,0:T(2,128)(2,1)S(1)}, u32[]{:S(2)}, u32[]{:S(2)}) collective-permute-start(bf16[2,2560]{1,0:T(2,128)(2,1)S(1)} %pad_maximum_fusion.2), channel_id=1, source_target_pairs={{0,8},{1,9},{2,10},{3,11},{4,12},{5,13},{6,14},{7,15},{8,0},{9,1},... | collective-permute-start | bytes 30728 | tf_op jit(solution)/shard_map/ppermute | solution.py:119
  7.4 1.7 %collective-permute-done = bf16[2,2560]{1,0:T(2,128)(2,1)S(1)} collective-permute-done((bf16[2,2560]{1,0:T(2,128)(2,1)S(1)}, bf16[2,2560]{1,0:T(2,128)(2,1)S(1)}, u32[]{:S(2)}, u32[]{:S(2)}) %collective-permute-start) | collective-permute-done | bytes 10272 | tf_op jit(solution)/shard_map/ppermute | solution.py:119
  9.1 2.0 %collective-permute-start.1 = (bf16[4,2560]{1,0:T(4,128)(2,1)S(1)}, bf16[4,2560]{1,0:T(4,128)(2,1)S(1)}, u32[]{:S(2)}, u32[]{:S(2)}) collective-permute-start(bf16[4,2560]{1,0:T(4,128)(2,1)S(1)} %maximum_select_fusion.5), channel_id=1, source_target_pairs={{0,4},{1,5},{2,6},{3,7},{4,0},{5,1},{6,2},{7,3},{8,12},{9,13},{10,... | collective-permute-start | bytes 61448 | tf_op jit(solution)/shard_map/ppermute | solution.py:119
  11.2 1.8 %collective-permute-done.1 = bf16[4,2560]{1,0:T(4,128)(2,1)S(1)} collective-permute-done((bf16[4,2560]{1,0:T(4,128)(2,1)S(1)}, bf16[4,2560]{1,0:T(4,128)(2,1)S(1)}, u32[]{:S(2)}, u32[]{:S(2)}) %collective-permute-start.1) | collective-permute-done | bytes 20512 | tf_op jit(solution)/shard_map/ppermute | solution.py:119
  13.0 1.9 %collective-permute-start.2 = (bf16[8,2560]{1,0:T(8,128)(2,1)S(1)}, bf16[8,2560]{1,0:T(8,128)(2,1)S(1)}, u32[]{:S(2)}, u32[]{:S(2)}) collective-permute-start(bf16[8,2560]{1,0:T(8,128)(2,1)S(1)} %maximum_select_fusion.4), channel_id=1, source_target_pairs={{0,2},{1,3},{2,0},{3,1},{4,6},{5,7},{6,4},{7,5},{8,10},{9,11},{10,... | collective-permute-start | bytes 122888 | tf_op jit(solution)/shard_map/ppermute | solution.py:119
  15.2 1.9 %collective-permute-done.2 = bf16[8,2560]{1,0:T(8,128)(2,1)S(1)} collective-permute-done((bf16[8,2560]{1,0:T(8,128)(2,1)S(1)}, bf16[8,2560]{1,0:T(8,128)(2,1)S(1)}, u32[]{:S(2)}, u32[]{:S(2)}) %collective-permute-start.2) | collective-permute-done | bytes 40992 | tf_op jit(solution)/shard_map/ppermute | solution.py:119
  17.3 1.2 %collective-permute-done.3 = bf16[16,2560]{1,0:T(8,128)(2,1)S(1)} collective-permute-done((bf16[16,2560]{1,0:T(8,128)(2,1)S(1)}, bf16[16,2560]{1,0:T(8,128)(2,1)S(1)}, u32[]{:S(2)}, u32[]{:S(2)}) %collective-permute-start.3) | collective-permute-done | bytes 81952 | tf_op jit(solution)/shard_map/ppermute | solution.py:119
  20.6 0.9 %add_convert_fusion = (bf16[768,512]{1,0:T(8,128)(2,1)S(1)}, f32[768,512]{1,0:T(8,128)S(1)}) fusion(bf16[32,24,512]{2,1,0:T(8,128)(2,1)S(1)} %multiply_convert_fusion, f32[768,512]{1,0:T(8,128)S(1)} %fusion.14, bf16[512,256]{1,0:T(8,128)(2,1)S(1)} %copy-done.5, f32[768,512]{1,0:T(8,128)S(1)} %fusion.44, f32[256]{0:T(256)S(1)} %bitcast.43, f32[256]{0:T(256)S(1)} %bitcast.39), kind=kOutput, calls=%fused_computation.14 | convolution fusion | flops 206831616 | bytes 6555648 | tf_op jit(solution)/shard_map/dot_general | solution.py:55
  23.7 1.2 %fusion.11 = f32[768,512]{1,0:T(8,128)S(1)} fusion(bf16[512,512]{1,0:T(8,128)(2,1)S(1)} %copy-done.4, f32[768,512]{1,0:T(8,128)S(1)} %get-tuple-element.11, f32[768,512]{1,0:T(8,128)S(1)} %convolution_add_fusion), kind=kOutput, calls=%fused_computation.30 | convolution fusion | flops 410517504 | bytes 5242880 | tf_op jit(solution)/shard_map/dot_general | solution.py:71
  26.6 1.4 %collective-permute-done.4 = bf16[280,512]{1,0:T(8,128)(2,1)S(1)} collective-permute-done((bf16[280,512]{1,0:T(8,128)(2,1)S(1)}, bf16[280,512]{1,0:T(8,128)(2,1)S(1)}, u32[]{:S(2)}, u32[]{:S(2)}) %collective-permute-start.4) | collective-permute-done | bytes 286752 | tf_op jit(solution)/shard_map/ppermute | solution.py:158
  28.3 1.9 %collective-permute-start.5 = (bf16[140,512]{1,0:T(8,128)(2,1)S(1)}, bf16[140,512]{1,0:T(8,128)(2,1)S(1)}, u32[]{:S(2)}, u32[]{:S(2)}) collective-permute-start(bf16[140,512]{1,0:T(8,128)(2,1)S(1)} %select_convert_fusion.1), channel_id=1, source_target_pairs={{0,2},{1,3},{2,0},{3,1},{4,6},{5,7},{6,4},{7,5},{8,10},{9,11},{10,... | collective-permute-start | bytes 430088 | tf_op jit(solution)/shard_map/ppermute | solution.py:158
  30.2 4.2 %collective-permute-done.5 = bf16[140,512]{1,0:T(8,128)(2,1)S(1)} collective-permute-done((bf16[140,512]{1,0:T(8,128)(2,1)S(1)}, bf16[140,512]{1,0:T(8,128)(2,1)S(1)}, u32[]{:S(2)}, u32[]{:S(2)}) %collective-permute-start.5) | collective-permute-done | bytes 143392 | tf_op jit(solution)/shard_map/ppermute | solution.py:158
  34.4 1.9 %collective-permute-start.6 = (bf16[140,512]{1,0:T(8,128)(2,1)S(1)}, bf16[140,512]{1,0:T(8,128)(2,1)S(1)}, u32[]{:S(2)}, u32[]{:S(2)}) collective-permute-start(bf16[140,512]{1,0:T(8,128)(2,1)S(1)} %add_convert_fusion.7), channel_id=1, source_target_pairs={{0,4},{1,5},{2,6},{3,7},{4,0},{5,1},{6,2},{7,3},{8,12},{9,13},{10,... | collective-permute-start | bytes 430088 | tf_op jit(solution)/shard_map/ppermute | solution.py:164
  36.3 3.4 %collective-permute-done.6 = bf16[140,512]{1,0:T(8,128)(2,1)S(1)} collective-permute-done((bf16[140,512]{1,0:T(8,128)(2,1)S(1)}, bf16[140,512]{1,0:T(8,128)(2,1)S(1)}, u32[]{:S(2)}, u32[]{:S(2)}) %collective-permute-start.6) | collective-permute-done | bytes 143392 | tf_op jit(solution)/shard_map/ppermute | solution.py:164
  39.7 2.8 %collective-permute-start.7 = (bf16[140,512]{1,0:T(8,128)(2,1)S(1)}, bf16[140,512]{1,0:T(8,128)(2,1)S(1)}, u32[]{:S(2)}, u32[]{:S(2)}) collective-permute-start(bf16[140,512]{1,0:T(8,128)(2,1)S(1)} %add_convert_fusion.6), channel_id=1, source_target_pairs={{0,8},{1,9},{2,10},{3,11},{4,12},{5,13},{6,14},{7,15},{8,0},{9,1},... | collective-permute-start | bytes 430088 | tf_op jit(solution)/shard_map/ppermute | solution.py:164
  42.5 5.3 %collective-permute-done.7 = bf16[140,512]{1,0:T(8,128)(2,1)S(1)} collective-permute-done((bf16[140,512]{1,0:T(8,128)(2,1)S(1)}, bf16[140,512]{1,0:T(8,128)(2,1)S(1)}, u32[]{:S(2)}, u32[]{:S(2)}) %collective-permute-start.7) | collective-permute-done | bytes 143392 | tf_op jit(solution)/shard_map/ppermute | solution.py:164
  47.9 1.6 %collective-permute-start.8 = (bf16[140,512]{1,0:T(8,128)(2,1)S(1)}, bf16[140,512]{1,0:T(8,128)(2,1)S(1)}, u32[]{:S(2)}, u32[]{:S(2)}) collective-permute-start(bf16[140,512]{1,0:T(8,128)(2,1)S(1)} %add_convert_fusion.5), channel_id=1, source_target_pairs={{0,2},{1,3},{2,0},{3,1},{4,6},{5,7},{6,4},{7,5},{8,10},{9,11},{10,... | collective-permute-start | bytes 430088 | tf_op jit(solution)/shard_map/ppermute | solution.py:169
  49.6 3.6 %collective-permute-done.8 = bf16[140,512]{1,0:T(8,128)(2,1)S(1)} collective-permute-done((bf16[140,512]{1,0:T(8,128)(2,1)S(1)}, bf16[140,512]{1,0:T(8,128)(2,1)S(1)}, u32[]{:S(2)}, u32[]{:S(2)}) %collective-permute-start.8) | collective-permute-done | bytes 143392 | tf_op jit(solution)/shard_map/ppermute | solution.py:169
  53.3 1.6 %collective-permute-done.9 = bf16[280,512]{1,0:T(8,128)(2,1)S(1)} collective-permute-done((bf16[280,512]{1,0:T(8,128)(2,1)S(1)}, bf16[280,512]{1,0:T(8,128)(2,1)S(1)}, u32[]{:S(2)}, u32[]{:S(2)}) %collective-permute-start.9) | collective-permute-done | bytes 286752 | tf_op jit(solution)/shard_map/ppermute | solution.py:169
  56.0 1.3 %fusion.30 = f32[512,512]{1,0:T(8,128)} fusion(bf16[32,512]{1,0:T(8,128)(2,1)S(1)} %convolution_convert_fusion.1, bf16[560,512]{1,0:T(8,128)(2,1)S(1)} %maximum_select_fusion), kind=kOutput, calls=%fused_computation.61 | convolution fusion | flops 16777216 | bytes 1114112 | tf_op jit(solution)/shard_map/dot_general | solution.py:91
  57.2 1.1 %slice_convert_fusion = f32[512,512]{1,0:T(8,128)} fusion(bf16[560,512]{1,0:T(8,128)(2,1)S(1)} %maximum_select_fusion), kind=kLoop, calls=%fused_computation.37 | loop fusion | flops 262144 | bytes 1572864 | tf_op jit(solution)/shard_map/convert_element_type | solution.py:242
  58.4 2.9 %fusion.8 = f32[2048,512]{1,0:T(8,128)} fusion(bf16[32,512]{1,0:T(8,128)(2,1)S(1)} %fusion.9, bf16[32,2560]{1,0:T(8,128)(2,1)S(1)} %maximum_select_fusion.2, s32[32]{0:T(128)S(1)} %eq.40), kind=kOutput, calls=%fused_computation.18 | convolution fusion | flops 71369728 | bytes 4358656 | tf_op jit(solution)/shard_map/dot_general | solution.py:98
  (59 shorter events, 8.0 us)
Async XLA Ops:
  0.6 1.6 %copy-start = (bf16[2048,512]{1,0:T(8,128)(2,1)S(1)}, bf16[2048,512]{1,0:T(8,128)(2,1)}, u32[]{:S(2)}) copy-start(bf16[2048,512]{1,0:T(8,128)(2,1)} %param.12) | copy-start | bytes 6291460
  0.6 2.7 %copy-start.6 = (bf16[2,2048]{1,0:T(2,128)(2,1)S(1)}, bf16[2,2048]{1,0:T(2,128)(2,1)}, u32[]{:S(2)}) copy-start(bf16[2,2048]{1,0:T(2,128)(2,1)} %param.9) | copy-start | bytes 24580
  0.7 10.5 %copy-start.7 = (bf16[24,512]{1,0:T(8,128)(2,1)S(1)}, bf16[24,512]{1,0:T(8,128)(2,1)}, u32[]{:S(2)}) copy-start(bf16[24,512]{1,0:T(8,128)(2,1)} %param.14) | copy-start | bytes 73732
  0.7 14.3 %copy-start.8 = (f32[2,256]{1,0:T(2,128)S(1)}, f32[2,256]{1,0:T(2,128)}, u32[]{:S(2)}) copy-start(f32[2,256]{1,0:T(2,128)} %param.15) | copy-start | bytes 6148
  0.7 14.3 %copy-start.9 = (s32[32]{0:T(128)S(1)}, s32[32]{0:T(128)}, u32[]{:S(2)}) copy-start(s32[32]{0:T(128)} %param.11) | copy-start | bytes 388
  0.7 17.9 %copy-start.1 = (bf16[512,512]{1,0:T(8,128)(2,1)S(1)}, bf16[512,512]{1,0:T(8,128)(2,1)}, u32[]{:S(2)}) copy-start(bf16[512,512]{1,0:T(8,128)(2,1)} %param.13) | copy-start | bytes 1572868
  3.3 15.7 %copy-start.4 = (bf16[512,512]{1,0:T(8,128)(2,1)S(1)}, bf16[512,512]{1,0:T(8,128)(2,1)}, u32[]{:S(2)}) copy-start(bf16[512,512]{1,0:T(8,128)(2,1)} %constant.107.clone) | copy-start | bytes 1572868
  3.3 5.8 %collective-permute-start = (bf16[2,2560]{1,0:T(2,128)(2,1)S(1)}, bf16[2,2560]{1,0:T(2,128)(2,1)S(1)}, u32[]{:S(2)}, u32[]{:S(2)}) collective-permute-start(bf16[2,2560]{1,0:T(2,128)(2,1)S(1)} %pad_maximum_fusion.2), channel_id=1, source_target_pairs={{0,8},{1,9},{2,10},{3,11},{4,12},{5,13},{6,14},{7,15},{8,0},{9,1},... | collective-permute-start | bytes 30728 | tf_op jit(solution)/shard_map/ppermute | solution.py:119
  9.1 3.8 %collective-permute-start.1 = (bf16[4,2560]{1,0:T(4,128)(2,1)S(1)}, bf16[4,2560]{1,0:T(4,128)(2,1)S(1)}, u32[]{:S(2)}, u32[]{:S(2)}) collective-permute-start(bf16[4,2560]{1,0:T(4,128)(2,1)S(1)} %maximum_select_fusion.5), channel_id=1, source_target_pairs={{0,4},{1,5},{2,6},{3,7},{4,0},{5,1},{6,2},{7,3},{8,12},{9,13},{10,... | collective-permute-start | bytes 61448 | tf_op jit(solution)/shard_map/ppermute | solution.py:119
  13.0 4.1 %collective-permute-start.2 = (bf16[8,2560]{1,0:T(8,128)(2,1)S(1)}, bf16[8,2560]{1,0:T(8,128)(2,1)S(1)}, u32[]{:S(2)}, u32[]{:S(2)}) collective-permute-start(bf16[8,2560]{1,0:T(8,128)(2,1)S(1)} %maximum_select_fusion.4), channel_id=1, source_target_pairs={{0,2},{1,3},{2,0},{3,1},{4,6},{5,7},{6,4},{7,5},{8,10},{9,11},{10,... | collective-permute-start | bytes 122888 | tf_op jit(solution)/shard_map/ppermute | solution.py:119
  17.1 1.3 %collective-permute-start.3 = (bf16[16,2560]{1,0:T(8,128)(2,1)S(1)}, bf16[16,2560]{1,0:T(8,128)(2,1)S(1)}, u32[]{:S(2)}, u32[]{:S(2)}) collective-permute-start(bf16[16,2560]{1,0:T(8,128)(2,1)S(1)} %maximum_select_fusion.3), channel_id=1, source_target_pairs={{0,1},{1,0},{2,3},{3,2},{4,5},{5,4},{6,7},{7,6},{8,9},{9,8},{10,11... | collective-permute-start | bytes 245768 | tf_op jit(solution)/shard_map/ppermute | solution.py:119
  19.0 1.0 %copy-start.2 = (bf16[512,256]{1,0:T(8,128)(2,1)S(1)}, bf16[512,256]{1,0:T(8,128)(2,1)}, u32[]{:S(2)}) copy-start(bf16[512,256]{1,0:T(8,128)(2,1)} %constant.113) | copy-start | bytes 786436
  19.6 1.0 %copy-start.5 = (bf16[512,256]{1,0:T(8,128)(2,1)S(1)}, bf16[512,256]{1,0:T(8,128)(2,1)}, u32[]{:S(2)}) copy-start(bf16[512,256]{1,0:T(8,128)(2,1)} %constant.114) | copy-start | bytes 786436
  20.5 1.0 %copy-start.3 = (bf16[512,512]{1,0:T(8,128)(2,1)S(1)}, bf16[512,512]{1,0:T(8,128)(2,1)}, u32[]{:S(2)}) copy-start(bf16[512,512]{1,0:T(8,128)(2,1)} %param.16) | copy-start | bytes 1572868
  20.5 1.3 %copy-start.10 = (bf16[32,24,512]{2,1,0:T(8,128)(2,1)S(1)}, bf16[32,24,512]{2,1,0:T(8,128)(2,1)}, u32[]{:S(2)}) copy-start(bf16[32,24,512]{2,1,0:T(8,128)(2,1)} %param.10) | copy-start | bytes 2359300
  26.4 1.6 %collective-permute-start.4 = (bf16[280,512]{1,0:T(8,128)(2,1)S(1)}, bf16[280,512]{1,0:T(8,128)(2,1)S(1)}, u32[]{:S(2)}, u32[]{:S(2)}) collective-permute-start(bf16[280,512]{1,0:T(8,128)(2,1)S(1)} %select_convert_fusion), channel_id=1, source_target_pairs={{0,1},{1,0},{2,3},{3,2},{4,5},{5,4},{6,7},{7,6},{8,9},{9,8},{10,11... | collective-permute-start | bytes 860168 | tf_op jit(solution)/shard_map/ppermute | solution.py:158
  28.3 6.1 %collective-permute-start.5 = (bf16[140,512]{1,0:T(8,128)(2,1)S(1)}, bf16[140,512]{1,0:T(8,128)(2,1)S(1)}, u32[]{:S(2)}, u32[]{:S(2)}) collective-permute-start(bf16[140,512]{1,0:T(8,128)(2,1)S(1)} %select_convert_fusion.1), channel_id=1, source_target_pairs={{0,2},{1,3},{2,0},{3,1},{4,6},{5,7},{6,4},{7,5},{8,10},{9,11},{10,... | collective-permute-start | bytes 430088 | tf_op jit(solution)/shard_map/ppermute | solution.py:158
  34.4 5.3 %collective-permute-start.6 = (bf16[140,512]{1,0:T(8,128)(2,1)S(1)}, bf16[140,512]{1,0:T(8,128)(2,1)S(1)}, u32[]{:S(2)}, u32[]{:S(2)}) collective-permute-start(bf16[140,512]{1,0:T(8,128)(2,1)S(1)} %add_convert_fusion.7), channel_id=1, source_target_pairs={{0,4},{1,5},{2,6},{3,7},{4,0},{5,1},{6,2},{7,3},{8,12},{9,13},{10,... | collective-permute-start | bytes 430088 | tf_op jit(solution)/shard_map/ppermute | solution.py:164
  39.7 8.1 %collective-permute-start.7 = (bf16[140,512]{1,0:T(8,128)(2,1)S(1)}, bf16[140,512]{1,0:T(8,128)(2,1)S(1)}, u32[]{:S(2)}, u32[]{:S(2)}) collective-permute-start(bf16[140,512]{1,0:T(8,128)(2,1)S(1)} %add_convert_fusion.6), channel_id=1, source_target_pairs={{0,8},{1,9},{2,10},{3,11},{4,12},{5,13},{6,14},{7,15},{8,0},{9,1},... | collective-permute-start | bytes 430088 | tf_op jit(solution)/shard_map/ppermute | solution.py:164
  47.9 5.2 %collective-permute-start.8 = (bf16[140,512]{1,0:T(8,128)(2,1)S(1)}, bf16[140,512]{1,0:T(8,128)(2,1)S(1)}, u32[]{:S(2)}, u32[]{:S(2)}) collective-permute-start(bf16[140,512]{1,0:T(8,128)(2,1)S(1)} %add_convert_fusion.5), channel_id=1, source_target_pairs={{0,2},{1,3},{2,0},{3,1},{4,6},{5,7},{6,4},{7,5},{8,10},{9,11},{10,... | collective-permute-start | bytes 430088 | tf_op jit(solution)/shard_map/ppermute | solution.py:169
  53.2 1.6 %collective-permute-start.9 = (bf16[280,512]{1,0:T(8,128)(2,1)S(1)}, bf16[280,512]{1,0:T(8,128)(2,1)S(1)}, u32[]{:S(2)}, u32[]{:S(2)}) collective-permute-start(bf16[280,512]{1,0:T(8,128)(2,1)S(1)} %maximum_select_fusion.1), channel_id=1, source_target_pairs={{0,1},{1,0},{2,3},{3,2},{4,5},{5,4},{6,7},{7,6},{8,9},{9,8},{10,11... | collective-permute-start | bytes 860168 | tf_op jit(solution)/shard_map/ppermute | solution.py:169

commit v17 on v13

--- a/solution.py
+++ b/solution.py
@@ -233,7 +233,10 @@
         ],
         0,
     )
-    packed = sum_halving(packed, "freq")
+    columns = packed.shape[1] // 2
+    packed = jnp.concatenate(
+        [sum_halving(packed[:, :columns], "freq"), sum_halving(packed[:, columns:], "freq")], 1
+    )
     rows_out = grad_out.shape[0]
     grad_out = packed[:rows_out].astype(jnp.float32)
     derivative_bottleneck = packed[rows_out : rows_out + samples].astype(jnp.float32)

time: 60.1 us -> 58.6 us (0.975)
  waiting for transfers between devices: 23.9 us -> 17.2 us
  starting transfers between devices: 16.6 us -> 21.6 us
    ppermute x2 -> x4, waiting for transfers between devices: 8.73 us -> 4.26 us  [sum_halving(): arrived = lax.ppermute(values, axis_name, _exchange_pairs(count, distance))]
    ppermute x2 -> x4, starting transfers between devices: 4.7 us -> 7.77 us  [sum_halving(): arrived = lax.ppermute(values, axis_name, _exchange_pairs(count, distance))]
    ppermute x2 -> x4, waiting for transfers between devices: 5.59 us -> 3.7 us  [sum_halving(): arrived = lax.ppermute(send, axis_name, _exchange_pairs(count, distance))]
    ppermute x2 -> x4, starting transfers between devices: 1.71 us -> 2.98 us  [sum_halving(): other = lax.ppermute(values, axis_name, _exchange_pairs(count, distance))]
    ppermute x2 -> x4, waiting for transfers between devices: 5.12 us -> 4.33 us  [sum_halving(): other = lax.ppermute(values, axis_name, _exchange_pairs(count, distance))]
    ppermute x2 -> x4, starting transfers between devices: 2.12 us -> 2.79 us  [sum_halving(): arrived = lax.ppermute(send, axis_name, _exchange_pairs(count, distance))]
  transfers between devices with their start and end apart: 10 -> 16, of which waited for: 10 -> 11; matrix products, arithmetic and copies ran while one was open for 4% -> 5% of each run, Pallas kernels for 0% -> 0%
where the time goes in v17:
time: 58.6 us; the launch traced here: 58.3 us
  starting transfers between devices  21.6 us (37%)
  waiting for transfers between devices  17.2 us (29%)
  matrix products  10.8 us (18%)
  other arithmetic  4.88 us (8%)
  local copies, waits for them, and re-layouts  2.81 us (5%)
  between operations  0.92 us (2%)
    ppermute x4, starting transfers between devices, gather_rows(): other = lax.ppermute(block, axis_name, _exchange_pairs(count, distance))  8.06 us
    ppermute x4, starting transfers between devices, sum_halving(): arrived = lax.ppermute(values, axis_name, _exchange_pairs(count, distance))  7.77 us
    ppermute x4, waiting for transfers between devices, gather_rows(): other = lax.ppermute(block, axis_name, _exchange_pairs(count, distance))  4.91 us
    ppermute x4, waiting for transfers between devices, sum_halving(): other = lax.ppermute(values, axis_name, _exchange_pairs(count, distance))  4.33 us
    ppermute x4, waiting for transfers between devices, sum_halving(): arrived = lax.ppermute(values, axis_name, _exchange_pairs(count, distance))  4.26 us
    ppermute x4, waiting for transfers between devices, sum_halving(): arrived = lax.ppermute(send, axis_name, _exchange_pairs(count, distance))  3.7 us
    ppermute x4, starting transfers between devices, sum_halving(): other = lax.ppermute(values, axis_name, _exchange_pairs(count, distance))  2.98 us
    dot_general x1, matrix products, encoder_grads(): lax.dot_general(inputs_rows, grad_pre, (((0,), (0,)), ((), ())), preferre...  2.96 us
  transfers between devices with their start and end apart: 16, of which 11 were waited for; matrix products, arithmetic and copies ran while one was open for 5% of the time, Pallas kernels for 0%

profile of v17, /device:TPU:0, one launch (start us, length us, event | category | flops | bytes accessed | tf_op | source)
XLA Modules:
  0.0 58.3 jit_solution(11135825184256026774)
XLA Ops:
  0.6 4.1 %collective-permute-start = (bf16[2,2048]{1,0:T(2,128)(2,1)}, bf16[2,2048]{1,0:T(2,128)(2,1)S(1)}, u32[]{:S(2)}, u32[]{:S(2)}) collective-permute-start(bf16[2,2048]{1,0:T(2,128)(2,1)} %param.9), channel_id=1, source_target_pairs={{0,8},{1,9},{2,10},{3,11},{4,12},{5,13},{6,14},{7,15},{8,0},{9,1},... | collective-permute-start | bytes 24584 | tf_op jit(solution)/shard_map/ppermute | solution.py:119
  4.7 1.8 %collective-permute-done = bf16[2,2048]{1,0:T(2,128)(2,1)S(1)} collective-permute-done((bf16[2,2048]{1,0:T(2,128)(2,1)}, bf16[2,2048]{1,0:T(2,128)(2,1)S(1)}, u32[]{:S(2)}, u32[]{:S(2)}) %collective-permute-start) | collective-permute-done | bytes 8224 | tf_op jit(solution)/shard_map/ppermute | solution.py:119
  7.4 2.0 %collective-permute-start.1 = (bf16[4,2048]{1,0:T(4,128)(2,1)S(1)}, bf16[4,2048]{1,0:T(4,128)(2,1)S(1)}, u32[]{:S(2)}, u32[]{:S(2)}) collective-permute-start(bf16[4,2048]{1,0:T(4,128)(2,1)S(1)} %maximum_select_fusion.8), channel_id=1, source_target_pairs={{0,4},{1,5},{2,6},{3,7},{4,0},{5,1},{6,2},{7,3},{8,12},{9,13},{10,... | collective-permute-start | bytes 49160 | tf_op jit(solution)/shard_map/ppermute | solution.py:119
  9.4 1.8 %collective-permute-done.1 = bf16[4,2048]{1,0:T(4,128)(2,1)S(1)} collective-permute-done((bf16[4,2048]{1,0:T(4,128)(2,1)S(1)}, bf16[4,2048]{1,0:T(4,128)(2,1)S(1)}, u32[]{:S(2)}, u32[]{:S(2)}) %collective-permute-start.1) | collective-permute-done | bytes 16416 | tf_op jit(solution)/shard_map/ppermute | solution.py:119
  11.3 1.9 %collective-permute-start.2 = (bf16[8,2048]{1,0:T(8,128)(2,1)S(1)}, bf16[8,2048]{1,0:T(8,128)(2,1)S(1)}, u32[]{:S(2)}, u32[]{:S(2)}) collective-permute-start(bf16[8,2048]{1,0:T(8,128)(2,1)S(1)} %maximum_select_fusion.7), channel_id=1, source_target_pairs={{0,2},{1,3},{2,0},{3,1},{4,6},{5,7},{6,4},{7,5},{8,10},{9,11},{10,... | collective-permute-start | bytes 98312 | tf_op jit(solution)/shard_map/ppermute | solution.py:119
  14.0 1.2 %collective-permute-done.2 = bf16[8,2048]{1,0:T(8,128)(2,1)S(1)} collective-permute-done((bf16[8,2048]{1,0:T(8,128)(2,1)S(1)}, bf16[8,2048]{1,0:T(8,128)(2,1)S(1)}, u32[]{:S(2)}, u32[]{:S(2)}) %collective-permute-start.2) | collective-permute-done | bytes 32800 | tf_op jit(solution)/shard_map/ppermute | solution.py:119
  23.0 1.2 %fusion.11 = f32[768,512]{1,0:T(8,128)S(1)} fusion(bf16[512,512]{1,0:T(8,128)(2,1)S(1)} %copy-done.4, f32[768,512]{1,0:T(8,128)S(1)} %get-tuple-element.15, f32[768,512]{1,0:T(8,128)S(1)} %convolution_add_fusion), kind=kOutput, calls=%fused_computation.30 | convolution fusion | flops 410517504 | bytes 5242880 | tf_op jit(solution)/shard_map/dot_general | solution.py:71
  26.4 0.9 %collective-permute-done.10 = bf16[280,256]{1,0:T(8,128)(2,1)S(1)} collective-permute-done((bf16[280,256]{1,0:T(8,128)(2,1)S(1)}, bf16[280,256]{1,0:T(8,128)(2,1)S(1)}, u32[]{:S(2)}, u32[]{:S(2)}) %collective-permute-start.10) | collective-permute-done | bytes 143392 | tf_op jit(solution)/shard_map/ppermute | solution.py:158
  27.8 1.9 %collective-permute-start.5 = (bf16[140,256]{1,0:T(8,128)(2,1)S(1)}, bf16[140,256]{1,0:T(8,128)(2,1)S(1)}, u32[]{:S(2)}, u32[]{:S(2)}) collective-permute-start(bf16[140,256]{1,0:T(8,128)(2,1)S(1)} %select_convert_fusion.3), channel_id=1, source_target_pairs={{0,2},{1,3},{2,0},{3,1},{4,6},{5,7},{6,4},{7,5},{8,10},{9,11},{10,... | collective-permute-start | bytes 215048 | tf_op jit(solution)/shard_map/ppermute | solution.py:158
  30.0 2.4 %collective-permute-done.5 = bf16[140,256]{1,0:T(8,128)(2,1)S(1)} collective-permute-done((bf16[140,256]{1,0:T(8,128)(2,1)S(1)}, bf16[140,256]{1,0:T(8,128)(2,1)S(1)}, u32[]{:S(2)}, u32[]{:S(2)}) %collective-permute-start.5) | collective-permute-done | bytes 71712 | tf_op jit(solution)/shard_map/ppermute | solution.py:158
  32.5 2.1 %collective-permute-start.6 = (bf16[140,256]{1,0:T(8,128)(2,1)S(1)}, bf16[140,256]{1,0:T(8,128)(2,1)S(1)}, u32[]{:S(2)}, u32[]{:S(2)}) collective-permute-start(bf16[140,256]{1,0:T(8,128)(2,1)S(1)} %add_convert_fusion.10), channel_id=1, source_target_pairs={{0,4},{1,5},{2,6},{3,7},{4,0},{5,1},{6,2},{7,3},{8,12},{9,13},{10,... | collective-permute-start | bytes 215048 | tf_op jit(solution)/shard_map/ppermute | solution.py:164
  34.6 1.3 %collective-permute-start.12 = (bf16[140,256]{1,0:T(8,128)(2,1)S(1)}, bf16[140,256]{1,0:T(8,128)(2,1)S(1)}, u32[]{:S(2)}, u32[]{:S(2)}) collective-permute-start(bf16[140,256]{1,0:T(8,128)(2,1)S(1)} %add_convert_fusion.7), channel_id=1, source_target_pairs={{0,4},{1,5},{2,6},{3,7},{4,0},{5,1},{6,2},{7,3},{8,12},{9,13},{10,... | collective-permute-start | bytes 215048 | tf_op jit(solution)/shard_map/ppermute | solution.py:164
  35.9 1.8 %collective-permute-done.6 = bf16[140,256]{1,0:T(8,128)(2,1)S(1)} collective-permute-done((bf16[140,256]{1,0:T(8,128)(2,1)S(1)}, bf16[140,256]{1,0:T(8,128)(2,1)S(1)}, u32[]{:S(2)}, u32[]{:S(2)}) %collective-permute-start.6) | collective-permute-done | bytes 71712 | tf_op jit(solution)/shard_map/ppermute | solution.py:164
  37.7 2.7 %collective-permute-start.7 = (bf16[140,256]{1,0:T(8,128)(2,1)S(1)}, bf16[140,256]{1,0:T(8,128)(2,1)S(1)}, u32[]{:S(2)}, u32[]{:S(2)}) collective-permute-start(bf16[140,256]{1,0:T(8,128)(2,1)S(1)} %add_convert_fusion.9), channel_id=1, source_target_pairs={{0,8},{1,9},{2,10},{3,11},{4,12},{5,13},{6,14},{7,15},{8,0},{9,1},... | collective-permute-start | bytes 215048 | tf_op jit(solution)/shard_map/ppermute | solution.py:164
  40.4 1.7 %collective-permute-start.13 = (bf16[140,256]{1,0:T(8,128)(2,1)S(1)}, bf16[140,256]{1,0:T(8,128)(2,1)S(1)}, u32[]{:S(2)}, u32[]{:S(2)}) collective-permute-start(bf16[140,256]{1,0:T(8,128)(2,1)S(1)} %add_convert_fusion.6), channel_id=1, source_target_pairs={{0,8},{1,9},{2,10},{3,11},{4,12},{5,13},{6,14},{7,15},{8,0},{9,1},... | collective-permute-start | bytes 215048 | tf_op jit(solution)/shard_map/ppermute | solution.py:164
  42.1 2.5 %collective-permute-done.7 = bf16[140,256]{1,0:T(8,128)(2,1)S(1)} collective-permute-done((bf16[140,256]{1,0:T(8,128)(2,1)S(1)}, bf16[140,256]{1,0:T(8,128)(2,1)S(1)}, u32[]{:S(2)}, u32[]{:S(2)}) %collective-permute-start.7) | collective-permute-done | bytes 71712 | tf_op jit(solution)/shard_map/ppermute | solution.py:164
  44.6 1.7 %collective-permute-start.8 = (bf16[140,256]{1,0:T(8,128)(2,1)S(1)}, bf16[140,256]{1,0:T(8,128)(2,1)S(1)}, u32[]{:S(2)}, u32[]{:S(2)}) collective-permute-start(bf16[140,256]{1,0:T(8,128)(2,1)S(1)} %add_convert_fusion.8), channel_id=1, source_target_pairs={{0,2},{1,3},{2,0},{3,1},{4,6},{5,7},{6,4},{7,5},{8,10},{9,11},{10,... | collective-permute-start | bytes 215048 | tf_op jit(solution)/shard_map/ppermute | solution.py:169
  46.3 1.2 %collective-permute-start.14 = (bf16[140,256]{1,0:T(8,128)(2,1)S(1)}, bf16[140,256]{1,0:T(8,128)(2,1)S(1)}, u32[]{:S(2)}, u32[]{:S(2)}) collective-permute-start(bf16[140,256]{1,0:T(8,128)(2,1)S(1)} %add_convert_fusion.5), channel_id=1, source_target_pairs={{0,2},{1,3},{2,0},{3,1},{4,6},{5,7},{6,4},{7,5},{8,10},{9,11},{10,... | collective-permute-start | bytes 215048 | tf_op jit(solution)/shard_map/ppermute | solution.py:169
  47.5 1.6 %collective-permute-done.8 = bf16[140,256]{1,0:T(8,128)(2,1)S(1)} collective-permute-done((bf16[140,256]{1,0:T(8,128)(2,1)S(1)}, bf16[140,256]{1,0:T(8,128)(2,1)S(1)}, u32[]{:S(2)}, u32[]{:S(2)}) %collective-permute-start.8) | collective-permute-done | bytes 71712 | tf_op jit(solution)/shard_map/ppermute | solution.py:169
  49.2 1.6 %collective-permute-done.14 = bf16[140,256]{1,0:T(8,128)(2,1)S(1)} collective-permute-done((bf16[140,256]{1,0:T(8,128)(2,1)S(1)}, bf16[140,256]{1,0:T(8,128)(2,1)S(1)}, u32[]{:S(2)}, u32[]{:S(2)}) %collective-permute-start.14) | collective-permute-done | bytes 71712 | tf_op jit(solution)/shard_map/ppermute | solution.py:169
  51.0 1.2 %collective-permute-done.15 = bf16[280,256]{1,0:T(8,128)(2,1)S(1)} collective-permute-done((bf16[280,256]{1,0:T(8,128)(2,1)S(1)}, bf16[280,256]{1,0:T(8,128)(2,1)S(1)}, u32[]{:S(2)}, u32[]{:S(2)}) %collective-permute-start.15) | collective-permute-done | bytes 143392 | tf_op jit(solution)/shard_map/ppermute | solution.py:169
  52.3 1.1 %fusion.13 = f32[512,512]{1,0:T(8,128)} fusion(bf16[560,256]{1,0:T(8,128)(2,1)S(1)} %maximum_select_fusion.1, bf16[560,256]{1,0:T(8,128)(2,1)S(1)} %maximum_select_fusion), kind=kLoop, calls=%fused_computation.32 | loop fusion | flops 1048576 | bytes 1622016 | tf_op jit(solution)/shard_map/convert_element_type | solution.py:241
  53.4 3.0 %fusion.10 = f32[2048,512]{1,0:T(8,128)} fusion(bf16[32,2048]{1,0:T(8,128)(2,1)S(1)} %convolution_convert_fusion, bf16[32,512]{1,0:T(8,128)(2,1)S(1)} %pad_maximum_fusion.1, bf16[512,512]{1,0:T(8,128)(2,1)S(1)} %copy-done.1, bf16[32,512]{1,0:T(8,128)(2,1)S(1)} %fusion.8), kind=kOutput, calls=%fused_computation.23 | convolution fusion | flops 83968000 | bytes 4915200 | tf_op jit(solution)/shard_map/dot_general | solution.py:98
  56.4 1.3 %fusion.49 = f32[512,512]{1,0:T(8,128)} fusion(bf16[32,512]{1,0:T(8,128)(2,1)S(1)} %fusion.8, bf16[32,512]{1,0:T(8,128)(2,1)S(1)} %pad_maximum_fusion.1), kind=kOutput, calls=%fused_computation.93 | convolution fusion | flops 16777216 | bytes 1114112 | tf_op jit(solution)/shard_map/dot_general | solution.py:91
  (68 shorter events, 13.4 us)
Async XLA Ops:
  0.6 16.6 %copy-start = (bf16[2048,512]{1,0:T(8,128)(2,1)S(1)}, bf16[2048,512]{1,0:T(8,128)(2,1)}, u32[]{:S(2)}) copy-start(bf16[2048,512]{1,0:T(8,128)(2,1)} %param.12) | copy-start | bytes 6291460
  0.6 5.9 %collective-permute-start = (bf16[2,2048]{1,0:T(2,128)(2,1)}, bf16[2,2048]{1,0:T(2,128)(2,1)S(1)}, u32[]{:S(2)}, u32[]{:S(2)}) collective-permute-start(bf16[2,2048]{1,0:T(2,128)(2,1)} %param.9), channel_id=1, source_target_pairs={{0,8},{1,9},{2,10},{3,11},{4,12},{5,13},{6,14},{7,15},{8,0},{9,1},... | collective-permute-start | bytes 24584 | tf_op jit(solution)/shard_map/ppermute | solution.py:119
  7.4 3.8 %collective-permute-start.1 = (bf16[4,2048]{1,0:T(4,128)(2,1)S(1)}, bf16[4,2048]{1,0:T(4,128)(2,1)S(1)}, u32[]{:S(2)}, u32[]{:S(2)}) collective-permute-start(bf16[4,2048]{1,0:T(4,128)(2,1)S(1)} %maximum_select_fusion.8), channel_id=1, source_target_pairs={{0,4},{1,5},{2,6},{3,7},{4,0},{5,1},{6,2},{7,3},{8,12},{9,13},{10,... | collective-permute-start | bytes 49160 | tf_op jit(solution)/shard_map/ppermute | solution.py:119
  11.2 6.5 %copy-start.1 = (bf16[512,512]{1,0:T(8,128)(2,1)S(1)}, bf16[512,512]{1,0:T(8,128)(2,1)}, u32[]{:S(2)}) copy-start(bf16[512,512]{1,0:T(8,128)(2,1)} %param.13) | copy-start | bytes 1572868
  11.3 4.0 %collective-permute-start.2 = (bf16[8,2048]{1,0:T(8,128)(2,1)S(1)}, bf16[8,2048]{1,0:T(8,128)(2,1)S(1)}, u32[]{:S(2)}, u32[]{:S(2)}) collective-permute-start(bf16[8,2048]{1,0:T(8,128)(2,1)S(1)} %maximum_select_fusion.7), channel_id=1, source_target_pairs={{0,2},{1,3},{2,0},{3,1},{4,6},{5,7},{6,4},{7,5},{8,10},{9,11},{10,... | collective-permute-start | bytes 98312 | tf_op jit(solution)/shard_map/ppermute | solution.py:119
  15.3 1.8 %collective-permute-start.3 = (bf16[16,2048]{1,0:T(8,128)(2,1)S(1)}, bf16[16,2048]{1,0:T(8,128)(2,1)S(1)}, u32[]{:S(2)}, u32[]{:S(2)}) collective-permute-start(bf16[16,2048]{1,0:T(8,128)(2,1)S(1)} %maximum_select_fusion.6), channel_id=1, source_target_pairs={{0,1},{1,0},{2,3},{3,2},{4,5},{5,4},{6,7},{7,6},{8,9},{9,8},{10,11... | collective-permute-start | bytes 196616 | tf_op jit(solution)/shard_map/ppermute | solution.py:119
  17.2 1.0 %copy-start.4 = (bf16[512,512]{1,0:T(8,128)(2,1)S(1)}, bf16[512,512]{1,0:T(8,128)(2,1)}, u32[]{:S(2)}) copy-start(bf16[512,512]{1,0:T(8,128)(2,1)} %constant.123.clone) | copy-start | bytes 1572868
  18.1 1.0 %copy-start.2 = (bf16[512,256]{1,0:T(8,128)(2,1)S(1)}, bf16[512,256]{1,0:T(8,128)(2,1)}, u32[]{:S(2)}) copy-start(bf16[512,256]{1,0:T(8,128)(2,1)} %constant.129) | copy-start | bytes 786436
  18.8 1.0 %copy-start.5 = (bf16[512,256]{1,0:T(8,128)(2,1)S(1)}, bf16[512,256]{1,0:T(8,128)(2,1)}, u32[]{:S(2)}) copy-start(bf16[512,256]{1,0:T(8,128)(2,1)} %constant.130) | copy-start | bytes 786436
  19.8 1.0 %copy-start.3 = (bf16[512,512]{1,0:T(8,128)(2,1)S(1)}, bf16[512,512]{1,0:T(8,128)(2,1)}, u32[]{:S(2)}) copy-start(bf16[512,512]{1,0:T(8,128)(2,1)} %param.16) | copy-start | bytes 1572868
  19.8 1.3 %copy-start.6 = (bf16[32,24,512]{2,1,0:T(8,128)(2,1)S(1)}, bf16[32,24,512]{2,1,0:T(8,128)(2,1)}, u32[]{:S(2)}) copy-start(bf16[32,24,512]{2,1,0:T(8,128)(2,1)} %param.10) | copy-start | bytes 2359300
  25.8 1.6 %collective-permute-start.10 = (bf16[280,256]{1,0:T(8,128)(2,1)S(1)}, bf16[280,256]{1,0:T(8,128)(2,1)S(1)}, u32[]{:S(2)}, u32[]{:S(2)}) collective-permute-start(bf16[280,256]{1,0:T(8,128)(2,1)S(1)} %get-tuple-element.9), channel_id=1, source_target_pairs={{0,1},{1,0},{2,3},{3,2},{4,5},{5,4},{6,7},{7,6},{8,9},{9,8},{10,11... | collective-permute-start | bytes 430088 | tf_op jit(solution)/shard_map/ppermute | solution.py:158
  26.3 1.4 %collective-permute-start.4 = (bf16[280,256]{1,0:T(8,128)(2,1)S(1)}, bf16[280,256]{1,0:T(8,128)(2,1)S(1)}, u32[]{:S(2)}, u32[]{:S(2)}) collective-permute-start(bf16[280,256]{1,0:T(8,128)(2,1)S(1)} %get-tuple-element.8), channel_id=1, source_target_pairs={{0,1},{1,0},{2,3},{3,2},{4,5},{5,4},{6,7},{7,6},{8,9},{9,8},{10,11... | collective-permute-start | bytes 430088 | tf_op jit(solution)/shard_map/ppermute | solution.py:158
  27.8 4.6 %collective-permute-start.5 = (bf16[140,256]{1,0:T(8,128)(2,1)S(1)}, bf16[140,256]{1,0:T(8,128)(2,1)S(1)}, u32[]{:S(2)}, u32[]{:S(2)}) collective-permute-start(bf16[140,256]{1,0:T(8,128)(2,1)S(1)} %select_convert_fusion.3), channel_id=1, source_target_pairs={{0,2},{1,3},{2,0},{3,1},{4,6},{5,7},{6,4},{7,5},{8,10},{9,11},{10,... | collective-permute-start | bytes 215048 | tf_op jit(solution)/shard_map/ppermute | solution.py:158
  29.8 4.8 %collective-permute-start.11 = (bf16[140,256]{1,0:T(8,128)(2,1)S(1)}, bf16[140,256]{1,0:T(8,128)(2,1)S(1)}, u32[]{:S(2)}, u32[]{:S(2)}) collective-permute-start(bf16[140,256]{1,0:T(8,128)(2,1)S(1)} %select_convert_fusion.2), channel_id=1, source_target_pairs={{0,2},{1,3},{2,0},{3,1},{4,6},{5,7},{6,4},{7,5},{8,10},{9,11},{10,... | collective-permute-start | bytes 215048 | tf_op jit(solution)/shard_map/ppermute | solution.py:158
  32.5 5.2 %collective-permute-start.6 = (bf16[140,256]{1,0:T(8,128)(2,1)S(1)}, bf16[140,256]{1,0:T(8,128)(2,1)S(1)}, u32[]{:S(2)}, u32[]{:S(2)}) collective-permute-start(bf16[140,256]{1,0:T(8,128)(2,1)S(1)} %add_convert_fusion.10), channel_id=1, source_target_pairs={{0,4},{1,5},{2,6},{3,7},{4,0},{5,1},{6,2},{7,3},{8,12},{9,13},{10,... | collective-permute-start | bytes 215048 | tf_op jit(solution)/shard_map/ppermute | solution.py:164
  34.6 5.7 %collective-permute-start.12 = (bf16[140,256]{1,0:T(8,128)(2,1)S(1)}, bf16[140,256]{1,0:T(8,128)(2,1)S(1)}, u32[]{:S(2)}, u32[]{:S(2)}) collective-permute-start(bf16[140,256]{1,0:T(8,128)(2,1)S(1)} %add_convert_fusion.7), channel_id=1, source_target_pairs={{0,4},{1,5},{2,6},{3,7},{4,0},{5,1},{6,2},{7,3},{8,12},{9,13},{10,... | collective-permute-start | bytes 215048 | tf_op jit(solution)/shard_map/ppermute | solution.py:164
  37.7 6.9 %collective-permute-start.7 = (bf16[140,256]{1,0:T(8,128)(2,1)S(1)}, bf16[140,256]{1,0:T(8,128)(2,1)S(1)}, u32[]{:S(2)}, u32[]{:S(2)}) collective-permute-start(bf16[140,256]{1,0:T(8,128)(2,1)S(1)} %add_convert_fusion.9), channel_id=1, source_target_pairs={{0,8},{1,9},{2,10},{3,11},{4,12},{5,13},{6,14},{7,15},{8,0},{9,1},... | collective-permute-start | bytes 215048 | tf_op jit(solution)/shard_map/ppermute | solution.py:164
  40.4 5.9 %collective-permute-start.13 = (bf16[140,256]{1,0:T(8,128)(2,1)S(1)}, bf16[140,256]{1,0:T(8,128)(2,1)S(1)}, u32[]{:S(2)}, u32[]{:S(2)}) collective-permute-start(bf16[140,256]{1,0:T(8,128)(2,1)S(1)} %add_convert_fusion.6), channel_id=1, source_target_pairs={{0,8},{1,9},{2,10},{3,11},{4,12},{5,13},{6,14},{7,15},{8,0},{9,1},... | collective-permute-start | bytes 215048 | tf_op jit(solution)/shard_map/ppermute | solution.py:164
  44.6 4.4 %collective-permute-start.8 = (bf16[140,256]{1,0:T(8,128)(2,1)S(1)}, bf16[140,256]{1,0:T(8,128)(2,1)S(1)}, u32[]{:S(2)}, u32[]{:S(2)}) collective-permute-start(bf16[140,256]{1,0:T(8,128)(2,1)S(1)} %add_convert_fusion.8), channel_id=1, source_target_pairs={{0,2},{1,3},{2,0},{3,1},{4,6},{5,7},{6,4},{7,5},{8,10},{9,11},{10,... | collective-permute-start | bytes 215048 | tf_op jit(solution)/shard_map/ppermute | solution.py:169
  46.3 4.4 %collective-permute-start.14 = (bf16[140,256]{1,0:T(8,128)(2,1)S(1)}, bf16[140,256]{1,0:T(8,128)(2,1)S(1)}, u32[]{:S(2)}, u32[]{:S(2)}) collective-permute-start(bf16[140,256]{1,0:T(8,128)(2,1)S(1)} %add_convert_fusion.5), channel_id=1, source_target_pairs={{0,2},{1,3},{2,0},{3,1},{4,6},{5,7},{6,4},{7,5},{8,10},{9,11},{10,... | collective-permute-start | bytes 215048 | tf_op jit(solution)/shard_map/ppermute | solution.py:169
  49.1 1.8 %collective-permute-start.9 = (bf16[280,256]{1,0:T(8,128)(2,1)S(1)}, bf16[280,256]{1,0:T(8,128)(2,1)S(1)}, u32[]{:S(2)}, u32[]{:S(2)}) collective-permute-start(bf16[280,256]{1,0:T(8,128)(2,1)S(1)} %maximum_select_fusion.2), channel_id=1, source_target_pairs={{0,1},{1,0},{2,3},{3,2},{4,5},{5,4},{6,7},{7,6},{8,9},{9,8},{10,11... | collective-permute-start | bytes 430088 | tf_op jit(solution)/shard_map/ppermute | solution.py:169
  50.8 1.4 %collective-permute-start.15 = (bf16[280,256]{1,0:T(8,128)(2,1)S(1)}, bf16[280,256]{1,0:T(8,128)(2,1)S(1)}, u32[]{:S(2)}, u32[]{:S(2)}) collective-permute-start(bf16[280,256]{1,0:T(8,128)(2,1)S(1)} %maximum_select_fusion.3), channel_id=1, source_target_pairs={{0,1},{1,0},{2,3},{3,2},{4,5},{5,4},{6,7},{7,6},{8,9},{9,8},{10,11... | collective-permute-start | bytes 430088 | tf_op jit(solution)/shard_map/ppermute | solution.py:169

commit v18 on v17

--- a/solution.py
+++ b/solution.py
@@ -233,9 +233,14 @@
         ],
         0,
     )
-    columns = packed.shape[1] // 2
+    pieces = 4 if width % (4 * 128) == 0 else 1
+    columns = width // pieces
     packed = jnp.concatenate(
-        [sum_halving(packed[:, :columns], "freq"), sum_halving(packed[:, columns:], "freq")], 1
+        [
+            sum_halving(packed[:, piece * columns : (piece + 1) * columns], "freq")
+            for piece in range(pieces)
+        ],
+        1,
     )
     rows_out = grad_out.shape[0]
     grad_out = packed[:rows_out].astype(jnp.float32)

time: 58.6 us -> 59.9 us (1.022)
  starting transfers between devices: 21.6 us -> 30.5 us
  waiting for transfers between devices: 17.2 us -> 9.61 us
    ppermute x4 -> x8, starting transfers between devices: 7.77 us -> 11.9 us  [sum_halving(): arrived = lax.ppermute(values, axis_name, _exchange_pairs(count, distance))]
    ppermute x4 -> x8, waiting for transfers between devices: 4.26 us -> 0.33 us  [sum_halving(): arrived = lax.ppermute(values, axis_name, _exchange_pairs(count, distance))]
    ppermute x4 -> x8, starting transfers between devices: 2.79 us -> 5.46 us  [sum_halving(): arrived = lax.ppermute(send, axis_name, _exchange_pairs(count, distance))]
    ppermute x4 -> x8, waiting for transfers between devices: 3.7 us -> 1.19 us  [sum_halving(): arrived = lax.ppermute(send, axis_name, _exchange_pairs(count, distance))]
    ppermute x4 -> x8, starting transfers between devices: 2.98 us -> 5.01 us  [sum_halving(): other = lax.ppermute(values, axis_name, _exchange_pairs(count, distance))]
    ppermute x4 -> x8, waiting for transfers between devices: 4.33 us -> 3.17 us  [sum_halving(): other = lax.ppermute(values, axis_name, _exchange_pairs(count, distance))]
  transfers between devices with their start and end apart: 16 -> 28, of which waited for: 11 -> 13; matrix products, arithmetic and copies ran while one was open for 5% -> 6% of each run, Pallas kernels for 0% -> 0%
where the time goes in v18:
time: 59.9 us; the launch traced here: 59.6 us
  starting transfers between devices  30.5 us (51%)
  matrix products  10.9 us (18%)
  waiting for transfers between devices  9.61 us (16%)
  other arithmetic  4.82 us (8%)
  local copies, waits for them, and re-layouts  2.81 us (5%)
  between operations  1.01 us (2%)
    ppermute x8, starting transfers between devices, sum_halving(): arrived = lax.ppermute(values, axis_name, _exchange_pairs(count, distance))  11.9 us
    ppermute x4, starting transfers between devices, gather_rows(): other = lax.ppermute(block, axis_name, _exchange_pairs(count, distance))  8.06 us
    ppermute x8, starting transfers between devices, sum_halving(): arrived = lax.ppermute(send, axis_name, _exchange_pairs(count, distance))  5.46 us
    ppermute x8, starting transfers between devices, sum_halving(): other = lax.ppermute(values, axis_name, _exchange_pairs(count, distance))  5.01 us
    ppermute x4, waiting for transfers between devices, gather_rows(): other = lax.ppermute(block, axis_name, _exchange_pairs(count, distance))  4.91 us
    ppermute x8, waiting for transfers between devices, sum_halving(): other = lax.ppermute(values, axis_name, _exchange_pairs(count, distance))  3.17 us
    dot_general x1, matrix products, encoder_grads(): lax.dot_general(inputs_rows, grad_pre, (((0,), (0,)), ((), ())), preferre...  2.96 us
    dot_general x2, matrix products, decode_rows(): lax.dot_general(filtered, forward_transform, (((1,), (1,)), ((), ())), pr...  1.32 us
  transfers between devices with their start and end apart: 28, of which 13 were waited for; matrix products, arithmetic and copies ran while one was open for 6% of the time, Pallas kernels for 0%

profile of v18, /device:TPU:0, one launch (start us, length us, event | category | flops | bytes accessed | tf_op | source)
XLA Modules:
  0.0 59.6 jit_solution(6825481144424831424)
XLA Ops:
  0.6 4.1 %collective-permute-start = (bf16[2,2048]{1,0:T(2,128)(2,1)}, bf16[2,2048]{1,0:T(2,128)(2,1)S(1)}, u32[]{:S(2)}, u32[]{:S(2)}) collective-permute-start(bf16[2,2048]{1,0:T(2,128)(2,1)} %param.9), channel_id=1, source_target_pairs={{0,8},{1,9},{2,10},{3,11},{4,12},{5,13},{6,14},{7,15},{8,0},{9,1},... | collective-permute-start | bytes 24584 | tf_op jit(solution)/shard_map/ppermute | solution.py:119
  4.7 1.8 %collective-permute-done = bf16[2,2048]{1,0:T(2,128)(2,1)S(1)} collective-permute-done((bf16[2,2048]{1,0:T(2,128)(2,1)}, bf16[2,2048]{1,0:T(2,128)(2,1)S(1)}, u32[]{:S(2)}, u32[]{:S(2)}) %collective-permute-start) | collective-permute-done | bytes 8224 | tf_op jit(solution)/shard_map/ppermute | solution.py:119
  7.4 2.0 %collective-permute-start.1 = (bf16[4,2048]{1,0:T(4,128)(2,1)S(1)}, bf16[4,2048]{1,0:T(4,128)(2,1)S(1)}, u32[]{:S(2)}, u32[]{:S(2)}) collective-permute-start(bf16[4,2048]{1,0:T(4,128)(2,1)S(1)} %maximum_select_fusion.12), channel_id=1, source_target_pairs={{0,4},{1,5},{2,6},{3,7},{4,0},{5,1},{6,2},{7,3},{8,12},{9,13},{10,... | collective-permute-start | bytes 49160 | tf_op jit(solution)/shard_map/ppermute | solution.py:119
  9.4 1.8 %collective-permute-done.1 = bf16[4,2048]{1,0:T(4,128)(2,1)S(1)} collective-permute-done((bf16[4,2048]{1,0:T(4,128)(2,1)S(1)}, bf16[4,2048]{1,0:T(4,128)(2,1)S(1)}, u32[]{:S(2)}, u32[]{:S(2)}) %collective-permute-start.1) | collective-permute-done | bytes 16416 | tf_op jit(solution)/shard_map/ppermute | solution.py:119
  11.3 1.9 %collective-permute-start.2 = (bf16[8,2048]{1,0:T(8,128)(2,1)S(1)}, bf16[8,2048]{1,0:T(8,128)(2,1)S(1)}, u32[]{:S(2)}, u32[]{:S(2)}) collective-permute-start(bf16[8,2048]{1,0:T(8,128)(2,1)S(1)} %maximum_select_fusion.11), channel_id=1, source_target_pairs={{0,2},{1,3},{2,0},{3,1},{4,6},{5,7},{6,4},{7,5},{8,10},{9,11},{10,... | collective-permute-start | bytes 98312 | tf_op jit(solution)/shard_map/ppermute | solution.py:119
  14.0 1.2 %collective-permute-done.2 = bf16[8,2048]{1,0:T(8,128)(2,1)S(1)} collective-permute-done((bf16[8,2048]{1,0:T(8,128)(2,1)S(1)}, bf16[8,2048]{1,0:T(8,128)(2,1)S(1)}, u32[]{:S(2)}, u32[]{:S(2)}) %collective-permute-start.2) | collective-permute-done | bytes 32800 | tf_op jit(solution)/shard_map/ppermute | solution.py:119
  19.8 0.9 %add_convert_fusion = (bf16[768,512]{1,0:T(8,128)(2,1)S(1)}, f32[768,512]{1,0:T(8,128)S(1)}) fusion(bf16[32,24,512]{2,1,0:T(8,128)(2,1)S(1)} %multiply_convert_fusion, f32[768,512]{1,0:T(8,128)S(1)} %fusion.14, bf16[512,256]{1,0:T(8,128)(2,1)S(1)} %copy-done.5, f32[768,512]{1,0:T(8,128)S(1)} %fusion.49, f32[256]{0:T(256)S(1)} %bitcast.44, f32[256]{0:T(256)S(1)} %bitcast.40), kind=kOutput, calls=%fused_computation.14 | convolution fusion | flops 206831616 | bytes 6555648 | tf_op jit(solution)/shard_map/dot_general | solution.py:55
  23.0 1.2 %fusion.11 = f32[768,512]{1,0:T(8,128)S(1)} fusion(bf16[512,512]{1,0:T(8,128)(2,1)S(1)} %copy-done.4, f32[768,512]{1,0:T(8,128)S(1)} %get-tuple-element.19, f32[768,512]{1,0:T(8,128)S(1)} %convolution_add_fusion), kind=kOutput, calls=%fused_computation.30 | convolution fusion | flops 410517504 | bytes 5242880 | tf_op jit(solution)/shard_map/dot_general | solution.py:71
  28.2 1.9 %collective-permute-start.5 = (bf16[140,128]{1,0:T(8,128)(2,1)S(1)}, bf16[140,128]{1,0:T(8,128)(2,1)S(1)}, u32[]{:S(2)}, u32[]{:S(2)}) collective-permute-start(bf16[140,128]{1,0:T(8,128)(2,1)S(1)} %select_convert_fusion.7), channel_id=1, source_target_pairs={{0,2},{1,3},{2,0},{3,1},{4,6},{5,7},{6,4},{7,5},{8,10},{9,11},{10,... | collective-permute-start | bytes 107528 | tf_op jit(solution)/shard_map/ppermute | solution.py:158
  30.4 1.9 %collective-permute-start.17 = (bf16[140,128]{1,0:T(8,128)(2,1)S(1)}, bf16[140,128]{1,0:T(8,128)(2,1)S(1)}, u32[]{:S(2)}, u32[]{:S(2)}) collective-permute-start(bf16[140,128]{1,0:T(8,128)(2,1)S(1)} %select_convert_fusion.5), channel_id=1, source_target_pairs={{0,2},{1,3},{2,0},{3,1},{4,6},{5,7},{6,4},{7,5},{8,10},{9,11},{10,... | collective-permute-start | bytes 107528 | tf_op jit(solution)/shard_map/ppermute | solution.py:158
  32.6 2.0 %collective-permute-start.6 = (bf16[140,128]{1,0:T(8,128)(2,1)S(1)}, bf16[140,128]{1,0:T(8,128)(2,1)S(1)}, u32[]{:S(2)}, u32[]{:S(2)}) collective-permute-start(bf16[140,128]{1,0:T(8,128)(2,1)S(1)} %add_convert_fusion.16), channel_id=1, source_target_pairs={{0,4},{1,5},{2,6},{3,7},{4,0},{5,1},{6,2},{7,3},{8,12},{9,13},{10,... | collective-permute-start | bytes 107528 | tf_op jit(solution)/shard_map/ppermute | solution.py:164
  34.6 1.2 %collective-permute-start.12 = (bf16[140,128]{1,0:T(8,128)(2,1)S(1)}, bf16[140,128]{1,0:T(8,128)(2,1)S(1)}, u32[]{:S(2)}, u32[]{:S(2)}) collective-permute-start(bf16[140,128]{1,0:T(8,128)(2,1)S(1)} %add_convert_fusion.13), channel_id=1, source_target_pairs={{0,4},{1,5},{2,6},{3,7},{4,0},{5,1},{6,2},{7,3},{8,12},{9,13},{10,... | collective-permute-start | bytes 107528 | tf_op jit(solution)/shard_map/ppermute | solution.py:164
  35.9 0.9 %collective-permute-start.18 = (bf16[140,128]{1,0:T(8,128)(2,1)S(1)}, bf16[140,128]{1,0:T(8,128)(2,1)S(1)}, u32[]{:S(2)}, u32[]{:S(2)}) collective-permute-start(bf16[140,128]{1,0:T(8,128)(2,1)S(1)} %add_convert_fusion.10), channel_id=1, source_target_pairs={{0,4},{1,5},{2,6},{3,7},{4,0},{5,1},{6,2},{7,3},{8,12},{9,13},{10,... | collective-permute-start | bytes 107528 | tf_op jit(solution)/shard_map/ppermute | solution.py:164
  36.8 1.2 %collective-permute-start.24 = (bf16[140,128]{1,0:T(8,128)(2,1)S(1)}, bf16[140,128]{1,0:T(8,128)(2,1)S(1)}, u32[]{:S(2)}, u32[]{:S(2)}) collective-permute-start(bf16[140,128]{1,0:T(8,128)(2,1)S(1)} %add_convert_fusion.7), channel_id=1, source_target_pairs={{0,4},{1,5},{2,6},{3,7},{4,0},{5,1},{6,2},{7,3},{8,12},{9,13},{10,... | collective-permute-start | bytes 107528 | tf_op jit(solution)/shard_map/ppermute | solution.py:164
  38.1 2.6 %collective-permute-start.7 = (bf16[140,128]{1,0:T(8,128)(2,1)S(1)}, bf16[140,128]{1,0:T(8,128)(2,1)S(1)}, u32[]{:S(2)}, u32[]{:S(2)}) collective-permute-start(bf16[140,128]{1,0:T(8,128)(2,1)S(1)} %add_convert_fusion.15), channel_id=1, source_target_pairs={{0,8},{1,9},{2,10},{3,11},{4,12},{5,13},{6,14},{7,15},{8,0},{9,1},... | collective-permute-start | bytes 107528 | tf_op jit(solution)/shard_map/ppermute | solution.py:164
  40.8 0.9 %collective-permute-start.13 = (bf16[140,128]{1,0:T(8,128)(2,1)S(1)}, bf16[140,128]{1,0:T(8,128)(2,1)S(1)}, u32[]{:S(2)}, u32[]{:S(2)}) collective-permute-start(bf16[140,128]{1,0:T(8,128)(2,1)S(1)} %add_convert_fusion.12), channel_id=1, source_target_pairs={{0,8},{1,9},{2,10},{3,11},{4,12},{5,13},{6,14},{7,15},{8,0},{9,1},... | collective-permute-start | bytes 107528 | tf_op jit(solution)/shard_map/ppermute | solution.py:164
  41.6 2.2 %collective-permute-start.19 = (bf16[140,128]{1,0:T(8,128)(2,1)S(1)}, bf16[140,128]{1,0:T(8,128)(2,1)S(1)}, u32[]{:S(2)}, u32[]{:S(2)}) collective-permute-start(bf16[140,128]{1,0:T(8,128)(2,1)S(1)} %add_convert_fusion.9), channel_id=1, source_target_pairs={{0,8},{1,9},{2,10},{3,11},{4,12},{5,13},{6,14},{7,15},{8,0},{9,1},... | collective-permute-start | bytes 107528 | tf_op jit(solution)/shard_map/ppermute | solution.py:164
  43.9 0.9 %collective-permute-start.25 = (bf16[140,128]{1,0:T(8,128)(2,1)S(1)}, bf16[140,128]{1,0:T(8,128)(2,1)S(1)}, u32[]{:S(2)}, u32[]{:S(2)}) collective-permute-start(bf16[140,128]{1,0:T(8,128)(2,1)S(1)} %add_convert_fusion.6), channel_id=1, source_target_pairs={{0,8},{1,9},{2,10},{3,11},{4,12},{5,13},{6,14},{7,15},{8,0},{9,1},... | collective-permute-start | bytes 107528 | tf_op jit(solution)/shard_map/ppermute | solution.py:164
  44.7 1.5 %collective-permute-start.8 = (bf16[140,128]{1,0:T(8,128)(2,1)S(1)}, bf16[140,128]{1,0:T(8,128)(2,1)S(1)}, u32[]{:S(2)}, u32[]{:S(2)}) collective-permute-start(bf16[140,128]{1,0:T(8,128)(2,1)S(1)} %add_convert_fusion.14), channel_id=1, source_target_pairs={{0,2},{1,3},{2,0},{3,1},{4,6},{5,7},{6,4},{7,5},{8,10},{9,11},{10,... | collective-permute-start | bytes 107528 | tf_op jit(solution)/shard_map/ppermute | solution.py:169
  47.0 1.7 %collective-permute-start.20 = (bf16[140,128]{1,0:T(8,128)(2,1)S(1)}, bf16[140,128]{1,0:T(8,128)(2,1)S(1)}, u32[]{:S(2)}, u32[]{:S(2)}) collective-permute-start(bf16[140,128]{1,0:T(8,128)(2,1)S(1)} %add_convert_fusion.8), channel_id=1, source_target_pairs={{0,2},{1,3},{2,0},{3,1},{4,6},{5,7},{6,4},{7,5},{8,10},{9,11},{10,... | collective-permute-start | bytes 107528 | tf_op jit(solution)/shard_map/ppermute | solution.py:169
  51.3 1.6 %collective-permute-done.26 = bf16[140,128]{1,0:T(8,128)(2,1)S(1)} collective-permute-done((bf16[140,128]{1,0:T(8,128)(2,1)S(1)}, bf16[140,128]{1,0:T(8,128)(2,1)S(1)}, u32[]{:S(2)}, u32[]{:S(2)}) %collective-permute-start.26) | collective-permute-done | bytes 35872 | tf_op jit(solution)/shard_map/ppermute | solution.py:169
  54.3 1.1 %fusion.13 = f32[512,512]{1,0:T(8,128)} fusion(bf16[560,128]{1,0:T(8,128)(2,1)S(1)} %maximum_select_fusion.3, bf16[560,128]{1,0:T(8,128)(2,1)S(1)} %maximum_select_fusion.2, bf16[560,128]{1,0:T(8,128)(2,1)S(1)} %maximum_select_fusion.1, bf16[560,128]{1,0:T(8,128)(2,1)S(1)} %maximum_select_fusion), kind=kLoop, calls=%fused_computation.32 | loop fusion | flops 2097152 | bytes 1622016 | tf_op jit(solution)/shard_map/convert_element_type | solution.py:246
  55.3 3.0 %fusion.10 = f32[2048,512]{1,0:T(8,128)} fusion(bf16[32,2048]{1,0:T(8,128)(2,1)S(1)} %convolution_convert_fusion, bf16[32,512]{1,0:T(8,128)(2,1)S(1)} %pad_maximum_fusion.3, bf16[512,512]{1,0:T(8,128)(2,1)S(1)} %copy-done.1, bf16[32,512]{1,0:T(8,128)(2,1)S(1)} %fusion.8), kind=kOutput, calls=%fused_computation.23 | convolution fusion | flops 83968000 | bytes 4915200 | tf_op jit(solution)/shard_map/dot_general | solution.py:98
  58.3 1.3 %fusion.50 = f32[512,512]{1,0:T(8,128)} fusion(bf16[32,512]{1,0:T(8,128)(2,1)S(1)} %fusion.8, bf16[32,512]{1,0:T(8,128)(2,1)S(1)} %pad_maximum_fusion.3), kind=kOutput, calls=%fused_computation.112 | convolution fusion | flops 16777216 | bytes 1114112 | tf_op jit(solution)/shard_map/dot_general | solution.py:91
  (104 shorter events, 17.6 us)
Async XLA Ops:
  0.6 5.9 %collective-permute-start = (bf16[2,2048]{1,0:T(2,128)(2,1)}, bf16[2,2048]{1,0:T(2,128)(2,1)S(1)}, u32[]{:S(2)}, u32[]{:S(2)}) collective-permute-start(bf16[2,2048]{1,0:T(2,128)(2,1)} %param.9), channel_id=1, source_target_pairs={{0,8},{1,9},{2,10},{3,11},{4,12},{5,13},{6,14},{7,15},{8,0},{9,1},... | collective-permute-start | bytes 24584 | tf_op jit(solution)/shard_map/ppermute | solution.py:119
  7.4 3.8 %collective-permute-start.1 = (bf16[4,2048]{1,0:T(4,128)(2,1)S(1)}, bf16[4,2048]{1,0:T(4,128)(2,1)S(1)}, u32[]{:S(2)}, u32[]{:S(2)}) collective-permute-start(bf16[4,2048]{1,0:T(4,128)(2,1)S(1)} %maximum_select_fusion.12), channel_id=1, source_target_pairs={{0,4},{1,5},{2,6},{3,7},{4,0},{5,1},{6,2},{7,3},{8,12},{9,13},{10,... | collective-permute-start | bytes 49160 | tf_op jit(solution)/shard_map/ppermute | solution.py:119
  11.3 4.0 %collective-permute-start.2 = (bf16[8,2048]{1,0:T(8,128)(2,1)S(1)}, bf16[8,2048]{1,0:T(8,128)(2,1)S(1)}, u32[]{:S(2)}, u32[]{:S(2)}) collective-permute-start(bf16[8,2048]{1,0:T(8,128)(2,1)S(1)} %maximum_select_fusion.11), channel_id=1, source_target_pairs={{0,2},{1,3},{2,0},{3,1},{4,6},{5,7},{6,4},{7,5},{8,10},{9,11},{10,... | collective-permute-start | bytes 98312 | tf_op jit(solution)/shard_map/ppermute | solution.py:119
  15.3 1.8 %collective-permute-start.3 = (bf16[16,2048]{1,0:T(8,128)(2,1)S(1)}, bf16[16,2048]{1,0:T(8,128)(2,1)S(1)}, u32[]{:S(2)}, u32[]{:S(2)}) collective-permute-start(bf16[16,2048]{1,0:T(8,128)(2,1)S(1)} %maximum_select_fusion.10), channel_id=1, source_target_pairs={{0,1},{1,0},{2,3},{3,2},{4,5},{5,4},{6,7},{7,6},{8,9},{9,8},{10,11... | collective-permute-start | bytes 196616 | tf_op jit(solution)/shard_map/ppermute | solution.py:119
  25.8 1.5 %collective-permute-start.10 = (bf16[280,128]{1,0:T(8,128)(2,1)S(1)}, bf16[280,128]{1,0:T(8,128)(2,1)S(1)}, u32[]{:S(2)}, u32[]{:S(2)}) collective-permute-start(bf16[280,128]{1,0:T(8,128)(2,1)S(1)} %get-tuple-element.11), channel_id=1, source_target_pairs={{0,1},{1,0},{2,3},{3,2},{4,5},{5,4},{6,7},{7,6},{8,9},{9,8},{10,11... | collective-permute-start | bytes 215048 | tf_op jit(solution)/shard_map/ppermute | solution.py:158
  28.2 4.4 %collective-permute-start.5 = (bf16[140,128]{1,0:T(8,128)(2,1)S(1)}, bf16[140,128]{1,0:T(8,128)(2,1)S(1)}, u32[]{:S(2)}, u32[]{:S(2)}) collective-permute-start(bf16[140,128]{1,0:T(8,128)(2,1)S(1)} %select_convert_fusion.7), channel_id=1, source_target_pairs={{0,2},{1,3},{2,0},{3,1},{4,6},{5,7},{6,4},{7,5},{8,10},{9,11},{10,... | collective-permute-start | bytes 107528 | tf_op jit(solution)/shard_map/ppermute | solution.py:158
  30.2 4.4 %collective-permute-start.11 = (bf16[140,128]{1,0:T(8,128)(2,1)S(1)}, bf16[140,128]{1,0:T(8,128)(2,1)S(1)}, u32[]{:S(2)}, u32[]{:S(2)}) collective-permute-start(bf16[140,128]{1,0:T(8,128)(2,1)S(1)} %select_convert_fusion.6), channel_id=1, source_target_pairs={{0,2},{1,3},{2,0},{3,1},{4,6},{5,7},{6,4},{7,5},{8,10},{9,11},{10,... | collective-permute-start | bytes 107528 | tf_op jit(solution)/shard_map/ppermute | solution.py:158
  30.4 5.4 %collective-permute-start.17 = (bf16[140,128]{1,0:T(8,128)(2,1)S(1)}, bf16[140,128]{1,0:T(8,128)(2,1)S(1)}, u32[]{:S(2)}, u32[]{:S(2)}) collective-permute-start(bf16[140,128]{1,0:T(8,128)(2,1)S(1)} %select_convert_fusion.5), channel_id=1, source_target_pairs={{0,2},{1,3},{2,0},{3,1},{4,6},{5,7},{6,4},{7,5},{8,10},{9,11},{10,... | collective-permute-start | bytes 107528 | tf_op jit(solution)/shard_map/ppermute | solution.py:158
  32.4 4.5 %collective-permute-start.23 = (bf16[140,128]{1,0:T(8,128)(2,1)S(1)}, bf16[140,128]{1,0:T(8,128)(2,1)S(1)}, u32[]{:S(2)}, u32[]{:S(2)}) collective-permute-start(bf16[140,128]{1,0:T(8,128)(2,1)S(1)} %select_convert_fusion.4), channel_id=1, source_target_pairs={{0,2},{1,3},{2,0},{3,1},{4,6},{5,7},{6,4},{7,5},{8,10},{9,11},{10,... | collective-permute-start | bytes 107528 | tf_op jit(solution)/shard_map/ppermute | solution.py:158
  32.6 5.5 %collective-permute-start.6 = (bf16[140,128]{1,0:T(8,128)(2,1)S(1)}, bf16[140,128]{1,0:T(8,128)(2,1)S(1)}, u32[]{:S(2)}, u32[]{:S(2)}) collective-permute-start(bf16[140,128]{1,0:T(8,128)(2,1)S(1)} %add_convert_fusion.16), channel_id=1, source_target_pairs={{0,4},{1,5},{2,6},{3,7},{4,0},{5,1},{6,2},{7,3},{8,12},{9,13},{10,... | collective-permute-start | bytes 107528 | tf_op jit(solution)/shard_map/ppermute | solution.py:164
  34.6 6.1 %collective-permute-start.12 = (bf16[140,128]{1,0:T(8,128)(2,1)S(1)}, bf16[140,128]{1,0:T(8,128)(2,1)S(1)}, u32[]{:S(2)}, u32[]{:S(2)}) collective-permute-start(bf16[140,128]{1,0:T(8,128)(2,1)S(1)} %add_convert_fusion.13), channel_id=1, source_target_pairs={{0,4},{1,5},{2,6},{3,7},{4,0},{5,1},{6,2},{7,3},{8,12},{9,13},{10,... | collective-permute-start | bytes 107528 | tf_op jit(solution)/shard_map/ppermute | solution.py:164
  35.9 5.7 %collective-permute-start.18 = (bf16[140,128]{1,0:T(8,128)(2,1)S(1)}, bf16[140,128]{1,0:T(8,128)(2,1)S(1)}, u32[]{:S(2)}, u32[]{:S(2)}) collective-permute-start(bf16[140,128]{1,0:T(8,128)(2,1)S(1)} %add_convert_fusion.10), channel_id=1, source_target_pairs={{0,4},{1,5},{2,6},{3,7},{4,0},{5,1},{6,2},{7,3},{8,12},{9,13},{10,... | collective-permute-start | bytes 107528 | tf_op jit(solution)/shard_map/ppermute | solution.py:164
  36.8 7.0 %collective-permute-start.24 = (bf16[140,128]{1,0:T(8,128)(2,1)S(1)}, bf16[140,128]{1,0:T(8,128)(2,1)S(1)}, u32[]{:S(2)}, u32[]{:S(2)}) collective-permute-start(bf16[140,128]{1,0:T(8,128)(2,1)S(1)} %add_convert_fusion.7), channel_id=1, source_target_pairs={{0,4},{1,5},{2,6},{3,7},{4,0},{5,1},{6,2},{7,3},{8,12},{9,13},{10,... | collective-permute-start | bytes 107528 | tf_op jit(solution)/shard_map/ppermute | solution.py:164
  38.1 6.6 %collective-permute-start.7 = (bf16[140,128]{1,0:T(8,128)(2,1)S(1)}, bf16[140,128]{1,0:T(8,128)(2,1)S(1)}, u32[]{:S(2)}, u32[]{:S(2)}) collective-permute-start(bf16[140,128]{1,0:T(8,128)(2,1)S(1)} %add_convert_fusion.15), channel_id=1, source_target_pairs={{0,8},{1,9},{2,10},{3,11},{4,12},{5,13},{6,14},{7,15},{8,0},{9,1},... | collective-permute-start | bytes 107528 | tf_op jit(solution)/shard_map/ppermute | solution.py:164
  40.8 5.8 %collective-permute-start.13 = (bf16[140,128]{1,0:T(8,128)(2,1)S(1)}, bf16[140,128]{1,0:T(8,128)(2,1)S(1)}, u32[]{:S(2)}, u32[]{:S(2)}) collective-permute-start(bf16[140,128]{1,0:T(8,128)(2,1)S(1)} %add_convert_fusion.12), channel_id=1, source_target_pairs={{0,8},{1,9},{2,10},{3,11},{4,12},{5,13},{6,14},{7,15},{8,0},{9,1},... | collective-permute-start | bytes 107528 | tf_op jit(solution)/shard_map/ppermute | solution.py:164
  41.6 5.3 %collective-permute-start.19 = (bf16[140,128]{1,0:T(8,128)(2,1)S(1)}, bf16[140,128]{1,0:T(8,128)(2,1)S(1)}, u32[]{:S(2)}, u32[]{:S(2)}) collective-permute-start(bf16[140,128]{1,0:T(8,128)(2,1)S(1)} %add_convert_fusion.9), channel_id=1, source_target_pairs={{0,8},{1,9},{2,10},{3,11},{4,12},{5,13},{6,14},{7,15},{8,0},{9,1},... | collective-permute-start | bytes 107528 | tf_op jit(solution)/shard_map/ppermute | solution.py:164
  43.9 4.9 %collective-permute-start.25 = (bf16[140,128]{1,0:T(8,128)(2,1)S(1)}, bf16[140,128]{1,0:T(8,128)(2,1)S(1)}, u32[]{:S(2)}, u32[]{:S(2)}) collective-permute-start(bf16[140,128]{1,0:T(8,128)(2,1)S(1)} %add_convert_fusion.6), channel_id=1, source_target_pairs={{0,8},{1,9},{2,10},{3,11},{4,12},{5,13},{6,14},{7,15},{8,0},{9,1},... | collective-permute-start | bytes 107528 | tf_op jit(solution)/shard_map/ppermute | solution.py:164
  44.7 4.9 %collective-permute-start.8 = (bf16[140,128]{1,0:T(8,128)(2,1)S(1)}, bf16[140,128]{1,0:T(8,128)(2,1)S(1)}, u32[]{:S(2)}, u32[]{:S(2)}) collective-permute-start(bf16[140,128]{1,0:T(8,128)(2,1)S(1)} %add_convert_fusion.14), channel_id=1, source_target_pairs={{0,2},{1,3},{2,0},{3,1},{4,6},{5,7},{6,4},{7,5},{8,10},{9,11},{10,... | collective-permute-start | bytes 107528 | tf_op jit(solution)/shard_map/ppermute | solution.py:169
  46.6 4.0 %collective-permute-start.14 = (bf16[140,128]{1,0:T(8,128)(2,1)S(1)}, bf16[140,128]{1,0:T(8,128)(2,1)S(1)}, u32[]{:S(2)}, u32[]{:S(2)}) collective-permute-start(bf16[140,128]{1,0:T(8,128)(2,1)S(1)} %add_convert_fusion.11), channel_id=1, source_target_pairs={{0,2},{1,3},{2,0},{3,1},{4,6},{5,7},{6,4},{7,5},{8,10},{9,11},{10,... | collective-permute-start | bytes 107528 | tf_op jit(solution)/shard_map/ppermute | solution.py:169
  47.0 4.0 %collective-permute-start.20 = (bf16[140,128]{1,0:T(8,128)(2,1)S(1)}, bf16[140,128]{1,0:T(8,128)(2,1)S(1)}, u32[]{:S(2)}, u32[]{:S(2)}) collective-permute-start(bf16[140,128]{1,0:T(8,128)(2,1)S(1)} %add_convert_fusion.8), channel_id=1, source_target_pairs={{0,2},{1,3},{2,0},{3,1},{4,6},{5,7},{6,4},{7,5},{8,10},{9,11},{10,... | collective-permute-start | bytes 107528 | tf_op jit(solution)/shard_map/ppermute | solution.py:169
  48.8 4.0 %collective-permute-start.26 = (bf16[140,128]{1,0:T(8,128)(2,1)S(1)}, bf16[140,128]{1,0:T(8,128)(2,1)S(1)}, u32[]{:S(2)}, u32[]{:S(2)}) collective-permute-start(bf16[140,128]{1,0:T(8,128)(2,1)S(1)} %add_convert_fusion.5), channel_id=1, source_target_pairs={{0,2},{1,3},{2,0},{3,1},{4,6},{5,7},{6,4},{7,5},{8,10},{9,11},{10,... | collective-permute-start | bytes 107528 | tf_op jit(solution)/shard_map/ppermute | solution.py:169
  49.7 3.3 %collective-permute-start.9 = (bf16[280,128]{1,0:T(8,128)(2,1)S(1)}, bf16[280,128]{1,0:T(8,128)(2,1)S(1)}, u32[]{:S(2)}, u32[]{:S(2)}) collective-permute-start(bf16[280,128]{1,0:T(8,128)(2,1)S(1)} %maximum_select_fusion.6), channel_id=1, source_target_pairs={{0,1},{1,0},{2,3},{3,2},{4,5},{5,4},{6,7},{7,6},{8,9},{9,8},{10,11... | collective-permute-start | bytes 215048 | tf_op jit(solution)/shard_map/ppermute | solution.py:169
  50.6 2.4 %collective-permute-start.15 = (bf16[280,128]{1,0:T(8,128)(2,1)S(1)}, bf16[280,128]{1,0:T(8,128)(2,1)S(1)}, u32[]{:S(2)}, u32[]{:S(2)}) collective-permute-start(bf16[280,128]{1,0:T(8,128)(2,1)S(1)} %maximum_select_fusion.7), channel_id=1, source_target_pairs={{0,1},{1,0},{2,3},{3,2},{4,5},{5,4},{6,7},{7,6},{8,9},{9,8},{10,11... | collective-permute-start | bytes 215048 | tf_op jit(solution)/shard_map/ppermute | solution.py:169
  51.0 2.0 %collective-permute-start.21 = (bf16[280,128]{1,0:T(8,128)(2,1)S(1)}, bf16[280,128]{1,0:T(8,128)(2,1)S(1)}, u32[]{:S(2)}, u32[]{:S(2)}) collective-permute-start(bf16[280,128]{1,0:T(8,128)(2,1)S(1)} %maximum_select_fusion.8), channel_id=1, source_target_pairs={{0,1},{1,0},{2,3},{3,2},{4,5},{5,4},{6,7},{7,6},{8,9},{9,8},{10,11... | collective-permute-start | bytes 215048 | tf_op jit(solution)/shard_map/ppermute | solution.py:169
  (11 other events, 33.6 us)

commit v19 on v17

--- a/solution.py
+++ b/solution.py
@@ -144,34 +144,32 @@
     return values
 
 
-def sum_halving(values, axis_name, wire=jnp.bfloat16, halving_levels=2):
+def sum_halving(values, axis_name, halving=(1, 2), wire=jnp.bfloat16):
     count = lax.axis_size(axis_name)
     if not _is_power_of_two(count) or values.shape[0] % count != 0:
         return lax.psum(values, axis_name)
+    halving = tuple(distance for distance in halving if distance < count)
     position = lax.axis_index(axis_name)
-    distance = 1
-    while distance < count and distance < 2**halving_levels:
+    for distance in halving:
         half = values.shape[0] // 2
         lower = (position // distance) % 2 == 0
         keep = jnp.where(lower, values[:half], values[half:])
         send = jnp.where(lower, values[half:], values[:half]).astype(wire)
         arrived = lax.ppermute(send, axis_name, _exchange_pairs(count, distance))
         values = keep + arrived.astype(keep.dtype)
+    values = values.astype(wire)
+    distance = 1
+    while distance < count:
+        if distance not in halving:
+            arrived = lax.ppermute(values, axis_name, _exchange_pairs(count, distance))
+            values = (values.astype(jnp.float32) + arrived.astype(jnp.float32)).astype(wire)
         distance *= 2
-    top = distance
-    values = values.astype(wire)
-    while distance < count:
-        arrived = lax.ppermute(values, axis_name, _exchange_pairs(count, distance))
-        values = (values.astype(jnp.float32) + arrived.astype(jnp.float32)).astype(wire)
-        distance *= 2
-    distance = top // 2
-    while distance >= 1:
+    for distance in reversed(halving):
         other = lax.ppermute(values, axis_name, _exchange_pairs(count, distance))
         lower = (position // distance) % 2 == 0
         values = jnp.where(
             lower, jnp.concatenate([values, other], 0), jnp.concatenate([other, values], 0)
         )
-        distance //= 2
     return values
 
 
@@ -235,7 +233,11 @@
     )
     columns = packed.shape[1] // 2
     packed = jnp.concatenate(
-        [sum_halving(packed[:, :columns], "freq"), sum_halving(packed[:, columns:], "freq")], 1
+        [
+            sum_halving(packed[:, :columns], "freq", (1, 2)),
+            sum_halving(packed[:, columns:], "freq", (1, 4)),
+        ],
+        1,
     )
     rows_out = grad_out.shape[0]
     grad_out = packed[:rows_out].astype(jnp.float32)

time: 58.6 us -> 58.4 us (level)
  waiting for transfers between devices: 17.2 us -> 15.9 us
  starting transfers between devices: 21.6 us -> 22.7 us
    ppermute x4, waiting for transfers between devices: 3.7 us -> 2.25 us  [sum_halving(): arrived = lax.ppermute(send, axis_name, _exchange_pairs(count, distance))]
    ppermute x4, starting transfers between devices: 2.79 us -> 4.2 us  [sum_halving(): arrived = lax.ppermute(send, axis_name, _exchange_pairs(count, distance))]
where the time goes in v19:
time: 58.4 us; the launch traced here: 58 us
  starting transfers between devices  22.7 us (39%)
  waiting for transfers between devices  15.9 us (27%)
  matrix products  10.8 us (18%)
  other arithmetic  4.88 us (8%)
  local copies, waits for them, and re-layouts  2.81 us (5%)
  between operations  0.92 us (2%)
    ppermute x4, starting transfers between devices, gather_rows(): other = lax.ppermute(block, axis_name, _exchange_pairs(count, distance))  8.06 us
    ppermute x4, starting transfers between devices, sum_halving(): arrived = lax.ppermute(values, axis_name, _exchange_pairs(count, distance))  7.99 us
    ppermute x4, waiting for transfers between devices, gather_rows(): other = lax.ppermute(block, axis_name, _exchange_pairs(count, distance))  4.91 us
    ppermute x4, waiting for transfers between devices, sum_halving(): other = lax.ppermute(values, axis_name, _exchange_pairs(count, distance))  4.77 us
    ppermute x4, starting transfers between devices, sum_halving(): arrived = lax.ppermute(send, axis_name, _exchange_pairs(count, distance))  4.2 us
    ppermute x4, waiting for transfers between devices, sum_halving(): arrived = lax.ppermute(values, axis_name, _exchange_pairs(count, distance))  3.94 us
    dot_general x1, matrix products, encoder_grads(): lax.dot_general(inputs_rows, grad_pre, (((0,), (0,)), ((), ())), preferre...  2.96 us
    ppermute x4, starting transfers between devices, sum_halving(): other = lax.ppermute(values, axis_name, _exchange_pairs(count, distance))  2.46 us
  transfers between devices with their start and end apart: 16, of which 11 were waited for; matrix products, arithmetic and copies ran while one was open for 5% of the time, Pallas kernels for 0%

profile of v19, /device:TPU:0, one launch (start us, length us, event | category | flops | bytes accessed | tf_op | source)
XLA Modules:
  0.0 58.0 jit_solution(8303865012165413771)
XLA Ops:
  0.6 4.1 %collective-permute-start = (bf16[2,2048]{1,0:T(2,128)(2,1)}, bf16[2,2048]{1,0:T(2,128)(2,1)S(1)}, u32[]{:S(2)}, u32[]{:S(2)}) collective-permute-start(bf16[2,2048]{1,0:T(2,128)(2,1)} %param.9), channel_id=1, source_target_pairs={{0,8},{1,9},{2,10},{3,11},{4,12},{5,13},{6,14},{7,15},{8,0},{9,1},... | collective-permute-start | bytes 24584 | tf_op jit(solution)/shard_map/ppermute | solution.py:119
  4.7 1.8 %collective-permute-done = bf16[2,2048]{1,0:T(2,128)(2,1)S(1)} collective-permute-done((bf16[2,2048]{1,0:T(2,128)(2,1)}, bf16[2,2048]{1,0:T(2,128)(2,1)S(1)}, u32[]{:S(2)}, u32[]{:S(2)}) %collective-permute-start) | collective-permute-done | bytes 8224 | tf_op jit(solution)/shard_map/ppermute | solution.py:119
  7.4 2.0 %collective-permute-start.1 = (bf16[4,2048]{1,0:T(4,128)(2,1)S(1)}, bf16[4,2048]{1,0:T(4,128)(2,1)S(1)}, u32[]{:S(2)}, u32[]{:S(2)}) collective-permute-start(bf16[4,2048]{1,0:T(4,128)(2,1)S(1)} %maximum_select_fusion.8), channel_id=1, source_target_pairs={{0,4},{1,5},{2,6},{3,7},{4,0},{5,1},{6,2},{7,3},{8,12},{9,13},{10,... | collective-permute-start | bytes 49160 | tf_op jit(solution)/shard_map/ppermute | solution.py:119
  9.4 1.8 %collective-permute-done.1 = bf16[4,2048]{1,0:T(4,128)(2,1)S(1)} collective-permute-done((bf16[4,2048]{1,0:T(4,128)(2,1)S(1)}, bf16[4,2048]{1,0:T(4,128)(2,1)S(1)}, u32[]{:S(2)}, u32[]{:S(2)}) %collective-permute-start.1) | collective-permute-done | bytes 16416 | tf_op jit(solution)/shard_map/ppermute | solution.py:119
  11.3 1.9 %collective-permute-start.2 = (bf16[8,2048]{1,0:T(8,128)(2,1)S(1)}, bf16[8,2048]{1,0:T(8,128)(2,1)S(1)}, u32[]{:S(2)}, u32[]{:S(2)}) collective-permute-start(bf16[8,2048]{1,0:T(8,128)(2,1)S(1)} %maximum_select_fusion.7), channel_id=1, source_target_pairs={{0,2},{1,3},{2,0},{3,1},{4,6},{5,7},{6,4},{7,5},{8,10},{9,11},{10,... | collective-permute-start | bytes 98312 | tf_op jit(solution)/shard_map/ppermute | solution.py:119
  14.0 1.2 %collective-permute-done.2 = bf16[8,2048]{1,0:T(8,128)(2,1)S(1)} collective-permute-done((bf16[8,2048]{1,0:T(8,128)(2,1)S(1)}, bf16[8,2048]{1,0:T(8,128)(2,1)S(1)}, u32[]{:S(2)}, u32[]{:S(2)}) %collective-permute-start.2) | collective-permute-done | bytes 32800 | tf_op jit(solution)/shard_map/ppermute | solution.py:119
  23.0 1.2 %fusion.11 = f32[768,512]{1,0:T(8,128)S(1)} fusion(bf16[512,512]{1,0:T(8,128)(2,1)S(1)} %copy-done.4, f32[768,512]{1,0:T(8,128)S(1)} %get-tuple-element.15, f32[768,512]{1,0:T(8,128)S(1)} %convolution_add_fusion), kind=kOutput, calls=%fused_computation.30 | convolution fusion | flops 410517504 | bytes 5242880 | tf_op jit(solution)/shard_map/dot_general | solution.py:71
  26.4 0.9 %collective-permute-done.10 = bf16[280,256]{1,0:T(8,128)(2,1)S(1)} collective-permute-done((bf16[280,256]{1,0:T(8,128)(2,1)S(1)}, bf16[280,256]{1,0:T(8,128)(2,1)S(1)}, u32[]{:S(2)}, u32[]{:S(2)}) %collective-permute-start.10) | collective-permute-done | bytes 143392 | tf_op jit(solution)/shard_map/ppermute | solution.py:158
  27.8 1.9 %collective-permute-start.5 = (bf16[140,256]{1,0:T(8,128)(2,1)S(1)}, bf16[140,256]{1,0:T(8,128)(2,1)S(1)}, u32[]{:S(2)}, u32[]{:S(2)}) collective-permute-start(bf16[140,256]{1,0:T(8,128)(2,1)S(1)} %select_convert_fusion.3), channel_id=1, source_target_pairs={{0,2},{1,3},{2,0},{3,1},{4,6},{5,7},{6,4},{7,5},{8,10},{9,11},{10,... | collective-permute-start | bytes 215048 | tf_op jit(solution)/shard_map/ppermute | solution.py:158
  29.8 1.7 %collective-permute-start.11 = (bf16[140,256]{1,0:T(8,128)(2,1)S(1)}, bf16[140,256]{1,0:T(8,128)(2,1)S(1)}, u32[]{:S(2)}, u32[]{:S(2)}) collective-permute-start(bf16[140,256]{1,0:T(8,128)(2,1)S(1)} %select_convert_fusion.2), channel_id=1, source_target_pairs={{0,4},{1,5},{2,6},{3,7},{4,0},{5,1},{6,2},{7,3},{8,12},{9,13},{10,... | collective-permute-start | bytes 215048 | tf_op jit(solution)/shard_map/ppermute | solution.py:158
  31.4 1.0 %collective-permute-done.5 = bf16[140,256]{1,0:T(8,128)(2,1)S(1)} collective-permute-done((bf16[140,256]{1,0:T(8,128)(2,1)S(1)}, bf16[140,256]{1,0:T(8,128)(2,1)S(1)}, u32[]{:S(2)}, u32[]{:S(2)}) %collective-permute-start.5) | collective-permute-done | bytes 71712 | tf_op jit(solution)/shard_map/ppermute | solution.py:158
  32.4 1.9 %collective-permute-start.6 = (bf16[140,256]{1,0:T(8,128)(2,1)S(1)}, bf16[140,256]{1,0:T(8,128)(2,1)S(1)}, u32[]{:S(2)}, u32[]{:S(2)}) collective-permute-start(bf16[140,256]{1,0:T(8,128)(2,1)S(1)} %add_convert_fusion.10), channel_id=1, source_target_pairs={{0,4},{1,5},{2,6},{3,7},{4,0},{5,1},{6,2},{7,3},{8,12},{9,13},{10,... | collective-permute-start | bytes 215048 | tf_op jit(solution)/shard_map/ppermute | solution.py:164
  34.3 1.6 %collective-permute-start.12 = (bf16[140,256]{1,0:T(8,128)(2,1)S(1)}, bf16[140,256]{1,0:T(8,128)(2,1)S(1)}, u32[]{:S(2)}, u32[]{:S(2)}) collective-permute-start(bf16[140,256]{1,0:T(8,128)(2,1)S(1)} %add_convert_fusion.7), channel_id=1, source_target_pairs={{0,2},{1,3},{2,0},{3,1},{4,6},{5,7},{6,4},{7,5},{8,10},{9,11},{10,... | collective-permute-start | bytes 215048 | tf_op jit(solution)/shard_map/ppermute | solution.py:164
  35.9 0.9 %collective-permute-done.6 = bf16[140,256]{1,0:T(8,128)(2,1)S(1)} collective-permute-done((bf16[140,256]{1,0:T(8,128)(2,1)S(1)}, bf16[140,256]{1,0:T(8,128)(2,1)S(1)}, u32[]{:S(2)}, u32[]{:S(2)}) %collective-permute-start.6) | collective-permute-done | bytes 71712 | tf_op jit(solution)/shard_map/ppermute | solution.py:164
  36.9 2.9 %collective-permute-start.7 = (bf16[140,256]{1,0:T(8,128)(2,1)S(1)}, bf16[140,256]{1,0:T(8,128)(2,1)S(1)}, u32[]{:S(2)}, u32[]{:S(2)}) collective-permute-start(bf16[140,256]{1,0:T(8,128)(2,1)S(1)} %add_convert_fusion.9), channel_id=1, source_target_pairs={{0,8},{1,9},{2,10},{3,11},{4,12},{5,13},{6,14},{7,15},{8,0},{9,1},... | collective-permute-start | bytes 215048 | tf_op jit(solution)/shard_map/ppermute | solution.py:164
  39.8 1.7 %collective-permute-start.13 = (bf16[140,256]{1,0:T(8,128)(2,1)S(1)}, bf16[140,256]{1,0:T(8,128)(2,1)S(1)}, u32[]{:S(2)}, u32[]{:S(2)}) collective-permute-start(bf16[140,256]{1,0:T(8,128)(2,1)S(1)} %add_convert_fusion.6), channel_id=1, source_target_pairs={{0,8},{1,9},{2,10},{3,11},{4,12},{5,13},{6,14},{7,15},{8,0},{9,1},... | collective-permute-start | bytes 215048 | tf_op jit(solution)/shard_map/ppermute | solution.py:164
  41.4 3.0 %collective-permute-done.7 = bf16[140,256]{1,0:T(8,128)(2,1)S(1)} collective-permute-done((bf16[140,256]{1,0:T(8,128)(2,1)S(1)}, bf16[140,256]{1,0:T(8,128)(2,1)S(1)}, u32[]{:S(2)}, u32[]{:S(2)}) %collective-permute-start.7) | collective-permute-done | bytes 71712 | tf_op jit(solution)/shard_map/ppermute | solution.py:164
  44.5 1.6 %collective-permute-start.8 = (bf16[140,256]{1,0:T(8,128)(2,1)S(1)}, bf16[140,256]{1,0:T(8,128)(2,1)S(1)}, u32[]{:S(2)}, u32[]{:S(2)}) collective-permute-start(bf16[140,256]{1,0:T(8,128)(2,1)S(1)} %add_convert_fusion.8), channel_id=1, source_target_pairs={{0,2},{1,3},{2,0},{3,1},{4,6},{5,7},{6,4},{7,5},{8,10},{9,11},{10,... | collective-permute-start | bytes 215048 | tf_op jit(solution)/shard_map/ppermute | solution.py:168
  46.8 2.1 %collective-permute-done.8 = bf16[140,256]{1,0:T(8,128)(2,1)S(1)} collective-permute-done((bf16[140,256]{1,0:T(8,128)(2,1)S(1)}, bf16[140,256]{1,0:T(8,128)(2,1)S(1)}, u32[]{:S(2)}, u32[]{:S(2)}) %collective-permute-start.8) | collective-permute-done | bytes 71712 | tf_op jit(solution)/shard_map/ppermute | solution.py:168
  49.0 1.5 %collective-permute-done.14 = bf16[140,256]{1,0:T(8,128)(2,1)S(1)} collective-permute-done((bf16[140,256]{1,0:T(8,128)(2,1)S(1)}, bf16[140,256]{1,0:T(8,128)(2,1)S(1)}, u32[]{:S(2)}, u32[]{:S(2)}) %collective-permute-start.14) | collective-permute-done | bytes 71712 | tf_op jit(solution)/shard_map/ppermute | solution.py:168
  50.8 1.2 %collective-permute-done.15 = bf16[280,256]{1,0:T(8,128)(2,1)S(1)} collective-permute-done((bf16[280,256]{1,0:T(8,128)(2,1)S(1)}, bf16[280,256]{1,0:T(8,128)(2,1)S(1)}, u32[]{:S(2)}, u32[]{:S(2)}) %collective-permute-start.15) | collective-permute-done | bytes 143392 | tf_op jit(solution)/shard_map/ppermute | solution.py:168
  52.1 1.1 %fusion.13 = f32[512,512]{1,0:T(8,128)} fusion(bf16[560,256]{1,0:T(8,128)(2,1)S(1)} %maximum_select_fusion.1, bf16[560,256]{1,0:T(8,128)(2,1)S(1)} %maximum_select_fusion), kind=kLoop, calls=%fused_computation.32 | loop fusion | flops 1048576 | bytes 1622016 | tf_op jit(solution)/shard_map/convert_element_type | solution.py:243
  53.2 3.0 %fusion.10 = f32[2048,512]{1,0:T(8,128)} fusion(bf16[32,2048]{1,0:T(8,128)(2,1)S(1)} %convolution_convert_fusion, bf16[32,512]{1,0:T(8,128)(2,1)S(1)} %pad_maximum_fusion.1, bf16[512,512]{1,0:T(8,128)(2,1)S(1)} %copy-done.1, bf16[32,512]{1,0:T(8,128)(2,1)S(1)} %fusion.8), kind=kOutput, calls=%fused_computation.23 | convolution fusion | flops 83968000 | bytes 4915200 | tf_op jit(solution)/shard_map/dot_general | solution.py:98
  56.2 1.3 %fusion.49 = f32[512,512]{1,0:T(8,128)} fusion(bf16[32,512]{1,0:T(8,128)(2,1)S(1)} %fusion.8, bf16[32,512]{1,0:T(8,128)(2,1)S(1)} %pad_maximum_fusion.1), kind=kOutput, calls=%fused_computation.93 | convolution fusion | flops 16777216 | bytes 1114112 | tf_op jit(solution)/shard_map/dot_general | solution.py:91
  (68 shorter events, 13.9 us)
Async XLA Ops:
  0.6 16.6 %copy-start = (bf16[2048,512]{1,0:T(8,128)(2,1)S(1)}, bf16[2048,512]{1,0:T(8,128)(2,1)}, u32[]{:S(2)}) copy-start(bf16[2048,512]{1,0:T(8,128)(2,1)} %param.12) | copy-start | bytes 6291460
  0.6 5.9 %collective-permute-start = (bf16[2,2048]{1,0:T(2,128)(2,1)}, bf16[2,2048]{1,0:T(2,128)(2,1)S(1)}, u32[]{:S(2)}, u32[]{:S(2)}) collective-permute-start(bf16[2,2048]{1,0:T(2,128)(2,1)} %param.9), channel_id=1, source_target_pairs={{0,8},{1,9},{2,10},{3,11},{4,12},{5,13},{6,14},{7,15},{8,0},{9,1},... | collective-permute-start | bytes 24584 | tf_op jit(solution)/shard_map/ppermute | solution.py:119
  7.4 3.8 %collective-permute-start.1 = (bf16[4,2048]{1,0:T(4,128)(2,1)S(1)}, bf16[4,2048]{1,0:T(4,128)(2,1)S(1)}, u32[]{:S(2)}, u32[]{:S(2)}) collective-permute-start(bf16[4,2048]{1,0:T(4,128)(2,1)S(1)} %maximum_select_fusion.8), channel_id=1, source_target_pairs={{0,4},{1,5},{2,6},{3,7},{4,0},{5,1},{6,2},{7,3},{8,12},{9,13},{10,... | collective-permute-start | bytes 49160 | tf_op jit(solution)/shard_map/ppermute | solution.py:119
  11.2 6.5 %copy-start.1 = (bf16[512,512]{1,0:T(8,128)(2,1)S(1)}, bf16[512,512]{1,0:T(8,128)(2,1)}, u32[]{:S(2)}) copy-start(bf16[512,512]{1,0:T(8,128)(2,1)} %param.13) | copy-start | bytes 1572868
  11.3 4.0 %collective-permute-start.2 = (bf16[8,2048]{1,0:T(8,128)(2,1)S(1)}, bf16[8,2048]{1,0:T(8,128)(2,1)S(1)}, u32[]{:S(2)}, u32[]{:S(2)}) collective-permute-start(bf16[8,2048]{1,0:T(8,128)(2,1)S(1)} %maximum_select_fusion.7), channel_id=1, source_target_pairs={{0,2},{1,3},{2,0},{3,1},{4,6},{5,7},{6,4},{7,5},{8,10},{9,11},{10,... | collective-permute-start | bytes 98312 | tf_op jit(solution)/shard_map/ppermute | solution.py:119
  15.3 1.8 %collective-permute-start.3 = (bf16[16,2048]{1,0:T(8,128)(2,1)S(1)}, bf16[16,2048]{1,0:T(8,128)(2,1)S(1)}, u32[]{:S(2)}, u32[]{:S(2)}) collective-permute-start(bf16[16,2048]{1,0:T(8,128)(2,1)S(1)} %maximum_select_fusion.6), channel_id=1, source_target_pairs={{0,1},{1,0},{2,3},{3,2},{4,5},{5,4},{6,7},{7,6},{8,9},{9,8},{10,11... | collective-permute-start | bytes 196616 | tf_op jit(solution)/shard_map/ppermute | solution.py:119
  17.2 1.0 %copy-start.4 = (bf16[512,512]{1,0:T(8,128)(2,1)S(1)}, bf16[512,512]{1,0:T(8,128)(2,1)}, u32[]{:S(2)}) copy-start(bf16[512,512]{1,0:T(8,128)(2,1)} %constant.123.clone) | copy-start | bytes 1572868
  18.1 1.0 %copy-start.2 = (bf16[512,256]{1,0:T(8,128)(2,1)S(1)}, bf16[512,256]{1,0:T(8,128)(2,1)}, u32[]{:S(2)}) copy-start(bf16[512,256]{1,0:T(8,128)(2,1)} %constant.129) | copy-start | bytes 786436
  18.8 1.0 %copy-start.5 = (bf16[512,256]{1,0:T(8,128)(2,1)S(1)}, bf16[512,256]{1,0:T(8,128)(2,1)}, u32[]{:S(2)}) copy-start(bf16[512,256]{1,0:T(8,128)(2,1)} %constant.130) | copy-start | bytes 786436
  19.8 1.0 %copy-start.3 = (bf16[512,512]{1,0:T(8,128)(2,1)S(1)}, bf16[512,512]{1,0:T(8,128)(2,1)}, u32[]{:S(2)}) copy-start(bf16[512,512]{1,0:T(8,128)(2,1)} %param.16) | copy-start | bytes 1572868
  19.8 1.3 %copy-start.6 = (bf16[32,24,512]{2,1,0:T(8,128)(2,1)S(1)}, bf16[32,24,512]{2,1,0:T(8,128)(2,1)}, u32[]{:S(2)}) copy-start(bf16[32,24,512]{2,1,0:T(8,128)(2,1)} %param.10) | copy-start | bytes 2359300
  25.8 1.6 %collective-permute-start.10 = (bf16[280,256]{1,0:T(8,128)(2,1)S(1)}, bf16[280,256]{1,0:T(8,128)(2,1)S(1)}, u32[]{:S(2)}, u32[]{:S(2)}) collective-permute-start(bf16[280,256]{1,0:T(8,128)(2,1)S(1)} %get-tuple-element.9), channel_id=1, source_target_pairs={{0,1},{1,0},{2,3},{3,2},{4,5},{5,4},{6,7},{7,6},{8,9},{9,8},{10,11... | collective-permute-start | bytes 430088 | tf_op jit(solution)/shard_map/ppermute | solution.py:158
  26.3 1.4 %collective-permute-start.4 = (bf16[280,256]{1,0:T(8,128)(2,1)S(1)}, bf16[280,256]{1,0:T(8,128)(2,1)S(1)}, u32[]{:S(2)}, u32[]{:S(2)}) collective-permute-start(bf16[280,256]{1,0:T(8,128)(2,1)S(1)} %get-tuple-element.8), channel_id=1, source_target_pairs={{0,1},{1,0},{2,3},{3,2},{4,5},{5,4},{6,7},{7,6},{8,9},{9,8},{10,11... | collective-permute-start | bytes 430088 | tf_op jit(solution)/shard_map/ppermute | solution.py:158
  27.8 4.6 %collective-permute-start.5 = (bf16[140,256]{1,0:T(8,128)(2,1)S(1)}, bf16[140,256]{1,0:T(8,128)(2,1)S(1)}, u32[]{:S(2)}, u32[]{:S(2)}) collective-permute-start(bf16[140,256]{1,0:T(8,128)(2,1)S(1)} %select_convert_fusion.3), channel_id=1, source_target_pairs={{0,2},{1,3},{2,0},{3,1},{4,6},{5,7},{6,4},{7,5},{8,10},{9,11},{10,... | collective-permute-start | bytes 215048 | tf_op jit(solution)/shard_map/ppermute | solution.py:158
  29.8 4.5 %collective-permute-start.11 = (bf16[140,256]{1,0:T(8,128)(2,1)S(1)}, bf16[140,256]{1,0:T(8,128)(2,1)S(1)}, u32[]{:S(2)}, u32[]{:S(2)}) collective-permute-start(bf16[140,256]{1,0:T(8,128)(2,1)S(1)} %select_convert_fusion.2), channel_id=1, source_target_pairs={{0,4},{1,5},{2,6},{3,7},{4,0},{5,1},{6,2},{7,3},{8,12},{9,13},{10,... | collective-permute-start | bytes 215048 | tf_op jit(solution)/shard_map/ppermute | solution.py:158
  32.4 4.4 %collective-permute-start.6 = (bf16[140,256]{1,0:T(8,128)(2,1)S(1)}, bf16[140,256]{1,0:T(8,128)(2,1)S(1)}, u32[]{:S(2)}, u32[]{:S(2)}) collective-permute-start(bf16[140,256]{1,0:T(8,128)(2,1)S(1)} %add_convert_fusion.10), channel_id=1, source_target_pairs={{0,4},{1,5},{2,6},{3,7},{4,0},{5,1},{6,2},{7,3},{8,12},{9,13},{10,... | collective-permute-start | bytes 215048 | tf_op jit(solution)/shard_map/ppermute | solution.py:164
  34.3 5.4 %collective-permute-start.12 = (bf16[140,256]{1,0:T(8,128)(2,1)S(1)}, bf16[140,256]{1,0:T(8,128)(2,1)S(1)}, u32[]{:S(2)}, u32[]{:S(2)}) collective-permute-start(bf16[140,256]{1,0:T(8,128)(2,1)S(1)} %add_convert_fusion.7), channel_id=1, source_target_pairs={{0,2},{1,3},{2,0},{3,1},{4,6},{5,7},{6,4},{7,5},{8,10},{9,11},{10,... | collective-permute-start | bytes 215048 | tf_op jit(solution)/shard_map/ppermute | solution.py:164
  36.9 7.6 %collective-permute-start.7 = (bf16[140,256]{1,0:T(8,128)(2,1)S(1)}, bf16[140,256]{1,0:T(8,128)(2,1)S(1)}, u32[]{:S(2)}, u32[]{:S(2)}) collective-permute-start(bf16[140,256]{1,0:T(8,128)(2,1)S(1)} %add_convert_fusion.9), channel_id=1, source_target_pairs={{0,8},{1,9},{2,10},{3,11},{4,12},{5,13},{6,14},{7,15},{8,0},{9,1},... | collective-permute-start | bytes 215048 | tf_op jit(solution)/shard_map/ppermute | solution.py:164
  39.8 6.3 %collective-permute-start.13 = (bf16[140,256]{1,0:T(8,128)(2,1)S(1)}, bf16[140,256]{1,0:T(8,128)(2,1)S(1)}, u32[]{:S(2)}, u32[]{:S(2)}) collective-permute-start(bf16[140,256]{1,0:T(8,128)(2,1)S(1)} %add_convert_fusion.6), channel_id=1, source_target_pairs={{0,8},{1,9},{2,10},{3,11},{4,12},{5,13},{6,14},{7,15},{8,0},{9,1},... | collective-permute-start | bytes 215048 | tf_op jit(solution)/shard_map/ppermute | solution.py:164
  44.5 4.4 %collective-permute-start.8 = (bf16[140,256]{1,0:T(8,128)(2,1)S(1)}, bf16[140,256]{1,0:T(8,128)(2,1)S(1)}, u32[]{:S(2)}, u32[]{:S(2)}) collective-permute-start(bf16[140,256]{1,0:T(8,128)(2,1)S(1)} %add_convert_fusion.8), channel_id=1, source_target_pairs={{0,2},{1,3},{2,0},{3,1},{4,6},{5,7},{6,4},{7,5},{8,10},{9,11},{10,... | collective-permute-start | bytes 215048 | tf_op jit(solution)/shard_map/ppermute | solution.py:168
  46.1 4.4 %collective-permute-start.14 = (bf16[140,256]{1,0:T(8,128)(2,1)S(1)}, bf16[140,256]{1,0:T(8,128)(2,1)S(1)}, u32[]{:S(2)}, u32[]{:S(2)}) collective-permute-start(bf16[140,256]{1,0:T(8,128)(2,1)S(1)} %add_convert_fusion.5), channel_id=1, source_target_pairs={{0,4},{1,5},{2,6},{3,7},{4,0},{5,1},{6,2},{7,3},{8,12},{9,13},{10,... | collective-permute-start | bytes 215048 | tf_op jit(solution)/shard_map/ppermute | solution.py:168
  48.9 1.7 %collective-permute-start.9 = (bf16[280,256]{1,0:T(8,128)(2,1)S(1)}, bf16[280,256]{1,0:T(8,128)(2,1)S(1)}, u32[]{:S(2)}, u32[]{:S(2)}) collective-permute-start(bf16[280,256]{1,0:T(8,128)(2,1)S(1)} %maximum_select_fusion.2), channel_id=1, source_target_pairs={{0,1},{1,0},{2,3},{3,2},{4,5},{5,4},{6,7},{7,6},{8,9},{9,8},{10,11... | collective-permute-start | bytes 430088 | tf_op jit(solution)/shard_map/ppermute | solution.py:168
  50.5 1.4 %collective-permute-start.15 = (bf16[280,256]{1,0:T(8,128)(2,1)S(1)}, bf16[280,256]{1,0:T(8,128)(2,1)S(1)}, u32[]{:S(2)}, u32[]{:S(2)}) collective-permute-start(bf16[280,256]{1,0:T(8,128)(2,1)S(1)} %maximum_select_fusion.3), channel_id=1, source_target_pairs={{0,1},{1,0},{2,3},{3,2},{4,5},{5,4},{6,7},{7,6},{8,9},{9,8},{10,11... | collective-permute-start | bytes 430088 | tf_op jit(solution)/shard_map/ppermute | solution.py:168

commit v20 on v13

--- a/solution.py
+++ b/solution.py
@@ -146,7 +146,7 @@
 
 def sum_halving(values, axis_name, wire=jnp.bfloat16, halving_levels=2):
     count = lax.axis_size(axis_name)
-    if not _is_power_of_two(count) or values.shape[0] % count != 0:
+    if not _is_power_of_two(count) or values.shape[0] % min(count, 2**halving_levels) != 0:
         return lax.psum(values, axis_name)
     position = lax.axis_index(axis_name)
     distance = 1
@@ -217,29 +217,29 @@
     derivative_bottleneck = jnp.einsum(
         "orm,rm->om", derivative_entering.reshape(samples, sub_dev, width), gain_row_values
     )
-    count = lax.axis_size("freq")
     half_width = grad_filter.shape[1]
     filter_rows = jnp.concatenate(
         [grad_filter, jnp.zeros((grad_filter.shape[0], width - half_width), jnp.float32)], 1
     )
-    packed_rows = grad_out.shape[0] + samples + filter_rows.shape[0]
-    padding = -packed_rows % count
+    rows_out = grad_out.shape[0]
+    small_rows = samples + filter_rows.shape[0]
+    packed_rows = rows_out + small_rows
+    padding = -packed_rows % 8
     packed = jnp.concatenate(
         [
-            grad_out,
             derivative_bottleneck,
             filter_rows,
+            grad_out,
             jnp.zeros((padding, width), jnp.float32),
         ],
         0,
     )
-    packed = sum_halving(packed, "freq")
-    rows_out = grad_out.shape[0]
-    grad_out = packed[:rows_out].astype(jnp.float32)
-    derivative_bottleneck = packed[rows_out : rows_out + samples].astype(jnp.float32)
-    grad_filter = packed[
-        rows_out + samples : rows_out + samples + filter_rows.shape[0], :half_width
-    ].astype(jnp.float32)
+    rows_each = packed.shape[0] // 2
+    first = sum_halving(packed[:rows_each], "freq")
+    second = sum_halving(packed[rows_each:], "freq")
+    derivative_bottleneck = first[:samples].astype(jnp.float32)
+    grad_filter = first[samples:small_rows, :half_width].astype(jnp.float32)
+    grad_out = jnp.concatenate([first[small_rows:], second], 0)[:rows_out].astype(jnp.float32)
     grad_enc, grad_dec = encoder_grads(
         inputs_by_sample, codes_by_sample, derivative_bottleneck, decoder_weight
     )

time: 60.1 us -> 58.4 us (0.972)
  waiting for transfers between devices: 23.9 us -> 16 us
  starting transfers between devices: 16.6 us -> 21.6 us
  other arithmetic: 4.81 us -> 5.83 us
    ppermute x2 -> x4, waiting for transfers between devices: 8.73 us -> 4.28 us  [sum_halving(): arrived = lax.ppermute(values, axis_name, _exchange_pairs(count, distance))]
    ppermute x2 -> x4, starting transfers between devices: 4.7 us -> 7.76 us  [sum_halving(): arrived = lax.ppermute(values, axis_name, _exchange_pairs(count, distance))]
    ppermute x2 -> x4, waiting for transfers between devices: 5.12 us -> 3.11 us  [sum_halving(): other = lax.ppermute(values, axis_name, _exchange_pairs(count, distance))]
    ppermute x2 -> x4, waiting for transfers between devices: 5.59 us -> 3.71 us  [sum_halving(): arrived = lax.ppermute(send, axis_name, _exchange_pairs(count, distance))]
    ppermute x2 -> x4, starting transfers between devices: 1.71 us -> 2.98 us  [sum_halving(): other = lax.ppermute(values, axis_name, _exchange_pairs(count, distance))]
    select_n x2 -> x4, other arithmetic: 0.32 us -> 1.29 us  [sum_halving(): jnp.where(lower, jnp.concatenate([values, other], 0), jnp.concatenate([ot...]
    ppermute x2 -> x4, starting transfers between devices: 2.12 us -> 2.79 us  [sum_halving(): arrived = lax.ppermute(send, axis_name, _exchange_pairs(count, distance))]
  transfers between devices with their start and end apart: 10 -> 16, of which waited for: 10 -> 10; matrix products, arithmetic and copies ran while one was open for 4% -> 13% of each run, Pallas kernels for 0% -> 0%
where the time goes in v20:
time: 58.4 us; the launch traced here: 58 us
  starting transfers between devices  21.6 us (37%)
  waiting for transfers between devices  16 us (27%)
  matrix products  10.8 us (18%)
  other arithmetic  5.83 us (10%)
  local copies, waits for them, and re-layouts  2.79 us (5%)
  between operations  0.93 us (2%)
    ppermute x4, starting transfers between devices, gather_rows(): other = lax.ppermute(block, axis_name, _exchange_pairs(count, distance))  8.06 us
    ppermute x4, starting transfers between devices, sum_halving(): arrived = lax.ppermute(values, axis_name, _exchange_pairs(count, distance))  7.76 us
    ppermute x4, waiting for transfers between devices, gather_rows(): other = lax.ppermute(block, axis_name, _exchange_pairs(count, distance))  4.91 us
    ppermute x4, waiting for transfers between devices, sum_halving(): arrived = lax.ppermute(values, axis_name, _exchange_pairs(count, distance))  4.28 us
    ppermute x4, waiting for transfers between devices, sum_halving(): arrived = lax.ppermute(send, axis_name, _exchange_pairs(count, distance))  3.71 us
    ppermute x4, waiting for transfers between devices, sum_halving(): other = lax.ppermute(values, axis_name, _exchange_pairs(count, distance))  3.11 us
    ppermute x4, starting transfers between devices, sum_halving(): other = lax.ppermute(values, axis_name, _exchange_pairs(count, distance))  2.98 us
    dot_general x1, matrix products, encoder_grads(): lax.dot_general(inputs_rows, grad_pre, (((0,), (0,)), ((), ())), preferre...  2.96 us
  transfers between devices with their start and end apart: 16, of which 10 were waited for; matrix products, arithmetic and copies ran while one was open for 13% of the time, Pallas kernels for 0%

profile of v20, /device:TPU:0, one launch (start us, length us, event | category | flops | bytes accessed | tf_op | source)
XLA Modules:
  0.0 58.0 jit_solution(345813438384346677)
XLA Ops:
  0.6 4.1 %collective-permute-start = (bf16[2,2048]{1,0:T(2,128)(2,1)}, bf16[2,2048]{1,0:T(2,128)(2,1)S(1)}, u32[]{:S(2)}, u32[]{:S(2)}) collective-permute-start(bf16[2,2048]{1,0:T(2,128)(2,1)} %param.9), channel_id=1, source_target_pairs={{0,8},{1,9},{2,10},{3,11},{4,12},{5,13},{6,14},{7,15},{8,0},{9,1},... | collective-permute-start | bytes 24584 | tf_op jit(solution)/shard_map/ppermute | solution.py:119
  4.7 1.8 %collective-permute-done = bf16[2,2048]{1,0:T(2,128)(2,1)S(1)} collective-permute-done((bf16[2,2048]{1,0:T(2,128)(2,1)}, bf16[2,2048]{1,0:T(2,128)(2,1)S(1)}, u32[]{:S(2)}, u32[]{:S(2)}) %collective-permute-start) | collective-permute-done | bytes 8224 | tf_op jit(solution)/shard_map/ppermute | solution.py:119
  7.4 2.0 %collective-permute-start.1 = (bf16[4,2048]{1,0:T(4,128)(2,1)S(1)}, bf16[4,2048]{1,0:T(4,128)(2,1)S(1)}, u32[]{:S(2)}, u32[]{:S(2)}) collective-permute-start(bf16[4,2048]{1,0:T(4,128)(2,1)S(1)} %maximum_select_fusion.8), channel_id=1, source_target_pairs={{0,4},{1,5},{2,6},{3,7},{4,0},{5,1},{6,2},{7,3},{8,12},{9,13},{10,... | collective-permute-start | bytes 49160 | tf_op jit(solution)/shard_map/ppermute | solution.py:119
  9.4 1.8 %collective-permute-done.1 = bf16[4,2048]{1,0:T(4,128)(2,1)S(1)} collective-permute-done((bf16[4,2048]{1,0:T(4,128)(2,1)S(1)}, bf16[4,2048]{1,0:T(4,128)(2,1)S(1)}, u32[]{:S(2)}, u32[]{:S(2)}) %collective-permute-start.1) | collective-permute-done | bytes 16416 | tf_op jit(solution)/shard_map/ppermute | solution.py:119
  11.3 1.9 %collective-permute-start.2 = (bf16[8,2048]{1,0:T(8,128)(2,1)S(1)}, bf16[8,2048]{1,0:T(8,128)(2,1)S(1)}, u32[]{:S(2)}, u32[]{:S(2)}) collective-permute-start(bf16[8,2048]{1,0:T(8,128)(2,1)S(1)} %maximum_select_fusion.7), channel_id=1, source_target_pairs={{0,2},{1,3},{2,0},{3,1},{4,6},{5,7},{6,4},{7,5},{8,10},{9,11},{10,... | collective-permute-start | bytes 98312 | tf_op jit(solution)/shard_map/ppermute | solution.py:119
  14.0 1.2 %collective-permute-done.2 = bf16[8,2048]{1,0:T(8,128)(2,1)S(1)} collective-permute-done((bf16[8,2048]{1,0:T(8,128)(2,1)S(1)}, bf16[8,2048]{1,0:T(8,128)(2,1)S(1)}, u32[]{:S(2)}, u32[]{:S(2)}) %collective-permute-start.2) | collective-permute-done | bytes 32800 | tf_op jit(solution)/shard_map/ppermute | solution.py:119
  22.9 1.2 %fusion.11 = f32[768,512]{1,0:T(8,128)S(1)} fusion(bf16[512,512]{1,0:T(8,128)(2,1)S(1)} %copy-done.4, f32[768,512]{1,0:T(8,128)S(1)} %get-tuple-element.16, f32[768,512]{1,0:T(8,128)S(1)} %convolution_add_fusion), kind=kOutput, calls=%fused_computation.30 | convolution fusion | flops 410517504 | bytes 5242880 | tf_op jit(solution)/shard_map/dot_general | solution.py:71
  26.3 0.9 %collective-permute-done.4 = bf16[138,512]{1,0:T(8,128)(2,1)S(1)} collective-permute-done((bf16[138,512]{1,0:T(8,128)(2,1)S(1)}, bf16[138,512]{1,0:T(8,128)(2,1)S(1)}, u32[]{:S(2)}, u32[]{:S(2)}) %collective-permute-start.4) | collective-permute-done | bytes 141344 | tf_op jit(solution)/shard_map/ppermute | solution.py:158
  27.7 1.9 %collective-permute-start.5 = (bf16[69,512]{1,0:T(8,128)(2,1)S(1)}, bf16[69,512]{1,0:T(8,128)(2,1)S(1)}, u32[]{:S(2)}, u32[]{:S(2)}) collective-permute-start(bf16[69,512]{1,0:T(8,128)(2,1)S(1)} %select_convert_fusion.3), channel_id=1, source_target_pairs={{0,2},{1,3},{2,0},{3,1},{4,6},{5,7},{6,4},{7,5},{8,10},{9,11},{10,... | collective-permute-start | bytes 211976 | tf_op jit(solution)/shard_map/ppermute | solution.py:158
  29.9 2.4 %collective-permute-done.5 = bf16[69,512]{1,0:T(8,128)(2,1)S(1)} collective-permute-done((bf16[69,512]{1,0:T(8,128)(2,1)S(1)}, bf16[69,512]{1,0:T(8,128)(2,1)S(1)}, u32[]{:S(2)}, u32[]{:S(2)}) %collective-permute-start.5) | collective-permute-done | bytes 70688 | tf_op jit(solution)/shard_map/ppermute | solution.py:158
  32.4 2.1 %collective-permute-start.6 = (bf16[69,512]{1,0:T(8,128)(2,1)S(1)}, bf16[69,512]{1,0:T(8,128)(2,1)S(1)}, u32[]{:S(2)}, u32[]{:S(2)}) collective-permute-start(bf16[69,512]{1,0:T(8,128)(2,1)S(1)} %add_convert_fusion.10), channel_id=1, source_target_pairs={{0,4},{1,5},{2,6},{3,7},{4,0},{5,1},{6,2},{7,3},{8,12},{9,13},{10,... | collective-permute-start | bytes 211976 | tf_op jit(solution)/shard_map/ppermute | solution.py:164
  34.5 1.2 %collective-permute-start.12 = (bf16[69,512]{1,0:T(8,128)(2,1)S(1)}, bf16[69,512]{1,0:T(8,128)(2,1)S(1)}, u32[]{:S(2)}, u32[]{:S(2)}) collective-permute-start(bf16[69,512]{1,0:T(8,128)(2,1)S(1)} %add_convert_fusion.7), channel_id=1, source_target_pairs={{0,4},{1,5},{2,6},{3,7},{4,0},{5,1},{6,2},{7,3},{8,12},{9,13},{10,... | collective-permute-start | bytes 211976 | tf_op jit(solution)/shard_map/ppermute | solution.py:164
  35.8 1.8 %collective-permute-done.6 = bf16[69,512]{1,0:T(8,128)(2,1)S(1)} collective-permute-done((bf16[69,512]{1,0:T(8,128)(2,1)S(1)}, bf16[69,512]{1,0:T(8,128)(2,1)S(1)}, u32[]{:S(2)}, u32[]{:S(2)}) %collective-permute-start.6) | collective-permute-done | bytes 70688 | tf_op jit(solution)/shard_map/ppermute | solution.py:164
  37.6 2.7 %collective-permute-start.7 = (bf16[69,512]{1,0:T(8,128)(2,1)S(1)}, bf16[69,512]{1,0:T(8,128)(2,1)S(1)}, u32[]{:S(2)}, u32[]{:S(2)}) collective-permute-start(bf16[69,512]{1,0:T(8,128)(2,1)S(1)} %add_convert_fusion.9), channel_id=1, source_target_pairs={{0,8},{1,9},{2,10},{3,11},{4,12},{5,13},{6,14},{7,15},{8,0},{9,1},... | collective-permute-start | bytes 211976 | tf_op jit(solution)/shard_map/ppermute | solution.py:164
  40.3 1.7 %collective-permute-start.13 = (bf16[69,512]{1,0:T(8,128)(2,1)S(1)}, bf16[69,512]{1,0:T(8,128)(2,1)S(1)}, u32[]{:S(2)}, u32[]{:S(2)}) collective-permute-start(bf16[69,512]{1,0:T(8,128)(2,1)S(1)} %add_convert_fusion.6), channel_id=1, source_target_pairs={{0,8},{1,9},{2,10},{3,11},{4,12},{5,13},{6,14},{7,15},{8,0},{9,1},... | collective-permute-start | bytes 211976 | tf_op jit(solution)/shard_map/ppermute | solution.py:164
  42.0 2.5 %collective-permute-done.7 = bf16[69,512]{1,0:T(8,128)(2,1)S(1)} collective-permute-done((bf16[69,512]{1,0:T(8,128)(2,1)S(1)}, bf16[69,512]{1,0:T(8,128)(2,1)S(1)}, u32[]{:S(2)}, u32[]{:S(2)}) %collective-permute-start.7) | collective-permute-done | bytes 70688 | tf_op jit(solution)/shard_map/ppermute | solution.py:164
  44.5 1.7 %collective-permute-start.8 = (bf16[69,512]{1,0:T(8,128)(2,1)S(1)}, bf16[69,512]{1,0:T(8,128)(2,1)S(1)}, u32[]{:S(2)}, u32[]{:S(2)}) collective-permute-start(bf16[69,512]{1,0:T(8,128)(2,1)S(1)} %add_convert_fusion.8), channel_id=1, source_target_pairs={{0,2},{1,3},{2,0},{3,1},{4,6},{5,7},{6,4},{7,5},{8,10},{9,11},{10,... | collective-permute-start | bytes 211976 | tf_op jit(solution)/shard_map/ppermute | solution.py:169
  46.2 1.2 %collective-permute-start.14 = (bf16[69,512]{1,0:T(8,128)(2,1)S(1)}, bf16[69,512]{1,0:T(8,128)(2,1)S(1)}, u32[]{:S(2)}, u32[]{:S(2)}) collective-permute-start(bf16[69,512]{1,0:T(8,128)(2,1)S(1)} %add_convert_fusion.5), channel_id=1, source_target_pairs={{0,2},{1,3},{2,0},{3,1},{4,6},{5,7},{6,4},{7,5},{8,10},{9,11},{10,... | collective-permute-start | bytes 211976 | tf_op jit(solution)/shard_map/ppermute | solution.py:169
  47.4 1.6 %collective-permute-done.8 = bf16[69,512]{1,0:T(8,128)(2,1)S(1)} collective-permute-done((bf16[69,512]{1,0:T(8,128)(2,1)S(1)}, bf16[69,512]{1,0:T(8,128)(2,1)S(1)}, u32[]{:S(2)}, u32[]{:S(2)}) %collective-permute-start.8) | collective-permute-done | bytes 70688 | tf_op jit(solution)/shard_map/ppermute | solution.py:169
  49.1 1.6 %collective-permute-done.14 = bf16[69,512]{1,0:T(8,128)(2,1)S(1)} collective-permute-done((bf16[69,512]{1,0:T(8,128)(2,1)S(1)}, bf16[69,512]{1,0:T(8,128)(2,1)S(1)}, u32[]{:S(2)}, u32[]{:S(2)}) %collective-permute-start.14) | collective-permute-done | bytes 70688 | tf_op jit(solution)/shard_map/ppermute | solution.py:169
  51.0 1.3 %fusion.37 = f32[512,512]{1,0:T(8,128)} fusion(bf16[32,512]{1,0:T(8,128)(2,1)S(1)} %fusion.8, bf16[276,512]{1,0:T(8,128)(2,1)S(1)} %maximum_select_fusion), kind=kOutput, calls=%fused_computation.77 | convolution fusion | flops 16777216 | bytes 1114112 | tf_op jit(solution)/shard_map/dot_general | solution.py:91
  52.2 3.0 %fusion.10 = f32[2048,512]{1,0:T(8,128)} fusion(bf16[32,2048]{1,0:T(8,128)(2,1)S(1)} %convolution_convert_fusion, bf16[512,512]{1,0:T(8,128)(2,1)S(1)} %copy-done.1, bf16[32,512]{1,0:T(8,128)(2,1)S(1)} %fusion.8, bf16[276,512]{1,0:T(8,128)(2,1)S(1)} %maximum_select_fusion), kind=kOutput, calls=%fused_computation.22 | convolution fusion | flops 83968000 | bytes 4915200 | tf_op jit(solution)/shard_map/dot_general | solution.py:98
  55.8 1.1 %maximum_select_fusion.1 = bf16[276,512]{1,0:T(8,128)(2,1)S(1)} fusion(bf16[138,512]{1,0:T(8,128)(2,1)} %collective-permute-done.15, bf16[138,512]{1,0:T(8,128)(2,1)S(1)} %maximum_select_fusion.3, pred[]{:T(512)S(6)} %eq.52), kind=kLoop, calls=%fused_computation.53 | loop fusion | flops 1271808 | bytes 565249 | tf_op jit(solution)/shard_map/jit(_where)/select_n | solution.py:171
  56.9 1.1 %fusion.13 = f32[512,512]{1,0:T(8,128)} fusion(bf16[276,512]{1,0:T(8,128)(2,1)S(1)} %maximum_select_fusion.1, bf16[242,512]{1,0:T(8,128)(2,1)S(1)} %slice.102), kind=kLoop, calls=%fused_computation.32 | loop fusion | flops 1048576 | bytes 1579008 | tf_op jit(solution)/shard_map/convert_element_type | solution.py:242
  (65 shorter events, 13.3 us)
Async XLA Ops:
  0.6 16.5 %copy-start = (bf16[2048,512]{1,0:T(8,128)(2,1)S(1)}, bf16[2048,512]{1,0:T(8,128)(2,1)}, u32[]{:S(2)}) copy-start(bf16[2048,512]{1,0:T(8,128)(2,1)} %param.12) | copy-start | bytes 6291460
  0.6 5.9 %collective-permute-start = (bf16[2,2048]{1,0:T(2,128)(2,1)}, bf16[2,2048]{1,0:T(2,128)(2,1)S(1)}, u32[]{:S(2)}, u32[]{:S(2)}) collective-permute-start(bf16[2,2048]{1,0:T(2,128)(2,1)} %param.9), channel_id=1, source_target_pairs={{0,8},{1,9},{2,10},{3,11},{4,12},{5,13},{6,14},{7,15},{8,0},{9,1},... | collective-permute-start | bytes 24584 | tf_op jit(solution)/shard_map/ppermute | solution.py:119
  7.4 3.8 %collective-permute-start.1 = (bf16[4,2048]{1,0:T(4,128)(2,1)S(1)}, bf16[4,2048]{1,0:T(4,128)(2,1)S(1)}, u32[]{:S(2)}, u32[]{:S(2)}) collective-permute-start(bf16[4,2048]{1,0:T(4,128)(2,1)S(1)} %maximum_select_fusion.8), channel_id=1, source_target_pairs={{0,4},{1,5},{2,6},{3,7},{4,0},{5,1},{6,2},{7,3},{8,12},{9,13},{10,... | collective-permute-start | bytes 49160 | tf_op jit(solution)/shard_map/ppermute | solution.py:119
  11.2 6.4 %copy-start.1 = (bf16[512,512]{1,0:T(8,128)(2,1)S(1)}, bf16[512,512]{1,0:T(8,128)(2,1)}, u32[]{:S(2)}) copy-start(bf16[512,512]{1,0:T(8,128)(2,1)} %param.13) | copy-start | bytes 1572868
  11.3 4.0 %collective-permute-start.2 = (bf16[8,2048]{1,0:T(8,128)(2,1)S(1)}, bf16[8,2048]{1,0:T(8,128)(2,1)S(1)}, u32[]{:S(2)}, u32[]{:S(2)}) collective-permute-start(bf16[8,2048]{1,0:T(8,128)(2,1)S(1)} %maximum_select_fusion.7), channel_id=1, source_target_pairs={{0,2},{1,3},{2,0},{3,1},{4,6},{5,7},{6,4},{7,5},{8,10},{9,11},{10,... | collective-permute-start | bytes 98312 | tf_op jit(solution)/shard_map/ppermute | solution.py:119
  15.3 1.7 %collective-permute-start.3 = (bf16[16,2048]{1,0:T(8,128)(2,1)S(1)}, bf16[16,2048]{1,0:T(8,128)(2,1)S(1)}, u32[]{:S(2)}, u32[]{:S(2)}) collective-permute-start(bf16[16,2048]{1,0:T(8,128)(2,1)S(1)} %maximum_select_fusion.6), channel_id=1, source_target_pairs={{0,1},{1,0},{2,3},{3,2},{4,5},{5,4},{6,7},{7,6},{8,9},{9,8},{10,11... | collective-permute-start | bytes 196616 | tf_op jit(solution)/shard_map/ppermute | solution.py:119
  17.1 1.0 %copy-start.4 = (bf16[512,512]{1,0:T(8,128)(2,1)S(1)}, bf16[512,512]{1,0:T(8,128)(2,1)}, u32[]{:S(2)}) copy-start(bf16[512,512]{1,0:T(8,128)(2,1)} %constant.123.clone) | copy-start | bytes 1572868
  18.0 1.0 %copy-start.2 = (bf16[512,256]{1,0:T(8,128)(2,1)S(1)}, bf16[512,256]{1,0:T(8,128)(2,1)}, u32[]{:S(2)}) copy-start(bf16[512,256]{1,0:T(8,128)(2,1)} %constant.131) | copy-start | bytes 786436
  18.8 1.0 %copy-start.5 = (bf16[512,256]{1,0:T(8,128)(2,1)S(1)}, bf16[512,256]{1,0:T(8,128)(2,1)}, u32[]{:S(2)}) copy-start(bf16[512,256]{1,0:T(8,128)(2,1)} %constant.132) | copy-start | bytes 786436
  19.7 1.0 %copy-start.3 = (bf16[512,512]{1,0:T(8,128)(2,1)S(1)}, bf16[512,512]{1,0:T(8,128)(2,1)}, u32[]{:S(2)}) copy-start(bf16[512,512]{1,0:T(8,128)(2,1)} %param.16) | copy-start | bytes 1572868
  19.7 1.3 %copy-start.6 = (bf16[32,24,512]{2,1,0:T(8,128)(2,1)S(1)}, bf16[32,24,512]{2,1,0:T(8,128)(2,1)}, u32[]{:S(2)}) copy-start(bf16[32,24,512]{2,1,0:T(8,128)(2,1)} %param.10) | copy-start | bytes 2359300
  25.6 1.6 %collective-permute-start.4 = (bf16[138,512]{1,0:T(8,128)(2,1)S(1)}, bf16[138,512]{1,0:T(8,128)(2,1)S(1)}, u32[]{:S(2)}, u32[]{:S(2)}) collective-permute-start(bf16[138,512]{1,0:T(8,128)(2,1)S(1)} %get-tuple-element.6), channel_id=1, source_target_pairs={{0,1},{1,0},{2,3},{3,2},{4,5},{5,4},{6,7},{7,6},{8,9},{9,8},{10,11... | collective-permute-start | bytes 423944 | tf_op jit(solution)/shard_map/ppermute | solution.py:158
  26.2 1.4 %collective-permute-start.10 = (bf16[138,512]{1,0:T(8,128)(2,1)S(1)}, bf16[138,512]{1,0:T(8,128)(2,1)S(1)}, u32[]{:S(2)}, u32[]{:S(2)}) collective-permute-start(bf16[138,512]{1,0:T(8,128)(2,1)S(1)} %get-tuple-element.10), channel_id=1, source_target_pairs={{0,1},{1,0},{2,3},{3,2},{4,5},{5,4},{6,7},{7,6},{8,9},{9,8},{10,11... | collective-permute-start | bytes 423944 | tf_op jit(solution)/shard_map/ppermute | solution.py:158
  27.7 4.6 %collective-permute-start.5 = (bf16[69,512]{1,0:T(8,128)(2,1)S(1)}, bf16[69,512]{1,0:T(8,128)(2,1)S(1)}, u32[]{:S(2)}, u32[]{:S(2)}) collective-permute-start(bf16[69,512]{1,0:T(8,128)(2,1)S(1)} %select_convert_fusion.3), channel_id=1, source_target_pairs={{0,2},{1,3},{2,0},{3,1},{4,6},{5,7},{6,4},{7,5},{8,10},{9,11},{10,... | collective-permute-start | bytes 211976 | tf_op jit(solution)/shard_map/ppermute | solution.py:158
  29.7 4.8 %collective-permute-start.11 = (bf16[69,512]{1,0:T(8,128)(2,1)S(1)}, bf16[69,512]{1,0:T(8,128)(2,1)S(1)}, u32[]{:S(2)}, u32[]{:S(2)}) collective-permute-start(bf16[69,512]{1,0:T(8,128)(2,1)S(1)} %select_convert_fusion.2), channel_id=1, source_target_pairs={{0,2},{1,3},{2,0},{3,1},{4,6},{5,7},{6,4},{7,5},{8,10},{9,11},{10,... | collective-permute-start | bytes 211976 | tf_op jit(solution)/shard_map/ppermute | solution.py:158
  32.4 5.2 %collective-permute-start.6 = (bf16[69,512]{1,0:T(8,128)(2,1)S(1)}, bf16[69,512]{1,0:T(8,128)(2,1)S(1)}, u32[]{:S(2)}, u32[]{:S(2)}) collective-permute-start(bf16[69,512]{1,0:T(8,128)(2,1)S(1)} %add_convert_fusion.10), channel_id=1, source_target_pairs={{0,4},{1,5},{2,6},{3,7},{4,0},{5,1},{6,2},{7,3},{8,12},{9,13},{10,... | collective-permute-start | bytes 211976 | tf_op jit(solution)/shard_map/ppermute | solution.py:164
  34.5 5.7 %collective-permute-start.12 = (bf16[69,512]{1,0:T(8,128)(2,1)S(1)}, bf16[69,512]{1,0:T(8,128)(2,1)S(1)}, u32[]{:S(2)}, u32[]{:S(2)}) collective-permute-start(bf16[69,512]{1,0:T(8,128)(2,1)S(1)} %add_convert_fusion.7), channel_id=1, source_target_pairs={{0,4},{1,5},{2,6},{3,7},{4,0},{5,1},{6,2},{7,3},{8,12},{9,13},{10,... | collective-permute-start | bytes 211976 | tf_op jit(solution)/shard_map/ppermute | solution.py:164
  37.6 6.9 %collective-permute-start.7 = (bf16[69,512]{1,0:T(8,128)(2,1)S(1)}, bf16[69,512]{1,0:T(8,128)(2,1)S(1)}, u32[]{:S(2)}, u32[]{:S(2)}) collective-permute-start(bf16[69,512]{1,0:T(8,128)(2,1)S(1)} %add_convert_fusion.9), channel_id=1, source_target_pairs={{0,8},{1,9},{2,10},{3,11},{4,12},{5,13},{6,14},{7,15},{8,0},{9,1},... | collective-permute-start | bytes 211976 | tf_op jit(solution)/shard_map/ppermute | solution.py:164
  40.3 5.9 %collective-permute-start.13 = (bf16[69,512]{1,0:T(8,128)(2,1)S(1)}, bf16[69,512]{1,0:T(8,128)(2,1)S(1)}, u32[]{:S(2)}, u32[]{:S(2)}) collective-permute-start(bf16[69,512]{1,0:T(8,128)(2,1)S(1)} %add_convert_fusion.6), channel_id=1, source_target_pairs={{0,8},{1,9},{2,10},{3,11},{4,12},{5,13},{6,14},{7,15},{8,0},{9,1},... | collective-permute-start | bytes 211976 | tf_op jit(solution)/shard_map/ppermute | solution.py:164
  44.5 4.4 %collective-permute-start.8 = (bf16[69,512]{1,0:T(8,128)(2,1)S(1)}, bf16[69,512]{1,0:T(8,128)(2,1)S(1)}, u32[]{:S(2)}, u32[]{:S(2)}) collective-permute-start(bf16[69,512]{1,0:T(8,128)(2,1)S(1)} %add_convert_fusion.8), channel_id=1, source_target_pairs={{0,2},{1,3},{2,0},{3,1},{4,6},{5,7},{6,4},{7,5},{8,10},{9,11},{10,... | collective-permute-start | bytes 211976 | tf_op jit(solution)/shard_map/ppermute | solution.py:169
  46.2 4.4 %collective-permute-start.14 = (bf16[69,512]{1,0:T(8,128)(2,1)S(1)}, bf16[69,512]{1,0:T(8,128)(2,1)S(1)}, u32[]{:S(2)}, u32[]{:S(2)}) collective-permute-start(bf16[69,512]{1,0:T(8,128)(2,1)S(1)} %add_convert_fusion.5), channel_id=1, source_target_pairs={{0,2},{1,3},{2,0},{3,1},{4,6},{5,7},{6,4},{7,5},{8,10},{9,11},{10,... | collective-permute-start | bytes 211976 | tf_op jit(solution)/shard_map/ppermute | solution.py:169
  49.0 1.8 %collective-permute-start.9 = (bf16[138,512]{1,0:T(8,128)(2,1)S(1)}, bf16[138,512]{1,0:T(8,128)(2,1)S(1)}, u32[]{:S(2)}, u32[]{:S(2)}) collective-permute-start(bf16[138,512]{1,0:T(8,128)(2,1)S(1)} %maximum_select_fusion.2), channel_id=1, source_target_pairs={{0,1},{1,0},{2,3},{3,2},{4,5},{5,4},{6,7},{7,6},{8,9},{9,8},{10,11... | collective-permute-start | bytes 423944 | tf_op jit(solution)/shard_map/ppermute | solution.py:169
  50.7 5.1 %collective-permute-start.15 = (bf16[138,512]{1,0:T(8,128)(2,1)S(1)}, bf16[138,512]{1,0:T(8,128)(2,1)}, u32[]{:S(2)}, u32[]{:S(2)}) collective-permute-start(bf16[138,512]{1,0:T(8,128)(2,1)S(1)} %maximum_select_fusion.3), channel_id=1, source_target_pairs={{0,1},{1,0},{2,3},{3,2},{4,5},{5,4},{6,7},{7,6},{8,9},{9,8},{10,11... | collective-permute-start | bytes 423944 | tf_op jit(solution)/shard_map/ppermute | solution.py:169

commit v21 on v20

--- a/solution.py
+++ b/solution.py
@@ -221,25 +221,10 @@
     filter_rows = jnp.concatenate(
         [grad_filter, jnp.zeros((grad_filter.shape[0], width - half_width), jnp.float32)], 1
     )
-    rows_out = grad_out.shape[0]
-    small_rows = samples + filter_rows.shape[0]
-    packed_rows = rows_out + small_rows
-    padding = -packed_rows % 8
-    packed = jnp.concatenate(
-        [
-            derivative_bottleneck,
-            filter_rows,
-            grad_out,
-            jnp.zeros((padding, width), jnp.float32),
-        ],
-        0,
-    )
-    rows_each = packed.shape[0] // 2
-    first = sum_halving(packed[:rows_each], "freq")
-    second = sum_halving(packed[rows_each:], "freq")
-    derivative_bottleneck = first[:samples].astype(jnp.float32)
-    grad_filter = first[samples:small_rows, :half_width].astype(jnp.float32)
-    grad_out = jnp.concatenate([first[small_rows:], second], 0)[:rows_out].astype(jnp.float32)
+    small = sum_whole(jnp.concatenate([derivative_bottleneck, filter_rows], 0), "freq")
+    grad_out = sum_halving(grad_out, "freq").astype(jnp.float32)
+    derivative_bottleneck = small[:samples]
+    grad_filter = small[samples:, :half_width]
     grad_enc, grad_dec = encoder_grads(
         inputs_by_sample, codes_by_sample, derivative_bottleneck, decoder_weight
     )

time: 58.4 us -> 62.4 us (1.068)
  waiting for transfers between devices: 16 us -> 22.1 us
  other arithmetic: 5.83 us -> 4 us
  starting transfers between devices: 21.6 us -> 20.8 us
    ppermute x0 -> x4, waiting for transfers between devices: none -> 10.7 us  [sum_whole(): lax.ppermute(values, axis_name, _exchange_pairs(count, distance))]
    ppermute x0 -> x4, starting transfers between devices: none -> 3.92 us  [sum_whole(): lax.ppermute(values, axis_name, _exchange_pairs(count, distance))]
    ppermute x4 -> x2, waiting for transfers between devices: 3.11 us -> 0.01 us  [sum_halving(): other = lax.ppermute(values, axis_name, _exchange_pairs(count, distance))]
    ppermute x4 -> x2, starting transfers between devices: 7.76 us -> 4.73 us  [sum_halving(): arrived = lax.ppermute(values, axis_name, _exchange_pairs(count, distance))]
    ppermute x4 -> x2, starting transfers between devices: 2.98 us -> 1.64 us  [sum_halving(): other = lax.ppermute(values, axis_name, _exchange_pairs(count, distance))]
    select_n x4 -> x1, other arithmetic: 1.29 us -> 0.06 us  [sum_halving(): jnp.where(lower, jnp.concatenate([values, other], 0), jnp.concatenate([ot...]
    ppermute x4 -> x2, waiting for transfers between devices: 4.28 us -> 3.07 us  [sum_halving(): arrived = lax.ppermute(values, axis_name, _exchange_pairs(count, distance))]
    convert_element_type x2 -> x1, other arithmetic: 1.69 us -> 1.18 us  [local(): grad_out = sum_halving(grad_out, 'freq').astype(jnp.float32)]
  transfers between devices with their start and end apart: 16 -> 14, of which waited for: 10 -> 8; matrix products, arithmetic and copies ran while one was open for 13% -> 16% of each run, Pallas kernels for 0% -> 0%
where the time goes in v21:
time: 62.4 us; the launch traced here: 62 us
  waiting for transfers between devices  22.1 us (35%)
  starting transfers between devices  20.8 us (33%)
  matrix products  10.8 us (17%)
  other arithmetic  4 us (6%)
  local copies, waits for them, and re-layouts  3.31 us (5%)
  between operations  0.91 us (1%)
    ppermute x4, waiting for transfers between devices, sum_whole(): lax.ppermute(values, axis_name, _exchange_pairs(count, distance))  10.7 us
    ppermute x4, starting transfers between devices, gather_rows(): other = lax.ppermute(block, axis_name, _exchange_pairs(count, distance))  8.06 us
    ppermute x4, waiting for transfers between devices, gather_rows(): other = lax.ppermute(block, axis_name, _exchange_pairs(count, distance))  4.91 us
    ppermute x2, starting transfers between devices, sum_halving(): arrived = lax.ppermute(values, axis_name, _exchange_pairs(count, distance))  4.73 us
    ppermute x4, starting transfers between devices, sum_whole(): lax.ppermute(values, axis_name, _exchange_pairs(count, distance))  3.92 us
    ppermute x2, waiting for transfers between devices, sum_halving(): arrived = lax.ppermute(send, axis_name, _exchange_pairs(count, distance))  3.39 us
    ppermute x2, waiting for transfers between devices, sum_halving(): arrived = lax.ppermute(values, axis_name, _exchange_pairs(count, distance))  3.07 us
    dot_general x1, matrix products, encoder_grads(): lax.dot_general(inputs_rows, grad_pre, (((0,), (0,)), ((), ())), preferre...  2.96 us
  transfers between devices with their start and end apart: 14, of which 8 were waited for; matrix products, arithmetic and copies ran while one was open for 16% of the time, Pallas kernels for 0%

profile of v21, /device:TPU:0, one launch (start us, length us, event | category | flops | bytes accessed | tf_op | source)
XLA Modules:
  0.0 62.0 jit_solution(16544979424836793418)
XLA Ops:
  0.6 4.1 %collective-permute-start = (bf16[2,2048]{1,0:T(2,128)(2,1)}, bf16[2,2048]{1,0:T(2,128)(2,1)S(1)}, u32[]{:S(2)}, u32[]{:S(2)}) collective-permute-start(bf16[2,2048]{1,0:T(2,128)(2,1)} %param.9), channel_id=1, source_target_pairs={{0,8},{1,9},{2,10},{3,11},{4,12},{5,13},{6,14},{7,15},{8,0},{9,1},... | collective-permute-start | bytes 24584 | tf_op jit(solution)/shard_map/ppermute | solution.py:119
  4.7 1.8 %collective-permute-done = bf16[2,2048]{1,0:T(2,128)(2,1)S(1)} collective-permute-done((bf16[2,2048]{1,0:T(2,128)(2,1)}, bf16[2,2048]{1,0:T(2,128)(2,1)S(1)}, u32[]{:S(2)}, u32[]{:S(2)}) %collective-permute-start) | collective-permute-done | bytes 8224 | tf_op jit(solution)/shard_map/ppermute | solution.py:119
  6.6 0.8 %maximum_select_fusion.6 = bf16[4,2048]{1,0:T(4,128)(2,1)S(1)} fusion(bf16[2,2048]{1,0:T(2,128)(2,1)S(1)} %collective-permute-done, bf16[2,2048]{1,0:T(2,128)(2,1)} %param.9, pred[]{:T(512)S(6)} %eq.47), kind=kLoop, calls=%fused_computation.68 | loop fusion | flops 73728 | bytes 32769 | tf_op jit(solution)/shard_map/jit(_where)/select_n | solution.py:121
  7.4 2.0 %collective-permute-start.1 = (bf16[4,2048]{1,0:T(4,128)(2,1)S(1)}, bf16[4,2048]{1,0:T(4,128)(2,1)S(1)}, u32[]{:S(2)}, u32[]{:S(2)}) collective-permute-start(bf16[4,2048]{1,0:T(4,128)(2,1)S(1)} %maximum_select_fusion.6), channel_id=1, source_target_pairs={{0,4},{1,5},{2,6},{3,7},{4,0},{5,1},{6,2},{7,3},{8,12},{9,13},{10,... | collective-permute-start | bytes 49160 | tf_op jit(solution)/shard_map/ppermute | solution.py:119
  9.4 1.8 %collective-permute-done.1 = bf16[4,2048]{1,0:T(4,128)(2,1)S(1)} collective-permute-done((bf16[4,2048]{1,0:T(4,128)(2,1)S(1)}, bf16[4,2048]{1,0:T(4,128)(2,1)S(1)}, u32[]{:S(2)}, u32[]{:S(2)}) %collective-permute-start.1) | collective-permute-done | bytes 16416 | tf_op jit(solution)/shard_map/ppermute | solution.py:119
  11.3 1.9 %collective-permute-start.2 = (bf16[8,2048]{1,0:T(8,128)(2,1)S(1)}, bf16[8,2048]{1,0:T(8,128)(2,1)S(1)}, u32[]{:S(2)}, u32[]{:S(2)}) collective-permute-start(bf16[8,2048]{1,0:T(8,128)(2,1)S(1)} %maximum_select_fusion.5), channel_id=1, source_target_pairs={{0,2},{1,3},{2,0},{3,1},{4,6},{5,7},{6,4},{7,5},{8,10},{9,11},{10,... | collective-permute-start | bytes 98312 | tf_op jit(solution)/shard_map/ppermute | solution.py:119
  13.2 0.8 %bitcast_convert_fusion = (f32[512,24]{0,1:T(8,128)S(1)}, f32[24,512]{1,0:T(8,128)S(1)}) fusion(bf16[24,512]{1,0:T(8,128)(2,1)} %param.14), kind=kLoop, calls=%fused_computation.67 | loop fusion | flops 24576 | bytes 122880
  14.0 1.2 %collective-permute-done.2 = bf16[8,2048]{1,0:T(8,128)(2,1)S(1)} collective-permute-done((bf16[8,2048]{1,0:T(8,128)(2,1)S(1)}, bf16[8,2048]{1,0:T(8,128)(2,1)S(1)}, u32[]{:S(2)}, u32[]{:S(2)}) %collective-permute-start.2) | collective-permute-done | bytes 32800 | tf_op jit(solution)/shard_map/ppermute | solution.py:119
  19.7 0.9 %add_convert_fusion = (bf16[768,512]{1,0:T(8,128)(2,1)S(1)}, f32[768,512]{1,0:T(8,128)S(1)}) fusion(bf16[32,24,512]{2,1,0:T(8,128)(2,1)S(1)} %multiply_convert_fusion, f32[768,512]{1,0:T(8,128)S(1)} %fusion.14, bf16[512,256]{1,0:T(8,128)(2,1)S(1)} %copy-done.5, f32[768,512]{1,0:T(8,128)S(1)} %fusion.50, f32[256]{0:T(256)S(1)} %bitcast.43, f32[256]{0:T(256)S(1)} %bitcast.39), kind=kOutput, calls=%fused_computation.14 | convolution fusion | flops 206831616 | bytes 6555648 | tf_op jit(solution)/shard_map/dot_general | solution.py:55
  23.5 1.2 %fusion.11 = f32[768,512]{1,0:T(8,128)S(1)} fusion(bf16[512,512]{1,0:T(8,128)(2,1)S(1)} %copy-done.4, f32[768,512]{1,0:T(8,128)S(1)} %get-tuple-element.11, f32[768,512]{1,0:T(8,128)S(1)} %convolution_add_fusion), kind=kOutput, calls=%fused_computation.29 | convolution fusion | flops 410517504 | bytes 5242880 | tf_op jit(solution)/shard_map/dot_general | solution.py:71
  26.0 1.9 %collective-permute-start.9 = (bf16[128,512]{1,0:T(8,128)(2,1)S(1)}, bf16[128,512]{1,0:T(8,128)(2,1)S(1)}, u32[]{:S(2)}, u32[]{:S(2)}) collective-permute-start(bf16[128,512]{1,0:T(8,128)(2,1)S(1)} %select_convert_fusion.1), channel_id=1, source_target_pairs={{0,2},{1,3},{2,0},{3,1},{4,6},{5,7},{6,4},{7,5},{8,10},{9,11},{10,... | collective-permute-start | bytes 393224 | tf_op jit(solution)/shard_map/ppermute | solution.py:158
  28.2 3.4 %collective-permute-done.9 = bf16[128,512]{1,0:T(8,128)(2,1)S(1)} collective-permute-done((bf16[128,512]{1,0:T(8,128)(2,1)S(1)}, bf16[128,512]{1,0:T(8,128)(2,1)S(1)}, u32[]{:S(2)}, u32[]{:S(2)}) %collective-permute-start.9) | collective-permute-done | bytes 131104 | tf_op jit(solution)/shard_map/ppermute | solution.py:158
  31.6 1.9 %collective-permute-start.10 = (bf16[128,512]{1,0:T(8,128)(2,1)S(1)}, bf16[128,512]{1,0:T(8,128)(2,1)S(1)}, u32[]{:S(2)}, u32[]{:S(2)}) collective-permute-start(bf16[128,512]{1,0:T(8,128)(2,1)S(1)} %add_convert_fusion.7), channel_id=1, source_target_pairs={{0,4},{1,5},{2,6},{3,7},{4,0},{5,1},{6,2},{7,3},{8,12},{9,13},{10,... | collective-permute-start | bytes 393224 | tf_op jit(solution)/shard_map/ppermute | solution.py:164
  33.6 3.1 %collective-permute-done.10 = bf16[128,512]{1,0:T(8,128)(2,1)S(1)} collective-permute-done((bf16[128,512]{1,0:T(8,128)(2,1)S(1)}, bf16[128,512]{1,0:T(8,128)(2,1)S(1)}, u32[]{:S(2)}, u32[]{:S(2)}) %collective-permute-start.10) | collective-permute-done | bytes 131104 | tf_op jit(solution)/shard_map/ppermute | solution.py:164
  36.7 2.9 %collective-permute-start.11 = (bf16[128,512]{1,0:T(8,128)(2,1)S(1)}, bf16[128,512]{1,0:T(8,128)(2,1)S(1)}, u32[]{:S(2)}, u32[]{:S(2)}) collective-permute-start(bf16[128,512]{1,0:T(8,128)(2,1)S(1)} %add_convert_fusion.6), channel_id=1, source_target_pairs={{0,8},{1,9},{2,10},{3,11},{4,12},{5,13},{6,14},{7,15},{8,0},{9,1},... | collective-permute-start | bytes 393224 | tf_op jit(solution)/shard_map/ppermute | solution.py:164
  39.6 1.6 %collective-permute-start.5 = (f32[34,512]{1,0:T(8,128)S(1)}, f32[34,512]{1,0:T(8,128)S(1)}, u32[]{:S(2)}, u32[]{:S(2)}) collective-permute-start(f32[34,512]{1,0:T(8,128)S(1)} %fusion.47), channel_id=1, source_target_pairs={{0,2},{1,3},{2,0},{3,1},{4,6},{5,7},{6,4},{7,5},{8,10},{9,11},{10,... | collective-permute-start | bytes 208904 | tf_op jit(solution)/shard_map/ppermute | solution.py:142
  41.2 2.9 %collective-permute-done.5 = f32[34,512]{1,0:T(8,128)S(1)} collective-permute-done((f32[34,512]{1,0:T(8,128)S(1)}, f32[34,512]{1,0:T(8,128)S(1)}, u32[]{:S(2)}, u32[]{:S(2)}) %collective-permute-start.5) | collective-permute-done | bytes 69664 | tf_op jit(solution)/shard_map/ppermute | solution.py:142
  44.1 2.2 %collective-permute-start.6 = (f32[34,512]{1,0:T(8,128)S(1)}, f32[34,512]{1,0:T(8,128)S(1)}, u32[]{:S(2)}, u32[]{:S(2)}) collective-permute-start(f32[34,512]{1,0:T(8,128)S(1)} %add.91), channel_id=1, source_target_pairs={{0,4},{1,5},{2,6},{3,7},{4,0},{5,1},{6,2},{7,3},{8,12},{9,13},{10,... | collective-permute-start | bytes 208904 | tf_op jit(solution)/shard_map/ppermute | solution.py:142
  46.3 1.6 %collective-permute-start.12 = (bf16[128,512]{1,0:T(8,128)(2,1)S(1)}, bf16[128,512]{1,0:T(8,128)(2,1)S(1)}, u32[]{:S(2)}, u32[]{:S(2)}) collective-permute-start(bf16[128,512]{1,0:T(8,128)(2,1)S(1)} %add_convert_fusion.5), channel_id=1, source_target_pairs={{0,2},{1,3},{2,0},{3,1},{4,6},{5,7},{6,4},{7,5},{8,10},{9,11},{10,... | collective-permute-start | bytes 393224 | tf_op jit(solution)/shard_map/ppermute | solution.py:169
  47.9 1.6 %collective-permute-done.6 = f32[34,512]{1,0:T(8,128)S(1)} collective-permute-done((f32[34,512]{1,0:T(8,128)S(1)}, f32[34,512]{1,0:T(8,128)S(1)}, u32[]{:S(2)}, u32[]{:S(2)}) %collective-permute-start.6) | collective-permute-done | bytes 69664 | tf_op jit(solution)/shard_map/ppermute | solution.py:142
  49.6 6.2 %collective-permute-done.7 = f32[34,512]{1,0:T(8,128)S(1)} collective-permute-done((f32[34,512]{1,0:T(8,128)S(1)}, f32[34,512]{1,0:T(8,128)S(1)}, u32[]{:S(2)}, u32[]{:S(2)}) %collective-permute-start.7) | collective-permute-done | bytes 69664 | tf_op jit(solution)/shard_map/ppermute | solution.py:142
  56.0 3.0 %fusion.10 = f32[2048,512]{1,0:T(8,128)} fusion(bf16[32,2048]{1,0:T(8,128)(2,1)S(1)} %convolution_convert_fusion, bf16[512,512]{1,0:T(8,128)(2,1)S(1)} %copy-done.1, bf16[32,512]{1,0:T(8,128)(2,1)S(1)} %fusion.8, f32[34,512]{1,0:T(8,128)S(1)} %add.93), kind=kOutput, calls=%fused_computation.22 | convolution fusion | flops 83968000 | bytes 4915200 | tf_op jit(solution)/shard_map/dot_general | solution.py:98
  59.5 1.3 %fusion.37 = f32[512,512]{1,0:T(8,128)} fusion(bf16[32,512]{1,0:T(8,128)(2,1)S(1)} %fusion.8, f32[34,512]{1,0:T(8,128)S(1)} %add.93), kind=kOutput, calls=%fused_computation.70 | convolution fusion | flops 16777216 | bytes 1114112 | tf_op jit(solution)/shard_map/dot_general | solution.py:91
  60.8 1.2 %fusion.13 = f32[512,512]{1,0:T(8,128)} fusion(bf16[256,512]{1,0:T(8,128)(2,1)S(1)} %collective-permute-done.13, bf16[256,512]{1,0:T(8,128)(2,1)S(1)} %maximum_select_fusion.1, pred[]{:T(512)S(6)} %eq.44), kind=kLoop, calls=%fused_computation.31 | loop fusion | flops 2621440 | bytes 1572865 | tf_op jit(solution)/shard_map/convert_element_type | solution.py:225
  (58 shorter events, 9.8 us)
Async XLA Ops:
  0.6 16.5 %copy-start = (bf16[2048,512]{1,0:T(8,128)(2,1)S(1)}, bf16[2048,512]{1,0:T(8,128)(2,1)}, u32[]{:S(2)}) copy-start(bf16[2048,512]{1,0:T(8,128)(2,1)} %param.12) | copy-start | bytes 6291460
  0.6 5.9 %collective-permute-start = (bf16[2,2048]{1,0:T(2,128)(2,1)}, bf16[2,2048]{1,0:T(2,128)(2,1)S(1)}, u32[]{:S(2)}, u32[]{:S(2)}) collective-permute-start(bf16[2,2048]{1,0:T(2,128)(2,1)} %param.9), channel_id=1, source_target_pairs={{0,8},{1,9},{2,10},{3,11},{4,12},{5,13},{6,14},{7,15},{8,0},{9,1},... | collective-permute-start | bytes 24584 | tf_op jit(solution)/shard_map/ppermute | solution.py:119
  7.4 3.8 %collective-permute-start.1 = (bf16[4,2048]{1,0:T(4,128)(2,1)S(1)}, bf16[4,2048]{1,0:T(4,128)(2,1)S(1)}, u32[]{:S(2)}, u32[]{:S(2)}) collective-permute-start(bf16[4,2048]{1,0:T(4,128)(2,1)S(1)} %maximum_select_fusion.6), channel_id=1, source_target_pairs={{0,4},{1,5},{2,6},{3,7},{4,0},{5,1},{6,2},{7,3},{8,12},{9,13},{10,... | collective-permute-start | bytes 49160 | tf_op jit(solution)/shard_map/ppermute | solution.py:119
  11.2 6.4 %copy-start.1 = (bf16[512,512]{1,0:T(8,128)(2,1)S(1)}, bf16[512,512]{1,0:T(8,128)(2,1)}, u32[]{:S(2)}) copy-start(bf16[512,512]{1,0:T(8,128)(2,1)} %param.13) | copy-start | bytes 1572868
  11.3 4.0 %collective-permute-start.2 = (bf16[8,2048]{1,0:T(8,128)(2,1)S(1)}, bf16[8,2048]{1,0:T(8,128)(2,1)S(1)}, u32[]{:S(2)}, u32[]{:S(2)}) collective-permute-start(bf16[8,2048]{1,0:T(8,128)(2,1)S(1)} %maximum_select_fusion.5), channel_id=1, source_target_pairs={{0,2},{1,3},{2,0},{3,1},{4,6},{5,7},{6,4},{7,5},{8,10},{9,11},{10,... | collective-permute-start | bytes 98312 | tf_op jit(solution)/shard_map/ppermute | solution.py:119
  15.3 1.7 %collective-permute-start.3 = (bf16[16,2048]{1,0:T(8,128)(2,1)S(1)}, bf16[16,2048]{1,0:T(8,128)(2,1)S(1)}, u32[]{:S(2)}, u32[]{:S(2)}) collective-permute-start(bf16[16,2048]{1,0:T(8,128)(2,1)S(1)} %maximum_select_fusion.4), channel_id=1, source_target_pairs={{0,1},{1,0},{2,3},{3,2},{4,5},{5,4},{6,7},{7,6},{8,9},{9,8},{10,11... | collective-permute-start | bytes 196616 | tf_op jit(solution)/shard_map/ppermute | solution.py:119
  17.1 1.0 %copy-start.4 = (bf16[512,512]{1,0:T(8,128)(2,1)S(1)}, bf16[512,512]{1,0:T(8,128)(2,1)}, u32[]{:S(2)}) copy-start(bf16[512,512]{1,0:T(8,128)(2,1)} %constant.106.clone) | copy-start | bytes 1572868
  18.0 1.0 %copy-start.2 = (bf16[512,256]{1,0:T(8,128)(2,1)S(1)}, bf16[512,256]{1,0:T(8,128)(2,1)}, u32[]{:S(2)}) copy-start(bf16[512,256]{1,0:T(8,128)(2,1)} %constant.112) | copy-start | bytes 786436
  18.8 1.0 %copy-start.5 = (bf16[512,256]{1,0:T(8,128)(2,1)S(1)}, bf16[512,256]{1,0:T(8,128)(2,1)}, u32[]{:S(2)}) copy-start(bf16[512,256]{1,0:T(8,128)(2,1)} %constant.113) | copy-start | bytes 786436
  19.7 1.0 %copy-start.3 = (bf16[512,512]{1,0:T(8,128)(2,1)S(1)}, bf16[512,512]{1,0:T(8,128)(2,1)}, u32[]{:S(2)}) copy-start(bf16[512,512]{1,0:T(8,128)(2,1)} %param.16) | copy-start | bytes 1572868
  19.7 1.3 %copy-start.6 = (bf16[32,24,512]{2,1,0:T(8,128)(2,1)S(1)}, bf16[32,24,512]{2,1,0:T(8,128)(2,1)}, u32[]{:S(2)}) copy-start(bf16[32,24,512]{2,1,0:T(8,128)(2,1)} %param.10) | copy-start | bytes 2359300
  22.9 2.8 %collective-permute-start.8 = (bf16[256,512]{1,0:T(8,128)(2,1)S(1)}, bf16[256,512]{1,0:T(8,128)(2,1)S(1)}, u32[]{:S(2)}, u32[]{:S(2)}) collective-permute-start(bf16[256,512]{1,0:T(8,128)(2,1)S(1)} %select_convert_fusion), channel_id=1, source_target_pairs={{0,1},{1,0},{2,3},{3,2},{4,5},{5,4},{6,7},{7,6},{8,9},{9,8},{10,11... | collective-permute-start | bytes 786440 | tf_op jit(solution)/shard_map/ppermute | solution.py:158
  26.0 5.6 %collective-permute-start.9 = (bf16[128,512]{1,0:T(8,128)(2,1)S(1)}, bf16[128,512]{1,0:T(8,128)(2,1)S(1)}, u32[]{:S(2)}, u32[]{:S(2)}) collective-permute-start(bf16[128,512]{1,0:T(8,128)(2,1)S(1)} %select_convert_fusion.1), channel_id=1, source_target_pairs={{0,2},{1,3},{2,0},{3,1},{4,6},{5,7},{6,4},{7,5},{8,10},{9,11},{10,... | collective-permute-start | bytes 393224 | tf_op jit(solution)/shard_map/ppermute | solution.py:158
  31.6 5.0 %collective-permute-start.10 = (bf16[128,512]{1,0:T(8,128)(2,1)S(1)}, bf16[128,512]{1,0:T(8,128)(2,1)S(1)}, u32[]{:S(2)}, u32[]{:S(2)}) collective-permute-start(bf16[128,512]{1,0:T(8,128)(2,1)S(1)} %add_convert_fusion.7), channel_id=1, source_target_pairs={{0,4},{1,5},{2,6},{3,7},{4,0},{5,1},{6,2},{7,3},{8,12},{9,13},{10,... | collective-permute-start | bytes 393224 | tf_op jit(solution)/shard_map/ppermute | solution.py:164
  33.5 6.1 %collective-permute-start.4 = (f32[34,512]{1,0:T(8,128)S(1)}, f32[34,512]{1,0:T(8,128)S(1)}, u32[]{:S(2)}, u32[]{:S(2)}) collective-permute-start(f32[34,512]{1,0:T(8,128)S(1)} %pad_maximum_fusion), channel_id=1, source_target_pairs={{0,1},{1,0},{2,3},{3,2},{4,5},{5,4},{6,7},{7,6},{8,9},{9,8},{10,11... | collective-permute-start | bytes 208904 | tf_op jit(solution)/shard_map/ppermute | solution.py:142
  36.7 9.6 %collective-permute-start.11 = (bf16[128,512]{1,0:T(8,128)(2,1)S(1)}, bf16[128,512]{1,0:T(8,128)(2,1)S(1)}, u32[]{:S(2)}, u32[]{:S(2)}) collective-permute-start(bf16[128,512]{1,0:T(8,128)(2,1)S(1)} %add_convert_fusion.6), channel_id=1, source_target_pairs={{0,8},{1,9},{2,10},{3,11},{4,12},{5,13},{6,14},{7,15},{8,0},{9,1},... | collective-permute-start | bytes 393224 | tf_op jit(solution)/shard_map/ppermute | solution.py:164
  39.6 4.5 %collective-permute-start.5 = (f32[34,512]{1,0:T(8,128)S(1)}, f32[34,512]{1,0:T(8,128)S(1)}, u32[]{:S(2)}, u32[]{:S(2)}) collective-permute-start(f32[34,512]{1,0:T(8,128)S(1)} %fusion.47), channel_id=1, source_target_pairs={{0,2},{1,3},{2,0},{3,1},{4,6},{5,7},{6,4},{7,5},{8,10},{9,11},{10,... | collective-permute-start | bytes 208904 | tf_op jit(solution)/shard_map/ppermute | solution.py:142
  44.1 5.4 %collective-permute-start.6 = (f32[34,512]{1,0:T(8,128)S(1)}, f32[34,512]{1,0:T(8,128)S(1)}, u32[]{:S(2)}, u32[]{:S(2)}) collective-permute-start(f32[34,512]{1,0:T(8,128)S(1)} %add.91), channel_id=1, source_target_pairs={{0,4},{1,5},{2,6},{3,7},{4,0},{5,1},{6,2},{7,3},{8,12},{9,13},{10,... | collective-permute-start | bytes 208904 | tf_op jit(solution)/shard_map/ppermute | solution.py:142
  46.3 9.5 %collective-permute-start.12 = (bf16[128,512]{1,0:T(8,128)(2,1)S(1)}, bf16[128,512]{1,0:T(8,128)(2,1)S(1)}, u32[]{:S(2)}, u32[]{:S(2)}) collective-permute-start(bf16[128,512]{1,0:T(8,128)(2,1)S(1)} %add_convert_fusion.5), channel_id=1, source_target_pairs={{0,2},{1,3},{2,0},{3,1},{4,6},{5,7},{6,4},{7,5},{8,10},{9,11},{10,... | collective-permute-start | bytes 393224 | tf_op jit(solution)/shard_map/ppermute | solution.py:169
  49.5 6.3 %collective-permute-start.7 = (f32[34,512]{1,0:T(8,128)S(1)}, f32[34,512]{1,0:T(8,128)S(1)}, u32[]{:S(2)}, u32[]{:S(2)}) collective-permute-start(f32[34,512]{1,0:T(8,128)S(1)} %add.92), channel_id=1, source_target_pairs={{0,8},{1,9},{2,10},{3,11},{4,12},{5,13},{6,14},{7,15},{8,0},{9,1},... | collective-permute-start | bytes 208904 | tf_op jit(solution)/shard_map/ppermute | solution.py:142
  55.9 4.9 %collective-permute-start.13 = (bf16[256,512]{1,0:T(8,128)(2,1)S(1)}, bf16[256,512]{1,0:T(8,128)(2,1)S(1)}, u32[]{:S(2)}, u32[]{:S(2)}) collective-permute-start(bf16[256,512]{1,0:T(8,128)(2,1)S(1)} %maximum_select_fusion.1), channel_id=1, source_target_pairs={{0,1},{1,0},{2,3},{3,2},{4,5},{5,4},{6,7},{7,6},{8,9},{9,8},{10,11... | collective-permute-start | bytes 786440 | tf_op jit(solution)/shard_map/ppermute | solution.py:169

commit v22 on v17

--- a/solution.py
+++ b/solution.py
@@ -146,7 +146,7 @@
 
 def sum_halving(values, axis_name, wire=jnp.bfloat16, halving_levels=2):
     count = lax.axis_size(axis_name)
-    if not _is_power_of_two(count) or values.shape[0] % count != 0:
+    if not _is_power_of_two(count) or values.shape[0] % min(count, 2**halving_levels) != 0:
         return lax.psum(values, axis_name)
     position = lax.axis_index(axis_name)
     distance = 1
@@ -223,7 +223,7 @@
         [grad_filter, jnp.zeros((grad_filter.shape[0], width - half_width), jnp.float32)], 1
     )
     packed_rows = grad_out.shape[0] + samples + filter_rows.shape[0]
-    padding = -packed_rows % count
+    padding = -packed_rows % 8
     packed = jnp.concatenate(
         [
             grad_out,

time: 58.6 us -> 58.6 us (level)
  no operation moved by 1% of the time
where the time goes in v22:
time: 58.6 us; the launch traced here: 58.3 us
  starting transfers between devices  21.6 us (37%)
  waiting for transfers between devices  17.2 us (29%)
  matrix products  10.8 us (18%)
  other arithmetic  4.89 us (8%)
  local copies, waits for them, and re-layouts  2.81 us (5%)
  between operations  0.93 us (2%)
    ppermute x4, starting transfers between devices, gather_rows(): other = lax.ppermute(block, axis_name, _exchange_pairs(count, distance))  8.06 us
    ppermute x4, starting transfers between devices, sum_halving(): arrived = lax.ppermute(values, axis_name, _exchange_pairs(count, distance))  7.77 us
    ppermute x4, waiting for transfers between devices, gather_rows(): other = lax.ppermute(block, axis_name, _exchange_pairs(count, distance))  4.91 us
    ppermute x4, waiting for transfers between devices, sum_halving(): other = lax.ppermute(values, axis_name, _exchange_pairs(count, distance))  4.35 us
    ppermute x4, waiting for transfers between devices, sum_halving(): arrived = lax.ppermute(values, axis_name, _exchange_pairs(count, distance))  4.25 us
    ppermute x4, waiting for transfers between devices, sum_halving(): arrived = lax.ppermute(send, axis_name, _exchange_pairs(count, distance))  3.7 us
    ppermute x4, starting transfers between devices, sum_halving(): other = lax.ppermute(values, axis_name, _exchange_pairs(count, distance))  2.98 us
    dot_general x1, matrix products, encoder_grads(): lax.dot_general(inputs_rows, grad_pre, (((0,), (0,)), ((), ())), preferre...  2.96 us
  transfers between devices with their start and end apart: 16, of which 11 were waited for; matrix products, arithmetic and copies ran while one was open for 5% of the time, Pallas kernels for 0%

profile of v22, /device:TPU:0, one launch (start us, length us, event | category | flops | bytes accessed | tf_op | source)
XLA Modules:
  0.0 58.3 jit_solution(15962321215134348404)
XLA Ops:
  0.6 4.1 %collective-permute-start = (bf16[2,2048]{1,0:T(2,128)(2,1)}, bf16[2,2048]{1,0:T(2,128)(2,1)S(1)}, u32[]{:S(2)}, u32[]{:S(2)}) collective-permute-start(bf16[2,2048]{1,0:T(2,128)(2,1)} %param.9), channel_id=1, source_target_pairs={{0,8},{1,9},{2,10},{3,11},{4,12},{5,13},{6,14},{7,15},{8,0},{9,1},... | collective-permute-start | bytes 24584 | tf_op jit(solution)/shard_map/ppermute | solution.py:119
  4.7 1.8 %collective-permute-done = bf16[2,2048]{1,0:T(2,128)(2,1)S(1)} collective-permute-done((bf16[2,2048]{1,0:T(2,128)(2,1)}, bf16[2,2048]{1,0:T(2,128)(2,1)S(1)}, u32[]{:S(2)}, u32[]{:S(2)}) %collective-permute-start) | collective-permute-done | bytes 8224 | tf_op jit(solution)/shard_map/ppermute | solution.py:119
  7.4 2.0 %collective-permute-start.1 = (bf16[4,2048]{1,0:T(4,128)(2,1)S(1)}, bf16[4,2048]{1,0:T(4,128)(2,1)S(1)}, u32[]{:S(2)}, u32[]{:S(2)}) collective-permute-start(bf16[4,2048]{1,0:T(4,128)(2,1)S(1)} %maximum_select_fusion.8), channel_id=1, source_target_pairs={{0,4},{1,5},{2,6},{3,7},{4,0},{5,1},{6,2},{7,3},{8,12},{9,13},{10,... | collective-permute-start | bytes 49160 | tf_op jit(solution)/shard_map/ppermute | solution.py:119
  9.4 1.8 %collective-permute-done.1 = bf16[4,2048]{1,0:T(4,128)(2,1)S(1)} collective-permute-done((bf16[4,2048]{1,0:T(4,128)(2,1)S(1)}, bf16[4,2048]{1,0:T(4,128)(2,1)S(1)}, u32[]{:S(2)}, u32[]{:S(2)}) %collective-permute-start.1) | collective-permute-done | bytes 16416 | tf_op jit(solution)/shard_map/ppermute | solution.py:119
  11.3 1.9 %collective-permute-start.2 = (bf16[8,2048]{1,0:T(8,128)(2,1)S(1)}, bf16[8,2048]{1,0:T(8,128)(2,1)S(1)}, u32[]{:S(2)}, u32[]{:S(2)}) collective-permute-start(bf16[8,2048]{1,0:T(8,128)(2,1)S(1)} %maximum_select_fusion.7), channel_id=1, source_target_pairs={{0,2},{1,3},{2,0},{3,1},{4,6},{5,7},{6,4},{7,5},{8,10},{9,11},{10,... | collective-permute-start | bytes 98312 | tf_op jit(solution)/shard_map/ppermute | solution.py:119
  14.0 1.2 %collective-permute-done.2 = bf16[8,2048]{1,0:T(8,128)(2,1)S(1)} collective-permute-done((bf16[8,2048]{1,0:T(8,128)(2,1)S(1)}, bf16[8,2048]{1,0:T(8,128)(2,1)S(1)}, u32[]{:S(2)}, u32[]{:S(2)}) %collective-permute-start.2) | collective-permute-done | bytes 32800 | tf_op jit(solution)/shard_map/ppermute | solution.py:119
  23.0 1.2 %fusion.11 = f32[768,512]{1,0:T(8,128)S(1)} fusion(bf16[512,512]{1,0:T(8,128)(2,1)S(1)} %copy-done.4, f32[768,512]{1,0:T(8,128)S(1)} %get-tuple-element.15, f32[768,512]{1,0:T(8,128)S(1)} %convolution_add_fusion), kind=kOutput, calls=%fused_computation.30 | convolution fusion | flops 410517504 | bytes 5242880 | tf_op jit(solution)/shard_map/dot_general | solution.py:71
  26.4 0.9 %collective-permute-done.10 = bf16[276,256]{1,0:T(8,128)(2,1)S(1)} collective-permute-done((bf16[276,256]{1,0:T(8,128)(2,1)S(1)}, bf16[276,256]{1,0:T(8,128)(2,1)S(1)}, u32[]{:S(2)}, u32[]{:S(2)}) %collective-permute-start.10) | collective-permute-done | bytes 141344 | tf_op jit(solution)/shard_map/ppermute | solution.py:158
  27.9 1.9 %collective-permute-start.5 = (bf16[138,256]{1,0:T(8,128)(2,1)S(1)}, bf16[138,256]{1,0:T(8,128)(2,1)S(1)}, u32[]{:S(2)}, u32[]{:S(2)}) collective-permute-start(bf16[138,256]{1,0:T(8,128)(2,1)S(1)} %select_convert_fusion.3), channel_id=1, source_target_pairs={{0,2},{1,3},{2,0},{3,1},{4,6},{5,7},{6,4},{7,5},{8,10},{9,11},{10,... | collective-permute-start | bytes 211976 | tf_op jit(solution)/shard_map/ppermute | solution.py:158
  30.1 2.4 %collective-permute-done.5 = bf16[138,256]{1,0:T(8,128)(2,1)S(1)} collective-permute-done((bf16[138,256]{1,0:T(8,128)(2,1)S(1)}, bf16[138,256]{1,0:T(8,128)(2,1)S(1)}, u32[]{:S(2)}, u32[]{:S(2)}) %collective-permute-start.5) | collective-permute-done | bytes 70688 | tf_op jit(solution)/shard_map/ppermute | solution.py:158
  32.5 2.1 %collective-permute-start.6 = (bf16[138,256]{1,0:T(8,128)(2,1)S(1)}, bf16[138,256]{1,0:T(8,128)(2,1)S(1)}, u32[]{:S(2)}, u32[]{:S(2)}) collective-permute-start(bf16[138,256]{1,0:T(8,128)(2,1)S(1)} %add_convert_fusion.10), channel_id=1, source_target_pairs={{0,4},{1,5},{2,6},{3,7},{4,0},{5,1},{6,2},{7,3},{8,12},{9,13},{10,... | collective-permute-start | bytes 211976 | tf_op jit(solution)/shard_map/ppermute | solution.py:164
  34.7 1.3 %collective-permute-start.12 = (bf16[138,256]{1,0:T(8,128)(2,1)S(1)}, bf16[138,256]{1,0:T(8,128)(2,1)S(1)}, u32[]{:S(2)}, u32[]{:S(2)}) collective-permute-start(bf16[138,256]{1,0:T(8,128)(2,1)S(1)} %add_convert_fusion.7), channel_id=1, source_target_pairs={{0,4},{1,5},{2,6},{3,7},{4,0},{5,1},{6,2},{7,3},{8,12},{9,13},{10,... | collective-permute-start | bytes 211976 | tf_op jit(solution)/shard_map/ppermute | solution.py:164
  35.9 1.8 %collective-permute-done.6 = bf16[138,256]{1,0:T(8,128)(2,1)S(1)} collective-permute-done((bf16[138,256]{1,0:T(8,128)(2,1)S(1)}, bf16[138,256]{1,0:T(8,128)(2,1)S(1)}, u32[]{:S(2)}, u32[]{:S(2)}) %collective-permute-start.6) | collective-permute-done | bytes 70688 | tf_op jit(solution)/shard_map/ppermute | solution.py:164
  37.7 2.7 %collective-permute-start.7 = (bf16[138,256]{1,0:T(8,128)(2,1)S(1)}, bf16[138,256]{1,0:T(8,128)(2,1)S(1)}, u32[]{:S(2)}, u32[]{:S(2)}) collective-permute-start(bf16[138,256]{1,0:T(8,128)(2,1)S(1)} %add_convert_fusion.9), channel_id=1, source_target_pairs={{0,8},{1,9},{2,10},{3,11},{4,12},{5,13},{6,14},{7,15},{8,0},{9,1},... | collective-permute-start | bytes 211976 | tf_op jit(solution)/shard_map/ppermute | solution.py:164
  40.4 1.7 %collective-permute-start.13 = (bf16[138,256]{1,0:T(8,128)(2,1)S(1)}, bf16[138,256]{1,0:T(8,128)(2,1)S(1)}, u32[]{:S(2)}, u32[]{:S(2)}) collective-permute-start(bf16[138,256]{1,0:T(8,128)(2,1)S(1)} %add_convert_fusion.6), channel_id=1, source_target_pairs={{0,8},{1,9},{2,10},{3,11},{4,12},{5,13},{6,14},{7,15},{8,0},{9,1},... | collective-permute-start | bytes 211976 | tf_op jit(solution)/shard_map/ppermute | solution.py:164
  42.2 2.5 %collective-permute-done.7 = bf16[138,256]{1,0:T(8,128)(2,1)S(1)} collective-permute-done((bf16[138,256]{1,0:T(8,128)(2,1)S(1)}, bf16[138,256]{1,0:T(8,128)(2,1)S(1)}, u32[]{:S(2)}, u32[]{:S(2)}) %collective-permute-start.7) | collective-permute-done | bytes 70688 | tf_op jit(solution)/shard_map/ppermute | solution.py:164
  44.6 1.7 %collective-permute-start.8 = (bf16[138,256]{1,0:T(8,128)(2,1)S(1)}, bf16[138,256]{1,0:T(8,128)(2,1)S(1)}, u32[]{:S(2)}, u32[]{:S(2)}) collective-permute-start(bf16[138,256]{1,0:T(8,128)(2,1)S(1)} %add_convert_fusion.8), channel_id=1, source_target_pairs={{0,2},{1,3},{2,0},{3,1},{4,6},{5,7},{6,4},{7,5},{8,10},{9,11},{10,... | collective-permute-start | bytes 211976 | tf_op jit(solution)/shard_map/ppermute | solution.py:169
  46.3 1.2 %collective-permute-start.14 = (bf16[138,256]{1,0:T(8,128)(2,1)S(1)}, bf16[138,256]{1,0:T(8,128)(2,1)S(1)}, u32[]{:S(2)}, u32[]{:S(2)}) collective-permute-start(bf16[138,256]{1,0:T(8,128)(2,1)S(1)} %add_convert_fusion.5), channel_id=1, source_target_pairs={{0,2},{1,3},{2,0},{3,1},{4,6},{5,7},{6,4},{7,5},{8,10},{9,11},{10,... | collective-permute-start | bytes 211976 | tf_op jit(solution)/shard_map/ppermute | solution.py:169
  47.5 1.6 %collective-permute-done.8 = bf16[138,256]{1,0:T(8,128)(2,1)S(1)} collective-permute-done((bf16[138,256]{1,0:T(8,128)(2,1)S(1)}, bf16[138,256]{1,0:T(8,128)(2,1)S(1)}, u32[]{:S(2)}, u32[]{:S(2)}) %collective-permute-start.8) | collective-permute-done | bytes 70688 | tf_op jit(solution)/shard_map/ppermute | solution.py:169
  49.2 1.6 %collective-permute-done.14 = bf16[138,256]{1,0:T(8,128)(2,1)S(1)} collective-permute-done((bf16[138,256]{1,0:T(8,128)(2,1)S(1)}, bf16[138,256]{1,0:T(8,128)(2,1)S(1)}, u32[]{:S(2)}, u32[]{:S(2)}) %collective-permute-start.14) | collective-permute-done | bytes 70688 | tf_op jit(solution)/shard_map/ppermute | solution.py:169
  51.0 1.2 %collective-permute-done.15 = bf16[276,256]{1,0:T(8,128)(2,1)S(1)} collective-permute-done((bf16[276,256]{1,0:T(8,128)(2,1)S(1)}, bf16[276,256]{1,0:T(8,128)(2,1)S(1)}, u32[]{:S(2)}, u32[]{:S(2)}) %collective-permute-start.15) | collective-permute-done | bytes 141344 | tf_op jit(solution)/shard_map/ppermute | solution.py:169
  52.4 1.1 %fusion.13 = f32[512,512]{1,0:T(8,128)} fusion(bf16[552,256]{1,0:T(8,128)(2,1)S(1)} %maximum_select_fusion.1, bf16[552,256]{1,0:T(8,128)(2,1)S(1)} %maximum_select_fusion), kind=kLoop, calls=%fused_computation.32 | loop fusion | flops 1048576 | bytes 1613824 | tf_op jit(solution)/shard_map/convert_element_type | solution.py:241
  53.5 3.0 %fusion.10 = f32[2048,512]{1,0:T(8,128)} fusion(bf16[32,2048]{1,0:T(8,128)(2,1)S(1)} %convolution_convert_fusion, bf16[32,512]{1,0:T(8,128)(2,1)S(1)} %pad_maximum_fusion.1, bf16[512,512]{1,0:T(8,128)(2,1)S(1)} %copy-done.1, bf16[32,512]{1,0:T(8,128)(2,1)S(1)} %fusion.8), kind=kOutput, calls=%fused_computation.23 | convolution fusion | flops 83968000 | bytes 4915200 | tf_op jit(solution)/shard_map/dot_general | solution.py:98
  56.4 1.3 %fusion.49 = f32[512,512]{1,0:T(8,128)} fusion(bf16[32,512]{1,0:T(8,128)(2,1)S(1)} %fusion.8, bf16[32,512]{1,0:T(8,128)(2,1)S(1)} %pad_maximum_fusion.1), kind=kOutput, calls=%fused_computation.93 | convolution fusion | flops 16777216 | bytes 1114112 | tf_op jit(solution)/shard_map/dot_general | solution.py:91
  (68 shorter events, 13.5 us)
Async XLA Ops:
  0.6 16.6 %copy-start = (bf16[2048,512]{1,0:T(8,128)(2,1)S(1)}, bf16[2048,512]{1,0:T(8,128)(2,1)}, u32[]{:S(2)}) copy-start(bf16[2048,512]{1,0:T(8,128)(2,1)} %param.12) | copy-start | bytes 6291460
  0.6 5.9 %collective-permute-start = (bf16[2,2048]{1,0:T(2,128)(2,1)}, bf16[2,2048]{1,0:T(2,128)(2,1)S(1)}, u32[]{:S(2)}, u32[]{:S(2)}) collective-permute-start(bf16[2,2048]{1,0:T(2,128)(2,1)} %param.9), channel_id=1, source_target_pairs={{0,8},{1,9},{2,10},{3,11},{4,12},{5,13},{6,14},{7,15},{8,0},{9,1},... | collective-permute-start | bytes 24584 | tf_op jit(solution)/shard_map/ppermute | solution.py:119
  7.4 3.8 %collective-permute-start.1 = (bf16[4,2048]{1,0:T(4,128)(2,1)S(1)}, bf16[4,2048]{1,0:T(4,128)(2,1)S(1)}, u32[]{:S(2)}, u32[]{:S(2)}) collective-permute-start(bf16[4,2048]{1,0:T(4,128)(2,1)S(1)} %maximum_select_fusion.8), channel_id=1, source_target_pairs={{0,4},{1,5},{2,6},{3,7},{4,0},{5,1},{6,2},{7,3},{8,12},{9,13},{10,... | collective-permute-start | bytes 49160 | tf_op jit(solution)/shard_map/ppermute | solution.py:119
  11.2 6.5 %copy-start.1 = (bf16[512,512]{1,0:T(8,128)(2,1)S(1)}, bf16[512,512]{1,0:T(8,128)(2,1)}, u32[]{:S(2)}) copy-start(bf16[512,512]{1,0:T(8,128)(2,1)} %param.13) | copy-start | bytes 1572868
  11.3 4.0 %collective-permute-start.2 = (bf16[8,2048]{1,0:T(8,128)(2,1)S(1)}, bf16[8,2048]{1,0:T(8,128)(2,1)S(1)}, u32[]{:S(2)}, u32[]{:S(2)}) collective-permute-start(bf16[8,2048]{1,0:T(8,128)(2,1)S(1)} %maximum_select_fusion.7), channel_id=1, source_target_pairs={{0,2},{1,3},{2,0},{3,1},{4,6},{5,7},{6,4},{7,5},{8,10},{9,11},{10,... | collective-permute-start | bytes 98312 | tf_op jit(solution)/shard_map/ppermute | solution.py:119
  15.3 1.8 %collective-permute-start.3 = (bf16[16,2048]{1,0:T(8,128)(2,1)S(1)}, bf16[16,2048]{1,0:T(8,128)(2,1)S(1)}, u32[]{:S(2)}, u32[]{:S(2)}) collective-permute-start(bf16[16,2048]{1,0:T(8,128)(2,1)S(1)} %maximum_select_fusion.6), channel_id=1, source_target_pairs={{0,1},{1,0},{2,3},{3,2},{4,5},{5,4},{6,7},{7,6},{8,9},{9,8},{10,11... | collective-permute-start | bytes 196616 | tf_op jit(solution)/shard_map/ppermute | solution.py:119
  17.2 1.0 %copy-start.4 = (bf16[512,512]{1,0:T(8,128)(2,1)S(1)}, bf16[512,512]{1,0:T(8,128)(2,1)}, u32[]{:S(2)}) copy-start(bf16[512,512]{1,0:T(8,128)(2,1)} %constant.123.clone) | copy-start | bytes 1572868
  18.1 1.0 %copy-start.2 = (bf16[512,256]{1,0:T(8,128)(2,1)S(1)}, bf16[512,256]{1,0:T(8,128)(2,1)}, u32[]{:S(2)}) copy-start(bf16[512,256]{1,0:T(8,128)(2,1)} %constant.129) | copy-start | bytes 786436
  18.8 1.0 %copy-start.5 = (bf16[512,256]{1,0:T(8,128)(2,1)S(1)}, bf16[512,256]{1,0:T(8,128)(2,1)}, u32[]{:S(2)}) copy-start(bf16[512,256]{1,0:T(8,128)(2,1)} %constant.130) | copy-start | bytes 786436
  19.8 1.0 %copy-start.3 = (bf16[512,512]{1,0:T(8,128)(2,1)S(1)}, bf16[512,512]{1,0:T(8,128)(2,1)}, u32[]{:S(2)}) copy-start(bf16[512,512]{1,0:T(8,128)(2,1)} %param.16) | copy-start | bytes 1572868
  19.8 1.3 %copy-start.6 = (bf16[32,24,512]{2,1,0:T(8,128)(2,1)S(1)}, bf16[32,24,512]{2,1,0:T(8,128)(2,1)}, u32[]{:S(2)}) copy-start(bf16[32,24,512]{2,1,0:T(8,128)(2,1)} %param.10) | copy-start | bytes 2359300
  25.8 1.6 %collective-permute-start.10 = (bf16[276,256]{1,0:T(8,128)(2,1)S(1)}, bf16[276,256]{1,0:T(8,128)(2,1)S(1)}, u32[]{:S(2)}, u32[]{:S(2)}) collective-permute-start(bf16[276,256]{1,0:T(8,128)(2,1)S(1)} %get-tuple-element.9), channel_id=1, source_target_pairs={{0,1},{1,0},{2,3},{3,2},{4,5},{5,4},{6,7},{7,6},{8,9},{9,8},{10,11... | collective-permute-start | bytes 423944 | tf_op jit(solution)/shard_map/ppermute | solution.py:158
  26.3 1.4 %collective-permute-start.4 = (bf16[276,256]{1,0:T(8,128)(2,1)S(1)}, bf16[276,256]{1,0:T(8,128)(2,1)S(1)}, u32[]{:S(2)}, u32[]{:S(2)}) collective-permute-start(bf16[276,256]{1,0:T(8,128)(2,1)S(1)} %get-tuple-element.8), channel_id=1, source_target_pairs={{0,1},{1,0},{2,3},{3,2},{4,5},{5,4},{6,7},{7,6},{8,9},{9,8},{10,11... | collective-permute-start | bytes 423944 | tf_op jit(solution)/shard_map/ppermute | solution.py:158
  27.9 4.6 %collective-permute-start.5 = (bf16[138,256]{1,0:T(8,128)(2,1)S(1)}, bf16[138,256]{1,0:T(8,128)(2,1)S(1)}, u32[]{:S(2)}, u32[]{:S(2)}) collective-permute-start(bf16[138,256]{1,0:T(8,128)(2,1)S(1)} %select_convert_fusion.3), channel_id=1, source_target_pairs={{0,2},{1,3},{2,0},{3,1},{4,6},{5,7},{6,4},{7,5},{8,10},{9,11},{10,... | collective-permute-start | bytes 211976 | tf_op jit(solution)/shard_map/ppermute | solution.py:158
  29.8 4.8 %collective-permute-start.11 = (bf16[138,256]{1,0:T(8,128)(2,1)S(1)}, bf16[138,256]{1,0:T(8,128)(2,1)S(1)}, u32[]{:S(2)}, u32[]{:S(2)}) collective-permute-start(bf16[138,256]{1,0:T(8,128)(2,1)S(1)} %select_convert_fusion.2), channel_id=1, source_target_pairs={{0,2},{1,3},{2,0},{3,1},{4,6},{5,7},{6,4},{7,5},{8,10},{9,11},{10,... | collective-permute-start | bytes 211976 | tf_op jit(solution)/shard_map/ppermute | solution.py:158
  32.5 5.2 %collective-permute-start.6 = (bf16[138,256]{1,0:T(8,128)(2,1)S(1)}, bf16[138,256]{1,0:T(8,128)(2,1)S(1)}, u32[]{:S(2)}, u32[]{:S(2)}) collective-permute-start(bf16[138,256]{1,0:T(8,128)(2,1)S(1)} %add_convert_fusion.10), channel_id=1, source_target_pairs={{0,4},{1,5},{2,6},{3,7},{4,0},{5,1},{6,2},{7,3},{8,12},{9,13},{10,... | collective-permute-start | bytes 211976 | tf_op jit(solution)/shard_map/ppermute | solution.py:164
  34.7 5.7 %collective-permute-start.12 = (bf16[138,256]{1,0:T(8,128)(2,1)S(1)}, bf16[138,256]{1,0:T(8,128)(2,1)S(1)}, u32[]{:S(2)}, u32[]{:S(2)}) collective-permute-start(bf16[138,256]{1,0:T(8,128)(2,1)S(1)} %add_convert_fusion.7), channel_id=1, source_target_pairs={{0,4},{1,5},{2,6},{3,7},{4,0},{5,1},{6,2},{7,3},{8,12},{9,13},{10,... | collective-permute-start | bytes 211976 | tf_op jit(solution)/shard_map/ppermute | solution.py:164
  37.7 6.9 %collective-permute-start.7 = (bf16[138,256]{1,0:T(8,128)(2,1)S(1)}, bf16[138,256]{1,0:T(8,128)(2,1)S(1)}, u32[]{:S(2)}, u32[]{:S(2)}) collective-permute-start(bf16[138,256]{1,0:T(8,128)(2,1)S(1)} %add_convert_fusion.9), channel_id=1, source_target_pairs={{0,8},{1,9},{2,10},{3,11},{4,12},{5,13},{6,14},{7,15},{8,0},{9,1},... | collective-permute-start | bytes 211976 | tf_op jit(solution)/shard_map/ppermute | solution.py:164
  40.4 5.9 %collective-permute-start.13 = (bf16[138,256]{1,0:T(8,128)(2,1)S(1)}, bf16[138,256]{1,0:T(8,128)(2,1)S(1)}, u32[]{:S(2)}, u32[]{:S(2)}) collective-permute-start(bf16[138,256]{1,0:T(8,128)(2,1)S(1)} %add_convert_fusion.6), channel_id=1, source_target_pairs={{0,8},{1,9},{2,10},{3,11},{4,12},{5,13},{6,14},{7,15},{8,0},{9,1},... | collective-permute-start | bytes 211976 | tf_op jit(solution)/shard_map/ppermute | solution.py:164
  44.6 4.4 %collective-permute-start.8 = (bf16[138,256]{1,0:T(8,128)(2,1)S(1)}, bf16[138,256]{1,0:T(8,128)(2,1)S(1)}, u32[]{:S(2)}, u32[]{:S(2)}) collective-permute-start(bf16[138,256]{1,0:T(8,128)(2,1)S(1)} %add_convert_fusion.8), channel_id=1, source_target_pairs={{0,2},{1,3},{2,0},{3,1},{4,6},{5,7},{6,4},{7,5},{8,10},{9,11},{10,... | collective-permute-start | bytes 211976 | tf_op jit(solution)/shard_map/ppermute | solution.py:169
  46.3 4.4 %collective-permute-start.14 = (bf16[138,256]{1,0:T(8,128)(2,1)S(1)}, bf16[138,256]{1,0:T(8,128)(2,1)S(1)}, u32[]{:S(2)}, u32[]{:S(2)}) collective-permute-start(bf16[138,256]{1,0:T(8,128)(2,1)S(1)} %add_convert_fusion.5), channel_id=1, source_target_pairs={{0,2},{1,3},{2,0},{3,1},{4,6},{5,7},{6,4},{7,5},{8,10},{9,11},{10,... | collective-permute-start | bytes 211976 | tf_op jit(solution)/shard_map/ppermute | solution.py:169
  49.1 1.8 %collective-permute-start.9 = (bf16[276,256]{1,0:T(8,128)(2,1)S(1)}, bf16[276,256]{1,0:T(8,128)(2,1)S(1)}, u32[]{:S(2)}, u32[]{:S(2)}) collective-permute-start(bf16[276,256]{1,0:T(8,128)(2,1)S(1)} %maximum_select_fusion.2), channel_id=1, source_target_pairs={{0,1},{1,0},{2,3},{3,2},{4,5},{5,4},{6,7},{7,6},{8,9},{9,8},{10,11... | collective-permute-start | bytes 423944 | tf_op jit(solution)/shard_map/ppermute | solution.py:169
  50.8 1.4 %collective-permute-start.15 = (bf16[276,256]{1,0:T(8,128)(2,1)S(1)}, bf16[276,256]{1,0:T(8,128)(2,1)S(1)}, u32[]{:S(2)}, u32[]{:S(2)}) collective-permute-start(bf16[276,256]{1,0:T(8,128)(2,1)S(1)} %maximum_select_fusion.3), channel_id=1, source_target_pairs={{0,1},{1,0},{2,3},{3,2},{4,5},{5,4},{6,7},{7,6},{8,9},{9,8},{10,11... | collective-permute-start | bytes 423944 | tf_op jit(solution)/shard_map/ppermute | solution.py:169

commit v23 on v20

--- a/solution.py
+++ b/solution.py
@@ -144,9 +144,11 @@
     return values
 
 
-def sum_halving(values, axis_name, wire=jnp.bfloat16, halving_levels=2):
+def sum_halving(values, axis_name, wire=jnp.bfloat16, halving_levels=2, trailing=None):
     count = lax.axis_size(axis_name)
     if not _is_power_of_two(count) or values.shape[0] % min(count, 2**halving_levels) != 0:
+        if trailing is not None:
+            return lax.psum(values, axis_name), trailing
         return lax.psum(values, axis_name)
     position = lax.axis_index(axis_name)
     distance = 1
@@ -157,6 +159,8 @@
         send = jnp.where(lower, values[half:], values[:half]).astype(wire)
         arrived = lax.ppermute(send, axis_name, _exchange_pairs(count, distance))
         values = keep + arrived.astype(keep.dtype)
+        if distance == 1 and trailing is not None:
+            values, trailing = lax.optimization_barrier((values, trailing))
         distance *= 2
     top = distance
     values = values.astype(wire)
@@ -172,6 +176,8 @@
             lower, jnp.concatenate([values, other], 0), jnp.concatenate([other, values], 0)
         )
         distance //= 2
+    if trailing is not None:
+        return values, trailing
     return values
 
 
@@ -235,8 +241,8 @@
         0,
     )
     rows_each = packed.shape[0] // 2
-    first = sum_halving(packed[:rows_each], "freq")
-    second = sum_halving(packed[rows_each:], "freq")
+    first, second_input = sum_halving(packed[:rows_each], "freq", trailing=packed[rows_each:])
+    second = sum_halving(second_input, "freq")
     derivative_bottleneck = first[:samples].astype(jnp.float32)
     grad_filter = first[samples:small_rows, :half_width].astype(jnp.float32)
     grad_out = jnp.concatenate([first[small_rows:], second], 0)[:rows_out].astype(jnp.float32)

time: 58.4 us -> 58.2 us (level)
  starting transfers between devices: 21.6 us -> 24.7 us
  waiting for transfers between devices: 16 us -> 13.7 us
  other arithmetic: 5.83 us -> 4.77 us
    ppermute x4, waiting for transfers between devices: 3.11 us -> 0.78 us  [sum_halving(): other = lax.ppermute(values, axis_name, _exchange_pairs(count, distance))]
    ppermute x4, starting transfers between devices: 2.79 us -> 4.21 us  [sum_halving(): arrived = lax.ppermute(send, axis_name, _exchange_pairs(count, distance))]
    ppermute x4, starting transfers between devices: 7.76 us -> 8.93 us  [sum_halving(): arrived = lax.ppermute(values, axis_name, _exchange_pairs(count, distance))]
    select_n x4, other arithmetic: 1.29 us -> 0.3 us  [sum_halving(): jnp.where(lower, jnp.concatenate([values, other], 0), jnp.concatenate([ot...]
where the time goes in v23:
time: 58.2 us; the launch traced here: 57.8 us
  starting transfers between devices  24.7 us (42%)
  waiting for transfers between devices  13.7 us (24%)
  matrix products  10.8 us (19%)
  other arithmetic  4.77 us (8%)
  local copies, waits for them, and re-layouts  2.84 us (5%)
  between operations  0.94 us (2%)
    ppermute x4, starting transfers between devices, sum_halving(): arrived = lax.ppermute(values, axis_name, _exchange_pairs(count, distance))  8.93 us
    ppermute x4, starting transfers between devices, gather_rows(): other = lax.ppermute(block, axis_name, _exchange_pairs(count, distance))  8.06 us
    ppermute x4, waiting for transfers between devices, gather_rows(): other = lax.ppermute(block, axis_name, _exchange_pairs(count, distance))  4.91 us
    ppermute x4, waiting for transfers between devices, sum_halving(): arrived = lax.ppermute(values, axis_name, _exchange_pairs(count, distance))  4.44 us
    ppermute x4, starting transfers between devices, sum_halving(): arrived = lax.ppermute(send, axis_name, _exchange_pairs(count, distance))  4.21 us
    ppermute x4, waiting for transfers between devices, sum_halving(): arrived = lax.ppermute(send, axis_name, _exchange_pairs(count, distance))  3.56 us
    ppermute x4, starting transfers between devices, sum_halving(): other = lax.ppermute(values, axis_name, _exchange_pairs(count, distance))  3.54 us
    dot_general x1, matrix products, encoder_grads(): lax.dot_general(inputs_rows, grad_pre, (((0,), (0,)), ((), ())), preferre...  2.96 us
  transfers between devices with their start and end apart: 16, of which 10 were waited for; matrix products, arithmetic and copies ran while one was open for 13% of the time, Pallas kernels for 0%

profile of v23, /device:TPU:0, one launch (start us, length us, event | category | flops | bytes accessed | tf_op | source)
XLA Modules:
  0.0 57.8 jit_solution(12296335427855384445)
XLA Ops:
  0.6 4.1 %collective-permute-start = (bf16[2,2048]{1,0:T(2,128)(2,1)}, bf16[2,2048]{1,0:T(2,128)(2,1)S(1)}, u32[]{:S(2)}, u32[]{:S(2)}) collective-permute-start(bf16[2,2048]{1,0:T(2,128)(2,1)} %param.9), channel_id=1, source_target_pairs={{0,8},{1,9},{2,10},{3,11},{4,12},{5,13},{6,14},{7,15},{8,0},{9,1},... | collective-permute-start | bytes 24584 | tf_op jit(solution)/shard_map/ppermute | solution.py:119
  4.7 1.8 %collective-permute-done = bf16[2,2048]{1,0:T(2,128)(2,1)S(1)} collective-permute-done((bf16[2,2048]{1,0:T(2,128)(2,1)}, bf16[2,2048]{1,0:T(2,128)(2,1)S(1)}, u32[]{:S(2)}, u32[]{:S(2)}) %collective-permute-start) | collective-permute-done | bytes 8224 | tf_op jit(solution)/shard_map/ppermute | solution.py:119
  7.4 2.0 %collective-permute-start.1 = (bf16[4,2048]{1,0:T(4,128)(2,1)S(1)}, bf16[4,2048]{1,0:T(4,128)(2,1)S(1)}, u32[]{:S(2)}, u32[]{:S(2)}) collective-permute-start(bf16[4,2048]{1,0:T(4,128)(2,1)S(1)} %maximum_select_fusion.8), channel_id=1, source_target_pairs={{0,4},{1,5},{2,6},{3,7},{4,0},{5,1},{6,2},{7,3},{8,12},{9,13},{10,... | collective-permute-start | bytes 49160 | tf_op jit(solution)/shard_map/ppermute | solution.py:119
  9.4 1.8 %collective-permute-done.1 = bf16[4,2048]{1,0:T(4,128)(2,1)S(1)} collective-permute-done((bf16[4,2048]{1,0:T(4,128)(2,1)S(1)}, bf16[4,2048]{1,0:T(4,128)(2,1)S(1)}, u32[]{:S(2)}, u32[]{:S(2)}) %collective-permute-start.1) | collective-permute-done | bytes 16416 | tf_op jit(solution)/shard_map/ppermute | solution.py:119
  11.3 1.9 %collective-permute-start.2 = (bf16[8,2048]{1,0:T(8,128)(2,1)S(1)}, bf16[8,2048]{1,0:T(8,128)(2,1)S(1)}, u32[]{:S(2)}, u32[]{:S(2)}) collective-permute-start(bf16[8,2048]{1,0:T(8,128)(2,1)S(1)} %maximum_select_fusion.7), channel_id=1, source_target_pairs={{0,2},{1,3},{2,0},{3,1},{4,6},{5,7},{6,4},{7,5},{8,10},{9,11},{10,... | collective-permute-start | bytes 98312 | tf_op jit(solution)/shard_map/ppermute | solution.py:119
  13.2 0.8 %bitcast_convert_fusion = (f32[512,24]{0,1:T(8,128)S(1)}, f32[24,512]{1,0:T(8,128)S(1)}) fusion(bf16[24,512]{1,0:T(8,128)(2,1)} %param.14), kind=kLoop, calls=%fused_computation.80 | loop fusion | flops 24576 | bytes 122880
  14.0 1.2 %collective-permute-done.2 = bf16[8,2048]{1,0:T(8,128)(2,1)S(1)} collective-permute-done((bf16[8,2048]{1,0:T(8,128)(2,1)S(1)}, bf16[8,2048]{1,0:T(8,128)(2,1)S(1)}, u32[]{:S(2)}, u32[]{:S(2)}) %collective-permute-start.2) | collective-permute-done | bytes 32800 | tf_op jit(solution)/shard_map/ppermute | solution.py:119
  19.7 0.9 %add_convert_fusion = (bf16[768,512]{1,0:T(8,128)(2,1)S(1)}, f32[768,512]{1,0:T(8,128)S(1)}) fusion(bf16[32,24,512]{2,1,0:T(8,128)(2,1)S(1)} %multiply_convert_fusion, f32[768,512]{1,0:T(8,128)S(1)} %fusion.14, bf16[512,256]{1,0:T(8,128)(2,1)S(1)} %copy-done.5, f32[768,512]{1,0:T(8,128)S(1)} %fusion.52, f32[256]{0:T(256)S(1)} %bitcast.42, f32[256]{0:T(256)S(1)} %bitcast.38), kind=kOutput, calls=%fused_computation.14 | convolution fusion | flops 206831616 | bytes 6555648 | tf_op jit(solution)/shard_map/dot_general | solution.py:55
  22.9 1.2 %fusion.11 = f32[768,512]{1,0:T(8,128)S(1)} fusion(bf16[512,512]{1,0:T(8,128)(2,1)S(1)} %copy-done.4, f32[768,512]{1,0:T(8,128)S(1)} %get-tuple-element.17, f32[768,512]{1,0:T(8,128)S(1)} %convolution_add_fusion), kind=kOutput, calls=%fused_computation.30 | convolution fusion | flops 410517504 | bytes 5242880 | tf_op jit(solution)/shard_map/dot_general | solution.py:71
  26.1 0.9 %collective-permute-done.4 = bf16[138,512]{1,0:T(8,128)(2,1)S(1)} collective-permute-done((bf16[138,512]{1,0:T(8,128)(2,1)S(1)}, bf16[138,512]{1,0:T(8,128)(2,1)S(1)}, u32[]{:S(2)}, u32[]{:S(2)}) %collective-permute-start.4) | collective-permute-done | bytes 141344 | tf_op jit(solution)/shard_map/ppermute | solution.py:160
  27.2 1.9 %collective-permute-start.5 = (bf16[69,512]{1,0:T(8,128)(2,1)S(1)}, bf16[69,512]{1,0:T(8,128)(2,1)S(1)}, u32[]{:S(2)}, u32[]{:S(2)}) collective-permute-start(bf16[69,512]{1,0:T(8,128)(2,1)S(1)} %select_convert_fusion.3), channel_id=1, source_target_pairs={{0,2},{1,3},{2,0},{3,1},{4,6},{5,7},{6,4},{7,5},{8,10},{9,11},{10,... | collective-permute-start | bytes 211976 | tf_op jit(solution)/shard_map/ppermute | solution.py:160
  29.3 2.6 %collective-permute-done.5 = bf16[69,512]{1,0:T(8,128)(2,1)S(1)} collective-permute-done((bf16[69,512]{1,0:T(8,128)(2,1)S(1)}, bf16[69,512]{1,0:T(8,128)(2,1)S(1)}, u32[]{:S(2)}, u32[]{:S(2)}) %collective-permute-start.5) | collective-permute-done | bytes 70688 | tf_op jit(solution)/shard_map/ppermute | solution.py:160
  31.9 1.9 %collective-permute-start.6 = (bf16[69,512]{1,0:T(8,128)(2,1)S(1)}, bf16[69,512]{1,0:T(8,128)(2,1)S(1)}, u32[]{:S(2)}, u32[]{:S(2)}) collective-permute-start(bf16[69,512]{1,0:T(8,128)(2,1)S(1)} %add_convert_fusion.10), channel_id=1, source_target_pairs={{0,4},{1,5},{2,6},{3,7},{4,0},{5,1},{6,2},{7,3},{8,12},{9,13},{10,... | collective-permute-start | bytes 211976 | tf_op jit(solution)/shard_map/ppermute | solution.py:168
  33.9 1.6 %collective-permute-start.11 = (bf16[69,512]{1,0:T(8,128)(2,1)S(1)}, bf16[69,512]{1,0:T(8,128)(2,1)S(1)}, u32[]{:S(2)}, u32[]{:S(2)}) collective-permute-start(bf16[69,512]{1,0:T(8,128)(2,1)S(1)} %select_convert_fusion.2), channel_id=1, source_target_pairs={{0,2},{1,3},{2,0},{3,1},{4,6},{5,7},{6,4},{7,5},{8,10},{9,11},{10,... | collective-permute-start | bytes 211976 | tf_op jit(solution)/shard_map/ppermute | solution.py:160
  35.5 0.9 %collective-permute-done.6 = bf16[69,512]{1,0:T(8,128)(2,1)S(1)} collective-permute-done((bf16[69,512]{1,0:T(8,128)(2,1)S(1)}, bf16[69,512]{1,0:T(8,128)(2,1)S(1)}, u32[]{:S(2)}, u32[]{:S(2)}) %collective-permute-start.6) | collective-permute-done | bytes 70688 | tf_op jit(solution)/shard_map/ppermute | solution.py:168
  36.4 2.9 %collective-permute-start.7 = (bf16[69,512]{1,0:T(8,128)(2,1)S(1)}, bf16[69,512]{1,0:T(8,128)(2,1)S(1)}, u32[]{:S(2)}, u32[]{:S(2)}) collective-permute-start(bf16[69,512]{1,0:T(8,128)(2,1)S(1)} %add_convert_fusion.9), channel_id=1, source_target_pairs={{0,8},{1,9},{2,10},{3,11},{4,12},{5,13},{6,14},{7,15},{8,0},{9,1},... | collective-permute-start | bytes 211976 | tf_op jit(solution)/shard_map/ppermute | solution.py:168
  39.3 1.6 %collective-permute-start.12 = (bf16[69,512]{1,0:T(8,128)(2,1)S(1)}, bf16[69,512]{1,0:T(8,128)(2,1)S(1)}, u32[]{:S(2)}, u32[]{:S(2)}) collective-permute-start(bf16[69,512]{1,0:T(8,128)(2,1)S(1)} %add_convert_fusion.7), channel_id=1, source_target_pairs={{0,4},{1,5},{2,6},{3,7},{4,0},{5,1},{6,2},{7,3},{8,12},{9,13},{10,... | collective-permute-start | bytes 211976 | tf_op jit(solution)/shard_map/ppermute | solution.py:168
  41.7 1.8 %collective-permute-start.8 = (bf16[69,512]{1,0:T(8,128)(2,1)S(1)}, bf16[69,512]{1,0:T(8,128)(2,1)S(1)}, u32[]{:S(2)}, u32[]{:S(2)}) collective-permute-start(bf16[69,512]{1,0:T(8,128)(2,1)S(1)} %add_convert_fusion.8), channel_id=1, source_target_pairs={{0,2},{1,3},{2,0},{3,1},{4,6},{5,7},{6,4},{7,5},{8,10},{9,11},{10,... | collective-permute-start | bytes 211976 | tf_op jit(solution)/shard_map/ppermute | solution.py:173
  43.7 2.6 %collective-permute-start.13 = (bf16[69,512]{1,0:T(8,128)(2,1)S(1)}, bf16[69,512]{1,0:T(8,128)(2,1)S(1)}, u32[]{:S(2)}, u32[]{:S(2)}) collective-permute-start(bf16[69,512]{1,0:T(8,128)(2,1)S(1)} %add_convert_fusion.6), channel_id=1, source_target_pairs={{0,8},{1,9},{2,10},{3,11},{4,12},{5,13},{6,14},{7,15},{8,0},{9,1},... | collective-permute-start | bytes 211976 | tf_op jit(solution)/shard_map/ppermute | solution.py:168
  46.4 2.6 %collective-permute-done.13 = bf16[69,512]{1,0:T(8,128)(2,1)S(1)} collective-permute-done((bf16[69,512]{1,0:T(8,128)(2,1)S(1)}, bf16[69,512]{1,0:T(8,128)(2,1)S(1)}, u32[]{:S(2)}, u32[]{:S(2)}) %collective-permute-start.13) | collective-permute-done | bytes 70688 | tf_op jit(solution)/shard_map/ppermute | solution.py:168
  49.1 1.6 %collective-permute-start.14 = (bf16[69,512]{1,0:T(8,128)(2,1)S(1)}, bf16[69,512]{1,0:T(8,128)(2,1)S(1)}, u32[]{:S(2)}, u32[]{:S(2)}) collective-permute-start(bf16[69,512]{1,0:T(8,128)(2,1)S(1)} %add_convert_fusion.5), channel_id=1, source_target_pairs={{0,2},{1,3},{2,0},{3,1},{4,6},{5,7},{6,4},{7,5},{8,10},{9,11},{10,... | collective-permute-start | bytes 211976 | tf_op jit(solution)/shard_map/ppermute | solution.py:173
  50.8 3.0 %fusion.10 = f32[2048,512]{1,0:T(8,128)} fusion(bf16[32,2048]{1,0:T(8,128)(2,1)S(1)} %convolution_convert_fusion, bf16[512,512]{1,0:T(8,128)(2,1)S(1)} %copy-done.1, bf16[32,512]{1,0:T(8,128)(2,1)S(1)} %fusion.8, bf16[276,512]{1,0:T(8,128)(2,1)S(1)} %maximum_select_fusion), kind=kOutput, calls=%fused_computation.22 | convolution fusion | flops 83968000 | bytes 4915200 | tf_op jit(solution)/shard_map/dot_general | solution.py:98
  53.7 1.3 %fusion.37 = f32[512,512]{1,0:T(8,128)} fusion(bf16[32,512]{1,0:T(8,128)(2,1)S(1)} %fusion.8, bf16[276,512]{1,0:T(8,128)(2,1)S(1)} %maximum_select_fusion), kind=kOutput, calls=%fused_computation.77 | convolution fusion | flops 16777216 | bytes 1114112 | tf_op jit(solution)/shard_map/dot_general | solution.py:91
  56.7 1.1 %fusion.13 = f32[512,512]{1,0:T(8,128)} fusion(bf16[276,512]{1,0:T(8,128)(2,1)S(1)} %maximum_select_fusion.1, bf16[242,512]{1,0:T(8,128)(2,1)S(1)} %slice.100), kind=kLoop, calls=%fused_computation.32 | loop fusion | flops 1048576 | bytes 1579008 | tf_op jit(solution)/shard_map/convert_element_type | solution.py:248
  (68 shorter events, 12.8 us)
Async XLA Ops:
  0.6 16.5 %copy-start = (bf16[2048,512]{1,0:T(8,128)(2,1)S(1)}, bf16[2048,512]{1,0:T(8,128)(2,1)}, u32[]{:S(2)}) copy-start(bf16[2048,512]{1,0:T(8,128)(2,1)} %param.12) | copy-start | bytes 6291460
  0.6 5.9 %collective-permute-start = (bf16[2,2048]{1,0:T(2,128)(2,1)}, bf16[2,2048]{1,0:T(2,128)(2,1)S(1)}, u32[]{:S(2)}, u32[]{:S(2)}) collective-permute-start(bf16[2,2048]{1,0:T(2,128)(2,1)} %param.9), channel_id=1, source_target_pairs={{0,8},{1,9},{2,10},{3,11},{4,12},{5,13},{6,14},{7,15},{8,0},{9,1},... | collective-permute-start | bytes 24584 | tf_op jit(solution)/shard_map/ppermute | solution.py:119
  7.4 3.8 %collective-permute-start.1 = (bf16[4,2048]{1,0:T(4,128)(2,1)S(1)}, bf16[4,2048]{1,0:T(4,128)(2,1)S(1)}, u32[]{:S(2)}, u32[]{:S(2)}) collective-permute-start(bf16[4,2048]{1,0:T(4,128)(2,1)S(1)} %maximum_select_fusion.8), channel_id=1, source_target_pairs={{0,4},{1,5},{2,6},{3,7},{4,0},{5,1},{6,2},{7,3},{8,12},{9,13},{10,... | collective-permute-start | bytes 49160 | tf_op jit(solution)/shard_map/ppermute | solution.py:119
  11.2 6.4 %copy-start.1 = (bf16[512,512]{1,0:T(8,128)(2,1)S(1)}, bf16[512,512]{1,0:T(8,128)(2,1)}, u32[]{:S(2)}) copy-start(bf16[512,512]{1,0:T(8,128)(2,1)} %param.13) | copy-start | bytes 1572868
  11.3 4.0 %collective-permute-start.2 = (bf16[8,2048]{1,0:T(8,128)(2,1)S(1)}, bf16[8,2048]{1,0:T(8,128)(2,1)S(1)}, u32[]{:S(2)}, u32[]{:S(2)}) collective-permute-start(bf16[8,2048]{1,0:T(8,128)(2,1)S(1)} %maximum_select_fusion.7), channel_id=1, source_target_pairs={{0,2},{1,3},{2,0},{3,1},{4,6},{5,7},{6,4},{7,5},{8,10},{9,11},{10,... | collective-permute-start | bytes 98312 | tf_op jit(solution)/shard_map/ppermute | solution.py:119
  15.3 1.7 %collective-permute-start.3 = (bf16[16,2048]{1,0:T(8,128)(2,1)S(1)}, bf16[16,2048]{1,0:T(8,128)(2,1)S(1)}, u32[]{:S(2)}, u32[]{:S(2)}) collective-permute-start(bf16[16,2048]{1,0:T(8,128)(2,1)S(1)} %maximum_select_fusion.6), channel_id=1, source_target_pairs={{0,1},{1,0},{2,3},{3,2},{4,5},{5,4},{6,7},{7,6},{8,9},{9,8},{10,11... | collective-permute-start | bytes 196616 | tf_op jit(solution)/shard_map/ppermute | solution.py:119
  17.1 1.0 %copy-start.4 = (bf16[512,512]{1,0:T(8,128)(2,1)S(1)}, bf16[512,512]{1,0:T(8,128)(2,1)}, u32[]{:S(2)}) copy-start(bf16[512,512]{1,0:T(8,128)(2,1)} %constant.123.clone) | copy-start | bytes 1572868
  18.0 1.0 %copy-start.2 = (bf16[512,256]{1,0:T(8,128)(2,1)S(1)}, bf16[512,256]{1,0:T(8,128)(2,1)}, u32[]{:S(2)}) copy-start(bf16[512,256]{1,0:T(8,128)(2,1)} %constant.131) | copy-start | bytes 786436
  18.8 1.0 %copy-start.5 = (bf16[512,256]{1,0:T(8,128)(2,1)S(1)}, bf16[512,256]{1,0:T(8,128)(2,1)}, u32[]{:S(2)}) copy-start(bf16[512,256]{1,0:T(8,128)(2,1)} %constant.132) | copy-start | bytes 786436
  19.7 1.0 %copy-start.3 = (bf16[512,512]{1,0:T(8,128)(2,1)S(1)}, bf16[512,512]{1,0:T(8,128)(2,1)}, u32[]{:S(2)}) copy-start(bf16[512,512]{1,0:T(8,128)(2,1)} %param.16) | copy-start | bytes 1572868
  19.7 1.3 %copy-start.6 = (bf16[32,24,512]{2,1,0:T(8,128)(2,1)S(1)}, bf16[32,24,512]{2,1,0:T(8,128)(2,1)}, u32[]{:S(2)}) copy-start(bf16[32,24,512]{2,1,0:T(8,128)(2,1)} %param.10) | copy-start | bytes 2359300
  25.5 1.6 %collective-permute-start.4 = (bf16[138,512]{1,0:T(8,128)(2,1)S(1)}, bf16[138,512]{1,0:T(8,128)(2,1)S(1)}, u32[]{:S(2)}, u32[]{:S(2)}) collective-permute-start(bf16[138,512]{1,0:T(8,128)(2,1)S(1)} %get-tuple-element.10), channel_id=1, source_target_pairs={{0,1},{1,0},{2,3},{3,2},{4,5},{5,4},{6,7},{7,6},{8,9},{9,8},{10,11... | collective-permute-start | bytes 423944 | tf_op jit(solution)/shard_map/ppermute | solution.py:160
  27.2 4.7 %collective-permute-start.5 = (bf16[69,512]{1,0:T(8,128)(2,1)S(1)}, bf16[69,512]{1,0:T(8,128)(2,1)S(1)}, u32[]{:S(2)}, u32[]{:S(2)}) collective-permute-start(bf16[69,512]{1,0:T(8,128)(2,1)S(1)} %select_convert_fusion.3), channel_id=1, source_target_pairs={{0,2},{1,3},{2,0},{3,1},{4,6},{5,7},{6,4},{7,5},{8,10},{9,11},{10,... | collective-permute-start | bytes 211976 | tf_op jit(solution)/shard_map/ppermute | solution.py:160
  29.2 4.7 %collective-permute-start.10 = (bf16[138,512]{1,0:T(8,128)(2,1)S(1)}, bf16[138,512]{1,0:T(8,128)(2,1)S(1)}, u32[]{:S(2)}, u32[]{:S(2)}) collective-permute-start(bf16[138,512]{1,0:T(8,128)(2,1)S(1)} %select_convert_fusion), channel_id=1, source_target_pairs={{0,1},{1,0},{2,3},{3,2},{4,5},{5,4},{6,7},{7,6},{8,9},{9,8},{10,11... | collective-permute-start | bytes 423944 | tf_op jit(solution)/shard_map/ppermute | solution.py:160
  31.9 4.4 %collective-permute-start.6 = (bf16[69,512]{1,0:T(8,128)(2,1)S(1)}, bf16[69,512]{1,0:T(8,128)(2,1)S(1)}, u32[]{:S(2)}, u32[]{:S(2)}) collective-permute-start(bf16[69,512]{1,0:T(8,128)(2,1)S(1)} %add_convert_fusion.10), channel_id=1, source_target_pairs={{0,4},{1,5},{2,6},{3,7},{4,0},{5,1},{6,2},{7,3},{8,12},{9,13},{10,... | collective-permute-start | bytes 211976 | tf_op jit(solution)/shard_map/ppermute | solution.py:168
  33.9 5.3 %collective-permute-start.11 = (bf16[69,512]{1,0:T(8,128)(2,1)S(1)}, bf16[69,512]{1,0:T(8,128)(2,1)S(1)}, u32[]{:S(2)}, u32[]{:S(2)}) collective-permute-start(bf16[69,512]{1,0:T(8,128)(2,1)S(1)} %select_convert_fusion.2), channel_id=1, source_target_pairs={{0,2},{1,3},{2,0},{3,1},{4,6},{5,7},{6,4},{7,5},{8,10},{9,11},{10,... | collective-permute-start | bytes 211976 | tf_op jit(solution)/shard_map/ppermute | solution.py:160
  36.4 5.3 %collective-permute-start.7 = (bf16[69,512]{1,0:T(8,128)(2,1)S(1)}, bf16[69,512]{1,0:T(8,128)(2,1)S(1)}, u32[]{:S(2)}, u32[]{:S(2)}) collective-permute-start(bf16[69,512]{1,0:T(8,128)(2,1)S(1)} %add_convert_fusion.9), channel_id=1, source_target_pairs={{0,8},{1,9},{2,10},{3,11},{4,12},{5,13},{6,14},{7,15},{8,0},{9,1},... | collective-permute-start | bytes 211976 | tf_op jit(solution)/shard_map/ppermute | solution.py:168
  39.3 4.4 %collective-permute-start.12 = (bf16[69,512]{1,0:T(8,128)(2,1)S(1)}, bf16[69,512]{1,0:T(8,128)(2,1)S(1)}, u32[]{:S(2)}, u32[]{:S(2)}) collective-permute-start(bf16[69,512]{1,0:T(8,128)(2,1)S(1)} %add_convert_fusion.7), channel_id=1, source_target_pairs={{0,4},{1,5},{2,6},{3,7},{4,0},{5,1},{6,2},{7,3},{8,12},{9,13},{10,... | collective-permute-start | bytes 211976 | tf_op jit(solution)/shard_map/ppermute | solution.py:168
  41.7 4.6 %collective-permute-start.8 = (bf16[69,512]{1,0:T(8,128)(2,1)S(1)}, bf16[69,512]{1,0:T(8,128)(2,1)S(1)}, u32[]{:S(2)}, u32[]{:S(2)}) collective-permute-start(bf16[69,512]{1,0:T(8,128)(2,1)S(1)} %add_convert_fusion.8), channel_id=1, source_target_pairs={{0,2},{1,3},{2,0},{3,1},{4,6},{5,7},{6,4},{7,5},{8,10},{9,11},{10,... | collective-permute-start | bytes 211976 | tf_op jit(solution)/shard_map/ppermute | solution.py:173
  43.7 5.3 %collective-permute-start.13 = (bf16[69,512]{1,0:T(8,128)(2,1)S(1)}, bf16[69,512]{1,0:T(8,128)(2,1)S(1)}, u32[]{:S(2)}, u32[]{:S(2)}) collective-permute-start(bf16[69,512]{1,0:T(8,128)(2,1)S(1)} %add_convert_fusion.6), channel_id=1, source_target_pairs={{0,8},{1,9},{2,10},{3,11},{4,12},{5,13},{6,14},{7,15},{8,0},{9,1},... | collective-permute-start | bytes 211976 | tf_op jit(solution)/shard_map/ppermute | solution.py:168
  46.4 4.3 %collective-permute-start.9 = (bf16[138,512]{1,0:T(8,128)(2,1)S(1)}, bf16[138,512]{1,0:T(8,128)(2,1)S(1)}, u32[]{:S(2)}, u32[]{:S(2)}) collective-permute-start(bf16[138,512]{1,0:T(8,128)(2,1)S(1)} %maximum_select_fusion.2), channel_id=1, source_target_pairs={{0,1},{1,0},{2,3},{3,2},{4,5},{5,4},{6,7},{7,6},{8,9},{9,8},{10,11... | collective-permute-start | bytes 423944 | tf_op jit(solution)/shard_map/ppermute | solution.py:173
  49.1 6.0 %collective-permute-start.14 = (bf16[69,512]{1,0:T(8,128)(2,1)S(1)}, bf16[69,512]{1,0:T(8,128)(2,1)S(1)}, u32[]{:S(2)}, u32[]{:S(2)}) collective-permute-start(bf16[69,512]{1,0:T(8,128)(2,1)S(1)} %add_convert_fusion.5), channel_id=1, source_target_pairs={{0,2},{1,3},{2,0},{3,1},{4,6},{5,7},{6,4},{7,5},{8,10},{9,11},{10,... | collective-permute-start | bytes 211976 | tf_op jit(solution)/shard_map/ppermute | solution.py:173
  55.2 1.4 %collective-permute-start.15 = (bf16[138,512]{1,0:T(8,128)(2,1)S(1)}, bf16[138,512]{1,0:T(8,128)(2,1)S(1)}, u32[]{:S(2)}, u32[]{:S(2)}) collective-permute-start(bf16[138,512]{1,0:T(8,128)(2,1)S(1)} %maximum_select_fusion.3), channel_id=1, source_target_pairs={{0,1},{1,0},{2,3},{3,2},{4,5},{5,4},{6,7},{7,6},{8,9},{9,8},{10,11... | collective-permute-start | bytes 423944 | tf_op jit(solution)/shard_map/ppermute | solution.py:173

commit v24 on v23

--- a/solution.py
+++ b/solution.py
@@ -240,7 +240,7 @@
         ],
         0,
     )
-    rows_each = packed.shape[0] // 2
+    rows_each = packed.shape[0] // 2 + 44 if packed.shape[0] % 8 == 0 and packed.shape[0] > 200 else packed.shape[0] // 2
     first, second_input = sum_halving(packed[:rows_each], "freq", trailing=packed[rows_each:])
     second = sum_halving(second_input, "freq")
     derivative_bottleneck = first[:samples].astype(jnp.float32)

time: 58.2 us -> 61 us (1.048)
  waiting for transfers between devices: 13.7 us -> 17.2 us
  starting transfers between devices: 24.7 us -> 23.1 us
  matrix products: 10.8 us -> 11.7 us
    ppermute x4, waiting for transfers between devices: 0.78 us -> 4.36 us  [sum_halving(): other = lax.ppermute(values, axis_name, _exchange_pairs(count, distance))]
    ppermute x4, starting transfers between devices: 4.21 us -> 3.17 us  [sum_halving(): arrived = lax.ppermute(send, axis_name, _exchange_pairs(count, distance))]
    dot_general x1, matrix products: 2.96 us -> 3.86 us  [encoder_grads(): lax.dot_general(inputs_rows, grad_pre, (((0,), (0,)), ((), ())), preferre...]
    ppermute x4, waiting for transfers between devices: 4.44 us -> 3.64 us  [sum_halving(): arrived = lax.ppermute(values, axis_name, _exchange_pairs(count, distance))]
    ppermute x4, waiting for transfers between devices: 3.56 us -> 4.31 us  [sum_halving(): arrived = lax.ppermute(send, axis_name, _exchange_pairs(count, distance))]
  transfers between devices with their start and end apart: 16 -> 16, of which waited for: 10 -> 11; matrix products, arithmetic and copies ran while one was open for 13% -> 5% of each run, Pallas kernels for 0% -> 0%
where the time goes in v24:
time: 61 us; the launch traced here: 60.6 us
  starting transfers between devices  23.1 us (38%)
  waiting for transfers between devices  17.2 us (28%)
  matrix products  11.7 us (19%)
  other arithmetic  4.71 us (8%)
  local copies, waits for them, and re-layouts  2.89 us (5%)
  between operations  0.95 us (2%)
    ppermute x4, starting transfers between devices, sum_halving(): arrived = lax.ppermute(values, axis_name, _exchange_pairs(count, distance))  8.44 us
    ppermute x4, starting transfers between devices, gather_rows(): other = lax.ppermute(block, axis_name, _exchange_pairs(count, distance))  8.06 us
    ppermute x4, waiting for transfers between devices, gather_rows(): other = lax.ppermute(block, axis_name, _exchange_pairs(count, distance))  4.91 us
    ppermute x4, waiting for transfers between devices, sum_halving(): other = lax.ppermute(values, axis_name, _exchange_pairs(count, distance))  4.36 us
    ppermute x4, waiting for transfers between devices, sum_halving(): arrived = lax.ppermute(send, axis_name, _exchange_pairs(count, distance))  4.31 us
    dot_general x1, matrix products, encoder_grads(): lax.dot_general(inputs_rows, grad_pre, (((0,), (0,)), ((), ())), preferre...  3.86 us
    ppermute x4, waiting for transfers between devices, sum_halving(): arrived = lax.ppermute(values, axis_name, _exchange_pairs(count, distance))  3.64 us
    ppermute x4, starting transfers between devices, sum_halving(): other = lax.ppermute(values, axis_name, _exchange_pairs(count, distance))  3.46 us
  transfers between devices with their start and end apart: 16, of which 11 were waited for; matrix products, arithmetic and copies ran while one was open for 5% of the time, Pallas kernels for 0%

profile of v24, /device:TPU:0, one launch (start us, length us, event | category | flops | bytes accessed | tf_op | source)
XLA Modules:
  0.0 60.6 jit_solution(3054694271160476951)
XLA Ops:
  0.6 4.1 %collective-permute-start = (bf16[2,2048]{1,0:T(2,128)(2,1)}, bf16[2,2048]{1,0:T(2,128)(2,1)S(1)}, u32[]{:S(2)}, u32[]{:S(2)}) collective-permute-start(bf16[2,2048]{1,0:T(2,128)(2,1)} %param.9), channel_id=1, source_target_pairs={{0,8},{1,9},{2,10},{3,11},{4,12},{5,13},{6,14},{7,15},{8,0},{9,1},... | collective-permute-start | bytes 24584 | tf_op jit(solution)/shard_map/ppermute | solution.py:119
  4.7 1.8 %collective-permute-done = bf16[2,2048]{1,0:T(2,128)(2,1)S(1)} collective-permute-done((bf16[2,2048]{1,0:T(2,128)(2,1)}, bf16[2,2048]{1,0:T(2,128)(2,1)S(1)}, u32[]{:S(2)}, u32[]{:S(2)}) %collective-permute-start) | collective-permute-done | bytes 8224 | tf_op jit(solution)/shard_map/ppermute | solution.py:119
  7.4 2.0 %collective-permute-start.1 = (bf16[4,2048]{1,0:T(4,128)(2,1)S(1)}, bf16[4,2048]{1,0:T(4,128)(2,1)S(1)}, u32[]{:S(2)}, u32[]{:S(2)}) collective-permute-start(bf16[4,2048]{1,0:T(4,128)(2,1)S(1)} %maximum_select_fusion.8), channel_id=1, source_target_pairs={{0,4},{1,5},{2,6},{3,7},{4,0},{5,1},{6,2},{7,3},{8,12},{9,13},{10,... | collective-permute-start | bytes 49160 | tf_op jit(solution)/shard_map/ppermute | solution.py:119
  9.4 1.8 %collective-permute-done.1 = bf16[4,2048]{1,0:T(4,128)(2,1)S(1)} collective-permute-done((bf16[4,2048]{1,0:T(4,128)(2,1)S(1)}, bf16[4,2048]{1,0:T(4,128)(2,1)S(1)}, u32[]{:S(2)}, u32[]{:S(2)}) %collective-permute-start.1) | collective-permute-done | bytes 16416 | tf_op jit(solution)/shard_map/ppermute | solution.py:119
  11.3 1.9 %collective-permute-start.2 = (bf16[8,2048]{1,0:T(8,128)(2,1)S(1)}, bf16[8,2048]{1,0:T(8,128)(2,1)S(1)}, u32[]{:S(2)}, u32[]{:S(2)}) collective-permute-start(bf16[8,2048]{1,0:T(8,128)(2,1)S(1)} %maximum_select_fusion.7), channel_id=1, source_target_pairs={{0,2},{1,3},{2,0},{3,1},{4,6},{5,7},{6,4},{7,5},{8,10},{9,11},{10,... | collective-permute-start | bytes 98312 | tf_op jit(solution)/shard_map/ppermute | solution.py:119
  14.0 1.2 %collective-permute-done.2 = bf16[8,2048]{1,0:T(8,128)(2,1)S(1)} collective-permute-done((bf16[8,2048]{1,0:T(8,128)(2,1)S(1)}, bf16[8,2048]{1,0:T(8,128)(2,1)S(1)}, u32[]{:S(2)}, u32[]{:S(2)}) %collective-permute-start.2) | collective-permute-done | bytes 32800 | tf_op jit(solution)/shard_map/ppermute | solution.py:119
  22.9 1.2 %fusion.11 = f32[768,512]{1,0:T(8,128)S(1)} fusion(bf16[512,512]{1,0:T(8,128)(2,1)S(1)} %copy-done.5, f32[768,512]{1,0:T(8,128)S(1)} %get-tuple-element.17, f32[768,512]{1,0:T(8,128)S(1)} %convolution_add_fusion), kind=kOutput, calls=%fused_computation.30 | convolution fusion | flops 410517504 | bytes 5242880 | tf_op jit(solution)/shard_map/dot_general | solution.py:71
  26.2 1.0 %collective-permute-done.4 = bf16[160,512]{1,0:T(8,128)(2,1)S(1)} collective-permute-done((bf16[160,512]{1,0:T(8,128)(2,1)S(1)}, bf16[160,512]{1,0:T(8,128)(2,1)S(1)}, u32[]{:S(2)}, u32[]{:S(2)}) %collective-permute-start.4) | collective-permute-done | bytes 163872 | tf_op jit(solution)/shard_map/ppermute | solution.py:160
  28.8 1.9 %collective-permute-start.11 = (bf16[58,512]{1,0:T(8,128)(2,1)S(1)}, bf16[58,512]{1,0:T(8,128)(2,1)S(1)}, u32[]{:S(2)}, u32[]{:S(2)}) collective-permute-start(bf16[58,512]{1,0:T(8,128)(2,1)S(1)} %select_convert_fusion.3), channel_id=1, source_target_pairs={{0,2},{1,3},{2,0},{3,1},{4,6},{5,7},{6,4},{7,5},{8,10},{9,11},{10,... | collective-permute-start | bytes 178184 | tf_op jit(solution)/shard_map/ppermute | solution.py:160
  31.0 2.4 %collective-permute-done.11 = bf16[58,512]{1,0:T(8,128)(2,1)S(1)} collective-permute-done((bf16[58,512]{1,0:T(8,128)(2,1)S(1)}, bf16[58,512]{1,0:T(8,128)(2,1)S(1)}, u32[]{:S(2)}, u32[]{:S(2)}) %collective-permute-start.11) | collective-permute-done | bytes 59424 | tf_op jit(solution)/shard_map/ppermute | solution.py:160
  33.4 2.0 %collective-permute-start.12 = (bf16[58,512]{1,0:T(8,128)(2,1)S(1)}, bf16[58,512]{1,0:T(8,128)(2,1)S(1)}, u32[]{:S(2)}, u32[]{:S(2)}) collective-permute-start(bf16[58,512]{1,0:T(8,128)(2,1)S(1)} %add_convert_fusion.10), channel_id=1, source_target_pairs={{0,4},{1,5},{2,6},{3,7},{4,0},{5,1},{6,2},{7,3},{8,12},{9,13},{10,... | collective-permute-start | bytes 178184 | tf_op jit(solution)/shard_map/ppermute | solution.py:168
  35.4 1.6 %collective-permute-start.6 = (bf16[80,512]{1,0:T(8,128)(2,1)S(1)}, bf16[80,512]{1,0:T(8,128)(2,1)S(1)}, u32[]{:S(2)}, u32[]{:S(2)}) collective-permute-start(bf16[80,512]{1,0:T(8,128)(2,1)S(1)} %add_convert_fusion.7), channel_id=1, source_target_pairs={{0,4},{1,5},{2,6},{3,7},{4,0},{5,1},{6,2},{7,3},{8,12},{9,13},{10,... | collective-permute-start | bytes 245768 | tf_op jit(solution)/shard_map/ppermute | solution.py:168
  37.0 1.2 %collective-permute-done.12 = bf16[58,512]{1,0:T(8,128)(2,1)S(1)} collective-permute-done((bf16[58,512]{1,0:T(8,128)(2,1)S(1)}, bf16[58,512]{1,0:T(8,128)(2,1)S(1)}, u32[]{:S(2)}, u32[]{:S(2)}) %collective-permute-start.12) | collective-permute-done | bytes 59424 | tf_op jit(solution)/shard_map/ppermute | solution.py:168
  38.2 3.2 %collective-permute-start.13 = (bf16[58,512]{1,0:T(8,128)(2,1)S(1)}, bf16[58,512]{1,0:T(8,128)(2,1)S(1)}, u32[]{:S(2)}, u32[]{:S(2)}) collective-permute-start(bf16[58,512]{1,0:T(8,128)(2,1)S(1)} %add_convert_fusion.9), channel_id=1, source_target_pairs={{0,8},{1,9},{2,10},{3,11},{4,12},{5,13},{6,14},{7,15},{8,0},{9,1},... | collective-permute-start | bytes 178184 | tf_op jit(solution)/shard_map/ppermute | solution.py:168
  41.4 1.7 %collective-permute-start.7 = (bf16[80,512]{1,0:T(8,128)(2,1)S(1)}, bf16[80,512]{1,0:T(8,128)(2,1)S(1)}, u32[]{:S(2)}, u32[]{:S(2)}) collective-permute-start(bf16[80,512]{1,0:T(8,128)(2,1)S(1)} %add_convert_fusion.6), channel_id=1, source_target_pairs={{0,8},{1,9},{2,10},{3,11},{4,12},{5,13},{6,14},{7,15},{8,0},{9,1},... | collective-permute-start | bytes 245768 | tf_op jit(solution)/shard_map/ppermute | solution.py:168
  43.1 2.4 %collective-permute-done.13 = bf16[58,512]{1,0:T(8,128)(2,1)S(1)} collective-permute-done((bf16[58,512]{1,0:T(8,128)(2,1)S(1)}, bf16[58,512]{1,0:T(8,128)(2,1)S(1)}, u32[]{:S(2)}, u32[]{:S(2)}) %collective-permute-start.13) | collective-permute-done | bytes 59424 | tf_op jit(solution)/shard_map/ppermute | solution.py:168
  45.6 2.0 %collective-permute-start.14 = (bf16[58,512]{1,0:T(8,128)(2,1)S(1)}, bf16[58,512]{1,0:T(8,128)(2,1)S(1)}, u32[]{:S(2)}, u32[]{:S(2)}) collective-permute-start(bf16[58,512]{1,0:T(8,128)(2,1)S(1)} %add_convert_fusion.8), channel_id=1, source_target_pairs={{0,2},{1,3},{2,0},{3,1},{4,6},{5,7},{6,4},{7,5},{8,10},{9,11},{10,... | collective-permute-start | bytes 178184 | tf_op jit(solution)/shard_map/ppermute | solution.py:173
  47.6 1.3 %collective-permute-start.8 = (bf16[80,512]{1,0:T(8,128)(2,1)S(1)}, bf16[80,512]{1,0:T(8,128)(2,1)S(1)}, u32[]{:S(2)}, u32[]{:S(2)}) collective-permute-start(bf16[80,512]{1,0:T(8,128)(2,1)S(1)} %add_convert_fusion.5), channel_id=1, source_target_pairs={{0,2},{1,3},{2,0},{3,1},{4,6},{5,7},{6,4},{7,5},{8,10},{9,11},{10,... | collective-permute-start | bytes 245768 | tf_op jit(solution)/shard_map/ppermute | solution.py:173
  48.9 1.0 %collective-permute-done.14 = bf16[58,512]{1,0:T(8,128)(2,1)S(1)} collective-permute-done((bf16[58,512]{1,0:T(8,128)(2,1)S(1)}, bf16[58,512]{1,0:T(8,128)(2,1)S(1)}, u32[]{:S(2)}, u32[]{:S(2)}) %collective-permute-start.14) | collective-permute-done | bytes 59424 | tf_op jit(solution)/shard_map/ppermute | solution.py:173
  50.0 2.1 %collective-permute-done.8 = bf16[80,512]{1,0:T(8,128)(2,1)S(1)} collective-permute-done((bf16[80,512]{1,0:T(8,128)(2,1)S(1)}, bf16[80,512]{1,0:T(8,128)(2,1)S(1)}, u32[]{:S(2)}, u32[]{:S(2)}) %collective-permute-start.8) | collective-permute-done | bytes 81952 | tf_op jit(solution)/shard_map/ppermute | solution.py:173
  52.3 1.3 %collective-permute-done.9 = bf16[160,512]{1,0:T(8,128)(2,1)S(1)} collective-permute-done((bf16[160,512]{1,0:T(8,128)(2,1)S(1)}, bf16[160,512]{1,0:T(8,128)(2,1)S(1)}, u32[]{:S(2)}, u32[]{:S(2)}) %collective-permute-start.9) | collective-permute-done | bytes 163872 | tf_op jit(solution)/shard_map/ppermute | solution.py:173
  54.4 1.3 %fusion.37 = f32[512,512]{1,0:T(8,128)} fusion(bf16[32,512]{1,0:T(8,128)(2,1)S(1)} %fusion.8, bf16[320,512]{1,0:T(8,128)(2,1)S(1)} %maximum_select_fusion), kind=kOutput, calls=%fused_computation.77 | convolution fusion | flops 16777216 | bytes 1114112 | tf_op jit(solution)/shard_map/dot_general | solution.py:91
  55.7 3.9 %fusion.10 = f32[2048,512]{1,0:T(8,128)} fusion(bf16[32,2048]{1,0:T(8,128)(2,1)} %copy-done.4, bf16[512,512]{1,0:T(8,128)(2,1)S(1)} %copy-done.1, bf16[32,512]{1,0:T(8,128)(2,1)S(1)} %fusion.8, bf16[320,512]{1,0:T(8,128)(2,1)S(1)} %maximum_select_fusion), kind=kOutput, calls=%fused_computation.22 | convolution fusion | flops 83968000 | bytes 4915200 | tf_op jit(solution)/shard_map/dot_general | solution.py:98
  59.5 1.1 %fusion.13 = f32[512,512]{1,0:T(8,128)} fusion(bf16[232,512]{1,0:T(8,128)(2,1)S(1)} %maximum_select_fusion.1, bf16[286,512]{1,0:T(8,128)(2,1)S(1)} %slice.100), kind=kLoop, calls=%fused_computation.32 | loop fusion | flops 1048576 | bytes 1579008 | tf_op jit(solution)/shard_map/convert_element_type | solution.py:248
  (70 shorter events, 14.3 us)
Async XLA Ops:
  0.6 16.5 %copy-start = (bf16[2048,512]{1,0:T(8,128)(2,1)S(1)}, bf16[2048,512]{1,0:T(8,128)(2,1)}, u32[]{:S(2)}) copy-start(bf16[2048,512]{1,0:T(8,128)(2,1)} %param.12) | copy-start | bytes 6291460
  0.6 5.9 %collective-permute-start = (bf16[2,2048]{1,0:T(2,128)(2,1)}, bf16[2,2048]{1,0:T(2,128)(2,1)S(1)}, u32[]{:S(2)}, u32[]{:S(2)}) collective-permute-start(bf16[2,2048]{1,0:T(2,128)(2,1)} %param.9), channel_id=1, source_target_pairs={{0,8},{1,9},{2,10},{3,11},{4,12},{5,13},{6,14},{7,15},{8,0},{9,1},... | collective-permute-start | bytes 24584 | tf_op jit(solution)/shard_map/ppermute | solution.py:119
  7.4 3.8 %collective-permute-start.1 = (bf16[4,2048]{1,0:T(4,128)(2,1)S(1)}, bf16[4,2048]{1,0:T(4,128)(2,1)S(1)}, u32[]{:S(2)}, u32[]{:S(2)}) collective-permute-start(bf16[4,2048]{1,0:T(4,128)(2,1)S(1)} %maximum_select_fusion.8), channel_id=1, source_target_pairs={{0,4},{1,5},{2,6},{3,7},{4,0},{5,1},{6,2},{7,3},{8,12},{9,13},{10,... | collective-permute-start | bytes 49160 | tf_op jit(solution)/shard_map/ppermute | solution.py:119
  11.2 6.4 %copy-start.1 = (bf16[512,512]{1,0:T(8,128)(2,1)S(1)}, bf16[512,512]{1,0:T(8,128)(2,1)}, u32[]{:S(2)}) copy-start(bf16[512,512]{1,0:T(8,128)(2,1)} %param.13) | copy-start | bytes 1572868
  11.3 4.0 %collective-permute-start.2 = (bf16[8,2048]{1,0:T(8,128)(2,1)S(1)}, bf16[8,2048]{1,0:T(8,128)(2,1)S(1)}, u32[]{:S(2)}, u32[]{:S(2)}) collective-permute-start(bf16[8,2048]{1,0:T(8,128)(2,1)S(1)} %maximum_select_fusion.7), channel_id=1, source_target_pairs={{0,2},{1,3},{2,0},{3,1},{4,6},{5,7},{6,4},{7,5},{8,10},{9,11},{10,... | collective-permute-start | bytes 98312 | tf_op jit(solution)/shard_map/ppermute | solution.py:119
  15.3 1.7 %collective-permute-start.3 = (bf16[16,2048]{1,0:T(8,128)(2,1)S(1)}, bf16[16,2048]{1,0:T(8,128)(2,1)S(1)}, u32[]{:S(2)}, u32[]{:S(2)}) collective-permute-start(bf16[16,2048]{1,0:T(8,128)(2,1)S(1)} %maximum_select_fusion.6), channel_id=1, source_target_pairs={{0,1},{1,0},{2,3},{3,2},{4,5},{5,4},{6,7},{7,6},{8,9},{9,8},{10,11... | collective-permute-start | bytes 196616 | tf_op jit(solution)/shard_map/ppermute | solution.py:119
  17.1 0.7 %copy-start.4 = (bf16[32,2048]{1,0:T(8,128)(2,1)}, bf16[32,2048]{1,0:T(8,128)(2,1)S(1)}, u32[]{:S(2)}) copy-start(bf16[32,2048]{1,0:T(8,128)(2,1)S(1)} %convolution_convert_fusion) | copy-start | bytes 393220
  17.2 1.1 %copy-start.5 = (bf16[512,512]{1,0:T(8,128)(2,1)S(1)}, bf16[512,512]{1,0:T(8,128)(2,1)}, u32[]{:S(2)}) copy-start(bf16[512,512]{1,0:T(8,128)(2,1)} %constant.123.clone) | copy-start | bytes 1572868
  18.0 1.0 %copy-start.2 = (bf16[512,256]{1,0:T(8,128)(2,1)S(1)}, bf16[512,256]{1,0:T(8,128)(2,1)}, u32[]{:S(2)}) copy-start(bf16[512,256]{1,0:T(8,128)(2,1)} %constant.131) | copy-start | bytes 786436
  18.8 1.0 %copy-start.6 = (bf16[512,256]{1,0:T(8,128)(2,1)S(1)}, bf16[512,256]{1,0:T(8,128)(2,1)}, u32[]{:S(2)}) copy-start(bf16[512,256]{1,0:T(8,128)(2,1)} %constant.132) | copy-start | bytes 786436
  19.8 1.0 %copy-start.3 = (bf16[512,512]{1,0:T(8,128)(2,1)S(1)}, bf16[512,512]{1,0:T(8,128)(2,1)}, u32[]{:S(2)}) copy-start(bf16[512,512]{1,0:T(8,128)(2,1)} %param.16) | copy-start | bytes 1572868
  19.8 1.3 %copy-start.7 = (bf16[32,24,512]{2,1,0:T(8,128)(2,1)S(1)}, bf16[32,24,512]{2,1,0:T(8,128)(2,1)}, u32[]{:S(2)}) copy-start(bf16[32,24,512]{2,1,0:T(8,128)(2,1)} %param.10) | copy-start | bytes 2359300
  25.6 1.6 %collective-permute-start.4 = (bf16[160,512]{1,0:T(8,128)(2,1)S(1)}, bf16[160,512]{1,0:T(8,128)(2,1)S(1)}, u32[]{:S(2)}, u32[]{:S(2)}) collective-permute-start(bf16[160,512]{1,0:T(8,128)(2,1)S(1)} %get-tuple-element.10), channel_id=1, source_target_pairs={{0,1},{1,0},{2,3},{3,2},{4,5},{5,4},{6,7},{7,6},{8,9},{9,8},{10,11... | collective-permute-start | bytes 491528 | tf_op jit(solution)/shard_map/ppermute | solution.py:160
  27.3 1.4 %collective-permute-start.10 = (bf16[116,512]{1,0:T(8,128)(2,1)S(1)}, bf16[116,512]{1,0:T(8,128)(2,1)S(1)}, u32[]{:S(2)}, u32[]{:S(2)}) collective-permute-start(bf16[116,512]{1,0:T(8,128)(2,1)S(1)} %select_convert_fusion.1), channel_id=1, source_target_pairs={{0,1},{1,0},{2,3},{3,2},{4,5},{5,4},{6,7},{7,6},{8,9},{9,8},{10,11... | collective-permute-start | bytes 356360 | tf_op jit(solution)/shard_map/ppermute | solution.py:160
  28.8 4.5 %collective-permute-start.11 = (bf16[58,512]{1,0:T(8,128)(2,1)S(1)}, bf16[58,512]{1,0:T(8,128)(2,1)S(1)}, u32[]{:S(2)}, u32[]{:S(2)}) collective-permute-start(bf16[58,512]{1,0:T(8,128)(2,1)S(1)} %select_convert_fusion.3), channel_id=1, source_target_pairs={{0,2},{1,3},{2,0},{3,1},{4,6},{5,7},{6,4},{7,5},{8,10},{9,11},{10,... | collective-permute-start | bytes 178184 | tf_op jit(solution)/shard_map/ppermute | solution.py:160
  30.8 4.6 %collective-permute-start.5 = (bf16[80,512]{1,0:T(8,128)(2,1)S(1)}, bf16[80,512]{1,0:T(8,128)(2,1)S(1)}, u32[]{:S(2)}, u32[]{:S(2)}) collective-permute-start(bf16[80,512]{1,0:T(8,128)(2,1)S(1)} %select_convert_fusion.2), channel_id=1, source_target_pairs={{0,2},{1,3},{2,0},{3,1},{4,6},{5,7},{6,4},{7,5},{8,10},{9,11},{10,... | collective-permute-start | bytes 245768 | tf_op jit(solution)/shard_map/ppermute | solution.py:160
  33.4 4.8 %collective-permute-start.12 = (bf16[58,512]{1,0:T(8,128)(2,1)S(1)}, bf16[58,512]{1,0:T(8,128)(2,1)S(1)}, u32[]{:S(2)}, u32[]{:S(2)}) collective-permute-start(bf16[58,512]{1,0:T(8,128)(2,1)S(1)} %add_convert_fusion.10), channel_id=1, source_target_pairs={{0,4},{1,5},{2,6},{3,7},{4,0},{5,1},{6,2},{7,3},{8,12},{9,13},{10,... | collective-permute-start | bytes 178184 | tf_op jit(solution)/shard_map/ppermute | solution.py:168
  35.4 6.0 %collective-permute-start.6 = (bf16[80,512]{1,0:T(8,128)(2,1)S(1)}, bf16[80,512]{1,0:T(8,128)(2,1)S(1)}, u32[]{:S(2)}, u32[]{:S(2)}) collective-permute-start(bf16[80,512]{1,0:T(8,128)(2,1)S(1)} %add_convert_fusion.7), channel_id=1, source_target_pairs={{0,4},{1,5},{2,6},{3,7},{4,0},{5,1},{6,2},{7,3},{8,12},{9,13},{10,... | collective-permute-start | bytes 245768 | tf_op jit(solution)/shard_map/ppermute | solution.py:168
  38.2 7.3 %collective-permute-start.13 = (bf16[58,512]{1,0:T(8,128)(2,1)S(1)}, bf16[58,512]{1,0:T(8,128)(2,1)S(1)}, u32[]{:S(2)}, u32[]{:S(2)}) collective-permute-start(bf16[58,512]{1,0:T(8,128)(2,1)S(1)} %add_convert_fusion.9), channel_id=1, source_target_pairs={{0,8},{1,9},{2,10},{3,11},{4,12},{5,13},{6,14},{7,15},{8,0},{9,1},... | collective-permute-start | bytes 178184 | tf_op jit(solution)/shard_map/ppermute | solution.py:168
  41.4 6.1 %collective-permute-start.7 = (bf16[80,512]{1,0:T(8,128)(2,1)S(1)}, bf16[80,512]{1,0:T(8,128)(2,1)S(1)}, u32[]{:S(2)}, u32[]{:S(2)}) collective-permute-start(bf16[80,512]{1,0:T(8,128)(2,1)S(1)} %add_convert_fusion.6), channel_id=1, source_target_pairs={{0,8},{1,9},{2,10},{3,11},{4,12},{5,13},{6,14},{7,15},{8,0},{9,1},... | collective-permute-start | bytes 245768 | tf_op jit(solution)/shard_map/ppermute | solution.py:168
  45.6 4.3 %collective-permute-start.14 = (bf16[58,512]{1,0:T(8,128)(2,1)S(1)}, bf16[58,512]{1,0:T(8,128)(2,1)S(1)}, u32[]{:S(2)}, u32[]{:S(2)}) collective-permute-start(bf16[58,512]{1,0:T(8,128)(2,1)S(1)} %add_convert_fusion.8), channel_id=1, source_target_pairs={{0,2},{1,3},{2,0},{3,1},{4,6},{5,7},{6,4},{7,5},{8,10},{9,11},{10,... | collective-permute-start | bytes 178184 | tf_op jit(solution)/shard_map/ppermute | solution.py:173
  47.6 4.5 %collective-permute-start.8 = (bf16[80,512]{1,0:T(8,128)(2,1)S(1)}, bf16[80,512]{1,0:T(8,128)(2,1)S(1)}, u32[]{:S(2)}, u32[]{:S(2)}) collective-permute-start(bf16[80,512]{1,0:T(8,128)(2,1)S(1)} %add_convert_fusion.5), channel_id=1, source_target_pairs={{0,2},{1,3},{2,0},{3,1},{4,6},{5,7},{6,4},{7,5},{8,10},{9,11},{10,... | collective-permute-start | bytes 245768 | tf_op jit(solution)/shard_map/ppermute | solution.py:173
  49.9 2.3 %collective-permute-start.15 = (bf16[116,512]{1,0:T(8,128)(2,1)S(1)}, bf16[116,512]{1,0:T(8,128)(2,1)S(1)}, u32[]{:S(2)}, u32[]{:S(2)}) collective-permute-start(bf16[116,512]{1,0:T(8,128)(2,1)S(1)} %maximum_select_fusion.5), channel_id=1, source_target_pairs={{0,1},{1,0},{2,3},{3,2},{4,5},{5,4},{6,7},{7,6},{8,9},{9,8},{10,11... | collective-permute-start | bytes 356360 | tf_op jit(solution)/shard_map/ppermute | solution.py:173
  52.1 1.5 %collective-permute-start.9 = (bf16[160,512]{1,0:T(8,128)(2,1)S(1)}, bf16[160,512]{1,0:T(8,128)(2,1)S(1)}, u32[]{:S(2)}, u32[]{:S(2)}) collective-permute-start(bf16[160,512]{1,0:T(8,128)(2,1)S(1)} %maximum_select_fusion.2), channel_id=1, source_target_pairs={{0,1},{1,0},{2,3},{3,2},{4,5},{5,4},{6,7},{7,6},{8,9},{9,8},{10,11... | collective-permute-start | bytes 491528 | tf_op jit(solution)/shard_map/ppermute | solution.py:173

commit v25 on v23

--- a/solution.py
+++ b/solution.py
@@ -159,7 +159,7 @@
         send = jnp.where(lower, values[half:], values[:half]).astype(wire)
         arrived = lax.ppermute(send, axis_name, _exchange_pairs(count, distance))
         values = keep + arrived.astype(keep.dtype)
-        if distance == 1 and trailing is not None:
+        if distance == 2 and trailing is not None:
             values, trailing = lax.optimization_barrier((values, trailing))
         distance *= 2
     top = distance

time: 58.2 us -> 61.5 us (1.057)
  waiting for transfers between devices: 13.7 us -> 17.1 us
    ppermute x4, waiting for transfers between devices: 0.78 us -> 3.11 us  [sum_halving(): other = lax.ppermute(values, axis_name, _exchange_pairs(count, distance))]
    ppermute x4, waiting for transfers between devices: 4.44 us -> 5.14 us  [sum_halving(): arrived = lax.ppermute(values, axis_name, _exchange_pairs(count, distance))]
  transfers between devices with their start and end apart: 16 -> 16, of which waited for: 10 -> 12; matrix products, arithmetic and copies ran while one was open for 13% -> 13% of each run, Pallas kernels for 0% -> 0%
where the time goes in v25:
time: 61.5 us; the launch traced here: 61.1 us
  starting transfers between devices  24.6 us (40%)
  waiting for transfers between devices  17.1 us (28%)
  matrix products  10.8 us (18%)
  other arithmetic  4.77 us (8%)
  local copies, waits for them, and re-layouts  2.84 us (5%)
  between operations  0.94 us (2%)
    ppermute x4, starting transfers between devices, sum_halving(): arrived = lax.ppermute(values, axis_name, _exchange_pairs(count, distance))  9.03 us
    ppermute x4, starting transfers between devices, gather_rows(): other = lax.ppermute(block, axis_name, _exchange_pairs(count, distance))  8.06 us
    ppermute x4, waiting for transfers between devices, sum_halving(): arrived = lax.ppermute(values, axis_name, _exchange_pairs(count, distance))  5.14 us
    ppermute x4, waiting for transfers between devices, gather_rows(): other = lax.ppermute(block, axis_name, _exchange_pairs(count, distance))  4.91 us
    ppermute x4, starting transfers between devices, sum_halving(): arrived = lax.ppermute(send, axis_name, _exchange_pairs(count, distance))  4.16 us
    ppermute x4, waiting for transfers between devices, sum_halving(): arrived = lax.ppermute(send, axis_name, _exchange_pairs(count, distance))  3.97 us
    ppermute x4, starting transfers between devices, sum_halving(): other = lax.ppermute(values, axis_name, _exchange_pairs(count, distance))  3.37 us
    ppermute x4, waiting for transfers between devices, sum_halving(): other = lax.ppermute(values, axis_name, _exchange_pairs(count, distance))  3.11 us
  transfers between devices with their start and end apart: 16, of which 12 were waited for; matrix products, arithmetic and copies ran while one was open for 13% of the time, Pallas kernels for 0%

profile of v25, /device:TPU:0, one launch (start us, length us, event | category | flops | bytes accessed | tf_op | source)
XLA Modules:
  0.0 61.1 jit_solution(10147845558039488045)
XLA Ops:
  0.6 4.1 %collective-permute-start = (bf16[2,2048]{1,0:T(2,128)(2,1)}, bf16[2,2048]{1,0:T(2,128)(2,1)S(1)}, u32[]{:S(2)}, u32[]{:S(2)}) collective-permute-start(bf16[2,2048]{1,0:T(2,128)(2,1)} %param.9), channel_id=1, source_target_pairs={{0,8},{1,9},{2,10},{3,11},{4,12},{5,13},{6,14},{7,15},{8,0},{9,1},... | collective-permute-start | bytes 24584 | tf_op jit(solution)/shard_map/ppermute | solution.py:119
  4.7 1.8 %collective-permute-done = bf16[2,2048]{1,0:T(2,128)(2,1)S(1)} collective-permute-done((bf16[2,2048]{1,0:T(2,128)(2,1)}, bf16[2,2048]{1,0:T(2,128)(2,1)S(1)}, u32[]{:S(2)}, u32[]{:S(2)}) %collective-permute-start) | collective-permute-done | bytes 8224 | tf_op jit(solution)/shard_map/ppermute | solution.py:119
  7.4 2.0 %collective-permute-start.1 = (bf16[4,2048]{1,0:T(4,128)(2,1)S(1)}, bf16[4,2048]{1,0:T(4,128)(2,1)S(1)}, u32[]{:S(2)}, u32[]{:S(2)}) collective-permute-start(bf16[4,2048]{1,0:T(4,128)(2,1)S(1)} %maximum_select_fusion.8), channel_id=1, source_target_pairs={{0,4},{1,5},{2,6},{3,7},{4,0},{5,1},{6,2},{7,3},{8,12},{9,13},{10,... | collective-permute-start | bytes 49160 | tf_op jit(solution)/shard_map/ppermute | solution.py:119
  9.4 1.8 %collective-permute-done.1 = bf16[4,2048]{1,0:T(4,128)(2,1)S(1)} collective-permute-done((bf16[4,2048]{1,0:T(4,128)(2,1)S(1)}, bf16[4,2048]{1,0:T(4,128)(2,1)S(1)}, u32[]{:S(2)}, u32[]{:S(2)}) %collective-permute-start.1) | collective-permute-done | bytes 16416 | tf_op jit(solution)/shard_map/ppermute | solution.py:119
  11.3 1.9 %collective-permute-start.2 = (bf16[8,2048]{1,0:T(8,128)(2,1)S(1)}, bf16[8,2048]{1,0:T(8,128)(2,1)S(1)}, u32[]{:S(2)}, u32[]{:S(2)}) collective-permute-start(bf16[8,2048]{1,0:T(8,128)(2,1)S(1)} %maximum_select_fusion.7), channel_id=1, source_target_pairs={{0,2},{1,3},{2,0},{3,1},{4,6},{5,7},{6,4},{7,5},{8,10},{9,11},{10,... | collective-permute-start | bytes 98312 | tf_op jit(solution)/shard_map/ppermute | solution.py:119
  14.0 1.2 %collective-permute-done.2 = bf16[8,2048]{1,0:T(8,128)(2,1)S(1)} collective-permute-done((bf16[8,2048]{1,0:T(8,128)(2,1)S(1)}, bf16[8,2048]{1,0:T(8,128)(2,1)S(1)}, u32[]{:S(2)}, u32[]{:S(2)}) %collective-permute-start.2) | collective-permute-done | bytes 32800 | tf_op jit(solution)/shard_map/ppermute | solution.py:119
  19.7 0.9 %add_convert_fusion = (bf16[768,512]{1,0:T(8,128)(2,1)S(1)}, f32[768,512]{1,0:T(8,128)S(1)}) fusion(bf16[32,24,512]{2,1,0:T(8,128)(2,1)S(1)} %multiply_convert_fusion, f32[768,512]{1,0:T(8,128)S(1)} %fusion.14, bf16[512,256]{1,0:T(8,128)(2,1)S(1)} %copy-done.5, f32[768,512]{1,0:T(8,128)S(1)} %fusion.52, f32[256]{0:T(256)S(1)} %bitcast.42, f32[256]{0:T(256)S(1)} %bitcast.38), kind=kOutput, calls=%fused_computation.14 | convolution fusion | flops 206831616 | bytes 6555648 | tf_op jit(solution)/shard_map/dot_general | solution.py:55
  22.9 1.2 %fusion.11 = f32[768,512]{1,0:T(8,128)S(1)} fusion(bf16[512,512]{1,0:T(8,128)(2,1)S(1)} %copy-done.4, f32[768,512]{1,0:T(8,128)S(1)} %get-tuple-element.17, f32[768,512]{1,0:T(8,128)S(1)} %convolution_add_fusion), kind=kOutput, calls=%fused_computation.30 | convolution fusion | flops 410517504 | bytes 5242880 | tf_op jit(solution)/shard_map/dot_general | solution.py:71
  26.1 1.0 %collective-permute-done.4 = bf16[138,512]{1,0:T(8,128)(2,1)S(1)} collective-permute-done((bf16[138,512]{1,0:T(8,128)(2,1)S(1)}, bf16[138,512]{1,0:T(8,128)(2,1)S(1)}, u32[]{:S(2)}, u32[]{:S(2)}) %collective-permute-start.4) | collective-permute-done | bytes 141344 | tf_op jit(solution)/shard_map/ppermute | solution.py:160
  27.2 1.9 %collective-permute-start.5 = (bf16[69,512]{1,0:T(8,128)(2,1)S(1)}, bf16[69,512]{1,0:T(8,128)(2,1)S(1)}, u32[]{:S(2)}, u32[]{:S(2)}) collective-permute-start(bf16[69,512]{1,0:T(8,128)(2,1)S(1)} %select_convert_fusion.3), channel_id=1, source_target_pairs={{0,2},{1,3},{2,0},{3,1},{4,6},{5,7},{6,4},{7,5},{8,10},{9,11},{10,... | collective-permute-start | bytes 211976 | tf_op jit(solution)/shard_map/ppermute | solution.py:160
  29.2 2.7 %collective-permute-done.5 = bf16[69,512]{1,0:T(8,128)(2,1)S(1)} collective-permute-done((bf16[69,512]{1,0:T(8,128)(2,1)S(1)}, bf16[69,512]{1,0:T(8,128)(2,1)S(1)}, u32[]{:S(2)}, u32[]{:S(2)}) %collective-permute-start.5) | collective-permute-done | bytes 70688 | tf_op jit(solution)/shard_map/ppermute | solution.py:160
  31.9 1.9 %collective-permute-start.6 = (bf16[69,512]{1,0:T(8,128)(2,1)S(1)}, bf16[69,512]{1,0:T(8,128)(2,1)S(1)}, u32[]{:S(2)}, u32[]{:S(2)}) collective-permute-start(bf16[69,512]{1,0:T(8,128)(2,1)S(1)} %convert_add_fusion.2), channel_id=1, source_target_pairs={{0,4},{1,5},{2,6},{3,7},{4,0},{5,1},{6,2},{7,3},{8,12},{9,13},{10,... | collective-permute-start | bytes 211976 | tf_op jit(solution)/shard_map/ppermute | solution.py:168
  33.9 2.4 %collective-permute-done.6 = bf16[69,512]{1,0:T(8,128)(2,1)S(1)} collective-permute-done((bf16[69,512]{1,0:T(8,128)(2,1)S(1)}, bf16[69,512]{1,0:T(8,128)(2,1)S(1)}, u32[]{:S(2)}, u32[]{:S(2)}) %collective-permute-start.6) | collective-permute-done | bytes 70688 | tf_op jit(solution)/shard_map/ppermute | solution.py:168
  36.4 2.9 %collective-permute-start.7 = (bf16[69,512]{1,0:T(8,128)(2,1)S(1)}, bf16[69,512]{1,0:T(8,128)(2,1)S(1)}, u32[]{:S(2)}, u32[]{:S(2)}) collective-permute-start(bf16[69,512]{1,0:T(8,128)(2,1)S(1)} %add_convert_fusion.9), channel_id=1, source_target_pairs={{0,8},{1,9},{2,10},{3,11},{4,12},{5,13},{6,14},{7,15},{8,0},{9,1},... | collective-permute-start | bytes 211976 | tf_op jit(solution)/shard_map/ppermute | solution.py:168
  39.4 1.6 %collective-permute-start.11 = (bf16[69,512]{1,0:T(8,128)(2,1)S(1)}, bf16[69,512]{1,0:T(8,128)(2,1)S(1)}, u32[]{:S(2)}, u32[]{:S(2)}) collective-permute-start(bf16[69,512]{1,0:T(8,128)(2,1)S(1)} %select_convert_fusion.2), channel_id=1, source_target_pairs={{0,2},{1,3},{2,0},{3,1},{4,6},{5,7},{6,4},{7,5},{8,10},{9,11},{10,... | collective-permute-start | bytes 211976 | tf_op jit(solution)/shard_map/ppermute | solution.py:160
  41.7 1.8 %collective-permute-start.8 = (bf16[69,512]{1,0:T(8,128)(2,1)S(1)}, bf16[69,512]{1,0:T(8,128)(2,1)S(1)}, u32[]{:S(2)}, u32[]{:S(2)}) collective-permute-start(bf16[69,512]{1,0:T(8,128)(2,1)S(1)} %add_convert_fusion.8), channel_id=1, source_target_pairs={{0,2},{1,3},{2,0},{3,1},{4,6},{5,7},{6,4},{7,5},{8,10},{9,11},{10,... | collective-permute-start | bytes 211976 | tf_op jit(solution)/shard_map/ppermute | solution.py:173
  43.8 1.6 %collective-permute-start.12 = (bf16[69,512]{1,0:T(8,128)(2,1)S(1)}, bf16[69,512]{1,0:T(8,128)(2,1)S(1)}, u32[]{:S(2)}, u32[]{:S(2)}) collective-permute-start(bf16[69,512]{1,0:T(8,128)(2,1)S(1)} %add_convert_fusion.7), channel_id=1, source_target_pairs={{0,4},{1,5},{2,6},{3,7},{4,0},{5,1},{6,2},{7,3},{8,12},{9,13},{10,... | collective-permute-start | bytes 211976 | tf_op jit(solution)/shard_map/ppermute | solution.py:168
  46.3 2.0 %collective-permute-done.12 = bf16[69,512]{1,0:T(8,128)(2,1)S(1)} collective-permute-done((bf16[69,512]{1,0:T(8,128)(2,1)S(1)}, bf16[69,512]{1,0:T(8,128)(2,1)S(1)}, u32[]{:S(2)}, u32[]{:S(2)}) %collective-permute-start.12) | collective-permute-done | bytes 70688 | tf_op jit(solution)/shard_map/ppermute | solution.py:168
  48.3 2.7 %collective-permute-start.13 = (bf16[69,512]{1,0:T(8,128)(2,1)S(1)}, bf16[69,512]{1,0:T(8,128)(2,1)S(1)}, u32[]{:S(2)}, u32[]{:S(2)}) collective-permute-start(bf16[69,512]{1,0:T(8,128)(2,1)S(1)} %add_convert_fusion.6), channel_id=1, source_target_pairs={{0,8},{1,9},{2,10},{3,11},{4,12},{5,13},{6,14},{7,15},{8,0},{9,1},... | collective-permute-start | bytes 211976 | tf_op jit(solution)/shard_map/ppermute | solution.py:168
  51.0 3.0 %fusion.10 = f32[2048,512]{1,0:T(8,128)} fusion(bf16[32,2048]{1,0:T(8,128)(2,1)S(1)} %convolution_convert_fusion, bf16[512,512]{1,0:T(8,128)(2,1)S(1)} %copy-done.1, bf16[32,512]{1,0:T(8,128)(2,1)S(1)} %fusion.8, bf16[276,512]{1,0:T(8,128)(2,1)S(1)} %maximum_select_fusion), kind=kOutput, calls=%fused_computation.22 | convolution fusion | flops 83968000 | bytes 4915200 | tf_op jit(solution)/shard_map/dot_general | solution.py:98
  54.0 1.4 %collective-permute-start.14 = (bf16[69,512]{1,0:T(8,128)(2,1)S(1)}, bf16[69,512]{1,0:T(8,128)(2,1)S(1)}, u32[]{:S(2)}, u32[]{:S(2)}) collective-permute-start(bf16[69,512]{1,0:T(8,128)(2,1)S(1)} %add_convert_fusion.5), channel_id=1, source_target_pairs={{0,2},{1,3},{2,0},{3,1},{4,6},{5,7},{6,4},{7,5},{8,10},{9,11},{10,... | collective-permute-start | bytes 211976 | tf_op jit(solution)/shard_map/ppermute | solution.py:173
  55.4 1.3 %fusion.37 = f32[512,512]{1,0:T(8,128)} fusion(bf16[32,512]{1,0:T(8,128)(2,1)S(1)} %fusion.8, bf16[276,512]{1,0:T(8,128)(2,1)S(1)} %maximum_select_fusion), kind=kOutput, calls=%fused_computation.77 | convolution fusion | flops 16777216 | bytes 1114112 | tf_op jit(solution)/shard_map/dot_general | solution.py:91
  56.8 1.6 %collective-permute-done.14 = bf16[69,512]{1,0:T(8,128)(2,1)S(1)} collective-permute-done((bf16[69,512]{1,0:T(8,128)(2,1)S(1)}, bf16[69,512]{1,0:T(8,128)(2,1)S(1)}, u32[]{:S(2)}, u32[]{:S(2)}) %collective-permute-start.14) | collective-permute-done | bytes 70688 | tf_op jit(solution)/shard_map/ppermute | solution.py:173
  60.0 1.1 %fusion.13 = f32[512,512]{1,0:T(8,128)} fusion(bf16[276,512]{1,0:T(8,128)(2,1)S(1)} %maximum_select_fusion.1, bf16[242,512]{1,0:T(8,128)(2,1)S(1)} %slice.102), kind=kLoop, calls=%fused_computation.32 | loop fusion | flops 1048576 | bytes 1579008 | tf_op jit(solution)/shard_map/convert_element_type | solution.py:248
  (68 shorter events, 14.3 us)
Async XLA Ops:
  0.6 16.5 %copy-start = (bf16[2048,512]{1,0:T(8,128)(2,1)S(1)}, bf16[2048,512]{1,0:T(8,128)(2,1)}, u32[]{:S(2)}) copy-start(bf16[2048,512]{1,0:T(8,128)(2,1)} %param.12) | copy-start | bytes 6291460
  0.6 5.9 %collective-permute-start = (bf16[2,2048]{1,0:T(2,128)(2,1)}, bf16[2,2048]{1,0:T(2,128)(2,1)S(1)}, u32[]{:S(2)}, u32[]{:S(2)}) collective-permute-start(bf16[2,2048]{1,0:T(2,128)(2,1)} %param.9), channel_id=1, source_target_pairs={{0,8},{1,9},{2,10},{3,11},{4,12},{5,13},{6,14},{7,15},{8,0},{9,1},... | collective-permute-start | bytes 24584 | tf_op jit(solution)/shard_map/ppermute | solution.py:119
  7.4 3.8 %collective-permute-start.1 = (bf16[4,2048]{1,0:T(4,128)(2,1)S(1)}, bf16[4,2048]{1,0:T(4,128)(2,1)S(1)}, u32[]{:S(2)}, u32[]{:S(2)}) collective-permute-start(bf16[4,2048]{1,0:T(4,128)(2,1)S(1)} %maximum_select_fusion.8), channel_id=1, source_target_pairs={{0,4},{1,5},{2,6},{3,7},{4,0},{5,1},{6,2},{7,3},{8,12},{9,13},{10,... | collective-permute-start | bytes 49160 | tf_op jit(solution)/shard_map/ppermute | solution.py:119
  11.2 6.4 %copy-start.1 = (bf16[512,512]{1,0:T(8,128)(2,1)S(1)}, bf16[512,512]{1,0:T(8,128)(2,1)}, u32[]{:S(2)}) copy-start(bf16[512,512]{1,0:T(8,128)(2,1)} %param.13) | copy-start | bytes 1572868
  11.3 4.0 %collective-permute-start.2 = (bf16[8,2048]{1,0:T(8,128)(2,1)S(1)}, bf16[8,2048]{1,0:T(8,128)(2,1)S(1)}, u32[]{:S(2)}, u32[]{:S(2)}) collective-permute-start(bf16[8,2048]{1,0:T(8,128)(2,1)S(1)} %maximum_select_fusion.7), channel_id=1, source_target_pairs={{0,2},{1,3},{2,0},{3,1},{4,6},{5,7},{6,4},{7,5},{8,10},{9,11},{10,... | collective-permute-start | bytes 98312 | tf_op jit(solution)/shard_map/ppermute | solution.py:119
  15.3 1.7 %collective-permute-start.3 = (bf16[16,2048]{1,0:T(8,128)(2,1)S(1)}, bf16[16,2048]{1,0:T(8,128)(2,1)S(1)}, u32[]{:S(2)}, u32[]{:S(2)}) collective-permute-start(bf16[16,2048]{1,0:T(8,128)(2,1)S(1)} %maximum_select_fusion.6), channel_id=1, source_target_pairs={{0,1},{1,0},{2,3},{3,2},{4,5},{5,4},{6,7},{7,6},{8,9},{9,8},{10,11... | collective-permute-start | bytes 196616 | tf_op jit(solution)/shard_map/ppermute | solution.py:119
  17.1 1.0 %copy-start.4 = (bf16[512,512]{1,0:T(8,128)(2,1)S(1)}, bf16[512,512]{1,0:T(8,128)(2,1)}, u32[]{:S(2)}) copy-start(bf16[512,512]{1,0:T(8,128)(2,1)} %constant.123.clone) | copy-start | bytes 1572868
  18.0 1.0 %copy-start.2 = (bf16[512,256]{1,0:T(8,128)(2,1)S(1)}, bf16[512,256]{1,0:T(8,128)(2,1)}, u32[]{:S(2)}) copy-start(bf16[512,256]{1,0:T(8,128)(2,1)} %constant.131) | copy-start | bytes 786436
  18.8 1.0 %copy-start.5 = (bf16[512,256]{1,0:T(8,128)(2,1)S(1)}, bf16[512,256]{1,0:T(8,128)(2,1)}, u32[]{:S(2)}) copy-start(bf16[512,256]{1,0:T(8,128)(2,1)} %constant.132) | copy-start | bytes 786436
  19.7 1.0 %copy-start.3 = (bf16[512,512]{1,0:T(8,128)(2,1)S(1)}, bf16[512,512]{1,0:T(8,128)(2,1)}, u32[]{:S(2)}) copy-start(bf16[512,512]{1,0:T(8,128)(2,1)} %param.16) | copy-start | bytes 1572868
  19.7 1.3 %copy-start.6 = (bf16[32,24,512]{2,1,0:T(8,128)(2,1)S(1)}, bf16[32,24,512]{2,1,0:T(8,128)(2,1)}, u32[]{:S(2)}) copy-start(bf16[32,24,512]{2,1,0:T(8,128)(2,1)} %param.10) | copy-start | bytes 2359300
  25.5 1.6 %collective-permute-start.4 = (bf16[138,512]{1,0:T(8,128)(2,1)S(1)}, bf16[138,512]{1,0:T(8,128)(2,1)S(1)}, u32[]{:S(2)}, u32[]{:S(2)}) collective-permute-start(bf16[138,512]{1,0:T(8,128)(2,1)S(1)} %get-tuple-element.10), channel_id=1, source_target_pairs={{0,1},{1,0},{2,3},{3,2},{4,5},{5,4},{6,7},{7,6},{8,9},{9,8},{10,11... | collective-permute-start | bytes 423944 | tf_op jit(solution)/shard_map/ppermute | solution.py:160
  27.2 4.7 %collective-permute-start.5 = (bf16[69,512]{1,0:T(8,128)(2,1)S(1)}, bf16[69,512]{1,0:T(8,128)(2,1)S(1)}, u32[]{:S(2)}, u32[]{:S(2)}) collective-permute-start(bf16[69,512]{1,0:T(8,128)(2,1)S(1)} %select_convert_fusion.3), channel_id=1, source_target_pairs={{0,2},{1,3},{2,0},{3,1},{4,6},{5,7},{6,4},{7,5},{8,10},{9,11},{10,... | collective-permute-start | bytes 211976 | tf_op jit(solution)/shard_map/ppermute | solution.py:160
  31.9 4.4 %collective-permute-start.6 = (bf16[69,512]{1,0:T(8,128)(2,1)S(1)}, bf16[69,512]{1,0:T(8,128)(2,1)S(1)}, u32[]{:S(2)}, u32[]{:S(2)}) collective-permute-start(bf16[69,512]{1,0:T(8,128)(2,1)S(1)} %convert_add_fusion.2), channel_id=1, source_target_pairs={{0,4},{1,5},{2,6},{3,7},{4,0},{5,1},{6,2},{7,3},{8,12},{9,13},{10,... | collective-permute-start | bytes 211976 | tf_op jit(solution)/shard_map/ppermute | solution.py:168
  33.9 5.4 %collective-permute-start.10 = (bf16[138,512]{1,0:T(8,128)(2,1)S(1)}, bf16[138,512]{1,0:T(8,128)(2,1)S(1)}, u32[]{:S(2)}, u32[]{:S(2)}) collective-permute-start(bf16[138,512]{1,0:T(8,128)(2,1)S(1)} %select_convert_fusion), channel_id=1, source_target_pairs={{0,1},{1,0},{2,3},{3,2},{4,5},{5,4},{6,7},{7,6},{8,9},{9,8},{10,11... | collective-permute-start | bytes 423944 | tf_op jit(solution)/shard_map/ppermute | solution.py:160
  36.4 5.3 %collective-permute-start.7 = (bf16[69,512]{1,0:T(8,128)(2,1)S(1)}, bf16[69,512]{1,0:T(8,128)(2,1)S(1)}, u32[]{:S(2)}, u32[]{:S(2)}) collective-permute-start(bf16[69,512]{1,0:T(8,128)(2,1)S(1)} %add_convert_fusion.9), channel_id=1, source_target_pairs={{0,8},{1,9},{2,10},{3,11},{4,12},{5,13},{6,14},{7,15},{8,0},{9,1},... | collective-permute-start | bytes 211976 | tf_op jit(solution)/shard_map/ppermute | solution.py:168
  39.4 4.4 %collective-permute-start.11 = (bf16[69,512]{1,0:T(8,128)(2,1)S(1)}, bf16[69,512]{1,0:T(8,128)(2,1)S(1)}, u32[]{:S(2)}, u32[]{:S(2)}) collective-permute-start(bf16[69,512]{1,0:T(8,128)(2,1)S(1)} %select_convert_fusion.2), channel_id=1, source_target_pairs={{0,2},{1,3},{2,0},{3,1},{4,6},{5,7},{6,4},{7,5},{8,10},{9,11},{10,... | collective-permute-start | bytes 211976 | tf_op jit(solution)/shard_map/ppermute | solution.py:160
  41.7 4.4 %collective-permute-start.8 = (bf16[69,512]{1,0:T(8,128)(2,1)S(1)}, bf16[69,512]{1,0:T(8,128)(2,1)S(1)}, u32[]{:S(2)}, u32[]{:S(2)}) collective-permute-start(bf16[69,512]{1,0:T(8,128)(2,1)S(1)} %add_convert_fusion.8), channel_id=1, source_target_pairs={{0,2},{1,3},{2,0},{3,1},{4,6},{5,7},{6,4},{7,5},{8,10},{9,11},{10,... | collective-permute-start | bytes 211976 | tf_op jit(solution)/shard_map/ppermute | solution.py:173
  43.8 4.4 %collective-permute-start.12 = (bf16[69,512]{1,0:T(8,128)(2,1)S(1)}, bf16[69,512]{1,0:T(8,128)(2,1)S(1)}, u32[]{:S(2)}, u32[]{:S(2)}) collective-permute-start(bf16[69,512]{1,0:T(8,128)(2,1)S(1)} %add_convert_fusion.7), channel_id=1, source_target_pairs={{0,4},{1,5},{2,6},{3,7},{4,0},{5,1},{6,2},{7,3},{8,12},{9,13},{10,... | collective-permute-start | bytes 211976 | tf_op jit(solution)/shard_map/ppermute | solution.py:168
  46.2 4.7 %collective-permute-start.9 = (bf16[138,512]{1,0:T(8,128)(2,1)S(1)}, bf16[138,512]{1,0:T(8,128)(2,1)S(1)}, u32[]{:S(2)}, u32[]{:S(2)}) collective-permute-start(bf16[138,512]{1,0:T(8,128)(2,1)S(1)} %maximum_select_fusion.2), channel_id=1, source_target_pairs={{0,1},{1,0},{2,3},{3,2},{4,5},{5,4},{6,7},{7,6},{8,9},{9,8},{10,11... | collective-permute-start | bytes 423944 | tf_op jit(solution)/shard_map/ppermute | solution.py:173
  48.3 5.7 %collective-permute-start.13 = (bf16[69,512]{1,0:T(8,128)(2,1)S(1)}, bf16[69,512]{1,0:T(8,128)(2,1)S(1)}, u32[]{:S(2)}, u32[]{:S(2)}) collective-permute-start(bf16[69,512]{1,0:T(8,128)(2,1)S(1)} %add_convert_fusion.6), channel_id=1, source_target_pairs={{0,8},{1,9},{2,10},{3,11},{4,12},{5,13},{6,14},{7,15},{8,0},{9,1},... | collective-permute-start | bytes 211976 | tf_op jit(solution)/shard_map/ppermute | solution.py:168
  54.0 4.4 %collective-permute-start.14 = (bf16[69,512]{1,0:T(8,128)(2,1)S(1)}, bf16[69,512]{1,0:T(8,128)(2,1)S(1)}, u32[]{:S(2)}, u32[]{:S(2)}) collective-permute-start(bf16[69,512]{1,0:T(8,128)(2,1)S(1)} %add_convert_fusion.5), channel_id=1, source_target_pairs={{0,2},{1,3},{2,0},{3,1},{4,6},{5,7},{6,4},{7,5},{8,10},{9,11},{10,... | collective-permute-start | bytes 211976 | tf_op jit(solution)/shard_map/ppermute | solution.py:173
  58.5 1.4 %collective-permute-start.15 = (bf16[138,512]{1,0:T(8,128)(2,1)S(1)}, bf16[138,512]{1,0:T(8,128)(2,1)S(1)}, u32[]{:S(2)}, u32[]{:S(2)}) collective-permute-start(bf16[138,512]{1,0:T(8,128)(2,1)S(1)} %maximum_select_fusion.3), channel_id=1, source_target_pairs={{0,1},{1,0},{2,3},{3,2},{4,5},{5,4},{6,7},{7,6},{8,9},{9,8},{10,11... | collective-permute-start | bytes 423944 | tf_op jit(solution)/shard_map/ppermute | solution.py:173
